TPU v7x, 512 devices: a whole 4x8x8 slice. The times are simulated.
512 devices in a mesh: section: 4 (over z_hi, core), seq: 32 (over x, y), head: 4 (over z_lo).
Axes of the slice: x: 4, y: 8, z: 8 (z_hi: 2, z_lo: 4; z = z_hi * 4 + z_lo), core: 2. Of those that a mesh axis runs over, the one named last changes fastest.
Arguments:
- query_heads: bfloat16 [4, 6144, 3072], P('section', 'seq', 'head'), may hold values from -6 to 6
- key_heads: bfloat16 [4, 6144, 3072], P('section', 'seq', 'head'), may hold values from -6 to 6
- value_heads: bfloat16 [4, 6144, 3072], P('section', 'seq', 'head'), may hold values from -6 to 6
- stream: bfloat16 [4, 6144, 3072], P('section', 'seq', 'head'), may hold values from -1.5 to 1.5
- out_weight: bfloat16 [4, 3072, 3072], P('section', 'head', 'seq'), may hold values from -0.109375 to 0.109375
- gate_scale: float32 [4, 3072], P('section', 'head'), may hold values from 0.5 to 1.5
- windows: int32 [16, 27], replicated, may hold values from -1 to 15, as said below
Outputs:
- handed: bfloat16 [4, 6144, 3072], P('section', 'seq', 'head')
Inputs may be any that keep to these rules, and one draw needn't show every extreme that they name: `windows`: row t lists, in an order drawn for each row, tile t + dt for every dt in -1, 0, 1 with 0 <= t + dt < 16 and tile t + dt in the same clip as t, and -1 in all its other slots; clips are runs of whole consecutive temporal tiles.
All inputs are finite; a program needn't handle non-finite values.
Results may differ from a plain program's by a relative error of at most 0.012.
Values may be sent and summed in bfloat16 or wider, within the bound.
No kernel may reach another device: no remote copies, remote signals or barrier semaphores. Data moves between devices by JAX's collectives and lax.ppermute only.
A program may use at most 64 MiB of HBM per device.

v0:
```python
from functools import partial
import math

import jax
import jax.numpy as jnp
from jax import lax
from jax.sharding import PartitionSpec as P

HD = 128
SPATIAL = 1


def shifted(block, axis, distance):
    devices = range(lax.axis_size(axis))
    route = [(i - distance, i) for i in devices if i - distance in devices]
    return lax.ppermute(block, axis, route)


def from_behind(value, axis, steps):
    count = lax.axis_size(axis)
    pairs = [(source, (source + steps) % count) for source in range(count)]
    return lax.ppermute(value, axis, pairs)


def split_heads(slab, head_count):
    return slab.reshape(slab.shape[0], head_count, slab.shape[1] // head_count)


def tile_maxima(key_slab, head_count, spatial_count):
    parts = split_heads(key_slab, head_count).astype(jnp.float32)
    lengths = jnp.sqrt(jnp.sum(parts * parts, axis=2))
    return jnp.max(lengths.reshape(spatial_count, -1, head_count), axis=1)


def slab_keep(nearby, slab_tile, in_range, spatial_count, temporal_count):
    first = jnp.clip(slab_tile, 0, temporal_count - 1) * spatial_count
    return lax.dynamic_slice_in_dim(nearby, first, spatial_count, 1) & in_range


def attend(
    running,
    slab_entry,
    keep,
    query_parts,
    row_bound,
    head_count,
    spatial_count,
    tile_rows,
    score_scale,
):
    weighted, summed = running
    row_count = query_parts.shape[0]
    slab_keys = split_heads(slab_entry[0], head_count)
    slab_values = split_heads(slab_entry[1], head_count)
    scores = (
        jnp.einsum("qhd,khd->hqk", query_parts, slab_keys, preferred_element_type=jnp.float32)
        * score_scale
    )
    row_keep = jnp.broadcast_to(
        keep[:, None, :, None], (spatial_count, tile_rows, spatial_count, tile_rows)
    )
    row_keep = row_keep.reshape(row_count, row_count)
    weights = jnp.where(row_keep[None], jnp.exp(scores - row_bound.T[:, :, None]), 0.0)
    summed = summed + jnp.sum(weights, axis=2)
    weighted = weighted + jnp.einsum(
        "hqk,khd->qhd",
        weights.astype(jnp.bfloat16),
        slab_values,
        preferred_element_type=jnp.float32,
    )
    return (weighted, summed)


def on_device(query_heads, key_heads, value_heads, stream, out_weight, gate_scale, windows):
    queries = query_heads[0]
    own_keys = key_heads[0]
    own_values = value_heads[0]
    row_count, feature_count = queries.shape
    head_count = feature_count // HD
    spatial_count = SPATIAL
    tile_rows = row_count // spatial_count
    tile_count = windows.shape[0]
    temporal_count = tile_count // spatial_count
    score_scale = 1.0 / math.sqrt(HD)
    seq_count = lax.axis_size("seq")
    position = lax.axis_index("seq")
    temporal = position // 2
    allowed = jnp.any(
        windows[:, :, None] == jnp.arange(tile_count, dtype=jnp.int32)[None, None, :], axis=1
    )
    nearby = lax.dynamic_slice_in_dim(allowed, temporal * spatial_count, spatial_count, 0)
    always = jnp.array(True)
    slabs = [(own_keys, own_values, temporal, always)]
    reach = min(3, seq_count - 1)
    offsets = list(range(1, reach + 1)) + list(range(-reach, 0))
    for offset in offsets:
        moved_keys, moved_values = shifted((own_keys, own_values), "seq", offset)
        source = position - offset
        in_range = (source >= 0) & (source < seq_count)
        slabs.append((moved_keys, moved_values, source // 2, in_range))
    keeps = [
        slab_keep(nearby, slab_entry[2], slab_entry[3], spatial_count, temporal_count)
        for slab_entry in slabs
    ]
    bound_tiles = jnp.zeros((spatial_count, head_count), jnp.float32)
    for slab_entry, keep in zip(slabs, keeps):
        maxima = tile_maxima(slab_entry[0], head_count, spatial_count)
        candidate = jnp.where(keep[:, :, None], maxima[None, :, :], 0.0)
        bound_tiles = jnp.maximum(bound_tiles, jnp.max(candidate, axis=1))
    query_parts = split_heads(queries, head_count)
    query_float = query_parts.astype(jnp.float32)
    query_lengths = jnp.sqrt(jnp.sum(query_float * query_float, axis=2))
    row_bound = query_lengths * jnp.repeat(bound_tiles, tile_rows, axis=0) * score_scale
    running = (
        jnp.zeros((row_count, head_count, HD), jnp.float32),
        jnp.zeros((head_count, row_count), jnp.float32),
    )
    for slab_entry, keep in zip(slabs, keeps):
        step_fn = partial(
            attend,
            slab_entry=slab_entry,
            keep=keep,
            query_parts=query_parts,
            row_bound=row_bound,
            head_count=head_count,
            spatial_count=spatial_count,
            tile_rows=tile_rows,
            score_scale=score_scale,
        )
        running = step_fn(running)
    weighted, summed = running
    attended = (
        (weighted / summed.T[:, :, None]).astype(jnp.bfloat16).reshape(row_count, feature_count)
    )
    head_terms = jnp.dot(
        attended,
        lax.all_gather(out_weight[0], "seq", axis=1, tiled=True),
        preferred_element_type=jnp.float32,
    )
    mixed = lax.psum_scatter(
        head_terms.astype(jnp.bfloat16), "head", scatter_dimension=1, tiled=True
    ).astype(jnp.float32)
    updated = (stream[0].astype(jnp.float32) + gate_scale[0][None, :] * mixed).astype(jnp.bfloat16)
    handed = from_behind(updated, "section", 1)
    return handed[None]


def solution(mesh):
    in_specs = (
        P("section", "seq", "head"),
        P("section", "seq", "head"),
        P("section", "seq", "head"),
        P("section", "seq", "head"),
        P("section", "head", "seq"),
        P("section", "head"),
        P(),
    )
    out_specs = P("section", "seq", "head")
    return jax.shard_map(
        on_device, mesh=mesh, in_specs=in_specs, out_specs=out_specs, check_vma=False
    )
```

profile of v0, /device:TPU:6, one launch (start us, length us, event | category | flops | bytes accessed | tf_op | source)
XLA Modules:
  0.0 199.7 jit_solution(8086827323401507072)
XLA Ops:
  7.3 6.4 %collective-permute-start.4 = (bf16[192,768]{1,0:T(8,128)(2,1)}, bf16[192,768]{1,0:T(8,128)(2,1)S(1)}, u32[]{:S(2)}, u32[]{:S(2)}) collective-permute-start(bf16[192,768]{1,0:T(8,128)(2,1)} %bitcast.145), channel_id=1, source_target_pairs={{8,0},{12,4},{16,8},{20,12},{24,16},{28,20},{32,24},{36,28},{40,32... | collective-permute-start | bytes 884744 | tf_op jit(solution)/shard_map/ppermute | solution.py:16
  13.7 3.3 %collective-permute-start.5 = (bf16[192,768]{1,0:T(8,128)(2,1)}, bf16[192,768]{1,0:T(8,128)(2,1)S(1)}, u32[]{:S(2)}, u32[]{:S(2)}) collective-permute-start(bf16[192,768]{1,0:T(8,128)(2,1)} %bitcast.146), channel_id=1, source_target_pairs={{4,0},{8,4},{12,8},{16,12},{20,16},{24,20},{28,24},{32,28},{36,32}... | collective-permute-start | bytes 884744 | tf_op jit(solution)/shard_map/ppermute | solution.py:16
  17.0 1.9 collective-permute-start.2
  18.9 7.8 %collective-permute-start.3 = (bf16[192,768]{1,0:T(8,128)(2,1)}, bf16[192,768]{1,0:T(8,128)(2,1)}, u32[]{:S(2)}, u32[]{:S(2)}) collective-permute-start(bf16[192,768]{1,0:T(8,128)(2,1)} %bitcast.148), channel_id=1, source_target_pairs={{12,0},{16,4},{20,8},{24,12},{28,16},{32,20},{36,24},{40,28},{44,3... | collective-permute-start | bytes 884744 | tf_op jit(solution)/shard_map/ppermute | solution.py:16
  26.8 2.6 %collective-permute-start = (bf16[192,768]{1,0:T(8,128)(2,1)}, bf16[192,768]{1,0:T(8,128)(2,1)S(1)}, u32[]{:S(2)}, u32[]{:S(2)}) collective-permute-start(bf16[192,768]{1,0:T(8,128)(2,1)} %bitcast.149), channel_id=1, source_target_pairs={{0,4},{4,8},{8,12},{12,16},{16,20},{20,24},{24,28},{28,32},{32,36}... | collective-permute-start | bytes 884744 | tf_op jit(solution)/shard_map/ppermute | solution.py:16
  29.4 1.3 reshape_squeeze.11
  30.7 1.4 reshape_squeeze.10
  38.3 2.0 %collective-permute-start.1 = (bf16[192,768]{1,0:T(8,128)(2,1)S(1)}, bf16[192,768]{1,0:T(8,128)(2,1)}, u32[]{:S(2)}, u32[]{:S(2)}) collective-permute-start(bf16[192,768]{1,0:T(8,128)(2,1)S(1)} %bitcast.150), channel_id=1, source_target_pairs={{0,8},{4,12},{8,16},{12,20},{16,24},{20,28},{24,32},{28,36},{32,40... | collective-permute-start | bytes 884744 | tf_op jit(solution)/shard_map/ppermute | solution.py:16
  41.0 2.5 %collective-permute-start.6 = (bf16[192,768]{1,0:T(8,128)(2,1)S(1)}, bf16[192,768]{1,0:T(8,128)(2,1)}, u32[]{:S(2)}, u32[]{:S(2)}) collective-permute-start(bf16[192,768]{1,0:T(8,128)(2,1)S(1)} %bitcast.151), channel_id=1, source_target_pairs={{0,4},{4,8},{8,12},{12,16},{16,20},{20,24},{24,28},{28,32},{32,36}... | collective-permute-start | bytes 884744 | tf_op jit(solution)/shard_map/ppermute | solution.py:16
  44.1 6.9 %collective-permute-start.10 = (bf16[192,768]{1,0:T(8,128)(2,1)S(1)}, bf16[192,768]{1,0:T(8,128)(2,1)}, u32[]{:S(2)}, u32[]{:S(2)}) collective-permute-start(bf16[192,768]{1,0:T(8,128)(2,1)S(1)} %bitcast.152), channel_id=1, source_target_pairs={{8,0},{12,4},{16,8},{20,12},{24,16},{28,20},{32,24},{36,28},{40,32... | collective-permute-start | bytes 884744 | tf_op jit(solution)/shard_map/ppermute | solution.py:16
  51.9 4.7 %collective-permute-done.3 = bf16[192,768]{1,0:T(8,128)(2,1)} collective-permute-done((bf16[192,768]{1,0:T(8,128)(2,1)}, bf16[192,768]{1,0:T(8,128)(2,1)}, u32[]{:S(2)}, u32[]{:S(2)}) %collective-permute-start.3) | collective-permute-done | bytes 294944 | tf_op jit(solution)/shard_map/ppermute | solution.py:16
  56.7 7.0 %collective-permute-start.9 = (bf16[192,768]{1,0:T(8,128)(2,1)S(1)}, bf16[192,768]{1,0:T(8,128)(2,1)}, u32[]{:S(2)}, u32[]{:S(2)}) collective-permute-start(bf16[192,768]{1,0:T(8,128)(2,1)S(1)} %bitcast.153), channel_id=1, source_target_pairs={{12,0},{16,4},{20,8},{24,12},{28,16},{32,20},{36,24},{40,28},{44,3... | collective-permute-start | bytes 884744 | tf_op jit(solution)/shard_map/ppermute | solution.py:16
  63.6 1.3 reshape.183
  65.3 3.2 %collective-permute-start.8 = (bf16[192,768]{1,0:T(8,128)(2,1)S(1)}, bf16[192,768]{1,0:T(8,128)(2,1)S(1)}, u32[]{:S(2)}, u32[]{:S(2)}) collective-permute-start(bf16[192,768]{1,0:T(8,128)(2,1)S(1)} %bitcast.154), channel_id=1, source_target_pairs={{0,12},{4,16},{8,20},{12,24},{16,28},{20,32},{24,36},{28,40},{32,4... | collective-permute-start | bytes 884744 | tf_op jit(solution)/shard_map/ppermute | solution.py:16
  69.3 4.0 %collective-permute-start.11 = (bf16[192,768]{1,0:T(8,128)(2,1)S(1)}, bf16[192,768]{1,0:T(8,128)(2,1)}, u32[]{:S(2)}, u32[]{:S(2)}) collective-permute-start(bf16[192,768]{1,0:T(8,128)(2,1)S(1)} %bitcast.155), channel_id=1, source_target_pairs={{4,0},{8,4},{12,8},{16,12},{20,16},{24,20},{28,24},{32,28},{36,32}... | collective-permute-start | bytes 884744 | tf_op jit(solution)/shard_map/ppermute | solution.py:16
  73.3 1.3 reshape.181
  76.2 1.2 fusion.96
  78.2 1.4 fusion.93
  80.2 3.6 %collective-permute-start.7 = (bf16[192,768]{1,0:T(8,128)(2,1)S(1)}, bf16[192,768]{1,0:T(8,128)(2,1)S(1)}, u32[]{:S(2)}, u32[]{:S(2)}) collective-permute-start(bf16[192,768]{1,0:T(8,128)(2,1)S(1)} %bitcast.156), channel_id=1, source_target_pairs={{0,8},{4,12},{8,16},{12,20},{16,24},{20,28},{24,32},{28,36},{32,40... | collective-permute-start | bytes 884744 | tf_op jit(solution)/shard_map/ppermute | solution.py:16
  83.8 1.4 fusion.37
  85.1 3.5 %collective-permute-done.9 = bf16[192,768]{1,0:T(8,128)(2,1)} collective-permute-done((bf16[192,768]{1,0:T(8,128)(2,1)S(1)}, bf16[192,768]{1,0:T(8,128)(2,1)}, u32[]{:S(2)}, u32[]{:S(2)}) %collective-permute-start.9) | collective-permute-done | bytes 294944 | tf_op jit(solution)/shard_map/ppermute | solution.py:16
  88.7 1.4 fusion.39
  90.0 1.4 fusion.95
  92.4 3.1 %collective-permute-done.11 = bf16[192,768]{1,0:T(8,128)(2,1)} collective-permute-done((bf16[192,768]{1,0:T(8,128)(2,1)S(1)}, bf16[192,768]{1,0:T(8,128)(2,1)}, u32[]{:S(2)}, u32[]{:S(2)}) %collective-permute-start.11) | collective-permute-done | bytes 294944 | tf_op jit(solution)/shard_map/ppermute | solution.py:16
  95.5 1.4 fusion.35
  97.3 1.4 convolution_add_fusion.1
  98.7 6.4 %collective-permute-done.7 = bf16[192,768]{1,0:T(8,128)(2,1)S(1)} collective-permute-done((bf16[192,768]{1,0:T(8,128)(2,1)S(1)}, bf16[192,768]{1,0:T(8,128)(2,1)S(1)}, u32[]{:S(2)}, u32[]{:S(2)}) %collective-permute-start.7) | collective-permute-done | bytes 294944 | tf_op jit(solution)/shard_map/ppermute | solution.py:16
  105.6 27.5 %all-gather.3.cloned.1.call-done = bf16[1,768,3072]{1,2,0:T(8,128)(2,1)} async-done(((bf16[1,768,96]{1,2,0:T(8,128)(2,1)}), bf16[1,768,3072]{1,2,0:T(8,128)(2,1)}) %all-gather.3.cloned.1.call-update) | async-done | bytes 4718608 | tf_op jit(solution)/shard_map/all_gather | solution.py:137
  133.1 5.1 %fusion.2 = bf16[192,3072]{1,0:T(8,128)(2,1)} fusion(bf16[1,768,3072]{1,2,0:T(8,128)(2,1)} %all-gather.3.cloned.1.call-done, bf16[6,24,8,128]{3,2,1,0:T(8,128)(2,1)S(1)} %fusion.33), kind=kOutput, calls=%fused_computation.2 | convolution fusion | flops 906559488 | bytes 6193152 | tf_op jit(solution)/shard_map/dot_general | solution.py:135
  138.9 37.4 %reduce-scatter.2.cloned.1.call-done = bf16[192,768]{1,0:T(8,128)(2,1)} async-done(((bf16[192,3072]{1,0:T(8,128)(2,1)}), bf16[192,768]{1,0:T(8,128)(2,1)}) %reduce-scatter.2.cloned.1.call-update) | async-done | bytes 294928 | tf_op jit(solution)/shard_map/reduce_scatter | solution.py:140
  177.3 1.9 collective-permute-start.12
  179.3 12.9 %collective-permute-done.12 = bf16[192,768]{1,0:T(8,128)(2,1)S(1)} collective-permute-done((bf16[192,768]{1,0:T(8,128)(2,1)S(1)}, bf16[192,768]{1,0:T(8,128)(2,1)S(1)}, u32[]{:S(2)}, u32[]{:S(2)}) %collective-permute-start.12) | collective-permute-done | bytes 294944 | tf_op jit(solution)/shard_map/ppermute | solution.py:22
  (66 shorter events, 13.4 us)
Async XLA Ops:
  6.5 126.6 %all-gather.3.cloned.1.call-start = ((), (), s32[]{:S(2)}) async-start(), calls=%async_computation.2 | async-start | bytes 4866048 | tf_op jit(solution)/shard_map/all_gather | solution.py:137
  7.3 169.0 %reduce-scatter.2.cloned.1.call-start = ((), (), s32[]{:S(2)}) async-start(), calls=%async_computation.1 | async-start | bytes 1474560 | tf_op jit(solution)/shard_map/reduce_scatter | solution.py:140
  7.3 25.4 %copy-start.5 = (s32[16,27]{1,0:T(8,128)S(1)}, s32[16,27]{1,0:T(8,128)}, u32[]{:S(2)}) copy-start(s32[16,27]{1,0:T(8,128)} %param.13) | copy-start | bytes 5188
  7.3 31.0 %collective-permute-start.4 = (bf16[192,768]{1,0:T(8,128)(2,1)}, bf16[192,768]{1,0:T(8,128)(2,1)S(1)}, u32[]{:S(2)}, u32[]{:S(2)}) collective-permute-start(bf16[192,768]{1,0:T(8,128)(2,1)} %bitcast.145), channel_id=1, source_target_pairs={{8,0},{12,4},{16,8},{20,12},{24,16},{28,20},{32,24},{36,28},{40,32... | collective-permute-start | bytes 884744 | tf_op jit(solution)/shard_map/ppermute | solution.py:16
  13.7 27.2 %collective-permute-start.5 = (bf16[192,768]{1,0:T(8,128)(2,1)}, bf16[192,768]{1,0:T(8,128)(2,1)S(1)}, u32[]{:S(2)}, u32[]{:S(2)}) collective-permute-start(bf16[192,768]{1,0:T(8,128)(2,1)} %bitcast.146), channel_id=1, source_target_pairs={{4,0},{8,4},{12,8},{16,12},{20,16},{24,20},{28,24},{32,28},{36,32}... | collective-permute-start | bytes 884744 | tf_op jit(solution)/shard_map/ppermute | solution.py:16
  17.0 27.1 %collective-permute-start.2 = (bf16[192,768]{1,0:T(8,128)(2,1)}, bf16[192,768]{1,0:T(8,128)(2,1)S(1)}, u32[]{:S(2)}, u32[]{:S(2)}) collective-permute-start(bf16[192,768]{1,0:T(8,128)(2,1)} %bitcast.147), channel_id=1, source_target_pairs={{0,12},{4,16},{8,20},{12,24},{16,28},{20,32},{24,36},{28,40},{32,4... | collective-permute-start | bytes 884744 | tf_op jit(solution)/shard_map/ppermute | solution.py:16
  18.9 37.7 %collective-permute-start.3 = (bf16[192,768]{1,0:T(8,128)(2,1)}, bf16[192,768]{1,0:T(8,128)(2,1)}, u32[]{:S(2)}, u32[]{:S(2)}) collective-permute-start(bf16[192,768]{1,0:T(8,128)(2,1)} %bitcast.148), channel_id=1, source_target_pairs={{12,0},{16,4},{20,8},{24,12},{28,16},{32,20},{36,24},{40,28},{44,3... | collective-permute-start | bytes 884744 | tf_op jit(solution)/shard_map/ppermute | solution.py:16
  26.8 38.5 %collective-permute-start = (bf16[192,768]{1,0:T(8,128)(2,1)}, bf16[192,768]{1,0:T(8,128)(2,1)S(1)}, u32[]{:S(2)}, u32[]{:S(2)}) collective-permute-start(bf16[192,768]{1,0:T(8,128)(2,1)} %bitcast.149), channel_id=1, source_target_pairs={{0,4},{4,8},{8,12},{12,16},{16,20},{20,24},{24,28},{28,32},{32,36}... | collective-permute-start | bytes 884744 | tf_op jit(solution)/shard_map/ppermute | solution.py:16
  30.7 2.8 %copy-start.2 = (bf16[1,192,768]{2,1,0:T(8,128)(2,1)S(1)}, bf16[1,192,768]{2,1,0:T(8,128)(2,1)}, u32[]{:S(2)}) copy-start(bf16[1,192,768]{2,1,0:T(8,128)(2,1)} %param.9) | copy-start | bytes 884740
  32.1 6.2 %copy-start.1 = (bf16[1,192,768]{2,1,0:T(8,128)(2,1)S(1)}, bf16[1,192,768]{2,1,0:T(8,128)(2,1)}, u32[]{:S(2)}) copy-start(bf16[1,192,768]{2,1,0:T(8,128)(2,1)} %param.8) | copy-start | bytes 884740
  38.3 2.7 %copy-start.3 = (bf16[192,768]{1,0:T(8,128)(2,1)}, bf16[192,768]{1,0:T(8,128)(2,1)S(1)}, u32[]{:S(2)}) copy-start(bf16[192,768]{1,0:T(8,128)(2,1)S(1)} %collective-permute-done.4) | copy-start | bytes 884740
  38.3 31.0 %collective-permute-start.1 = (bf16[192,768]{1,0:T(8,128)(2,1)S(1)}, bf16[192,768]{1,0:T(8,128)(2,1)}, u32[]{:S(2)}, u32[]{:S(2)}) collective-permute-start(bf16[192,768]{1,0:T(8,128)(2,1)S(1)} %bitcast.150), channel_id=1, source_target_pairs={{0,8},{4,12},{8,16},{12,20},{16,24},{20,28},{24,32},{28,36},{32,40... | collective-permute-start | bytes 884744 | tf_op jit(solution)/shard_map/ppermute | solution.py:16
  41.0 56.3 %collective-permute-start.6 = (bf16[192,768]{1,0:T(8,128)(2,1)S(1)}, bf16[192,768]{1,0:T(8,128)(2,1)}, u32[]{:S(2)}, u32[]{:S(2)}) collective-permute-start(bf16[192,768]{1,0:T(8,128)(2,1)S(1)} %bitcast.151), channel_id=1, source_target_pairs={{0,4},{4,8},{8,12},{12,16},{16,20},{20,24},{24,28},{28,32},{32,36}... | collective-permute-start | bytes 884744 | tf_op jit(solution)/shard_map/ppermute | solution.py:16
  44.1 36.1 %collective-permute-start.10 = (bf16[192,768]{1,0:T(8,128)(2,1)S(1)}, bf16[192,768]{1,0:T(8,128)(2,1)}, u32[]{:S(2)}, u32[]{:S(2)}) collective-permute-start(bf16[192,768]{1,0:T(8,128)(2,1)S(1)} %bitcast.152), channel_id=1, source_target_pairs={{8,0},{12,4},{16,8},{20,12},{24,16},{28,20},{32,24},{36,28},{40,32... | collective-permute-start | bytes 884744 | tf_op jit(solution)/shard_map/ppermute | solution.py:16
  56.7 32.0 %collective-permute-start.9 = (bf16[192,768]{1,0:T(8,128)(2,1)S(1)}, bf16[192,768]{1,0:T(8,128)(2,1)}, u32[]{:S(2)}, u32[]{:S(2)}) collective-permute-start(bf16[192,768]{1,0:T(8,128)(2,1)S(1)} %bitcast.153), channel_id=1, source_target_pairs={{12,0},{16,4},{20,8},{24,12},{28,16},{32,20},{36,24},{40,28},{44,3... | collective-permute-start | bytes 884744 | tf_op jit(solution)/shard_map/ppermute | solution.py:16
  65.3 26.7 %collective-permute-start.8 = (bf16[192,768]{1,0:T(8,128)(2,1)S(1)}, bf16[192,768]{1,0:T(8,128)(2,1)S(1)}, u32[]{:S(2)}, u32[]{:S(2)}) collective-permute-start(bf16[192,768]{1,0:T(8,128)(2,1)S(1)} %bitcast.154), channel_id=1, source_target_pairs={{0,12},{4,16},{8,20},{12,24},{16,28},{20,32},{24,36},{28,40},{32,4... | collective-permute-start | bytes 884744 | tf_op jit(solution)/shard_map/ppermute | solution.py:16
  69.3 26.2 %collective-permute-start.11 = (bf16[192,768]{1,0:T(8,128)(2,1)S(1)}, bf16[192,768]{1,0:T(8,128)(2,1)}, u32[]{:S(2)}, u32[]{:S(2)}) collective-permute-start(bf16[192,768]{1,0:T(8,128)(2,1)S(1)} %bitcast.155), channel_id=1, source_target_pairs={{4,0},{8,4},{12,8},{16,12},{20,16},{24,20},{28,24},{32,28},{36,32}... | collective-permute-start | bytes 884744 | tf_op jit(solution)/shard_map/ppermute | solution.py:16
  76.2 1.2 copy-start.4
  80.2 25.0 %collective-permute-start.7 = (bf16[192,768]{1,0:T(8,128)(2,1)S(1)}, bf16[192,768]{1,0:T(8,128)(2,1)S(1)}, u32[]{:S(2)}, u32[]{:S(2)}) collective-permute-start(bf16[192,768]{1,0:T(8,128)(2,1)S(1)} %bitcast.156), channel_id=1, source_target_pairs={{0,8},{4,12},{8,16},{12,20},{16,24},{20,28},{24,32},{28,36},{32,40... | collective-permute-start | bytes 884744 | tf_op jit(solution)/shard_map/ppermute | solution.py:16
  138.2 0.7 copy-start.6
  138.2 38.1 %copy-start = (bf16[1,192,768]{2,1,0:T(8,128)(2,1)S(1)}, bf16[1,192,768]{2,1,0:T(8,128)(2,1)}, u32[]{:S(2)}) copy-start(bf16[1,192,768]{2,1,0:T(8,128)(2,1)} %param.10) | copy-start | bytes 884740
  177.3 14.9 %collective-permute-start.12 = (bf16[192,768]{1,0:T(8,128)(2,1)S(1)}, bf16[192,768]{1,0:T(8,128)(2,1)S(1)}, u32[]{:S(2)}, u32[]{:S(2)}) collective-permute-start(bf16[192,768]{1,0:T(8,128)(2,1)S(1)} %fusion.34), channel_id=1, source_target_pairs={{0,128},{128,256},{256,384},{384,0},{1,129},{129,257},{257,385},{3... | collective-permute-start | bytes 884744 | tf_op jit(solution)/shard_map/ppermute | solution.py:22
Sparse Core Ops, SparseCore 0:
  10.5 122.5 all-gather.2
  138.3 37.9 reduce-scatter.1
where the time goes:
time: 201 us; the launch traced here: 200 us
  waiting for transfers between devices  96.3 us (48%)
  starting transfers between devices  53.2 us (26%)
  matrix products  17.7 us (9%)
  between operations  17.7 us (9%)
  local copies, waits for them, and re-layouts  9.78 us (5%)
  other arithmetic  4.97 us (2%)
    ppermute x12, starting transfers between devices, shifted(): return lax.ppermute(block, axis, route)  51.3 us
    reduce_scatter x1, waiting for transfers between devices, on_device(): lax.psum_scatter(head_terms.astype(jnp.bfloat16), 'head', scatter_dimensi...  37.4 us
    all_gather x1, waiting for transfers between devices, on_device(): lax.all_gather(out_weight[0], 'seq', axis=1, tiled=True)  27.5 us
    ppermute x12, waiting for transfers between devices, shifted(): return lax.ppermute(block, axis, route)  17.8 us
    ppermute x1, waiting for transfers between devices, from_behind(): return lax.ppermute(value, axis, pairs)  12.9 us
    dot_general x7, matrix products, attend(): jnp.einsum('hqk,khd->qhd', weights.astype(jnp.bfloat16), slab_values, pre...  6.69 us
    dot_general x7, matrix products, attend(): jnp.einsum('qhd,khd->hqk', query_parts, slab_keys, preferred_element_type...  5.97 us
    dot_general x1, matrix products, on_device(): jnp.dot(attended, lax.all_gather(out_weight[0], 'seq', axis=1, tiled=True...  5.06 us
  transfers between devices with their start and end apart: 15, of which 7 were waited for; matrix products, arithmetic and copies ran while one was open for 12% of the time, Pallas kernels for 0%

commit v1 on v0

--- a/solution.py
+++ b/solution.py
@@ -4,16 +4,37 @@
 import jax
 import jax.numpy as jnp
 from jax import lax
-from jax.sharding import PartitionSpec as P
+from jax.sharding import Mesh, PartitionSpec as P
 
 HD = 128
 SPATIAL = 1
 
 
-def shifted(block, axis, distance):
-    devices = range(lax.axis_size(axis))
-    route = [(i - distance, i) for i in devices if i - distance in devices]
+def shifted(block, axis, count, distance, wanted):
+    devices = range(count)
+    route = [(i - distance, i) for i in devices if i - distance in devices and wanted(i)]
     return lax.ppermute(block, axis, route)
+
+
+def needs(offset):
+    if offset == 3:
+        return lambda i: i % 2 == 1
+    if offset == -3:
+        return lambda i: i % 2 == 0
+    return lambda i: True
+
+
+def linear_pairs(sizes, mapping):
+    def flat(index):
+        value = 0
+        for part, size in zip(index, sizes):
+            value = value * size + part
+        return value
+
+    grid = [[]]
+    for size in sizes:
+        grid = [index + [part] for index in grid for part in range(size)]
+    return [(flat(index), flat(mapping(*index))) for index in grid]
 
 
 def from_behind(value, axis, steps):
@@ -82,8 +103,14 @@
     tile_count = windows.shape[0]
     temporal_count = tile_count // spatial_count
     score_scale = 1.0 / math.sqrt(HD)
-    seq_count = lax.axis_size("seq")
-    position = lax.axis_index("seq")
+    x_count = lax.axis_size("sx")
+    y_count = lax.axis_size("sy")
+    head_groups = lax.axis_size("head")
+    sections = lax.axis_size("section")
+    seq_count = x_count * y_count
+    x_index = lax.axis_index("sx")
+    y_index = lax.axis_index("sy")
+    position = x_index * y_count + y_index
     temporal = position // 2
     allowed = jnp.any(
         windows[:, :, None] == jnp.arange(tile_count, dtype=jnp.int32)[None, None, :], axis=1
@@ -94,7 +121,9 @@
     reach = min(3, seq_count - 1)
     offsets = list(range(1, reach + 1)) + list(range(-reach, 0))
     for offset in offsets:
-        moved_keys, moved_values = shifted((own_keys, own_values), "seq", offset)
+        moved_keys, moved_values = shifted(
+            (own_keys, own_values), ("sx", "sy"), seq_count, offset, needs(offset)
+        )
         source = position - offset
         in_range = (source >= 0) & (source < seq_count)
         slabs.append((moved_keys, moved_values, source // 2, in_range))
@@ -132,30 +161,41 @@
     attended = (
         (weighted / summed.T[:, :, None]).astype(jnp.bfloat16).reshape(row_count, feature_count)
     )
-    head_terms = jnp.dot(
-        attended,
-        lax.all_gather(out_weight[0], "seq", axis=1, tiled=True),
-        preferred_element_type=jnp.float32,
-    )
+    token_block = lax.all_gather(attended, "sx", axis=0, tiled=True)
+    weight_block = lax.all_gather(out_weight[0], "sy", axis=1, tiled=True)
+    group_term = jnp.dot(token_block, weight_block, preferred_element_type=jnp.float32)
     mixed = lax.psum_scatter(
-        head_terms.astype(jnp.bfloat16), "head", scatter_dimension=1, tiled=True
+        group_term.astype(jnp.bfloat16), "head", scatter_dimension=0, tiled=True
     ).astype(jnp.float32)
-    updated = (stream[0].astype(jnp.float32) + gate_scale[0][None, :] * mixed).astype(jnp.bfloat16)
-    handed = from_behind(updated, "section", 1)
+    swap = linear_pairs((x_count, head_groups), lambda a, b: (b, a))
+    stream_block = lax.ppermute(stream[0], ("sx", "head"), swap)
+    gate_block = lax.ppermute(gate_scale[0], ("sx", "head"), swap)
+    updated = (stream_block.astype(jnp.float32) + gate_block[None, :] * mixed).astype(jnp.bfloat16)
+    hand = linear_pairs(
+        (sections, x_count, head_groups), lambda s, a, b: ((s + 1) % sections, b, a)
+    )
+    handed = lax.ppermute(updated, ("section", "sx", "head"), hand)
     return handed[None]
 
 
 def solution(mesh):
+    sections, seq_count, head_count = mesh.devices.shape
+    x_count = 4 if seq_count % 4 == 0 else 1
+    split_mesh = Mesh(
+        mesh.devices.reshape(sections, x_count, seq_count // x_count, head_count),
+        ("section", "sx", "sy", "head"),
+    )
+    seq = ("sx", "sy")
     in_specs = (
-        P("section", "seq", "head"),
-        P("section", "seq", "head"),
-        P("section", "seq", "head"),
-        P("section", "seq", "head"),
-        P("section", "head", "seq"),
+        P("section", seq, "head"),
+        P("section", seq, "head"),
+        P("section", seq, "head"),
+        P("section", seq, "head"),
+        P("section", "head", seq),
         P("section", "head"),
         P(),
     )
-    out_specs = P("section", "seq", "head")
+    out_specs = P("section", seq, "head")
     return jax.shard_map(
-        on_device, mesh=mesh, in_specs=in_specs, out_specs=out_specs, check_vma=False
-    )
+        on_device, mesh=split_mesh, in_specs=in_specs, out_specs=out_specs, check_vma=False
+    )

time: 201 us -> 243 us (1.21)
  waiting for transfers between devices: 96.3 us -> 132 us
  starting transfers between devices: 53.2 us -> 60.4 us
    all_gather x1 -> x2, waiting for transfers between devices: 27.5 us -> 75.2 us  [the longest x1 45.2 us: on_device(): weight_block = lax.all_gather(out_weight[0], 'sy', axis=1, tiled=True)]
    reduce_scatter x1, waiting for transfers between devices: 37.4 us -> 26.5 us  [on_device(): lax.psum_scatter(group_term.astype(jnp.bfloat16), 'head', scatter_dimensi...]
    ppermute x1 -> x3, starting transfers between devices: 1.92 us -> 11.9 us  [the longest x1 5.69 us: on_device(): stream_block = lax.ppermute(stream[0], ('sx', 'head'), swap)]
    ppermute x12, waiting for transfers between devices: 17.8 us -> 8.34 us  [shifted(): return lax.ppermute(block, axis, route)]
    ppermute x1 -> x3, waiting for transfers between devices: 12.9 us -> 21.1 us  [the longest x1 15.5 us: on_device(): handed = lax.ppermute(updated, ('section', 'sx', 'head'), hand)]
    ppermute x12, starting transfers between devices: 51.3 us -> 48.5 us  [shifted(): return lax.ppermute(block, axis, route)]
  transfers between devices with their start and end apart: 15 -> 18, of which waited for: 7 -> 6; matrix products, arithmetic and copies ran while one was open for 12% -> 10% of each run, Pallas kernels for 0% -> 0%
where the time goes in v1:
time: 243 us; the launch traced here: 242 us
  waiting for transfers between devices  132 us (54%)
  starting transfers between devices  60.4 us (25%)
  between operations  17.5 us (7%)
  matrix products  16.3 us (7%)
  local copies, waits for them, and re-layouts  11.3 us (5%)
  other arithmetic  4.96 us (2%)
    ppermute x12, starting transfers between devices, shifted(): return lax.ppermute(block, axis, route)  48.5 us
    all_gather x1, waiting for transfers between devices, on_device(): weight_block = lax.all_gather(out_weight[0], 'sy', axis=1, tiled=True)  45.2 us
    all_gather x1, waiting for transfers between devices, on_device(): token_block = lax.all_gather(attended, 'sx', axis=0, tiled=True)  30.1 us
    reduce_scatter x1, waiting for transfers between devices, on_device(): lax.psum_scatter(group_term.astype(jnp.bfloat16), 'head', scatter_dimensi...  26.5 us
    ppermute x1, waiting for transfers between devices, on_device(): handed = lax.ppermute(updated, ('section', 'sx', 'head'), hand)  15.5 us
    ppermute x12, waiting for transfers between devices, shifted(): return lax.ppermute(block, axis, route)  8.34 us
    dot_general x7, matrix products, attend(): jnp.einsum('hqk,khd->qhd', weights.astype(jnp.bfloat16), slab_values, pre...  6.69 us
    dot_general x7, matrix products, attend(): jnp.einsum('qhd,khd->hqk', query_parts, slab_keys, preferred_element_type...  5.9 us
  transfers between devices with their start and end apart: 18, of which 6 were waited for; matrix products, arithmetic and copies ran while one was open for 10% of the time, Pallas kernels for 0%

profile of v1, /device:TPU:6, one launch (start us, length us, event | category | flops | bytes accessed | tf_op | source)
XLA Modules:
  0.0 242.4 jit_solution(3688263939341048570)
XLA Ops:
  6.5 5.8 %collective-permute-start.7 = (bf16[192,768]{1,0:T(8,128)(2,1)}, bf16[192,768]{1,0:T(8,128)(2,1)S(1)}, u32[]{:S(2)}, u32[]{:S(2)}) collective-permute-start(bf16[192,768]{1,0:T(8,128)(2,1)} %bitcast.143), channel_id=1, source_target_pairs={{4,0},{8,4},{12,8},{16,12},{20,16},{24,20},{28,24},{32,28},{36,32}... | collective-permute-start | bytes 884744 | tf_op jit(solution)/shard_map/ppermute | solution.py:16
  12.3 4.0 %collective-permute-start.6 = (bf16[192,768]{1,0:T(8,128)(2,1)}, bf16[192,768]{1,0:T(8,128)(2,1)}, u32[]{:S(2)}, u32[]{:S(2)}) collective-permute-start(bf16[192,768]{1,0:T(8,128)(2,1)} %bitcast.144), channel_id=1, source_target_pairs={{8,0},{12,4},{16,8},{20,12},{24,16},{28,20},{32,24},{36,28},{40,32... | collective-permute-start | bytes 884744 | tf_op jit(solution)/shard_map/ppermute | solution.py:16
  16.4 1.3 collective-permute-start.5
  17.7 6.4 %collective-permute-start.4 = (bf16[192,768]{1,0:T(8,128)(2,1)}, bf16[192,768]{1,0:T(8,128)(2,1)S(1)}, u32[]{:S(2)}, u32[]{:S(2)}) collective-permute-start(bf16[192,768]{1,0:T(8,128)(2,1)} %bitcast.146), channel_id=1, source_target_pairs={{0,12},{8,20},{16,28},{24,36},{32,44},{40,52},{48,60},{56,68},{64,... | collective-permute-start | bytes 884744 | tf_op jit(solution)/shard_map/ppermute | solution.py:16
  24.1 3.9 %collective-permute-start.3 = (bf16[192,768]{1,0:T(8,128)(2,1)}, bf16[192,768]{1,0:T(8,128)(2,1)S(1)}, u32[]{:S(2)}, u32[]{:S(2)}) collective-permute-start(bf16[192,768]{1,0:T(8,128)(2,1)} %bitcast.147), channel_id=1, source_target_pairs={{0,8},{4,12},{8,16},{12,20},{16,24},{20,28},{24,32},{28,36},{32,40... | collective-permute-start | bytes 884744 | tf_op jit(solution)/shard_map/ppermute | solution.py:16
  28.0 1.3 reshape_squeeze.11
  29.3 1.4 reshape_squeeze.10
  36.9 1.9 collective-permute-start.2
  39.5 6.0 %collective-permute-start.13 = (bf16[192,768]{1,0:T(8,128)(2,1)S(1)}, bf16[192,768]{1,0:T(8,128)(2,1)}, u32[]{:S(2)}, u32[]{:S(2)}) collective-permute-start(bf16[192,768]{1,0:T(8,128)(2,1)S(1)} %bitcast.149), channel_id=1, source_target_pairs={{4,0},{8,4},{12,8},{16,12},{20,16},{24,20},{28,24},{32,28},{36,32}... | collective-permute-start | bytes 884744 | tf_op jit(solution)/shard_map/ppermute | solution.py:16
  45.5 1.3 reshape.183
  47.1 2.8 %collective-permute-start.12 = (bf16[192,768]{1,0:T(8,128)(2,1)S(1)}, bf16[192,768]{1,0:T(8,128)(2,1)}, u32[]{:S(2)}, u32[]{:S(2)}) collective-permute-start(bf16[192,768]{1,0:T(8,128)(2,1)S(1)} %bitcast.150), channel_id=1, source_target_pairs={{8,0},{12,4},{16,8},{20,12},{24,16},{28,20},{32,24},{36,28},{40,32... | collective-permute-start | bytes 884744 | tf_op jit(solution)/shard_map/ppermute | solution.py:16
  50.9 1.3 collective-permute-start.11
  52.9 7.8 %collective-permute-start.10 = (bf16[192,768]{1,0:T(8,128)(2,1)S(1)}, bf16[192,768]{1,0:T(8,128)(2,1)}, u32[]{:S(2)}, u32[]{:S(2)}) collective-permute-start(bf16[192,768]{1,0:T(8,128)(2,1)S(1)} %bitcast.152), channel_id=1, source_target_pairs={{0,12},{8,20},{16,28},{24,36},{32,44},{40,52},{48,60},{56,68},{64,... | collective-permute-start | bytes 884744 | tf_op jit(solution)/shard_map/ppermute | solution.py:16
  61.3 1.9 collective-permute-start.8
  63.3 1.3 reshape.179
  68.7 1.4 fusion.85
  70.6 5.3 %collective-permute-start.9 = (bf16[192,768]{1,0:T(8,128)(2,1)S(1)}, bf16[192,768]{1,0:T(8,128)(2,1)S(1)}, u32[]{:S(2)}, u32[]{:S(2)}) collective-permute-start(bf16[192,768]{1,0:T(8,128)(2,1)S(1)} %bitcast.154), channel_id=1, source_target_pairs={{0,8},{4,12},{8,16},{12,20},{16,24},{20,28},{24,32},{28,36},{32,40... | collective-permute-start | bytes 884744 | tf_op jit(solution)/shard_map/ppermute | solution.py:16
  75.9 1.4 fusion.30
  77.3 1.4 fusion.32
  79.2 1.4 fusion.90
  80.6 1.4 fusion.34
  82.0 1.4 fusion.36
  84.3 8.3 %collective-permute-done.9 = bf16[192,768]{1,0:T(8,128)(2,1)S(1)} collective-permute-done((bf16[192,768]{1,0:T(8,128)(2,1)S(1)}, bf16[192,768]{1,0:T(8,128)(2,1)S(1)}, u32[]{:S(2)}, u32[]{:S(2)}) %collective-permute-start.9) | collective-permute-done | bytes 294944 | tf_op jit(solution)/shard_map/ppermute | solution.py:16
  94.7 30.1 %all-gather.4.cloned.1.call-done = bf16[768,768]{1,0:T(8,128)(2,1)} async-done(((bf16[192,768]{1,0:T(8,128)(2,1)}), bf16[768,768]{1,0:T(8,128)(2,1)}) %all-gather.4.cloned.1.call-update) | async-done | bytes 1179664 | tf_op jit(solution)/shard_map/all_gather | solution.py:164
  124.7 45.2 %all-gather.6.cloned.1.call-done = bf16[1,768,768]{1,2,0:T(8,128)(2,1)} async-done(((bf16[1,768,96]{1,2,0:T(8,128)(2,1)}), bf16[1,768,768]{1,2,0:T(8,128)(2,1)}) %all-gather.6.cloned.1.call-update) | async-done | bytes 1179664 | tf_op jit(solution)/shard_map/all_gather | solution.py:165
  169.9 3.7 %convolution_convert_fusion = bf16[768,768]{1,0:T(8,128)(2,1)} fusion(bf16[768,768]{1,0:T(8,128)(2,1)} %all-gather.4.cloned.1.call-done, bf16[1,768,768]{1,2,0:T(8,128)(2,1)} %all-gather.6.cloned.1.call-done), kind=kOutput, calls=%fused_computation | convolution fusion | flops 906559488 | bytes 3538944 | tf_op jit(solution)/shard_map/dot_general | solution.py:166
  174.6 5.7 %collective-permute-start = (bf16[192,768]{1,0:T(8,128)(2,1)S(1)}, bf16[192,768]{1,0:T(8,128)(2,1)S(1)}, u32[]{:S(2)}, u32[]{:S(2)}) collective-permute-start(bf16[192,768]{1,0:T(8,128)(2,1)S(1)} %bitcast.155), channel_id=1, source_target_pairs={{0,0},{1,32},{2,64},{3,96},{32,1},{33,33},{34,65},{35,97},{64,2},{... | collective-permute-start | bytes 884744 | tf_op jit(solution)/shard_map/ppermute | solution.py:171
  180.3 4.1 %collective-permute-start.1 = (f32[768]{0:T(1024)S(1)}, f32[768]{0:T(1024)S(1)}, u32[]{:S(2)}, u32[]{:S(2)}) collective-permute-start(f32[768]{0:T(1024)S(1)} %reduce.7), channel_id=1, source_target_pairs={{0,0},{1,32},{2,64},{3,96},{32,1},{33,33},{34,65},{35,97},{64,2},{... | collective-permute-start | bytes 9224 | tf_op jit(solution)/shard_map/ppermute | solution.py:172
  184.4 5.5 %collective-permute-done.1 = f32[768]{0:T(1024)S(1)} collective-permute-done((f32[768]{0:T(1024)S(1)}, f32[768]{0:T(1024)S(1)}, u32[]{:S(2)}, u32[]{:S(2)}) %collective-permute-start.1) | collective-permute-done | bytes 3104 | tf_op jit(solution)/shard_map/ppermute | solution.py:172
  189.9 26.5 %reduce-scatter.2.cloned.1.call-done = bf16[192,768]{1,0:T(8,128)(2,1)} async-done(((bf16[768,768]{1,0:T(8,128)(2,1)}), bf16[192,768]{1,0:T(8,128)(2,1)}) %reduce-scatter.2.cloned.1.call-update) | async-done | bytes 294928 | tf_op jit(solution)/shard_map/reduce_scatter | solution.py:167
  217.4 2.2 collective-permute-start.14
  219.6 15.5 %collective-permute-done.14 = bf16[192,768]{1,0:T(8,128)(2,1)S(1)} collective-permute-done((bf16[192,768]{1,0:T(8,128)(2,1)S(1)}, bf16[192,768]{1,0:T(8,128)(2,1)S(1)}, u32[]{:S(2)}, u32[]{:S(2)}) %collective-permute-start.14) | collective-permute-done | bytes 294944 | tf_op jit(solution)/shard_map/ppermute | solution.py:177
  (74 shorter events, 16.1 us)
Async XLA Ops:
  6.5 118.2 %all-gather.4.cloned.1.call-start = ((), (), s32[]{:S(2)}) async-start(), calls=%async_computation.1 | async-start | bytes 1474560 | tf_op jit(solution)/shard_map/all_gather | solution.py:164
  6.5 24.7 %copy-start.4 = (s32[16,27]{1,0:T(8,128)S(1)}, s32[16,27]{1,0:T(8,128)}, u32[]{:S(2)}) copy-start(s32[16,27]{1,0:T(8,128)} %param.13) | copy-start | bytes 5188
  6.5 30.3 %collective-permute-start.7 = (bf16[192,768]{1,0:T(8,128)(2,1)}, bf16[192,768]{1,0:T(8,128)(2,1)S(1)}, u32[]{:S(2)}, u32[]{:S(2)}) collective-permute-start(bf16[192,768]{1,0:T(8,128)(2,1)} %bitcast.143), channel_id=1, source_target_pairs={{4,0},{8,4},{12,8},{16,12},{20,16},{24,20},{28,24},{32,28},{36,32}... | collective-permute-start | bytes 884744 | tf_op jit(solution)/shard_map/ppermute | solution.py:16
  12.3 27.2 %collective-permute-start.6 = (bf16[192,768]{1,0:T(8,128)(2,1)}, bf16[192,768]{1,0:T(8,128)(2,1)}, u32[]{:S(2)}, u32[]{:S(2)}) collective-permute-start(bf16[192,768]{1,0:T(8,128)(2,1)} %bitcast.144), channel_id=1, source_target_pairs={{8,0},{12,4},{16,8},{20,12},{24,16},{28,20},{32,24},{36,28},{40,32... | collective-permute-start | bytes 884744 | tf_op jit(solution)/shard_map/ppermute | solution.py:16
  16.4 30.8 %collective-permute-start.5 = (bf16[192,768]{1,0:T(8,128)(2,1)}, bf16[192,768]{1,0:T(8,128)(2,1)S(1)}, u32[]{:S(2)}, u32[]{:S(2)}) collective-permute-start(bf16[192,768]{1,0:T(8,128)(2,1)} %bitcast.145), channel_id=1, source_target_pairs={{12,0},{20,8},{28,16},{36,24},{44,32},{52,40},{60,48},{68,56},{76,... | collective-permute-start | bytes 884744 | tf_op jit(solution)/shard_map/ppermute | solution.py:16
  17.7 33.2 %collective-permute-start.4 = (bf16[192,768]{1,0:T(8,128)(2,1)}, bf16[192,768]{1,0:T(8,128)(2,1)S(1)}, u32[]{:S(2)}, u32[]{:S(2)}) collective-permute-start(bf16[192,768]{1,0:T(8,128)(2,1)} %bitcast.146), channel_id=1, source_target_pairs={{0,12},{8,20},{16,28},{24,36},{32,44},{40,52},{48,60},{56,68},{64,... | collective-permute-start | bytes 884744 | tf_op jit(solution)/shard_map/ppermute | solution.py:16
  24.1 28.8 %collective-permute-start.3 = (bf16[192,768]{1,0:T(8,128)(2,1)}, bf16[192,768]{1,0:T(8,128)(2,1)S(1)}, u32[]{:S(2)}, u32[]{:S(2)}) collective-permute-start(bf16[192,768]{1,0:T(8,128)(2,1)} %bitcast.147), channel_id=1, source_target_pairs={{0,8},{4,12},{8,16},{12,20},{16,24},{20,28},{24,32},{28,36},{32,40... | collective-permute-start | bytes 884744 | tf_op jit(solution)/shard_map/ppermute | solution.py:16
  29.3 2.8 %copy-start.1 = (bf16[1,192,768]{2,1,0:T(8,128)(2,1)S(1)}, bf16[1,192,768]{2,1,0:T(8,128)(2,1)}, u32[]{:S(2)}) copy-start(bf16[1,192,768]{2,1,0:T(8,128)(2,1)} %param.9) | copy-start | bytes 884740
  30.7 6.2 %copy-start = (bf16[1,192,768]{2,1,0:T(8,128)(2,1)S(1)}, bf16[1,192,768]{2,1,0:T(8,128)(2,1)}, u32[]{:S(2)}) copy-start(bf16[1,192,768]{2,1,0:T(8,128)(2,1)} %param.8) | copy-start | bytes 884740
  36.9 2.6 %copy-start.2 = (bf16[192,768]{1,0:T(8,128)(2,1)}, bf16[192,768]{1,0:T(8,128)(2,1)S(1)}, u32[]{:S(2)}) copy-start(bf16[192,768]{1,0:T(8,128)(2,1)S(1)} %collective-permute-done.7) | copy-start | bytes 884740
  36.9 24.4 %collective-permute-start.2 = (bf16[192,768]{1,0:T(8,128)(2,1)S(1)}, bf16[192,768]{1,0:T(8,128)(2,1)}, u32[]{:S(2)}, u32[]{:S(2)}) collective-permute-start(bf16[192,768]{1,0:T(8,128)(2,1)S(1)} %bitcast.148), channel_id=1, source_target_pairs={{0,4},{4,8},{8,12},{12,16},{16,20},{20,24},{24,28},{28,32},{32,36}... | collective-permute-start | bytes 884744 | tf_op jit(solution)/shard_map/ppermute | solution.py:16
  39.5 31.1 %collective-permute-start.13 = (bf16[192,768]{1,0:T(8,128)(2,1)S(1)}, bf16[192,768]{1,0:T(8,128)(2,1)}, u32[]{:S(2)}, u32[]{:S(2)}) collective-permute-start(bf16[192,768]{1,0:T(8,128)(2,1)S(1)} %bitcast.149), channel_id=1, source_target_pairs={{4,0},{8,4},{12,8},{16,12},{20,16},{24,20},{28,24},{32,28},{36,32}... | collective-permute-start | bytes 884744 | tf_op jit(solution)/shard_map/ppermute | solution.py:16
  47.1 30.2 %collective-permute-start.12 = (bf16[192,768]{1,0:T(8,128)(2,1)S(1)}, bf16[192,768]{1,0:T(8,128)(2,1)}, u32[]{:S(2)}, u32[]{:S(2)}) collective-permute-start(bf16[192,768]{1,0:T(8,128)(2,1)S(1)} %bitcast.150), channel_id=1, source_target_pairs={{8,0},{12,4},{16,8},{20,12},{24,16},{28,20},{32,24},{36,28},{40,32... | collective-permute-start | bytes 884744 | tf_op jit(solution)/shard_map/ppermute | solution.py:16
  50.9 29.8 %collective-permute-start.11 = (bf16[192,768]{1,0:T(8,128)(2,1)S(1)}, bf16[192,768]{1,0:T(8,128)(2,1)}, u32[]{:S(2)}, u32[]{:S(2)}) collective-permute-start(bf16[192,768]{1,0:T(8,128)(2,1)S(1)} %bitcast.151), channel_id=1, source_target_pairs={{12,0},{20,8},{28,16},{36,24},{44,32},{52,40},{60,48},{68,56},{76,... | collective-permute-start | bytes 884744 | tf_op jit(solution)/shard_map/ppermute | solution.py:16
  52.9 29.1 %collective-permute-start.10 = (bf16[192,768]{1,0:T(8,128)(2,1)S(1)}, bf16[192,768]{1,0:T(8,128)(2,1)}, u32[]{:S(2)}, u32[]{:S(2)}) collective-permute-start(bf16[192,768]{1,0:T(8,128)(2,1)S(1)} %bitcast.152), channel_id=1, source_target_pairs={{0,12},{8,20},{16,28},{24,36},{32,44},{40,52},{48,60},{56,68},{64,... | collective-permute-start | bytes 884744 | tf_op jit(solution)/shard_map/ppermute | solution.py:16
  61.3 22.5 %collective-permute-start.8 = (bf16[192,768]{1,0:T(8,128)(2,1)S(1)}, bf16[192,768]{1,0:T(8,128)(2,1)S(1)}, u32[]{:S(2)}, u32[]{:S(2)}) collective-permute-start(bf16[192,768]{1,0:T(8,128)(2,1)S(1)} %bitcast.153), channel_id=1, source_target_pairs={{0,4},{4,8},{8,12},{12,16},{16,20},{20,24},{24,28},{28,32},{32,36}... | collective-permute-start | bytes 884744 | tf_op jit(solution)/shard_map/ppermute | solution.py:16
  67.2 1.0 copy-start.3
  70.6 22.0 %collective-permute-start.9 = (bf16[192,768]{1,0:T(8,128)(2,1)S(1)}, bf16[192,768]{1,0:T(8,128)(2,1)S(1)}, u32[]{:S(2)}, u32[]{:S(2)}) collective-permute-start(bf16[192,768]{1,0:T(8,128)(2,1)S(1)} %bitcast.154), channel_id=1, source_target_pairs={{0,8},{4,12},{8,16},{12,20},{16,24},{20,28},{24,32},{28,36},{32,40... | collective-permute-start | bytes 884744 | tf_op jit(solution)/shard_map/ppermute | solution.py:16
  93.9 76.0 %all-gather.6.cloned.1.call-start = ((), (), s32[]{:S(2)}) async-start(), calls=%async_computation.3 | async-start | bytes 1327104 | tf_op jit(solution)/shard_map/all_gather | solution.py:165
  94.6 121.8 %reduce-scatter.2.cloned.1.call-start = ((), (), s32[]{:S(2)}) async-start(), calls=%async_computation.2 | async-start | bytes 1474560 | tf_op jit(solution)/shard_map/reduce_scatter | solution.py:167
  173.6 1.0 copy-start.6
  173.6 6.7 %copy-start.5 = (f32[1,768]{1,0:T(1,128)S(1)}, f32[1,768]{1,0:T(1,128)}, u32[]{:S(2)}) copy-start(f32[1,768]{1,0:T(1,128)} %param.12) | copy-start | bytes 9220
  174.6 15.3 %collective-permute-start = (bf16[192,768]{1,0:T(8,128)(2,1)S(1)}, bf16[192,768]{1,0:T(8,128)(2,1)S(1)}, u32[]{:S(2)}, u32[]{:S(2)}) collective-permute-start(bf16[192,768]{1,0:T(8,128)(2,1)S(1)} %bitcast.155), channel_id=1, source_target_pairs={{0,0},{1,32},{2,64},{3,96},{32,1},{33,33},{34,65},{35,97},{64,2},{... | collective-permute-start | bytes 884744 | tf_op jit(solution)/shard_map/ppermute | solution.py:171
  180.3 9.6 %collective-permute-start.1 = (f32[768]{0:T(1024)S(1)}, f32[768]{0:T(1024)S(1)}, u32[]{:S(2)}, u32[]{:S(2)}) collective-permute-start(f32[768]{0:T(1024)S(1)} %reduce.7), channel_id=1, source_target_pairs={{0,0},{1,32},{2,64},{3,96},{32,1},{33,33},{34,65},{35,97},{64,2},{... | collective-permute-start | bytes 9224 | tf_op jit(solution)/shard_map/ppermute | solution.py:172
  217.4 17.7 %collective-permute-start.14 = (bf16[192,768]{1,0:T(8,128)(2,1)S(1)}, bf16[192,768]{1,0:T(8,128)(2,1)S(1)}, u32[]{:S(2)}, u32[]{:S(2)}) collective-permute-start(bf16[192,768]{1,0:T(8,128)(2,1)S(1)} %add_convert_fusion), channel_id=1, source_target_pairs={{0,128},{1,160},{2,192},{3,224},{32,129},{33,161},{34,193},{35,225... | collective-permute-start | bytes 884744 | tf_op jit(solution)/shard_map/ppermute | solution.py:177
Sparse Core Ops, SparseCore 0:
  94.0 30.6 all-gather.3
  126.8 43.0 all-gather.5
  173.8 42.5 reduce-scatter.1

commit v2 on v1

--- a/solution.py
+++ b/solution.py
@@ -161,20 +161,44 @@
     attended = (
         (weighted / summed.T[:, :, None]).astype(jnp.bfloat16).reshape(row_count, feature_count)
     )
-    token_block = lax.all_gather(attended, "sx", axis=0, tiled=True)
-    weight_block = lax.all_gather(out_weight[0], "sy", axis=1, tiled=True)
-    group_term = jnp.dot(token_block, weight_block, preferred_element_type=jnp.float32)
-    mixed = lax.psum_scatter(
-        group_term.astype(jnp.bfloat16), "head", scatter_dimension=0, tiled=True
-    ).astype(jnp.float32)
-    swap = linear_pairs((x_count, head_groups), lambda a, b: (b, a))
-    stream_block = lax.ppermute(stream[0], ("sx", "head"), swap)
-    gate_block = lax.ppermute(gate_scale[0], ("sx", "head"), swap)
-    updated = (stream_block.astype(jnp.float32) + gate_block[None, :] * mixed).astype(jnp.bfloat16)
-    hand = linear_pairs(
-        (sections, x_count, head_groups), lambda s, a, b: ((s + 1) % sections, b, a)
-    )
-    handed = lax.ppermute(updated, ("section", "sx", "head"), hand)
+    weight = out_weight[0]
+    forward = weight
+    backward = weight
+    weight_parts = {0: weight}
+    for step in range(1, y_count // 2 + 1):
+        forward = lax.ppermute(forward, "sy", [(i, (i + 1) % y_count) for i in range(y_count)])
+        weight_parts[(-step) % y_count] = forward
+        if step < y_count - step:
+            backward = lax.ppermute(
+                backward, "sy", [(i, (i - 1) % y_count) for i in range(y_count)]
+            )
+            weight_parts[step] = backward
+    relative_weight = jnp.concatenate([weight_parts[r] for r in range(y_count)], axis=1)
+    weight_block = jnp.roll(relative_weight, y_index * weight.shape[1], axis=1)
+    token_parts = [attended] + [
+        lax.ppermute(attended, "sx", [(i, (i + d) % x_count) for i in range(x_count)])
+        for d in range(1, x_count)
+    ]
+    terms = jnp.stack(
+        [
+            jnp.dot(part, weight_block, preferred_element_type=jnp.float32).astype(jnp.bfloat16)
+            for part in token_parts
+        ]
+    )
+    group_index = lax.axis_index("head")
+    mixed = jnp.zeros(terms.shape[1:], jnp.float32)
+    for step in range(head_groups):
+        pick = (x_index - group_index - step) % head_groups
+        outgoing = lax.dynamic_index_in_dim(terms, pick, 0, keepdims=False)
+        route = linear_pairs(
+            (x_count, head_groups), lambda a, b: ((b + step) % head_groups, a)
+        )
+        mixed = mixed + lax.ppermute(outgoing, ("sx", "head"), route).astype(jnp.float32)
+    updated = (
+        stream[0].astype(jnp.float32) + gate_scale[0][None, :] * mixed
+    ).astype(jnp.bfloat16)
+    hand = [(s, (s + 1) % sections) for s in range(sections)]
+    handed = lax.ppermute(updated, "section", hand)
     return handed[None]
 
 

time: 243 us -> 249 us (1.025)
  the two profiles are of different devices: /device:TPU:6 before, /device:TPU:219 now
where the time goes in v2:
time: 249 us; the launch traced here: 247 us
  starting transfers between devices  107 us (43%)
  waiting for transfers between devices  80.6 us (32%)
  local copies, waits for them, and re-layouts  24 us (10%)
  matrix products  19.8 us (8%)
  other arithmetic  11.3 us (5%)
  between operations  4.64 us (2%)
    ppermute x4, waiting for transfers between devices, on_device(): lax.ppermute(outgoing, ('sx', 'head'), route).astype(jnp.float32)  66.8 us
    ppermute x12, starting transfers between devices, shifted(): return lax.ppermute(block, axis, route)  45.2 us
    ppermute x1, starting transfers between devices, on_device(): handed = lax.ppermute(updated, 'section', hand)  16 us
    ppermute x4, starting transfers between devices, on_device(): lax.ppermute(forward, 'sy', [(i, (i + 1) % y_count) for i in range(y_coun...  14.2 us
    ppermute x3, starting transfers between devices, on_device(): lax.ppermute(attended, 'sx', [(i, (i + d) % x_count) for i in range(x_cou...  12.9 us
    ppermute x4, starting transfers between devices, on_device(): lax.ppermute(outgoing, ('sx', 'head'), route).astype(jnp.float32)  11 us
    dot_general x7, matrix products, attend(): jnp.einsum('qhd,khd->hqk', query_parts, slab_keys, preferred_element_type...  9.91 us
    reduce_sum x7, local copies, waits for them, and re-layouts, tile_maxima(): lengths = jnp.sqrt(jnp.sum(parts * parts, axis=2))  8.27 us
  transfers between devices with their start and end apart: 27, of which 5 were waited for; matrix products, arithmetic and copies ran while one was open for 21% of the time, Pallas kernels for 0%

profile of v2, /device:TPU:219, one launch (start us, length us, event | category | flops | bytes accessed | tf_op | source)
XLA Modules:
  0.0 247.0 jit_solution(4822284955609196690)
XLA Ops:
  0.0 2.0 collective-permute-start.4
  2.0 2.1 collective-permute-start.5
  5.4 8.1 %collective-permute-start.3 = (bf16[192,768]{1,0:T(8,128)(2,1)}, bf16[192,768]{1,0:T(8,128)(2,1)}, u32[]{:S(2)}, u32[]{:S(2)}) collective-permute-start(bf16[192,768]{1,0:T(8,128)(2,1)} %bitcast.171), channel_id=1, source_target_pairs={{12,0},{20,8},{28,16},{36,24},{44,32},{52,40},{60,48},{68,56},{76,... | collective-permute-start | bytes 884744 | tf_op jit(solution)/shard_map/ppermute | solution.py:16
  13.4 2.0 collective-permute-start.12
  20.8 2.1 reshape_squeeze.12
  27.4 5.9 %collective-permute-done.12 = bf16[768,96]{0,1:T(8,128)(2,1)S(1)} collective-permute-done((bf16[768,96]{0,1:T(8,128)(2,1)}, bf16[768,96]{0,1:T(8,128)(2,1)S(1)}, u32[]{:S(2)}, u32[]{:S(2)}) %collective-permute-start.12) | collective-permute-done | bytes 147488 | tf_op jit(solution)/shard_map/ppermute | solution.py:172
  33.3 9.5 %collective-permute-start = (bf16[192,768]{1,0:T(8,128)(2,1)}, bf16[192,768]{1,0:T(8,128)(2,1)}, u32[]{:S(2)}, u32[]{:S(2)}) collective-permute-start(bf16[192,768]{1,0:T(8,128)(2,1)} %bitcast.172), channel_id=1, source_target_pairs={{0,4},{4,8},{8,12},{12,16},{16,20},{20,24},{24,28},{28,32},{32,36}... | collective-permute-start | bytes 884744 | tf_op jit(solution)/shard_map/ppermute | solution.py:16
  42.9 3.4 %collective-permute-start.1 = (bf16[192,768]{1,0:T(8,128)(2,1)}, bf16[192,768]{1,0:T(8,128)(2,1)}, u32[]{:S(2)}, u32[]{:S(2)}) collective-permute-start(bf16[192,768]{1,0:T(8,128)(2,1)} %bitcast.173), channel_id=1, source_target_pairs={{0,8},{4,12},{8,16},{12,20},{16,24},{20,28},{24,32},{28,36},{32,40... | collective-permute-start | bytes 884744 | tf_op jit(solution)/shard_map/ppermute | solution.py:16
  48.5 1.9 collective-permute-start.6
  52.7 4.6 %collective-permute-start.9 = (bf16[192,768]{1,0:T(8,128)(2,1)}, bf16[192,768]{1,0:T(8,128)(2,1)}, u32[]{:S(2)}, u32[]{:S(2)}) collective-permute-start(bf16[192,768]{1,0:T(8,128)(2,1)} %bitcast.175), channel_id=1, source_target_pairs={{12,0},{20,8},{28,16},{36,24},{44,32},{52,40},{60,48},{68,56},{76,... | collective-permute-start | bytes 884744 | tf_op jit(solution)/shard_map/ppermute | solution.py:16
  59.6 1.6 copy.158
  68.7 2.4 collective-permute-start.10
  75.0 6.6 %collective-permute-start.11 = (bf16[192,768]{1,0:T(8,128)(2,1)}, bf16[192,768]{1,0:T(8,128)(2,1)}, u32[]{:S(2)}, u32[]{:S(2)}) collective-permute-start(bf16[192,768]{1,0:T(8,128)(2,1)} %bitcast.178), channel_id=1, source_target_pairs={{4,0},{8,4},{12,8},{16,12},{20,16},{24,20},{28,24},{32,28},{36,32}... | collective-permute-start | bytes 884744 | tf_op jit(solution)/shard_map/ppermute | solution.py:16
  95.2 4.3 %collective-permute-start.15 = (bf16[768,96]{0,1:T(8,128)(2,1)S(1)}, bf16[768,96]{0,1:T(8,128)(2,1)S(1)}, u32[]{:S(2)}, u32[]{:S(2)}) collective-permute-start(bf16[768,96]{0,1:T(8,128)(2,1)S(1)} %bitcast.163), channel_id=1, source_target_pairs={{0,4},{4,8},{8,12},{12,16},{16,20},{20,24},{24,28},{28,0},{1,5},{5... | collective-permute-start | bytes 442376 | tf_op jit(solution)/shard_map/ppermute | solution.py:169
  103.8 1.9 collective-permute-start.13
  105.8 4.6 %collective-permute-start.16 = (bf16[768,96]{0,1:T(8,128)(2,1)S(1)}, bf16[768,96]{0,1:T(8,128)(2,1)S(1)}, u32[]{:S(2)}, u32[]{:S(2)}) collective-permute-start(bf16[768,96]{0,1:T(8,128)(2,1)S(1)} %collective-permute-done.15), channel_id=1, source_target_pairs={{0,4},{4,8},{8,12},{12,16},{16,20},{20,24},{24,28},{28,0},{1,5},{5... | collective-permute-start | bytes 442376 | tf_op jit(solution)/shard_map/ppermute | solution.py:169
  113.3 1.9 collective-permute-start.7
  115.2 3.3 %collective-permute-start.14 = (bf16[768,96]{0,1:T(8,128)(2,1)S(1)}, bf16[768,96]{0,1:T(8,128)(2,1)S(1)}, u32[]{:S(2)}, u32[]{:S(2)}) collective-permute-start(bf16[768,96]{0,1:T(8,128)(2,1)S(1)} %collective-permute-done.13), channel_id=1, source_target_pairs={{0,28},{4,0},{8,4},{12,8},{16,12},{20,16},{24,20},{28,24},{1,29},{... | collective-permute-start | bytes 442376 | tf_op jit(solution)/shard_map/ppermute | solution.py:172
  118.5 3.4 %collective-permute-start.17 = (bf16[768,96]{0,1:T(8,128)(2,1)S(1)}, bf16[768,96]{0,1:T(8,128)(2,1)S(1)}, u32[]{:S(2)}, u32[]{:S(2)}) collective-permute-start(bf16[768,96]{0,1:T(8,128)(2,1)S(1)} %collective-permute-done.16), channel_id=1, source_target_pairs={{0,4},{4,8},{8,12},{12,16},{16,20},{20,24},{24,28},{28,0},{1,5},{5... | collective-permute-start | bytes 442376 | tf_op jit(solution)/shard_map/ppermute | solution.py:169
  126.6 3.1 %collective-permute-start.19 = (bf16[192,768]{1,0:T(8,128)(2,1)S(1)}, bf16[192,768]{1,0:T(8,128)(2,1)S(1)}, u32[]{:S(2)}, u32[]{:S(2)}) collective-permute-start(bf16[192,768]{1,0:T(8,128)(2,1)S(1)} %bitcast.164), channel_id=1, source_target_pairs={{0,32},{32,64},{64,96},{96,0},{1,33},{33,65},{65,97},{97,1},{2,34}... | collective-permute-start | bytes 884744 | tf_op jit(solution)/shard_map/ppermute | solution.py:179
  129.7 5.8 %collective-permute-start.20 = (bf16[192,768]{1,0:T(8,128)(2,1)S(1)}, bf16[192,768]{1,0:T(8,128)(2,1)S(1)}, u32[]{:S(2)}, u32[]{:S(2)}) collective-permute-start(bf16[192,768]{1,0:T(8,128)(2,1)S(1)} %bitcast.165), channel_id=1, source_target_pairs={{0,64},{32,96},{64,0},{96,32},{1,65},{33,97},{65,1},{97,33},{2,66}... | collective-permute-start | bytes 884744 | tf_op jit(solution)/shard_map/ppermute | solution.py:179
  135.5 4.0 %collective-permute-start.21 = (bf16[192,768]{1,0:T(8,128)(2,1)S(1)}, bf16[192,768]{1,0:T(8,128)(2,1)S(1)}, u32[]{:S(2)}, u32[]{:S(2)}) collective-permute-start(bf16[192,768]{1,0:T(8,128)(2,1)S(1)} %bitcast.166), channel_id=1, source_target_pairs={{0,96},{32,0},{64,32},{96,64},{1,97},{33,1},{65,33},{97,65},{2,98}... | collective-permute-start | bytes 884744 | tf_op jit(solution)/shard_map/ppermute | solution.py:179
  139.5 1.9 collective-permute-start.18
  141.4 4.2 %collective-permute-done.18 = bf16[768,96]{0,1:T(8,128)(2,1)S(1)} collective-permute-done((bf16[768,96]{0,1:T(8,128)(2,1)S(1)}, bf16[768,96]{0,1:T(8,128)(2,1)S(1)}, u32[]{:S(2)}, u32[]{:S(2)}) %collective-permute-start.18) | collective-permute-done | bytes 147488 | tf_op jit(solution)/shard_map/ppermute | solution.py:169
  148.5 2.3 collective-permute-start.22
  150.8 1.9 collective-permute-start.23
  152.7 3.2 %collective-permute-start.24 = (bf16[192,768]{1,0:T(8,128)(2,1)S(1)}, bf16[192,768]{1,0:T(8,128)(2,1)S(1)}, u32[]{:S(2)}, u32[]{:S(2)}) collective-permute-start(bf16[192,768]{1,0:T(8,128)(2,1)S(1)} %get-tuple-element.7), channel_id=1, source_target_pairs={{0,64},{1,96},{2,0},{3,32},{32,65},{33,97},{34,1},{35,33},{64,66},... | collective-permute-start | bytes 884744 | tf_op jit(solution)/shard_map/ppermute | solution.py:196
  155.9 3.6 %collective-permute-start.25 = (bf16[192,768]{1,0:T(8,128)(2,1)S(1)}, bf16[192,768]{1,0:T(8,128)(2,1)S(1)}, u32[]{:S(2)}, u32[]{:S(2)}) collective-permute-start(bf16[192,768]{1,0:T(8,128)(2,1)S(1)} %get-tuple-element.6), channel_id=1, source_target_pairs={{0,96},{1,0},{2,32},{3,64},{32,97},{33,1},{34,33},{35,65},{64,98},... | collective-permute-start | bytes 884744 | tf_op jit(solution)/shard_map/ppermute | solution.py:196
  159.6 27.8 %collective-permute-done.22 = bf16[192,768]{1,0:T(8,128)(2,1)S(1)} collective-permute-done((bf16[192,768]{1,0:T(8,128)(2,1)S(1)}, bf16[192,768]{1,0:T(8,128)(2,1)S(1)}, u32[]{:S(2)}, u32[]{:S(2)}) %collective-permute-start.22) | collective-permute-done | bytes 294944 | tf_op jit(solution)/shard_map/ppermute | solution.py:196
  187.4 39.0 %collective-permute-done.25 = bf16[192,768]{1,0:T(8,128)(2,1)S(1)} collective-permute-done((bf16[192,768]{1,0:T(8,128)(2,1)S(1)}, bf16[192,768]{1,0:T(8,128)(2,1)S(1)}, u32[]{:S(2)}, u32[]{:S(2)}) %collective-permute-start.25) | collective-permute-done | bytes 294944 | tf_op jit(solution)/shard_map/ppermute | solution.py:196
  226.6 16.0 %collective-permute-start.26 = (bf16[192,768]{1,0:T(8,128)(2,1)S(1)}, bf16[192,768]{1,0:T(8,128)(2,1)S(1)}, u32[]{:S(2)}, u32[]{:S(2)}) collective-permute-start(bf16[192,768]{1,0:T(8,128)(2,1)S(1)} %fusion.37), channel_id=1, source_target_pairs={{0,128},{128,256},{256,384},{384,0},{1,129},{129,257},{257,385},{3... | collective-permute-start | bytes 884744 | tf_op jit(solution)/shard_map/ppermute | solution.py:201
  242.6 3.6 %collective-permute-done.26 = bf16[192,768]{1,0:T(8,128)(2,1)S(1)} collective-permute-done((bf16[192,768]{1,0:T(8,128)(2,1)S(1)}, bf16[192,768]{1,0:T(8,128)(2,1)S(1)}, u32[]{:S(2)}, u32[]{:S(2)}) %collective-permute-start.26) | collective-permute-done | bytes 294944 | tf_op jit(solution)/shard_map/ppermute | solution.py:201
  (112 shorter events, 54.2 us)
Async XLA Ops:
  0.0 42.9 %collective-permute-start.4 = (bf16[192,768]{1,0:T(8,128)(2,1)}, bf16[192,768]{1,0:T(8,128)(2,1)}, u32[]{:S(2)}, u32[]{:S(2)}) collective-permute-start(bf16[192,768]{1,0:T(8,128)(2,1)} %bitcast.168), channel_id=1, source_target_pairs={{8,0},{12,4},{16,8},{20,12},{24,16},{28,20},{32,24},{36,28},{40,32... | collective-permute-start | bytes 884744 | tf_op jit(solution)/shard_map/ppermute | solution.py:16
  2.0 46.6 %collective-permute-start.5 = (bf16[192,768]{1,0:T(8,128)(2,1)}, bf16[192,768]{1,0:T(8,128)(2,1)}, u32[]{:S(2)}, u32[]{:S(2)}) collective-permute-start(bf16[192,768]{1,0:T(8,128)(2,1)} %bitcast.169), channel_id=1, source_target_pairs={{4,0},{8,4},{12,8},{16,12},{20,16},{24,20},{28,24},{32,28},{36,32}... | collective-permute-start | bytes 884744 | tf_op jit(solution)/shard_map/ppermute | solution.py:16
  4.1 48.6 %collective-permute-start.2 = (bf16[192,768]{1,0:T(8,128)(2,1)}, bf16[192,768]{1,0:T(8,128)(2,1)}, u32[]{:S(2)}, u32[]{:S(2)}) collective-permute-start(bf16[192,768]{1,0:T(8,128)(2,1)} %bitcast.170), channel_id=1, source_target_pairs={{0,12},{8,20},{16,28},{24,36},{32,44},{40,52},{48,60},{56,68},{64,... | collective-permute-start | bytes 884744 | tf_op jit(solution)/shard_map/ppermute | solution.py:16
  5.4 58.3 %collective-permute-start.3 = (bf16[192,768]{1,0:T(8,128)(2,1)}, bf16[192,768]{1,0:T(8,128)(2,1)}, u32[]{:S(2)}, u32[]{:S(2)}) collective-permute-start(bf16[192,768]{1,0:T(8,128)(2,1)} %bitcast.171), channel_id=1, source_target_pairs={{12,0},{20,8},{28,16},{36,24},{44,32},{52,40},{60,48},{68,56},{76,... | collective-permute-start | bytes 884744 | tf_op jit(solution)/shard_map/ppermute | solution.py:16
  13.4 6.2 %copy-start.6 = (s32[16,27]{1,0:T(8,128)S(1)}, s32[16,27]{1,0:T(8,128)}, u32[]{:S(2)}) copy-start(s32[16,27]{1,0:T(8,128)} %param.13) | copy-start | bytes 5188
  13.4 19.9 %collective-permute-start.12 = (bf16[768,96]{0,1:T(8,128)(2,1)}, bf16[768,96]{0,1:T(8,128)(2,1)S(1)}, u32[]{:S(2)}, u32[]{:S(2)}) collective-permute-start(bf16[768,96]{0,1:T(8,128)(2,1)} %bitcast.162), channel_id=1, source_target_pairs={{0,28},{4,0},{8,4},{12,8},{16,12},{20,16},{24,20},{28,24},{1,29},{... | collective-permute-start | bytes 442376 | tf_op jit(solution)/shard_map/ppermute | solution.py:172
  33.3 9.5 %copy-start.2 = (bf16[768,96]{0,1:T(8,128)(2,1)}, bf16[768,96]{0,1:T(8,128)(2,1)S(1)}, u32[]{:S(2)}) copy-start(bf16[768,96]{0,1:T(8,128)(2,1)S(1)} %collective-permute-done.12) | copy-start | bytes 442372
  33.3 35.4 %collective-permute-start = (bf16[192,768]{1,0:T(8,128)(2,1)}, bf16[192,768]{1,0:T(8,128)(2,1)}, u32[]{:S(2)}, u32[]{:S(2)}) collective-permute-start(bf16[192,768]{1,0:T(8,128)(2,1)} %bitcast.172), channel_id=1, source_target_pairs={{0,4},{4,8},{8,12},{12,16},{16,20},{20,24},{24,28},{28,32},{32,36}... | collective-permute-start | bytes 884744 | tf_op jit(solution)/shard_map/ppermute | solution.py:16
  42.9 32.1 %collective-permute-start.1 = (bf16[192,768]{1,0:T(8,128)(2,1)}, bf16[192,768]{1,0:T(8,128)(2,1)}, u32[]{:S(2)}, u32[]{:S(2)}) collective-permute-start(bf16[192,768]{1,0:T(8,128)(2,1)} %bitcast.173), channel_id=1, source_target_pairs={{0,8},{4,12},{8,16},{12,20},{16,24},{20,28},{24,32},{28,36},{32,40... | collective-permute-start | bytes 884744 | tf_op jit(solution)/shard_map/ppermute | solution.py:16
  48.5 76.1 %collective-permute-start.6 = (bf16[192,768]{1,0:T(8,128)(2,1)}, bf16[192,768]{1,0:T(8,128)(2,1)}, u32[]{:S(2)}, u32[]{:S(2)}) collective-permute-start(bf16[192,768]{1,0:T(8,128)(2,1)} %bitcast.174), channel_id=1, source_target_pairs={{0,4},{4,8},{8,12},{12,16},{16,20},{20,24},{24,28},{28,32},{32,36}... | collective-permute-start | bytes 884744 | tf_op jit(solution)/shard_map/ppermute | solution.py:16
  52.7 42.0 %collective-permute-start.9 = (bf16[192,768]{1,0:T(8,128)(2,1)}, bf16[192,768]{1,0:T(8,128)(2,1)}, u32[]{:S(2)}, u32[]{:S(2)}) collective-permute-start(bf16[192,768]{1,0:T(8,128)(2,1)} %bitcast.175), channel_id=1, source_target_pairs={{12,0},{20,8},{28,16},{36,24},{44,32},{52,40},{60,48},{68,56},{76,... | collective-permute-start | bytes 884744 | tf_op jit(solution)/shard_map/ppermute | solution.py:16
  63.7 42.1 %collective-permute-start.8 = (bf16[192,768]{1,0:T(8,128)(2,1)}, bf16[192,768]{1,0:T(8,128)(2,1)}, u32[]{:S(2)}, u32[]{:S(2)}) collective-permute-start(bf16[192,768]{1,0:T(8,128)(2,1)} %bitcast.176), channel_id=1, source_target_pairs={{0,12},{8,20},{16,28},{24,36},{32,44},{40,52},{48,60},{56,68},{64,... | collective-permute-start | bytes 884744 | tf_op jit(solution)/shard_map/ppermute | solution.py:16
  68.7 44.5 %collective-permute-start.10 = (bf16[192,768]{1,0:T(8,128)(2,1)}, bf16[192,768]{1,0:T(8,128)(2,1)}, u32[]{:S(2)}, u32[]{:S(2)}) collective-permute-start(bf16[192,768]{1,0:T(8,128)(2,1)} %bitcast.177), channel_id=1, source_target_pairs={{8,0},{12,4},{16,8},{20,12},{24,16},{28,20},{32,24},{36,28},{40,32... | collective-permute-start | bytes 884744 | tf_op jit(solution)/shard_map/ppermute | solution.py:16
  75.0 48.3 %collective-permute-start.11 = (bf16[192,768]{1,0:T(8,128)(2,1)}, bf16[192,768]{1,0:T(8,128)(2,1)}, u32[]{:S(2)}, u32[]{:S(2)}) collective-permute-start(bf16[192,768]{1,0:T(8,128)(2,1)} %bitcast.178), channel_id=1, source_target_pairs={{4,0},{8,4},{12,8},{16,12},{20,16},{24,20},{28,24},{32,28},{36,32}... | collective-permute-start | bytes 884744 | tf_op jit(solution)/shard_map/ppermute | solution.py:16
  95.2 8.6 %collective-permute-start.15 = (bf16[768,96]{0,1:T(8,128)(2,1)S(1)}, bf16[768,96]{0,1:T(8,128)(2,1)S(1)}, u32[]{:S(2)}, u32[]{:S(2)}) collective-permute-start(bf16[768,96]{0,1:T(8,128)(2,1)S(1)} %bitcast.163), channel_id=1, source_target_pairs={{0,4},{4,8},{8,12},{12,16},{16,20},{20,24},{24,28},{28,0},{1,5},{5... | collective-permute-start | bytes 442376 | tf_op jit(solution)/shard_map/ppermute | solution.py:169
  103.8 11.4 %collective-permute-start.13 = (bf16[768,96]{0,1:T(8,128)(2,1)S(1)}, bf16[768,96]{0,1:T(8,128)(2,1)S(1)}, u32[]{:S(2)}, u32[]{:S(2)}) collective-permute-start(bf16[768,96]{0,1:T(8,128)(2,1)S(1)} %copy-done.3), channel_id=1, source_target_pairs={{0,28},{4,0},{8,4},{12,8},{16,12},{20,16},{24,20},{28,24},{1,29},{... | collective-permute-start | bytes 442376 | tf_op jit(solution)/shard_map/ppermute | solution.py:172
  105.8 12.7 %collective-permute-start.16 = (bf16[768,96]{0,1:T(8,128)(2,1)S(1)}, bf16[768,96]{0,1:T(8,128)(2,1)S(1)}, u32[]{:S(2)}, u32[]{:S(2)}) collective-permute-start(bf16[768,96]{0,1:T(8,128)(2,1)S(1)} %collective-permute-done.15), channel_id=1, source_target_pairs={{0,4},{4,8},{8,12},{12,16},{16,20},{20,24},{24,28},{28,0},{1,5},{5... | collective-permute-start | bytes 442376 | tf_op jit(solution)/shard_map/ppermute | solution.py:169
  111.7 1.5 copy-start.5
  113.3 12.8 %collective-permute-start.7 = (bf16[192,768]{1,0:T(8,128)(2,1)S(1)}, bf16[192,768]{1,0:T(8,128)(2,1)S(1)}, u32[]{:S(2)}, u32[]{:S(2)}) collective-permute-start(bf16[192,768]{1,0:T(8,128)(2,1)S(1)} %bitcast.179), channel_id=1, source_target_pairs={{0,8},{4,12},{8,16},{12,20},{16,24},{20,28},{24,32},{28,36},{32,40... | collective-permute-start | bytes 884744 | tf_op jit(solution)/shard_map/ppermute | solution.py:16
  115.2 26.2 %collective-permute-start.14 = (bf16[768,96]{0,1:T(8,128)(2,1)S(1)}, bf16[768,96]{0,1:T(8,128)(2,1)S(1)}, u32[]{:S(2)}, u32[]{:S(2)}) collective-permute-start(bf16[768,96]{0,1:T(8,128)(2,1)S(1)} %collective-permute-done.13), channel_id=1, source_target_pairs={{0,28},{4,0},{8,4},{12,8},{16,12},{20,16},{24,20},{28,24},{1,29},{... | collective-permute-start | bytes 442376 | tf_op jit(solution)/shard_map/ppermute | solution.py:172
  118.5 20.9 %collective-permute-start.17 = (bf16[768,96]{0,1:T(8,128)(2,1)S(1)}, bf16[768,96]{0,1:T(8,128)(2,1)S(1)}, u32[]{:S(2)}, u32[]{:S(2)}) collective-permute-start(bf16[768,96]{0,1:T(8,128)(2,1)S(1)} %collective-permute-done.16), channel_id=1, source_target_pairs={{0,4},{4,8},{8,12},{12,16},{16,20},{20,24},{24,28},{28,0},{1,5},{5... | collective-permute-start | bytes 442376 | tf_op jit(solution)/shard_map/ppermute | solution.py:169
  126.6 19.3 %collective-permute-start.19 = (bf16[192,768]{1,0:T(8,128)(2,1)S(1)}, bf16[192,768]{1,0:T(8,128)(2,1)S(1)}, u32[]{:S(2)}, u32[]{:S(2)}) collective-permute-start(bf16[192,768]{1,0:T(8,128)(2,1)S(1)} %bitcast.164), channel_id=1, source_target_pairs={{0,32},{32,64},{64,96},{96,0},{1,33},{33,65},{65,97},{97,1},{2,34}... | collective-permute-start | bytes 884744 | tf_op jit(solution)/shard_map/ppermute | solution.py:179
  129.7 16.8 %collective-permute-start.20 = (bf16[192,768]{1,0:T(8,128)(2,1)S(1)}, bf16[192,768]{1,0:T(8,128)(2,1)S(1)}, u32[]{:S(2)}, u32[]{:S(2)}) collective-permute-start(bf16[192,768]{1,0:T(8,128)(2,1)S(1)} %bitcast.165), channel_id=1, source_target_pairs={{0,64},{32,96},{64,0},{96,32},{1,65},{33,97},{65,1},{97,33},{2,66}... | collective-permute-start | bytes 884744 | tf_op jit(solution)/shard_map/ppermute | solution.py:179
  135.5 12.1 %collective-permute-start.21 = (bf16[192,768]{1,0:T(8,128)(2,1)S(1)}, bf16[192,768]{1,0:T(8,128)(2,1)S(1)}, u32[]{:S(2)}, u32[]{:S(2)}) collective-permute-start(bf16[192,768]{1,0:T(8,128)(2,1)S(1)} %bitcast.166), channel_id=1, source_target_pairs={{0,96},{32,0},{64,32},{96,64},{1,97},{33,1},{65,33},{97,65},{2,98}... | collective-permute-start | bytes 884744 | tf_op jit(solution)/shard_map/ppermute | solution.py:179
  139.5 6.2 %collective-permute-start.18 = (bf16[768,96]{0,1:T(8,128)(2,1)S(1)}, bf16[768,96]{0,1:T(8,128)(2,1)S(1)}, u32[]{:S(2)}, u32[]{:S(2)}) collective-permute-start(bf16[768,96]{0,1:T(8,128)(2,1)S(1)} %collective-permute-done.17), channel_id=1, source_target_pairs={{0,4},{4,8},{8,12},{12,16},{16,20},{20,24},{24,28},{28,0},{1,5},{5... | collective-permute-start | bytes 442376 | tf_op jit(solution)/shard_map/ppermute | solution.py:169
  148.3 11.2 %copy-start.7 = (f32[1,768]{1,0:T(1,128)S(1)}, f32[1,768]{1,0:T(1,128)}, u32[]{:S(2)}) copy-start(f32[1,768]{1,0:T(1,128)} %param.12) | copy-start | bytes 9220
  148.3 78.0 %copy-start.4 = (bf16[1,192,768]{2,1,0:T(8,128)(2,1)S(1)}, bf16[1,192,768]{2,1,0:T(8,128)(2,1)}, u32[]{:S(2)}) copy-start(bf16[1,192,768]{2,1,0:T(8,128)(2,1)} %param.10) | copy-start | bytes 884740
  148.5 38.9 %collective-permute-start.22 = (bf16[192,768]{1,0:T(8,128)(2,1)S(1)}, bf16[192,768]{1,0:T(8,128)(2,1)S(1)}, u32[]{:S(2)}, u32[]{:S(2)}) collective-permute-start(bf16[192,768]{1,0:T(8,128)(2,1)S(1)} %get-tuple-element.5), channel_id=1, source_target_pairs={{0,0},{1,32},{2,64},{3,96},{32,1},{33,33},{34,65},{35,97},{64,2},{... | collective-permute-start | bytes 884744 | tf_op jit(solution)/shard_map/ppermute | solution.py:196
  150.8 36.6 %collective-permute-start.23 = (bf16[192,768]{1,0:T(8,128)(2,1)S(1)}, bf16[192,768]{1,0:T(8,128)(2,1)S(1)}, u32[]{:S(2)}, u32[]{:S(2)}) collective-permute-start(bf16[192,768]{1,0:T(8,128)(2,1)S(1)} %get-tuple-element.8), channel_id=1, source_target_pairs={{0,32},{1,64},{2,96},{3,0},{32,33},{33,65},{34,97},{35,1},{64,34},... | collective-permute-start | bytes 884744 | tf_op jit(solution)/shard_map/ppermute | solution.py:196
  152.7 34.6 %collective-permute-start.24 = (bf16[192,768]{1,0:T(8,128)(2,1)S(1)}, bf16[192,768]{1,0:T(8,128)(2,1)S(1)}, u32[]{:S(2)}, u32[]{:S(2)}) collective-permute-start(bf16[192,768]{1,0:T(8,128)(2,1)S(1)} %get-tuple-element.7), channel_id=1, source_target_pairs={{0,64},{1,96},{2,0},{3,32},{32,65},{33,97},{34,1},{35,33},{64,66},... | collective-permute-start | bytes 884744 | tf_op jit(solution)/shard_map/ppermute | solution.py:196
  155.9 70.4 %collective-permute-start.25 = (bf16[192,768]{1,0:T(8,128)(2,1)S(1)}, bf16[192,768]{1,0:T(8,128)(2,1)S(1)}, u32[]{:S(2)}, u32[]{:S(2)}) collective-permute-start(bf16[192,768]{1,0:T(8,128)(2,1)S(1)} %get-tuple-element.6), channel_id=1, source_target_pairs={{0,96},{1,0},{2,32},{3,64},{32,97},{33,1},{34,33},{35,65},{64,98},... | collective-permute-start | bytes 884744 | tf_op jit(solution)/shard_map/ppermute | solution.py:196
  226.6 19.7 %collective-permute-start.26 = (bf16[192,768]{1,0:T(8,128)(2,1)S(1)}, bf16[192,768]{1,0:T(8,128)(2,1)S(1)}, u32[]{:S(2)}, u32[]{:S(2)}) collective-permute-start(bf16[192,768]{1,0:T(8,128)(2,1)S(1)} %fusion.37), channel_id=1, source_target_pairs={{0,128},{128,256},{256,384},{384,0},{1,129},{129,257},{257,385},{3... | collective-permute-start | bytes 884744 | tf_op jit(solution)/shard_map/ppermute | solution.py:201
  (3 other events, 3.9 us)

commit v3 on v1

--- a/solution.py
+++ b/solution.py
@@ -140,6 +140,8 @@
     query_float = query_parts.astype(jnp.float32)
     query_lengths = jnp.sqrt(jnp.sum(query_float * query_float, axis=2))
     row_bound = query_lengths * jnp.repeat(bound_tiles, tile_rows, axis=0) * score_scale
+    weight_block = lax.all_gather(out_weight[0], "sy", axis=1, tiled=True)
+    weight_block, row_bound = lax.optimization_barrier((weight_block, row_bound))
     running = (
         jnp.zeros((row_count, head_count, HD), jnp.float32),
         jnp.zeros((head_count, row_count), jnp.float32),
@@ -161,12 +163,41 @@
     attended = (
         (weighted / summed.T[:, :, None]).astype(jnp.bfloat16).reshape(row_count, feature_count)
     )
-    token_block = lax.all_gather(attended, "sx", axis=0, tiled=True)
-    weight_block = lax.all_gather(out_weight[0], "sy", axis=1, tiled=True)
-    group_term = jnp.dot(token_block, weight_block, preferred_element_type=jnp.float32)
-    mixed = lax.psum_scatter(
-        group_term.astype(jnp.bfloat16), "head", scatter_dimension=0, tiled=True
-    ).astype(jnp.float32)
+    token_parts = [attended] + [
+        lax.ppermute(attended, "sx", [(i, (i + d) % x_count) for i in range(x_count)])
+        for d in range(1, x_count)
+    ]
+    terms = jnp.stack(
+        [
+            jnp.dot(part, weight_block, preferred_element_type=jnp.float32).astype(jnp.bfloat16)
+            for part in token_parts
+        ]
+    )
+    group_index = lax.axis_index("head")
+
+    def term_for(slab_x):
+        pick = (x_index - jnp.clip(slab_x, 0, head_groups - 1)) % x_count
+        return lax.dynamic_index_in_dim(terms, pick, 0, keepdims=False).astype(jnp.float32)
+
+    last = head_groups - 1
+    upward = None
+    downward = None
+    for step in range(1, head_groups):
+        send_up = term_for(group_index + head_groups - step)
+        if upward is not None:
+            send_up = send_up + upward
+        upward = lax.ppermute(
+            send_up.astype(jnp.bfloat16), "head", [(g, g + 1) for g in range(step)]
+        ).astype(jnp.float32)
+        send_down = term_for(group_index - head_groups + step)
+        if downward is not None:
+            send_down = send_down + downward
+        downward = lax.ppermute(
+            send_down.astype(jnp.bfloat16),
+            "head",
+            [(g, g - 1) for g in range(last, last - step, -1)],
+        ).astype(jnp.float32)
+    mixed = term_for(group_index) + upward + downward
     swap = linear_pairs((x_count, head_groups), lambda a, b: (b, a))
     stream_block = lax.ppermute(stream[0], ("sx", "head"), swap)
     gate_block = lax.ppermute(gate_scale[0], ("sx", "head"), swap)

time: 243 us -> 209 us (0.86)
  the two profiles are of different devices: /device:TPU:6 before, /device:TPU:161 now
where the time goes in v3:
time: 209 us; the launch traced here: 207 us
  starting transfers between devices  83.8 us (40%)
  waiting for transfers between devices  76.5 us (37%)
  between operations  18.2 us (9%)
  matrix products  14.8 us (7%)
  local copies, waits for them, and re-layouts  9.74 us (5%)
  other arithmetic  4.51 us (2%)
    ppermute x12, starting transfers between devices, shifted(): return lax.ppermute(block, axis, route)  41.6 us
    all_gather x1, waiting for transfers between devices, on_device(): weight_block = lax.all_gather(out_weight[0], 'sy', axis=1, tiled=True)  20.1 us
    ppermute x1, starting transfers between devices, on_device(): handed = lax.ppermute(updated, ('section', 'sx', 'head'), hand)  18 us
    ppermute x3, waiting for transfers between devices, on_device(): lax.ppermute(attended, 'sx', [(i, (i + d) % x_count) for i in range(x_cou...  11.7 us
    ppermute x1, waiting for transfers between devices, on_device(): handed = lax.ppermute(updated, ('section', 'sx', 'head'), hand)  11.4 us
    ppermute x1, waiting for transfers between devices, on_device(): gate_block = lax.ppermute(gate_scale[0], ('sx', 'head'), swap)  11.3 us
    ppermute x3, waiting for transfers between devices, on_device(): lax.ppermute(send_down.astype(jnp.bfloat16), 'head', [(g, g - 1) for g in...  9.61 us
    ppermute x3, starting transfers between devices, on_device(): lax.ppermute(send_down.astype(jnp.bfloat16), 'head', [(g, g - 1) for g in...  7.31 us
  transfers between devices with their start and end apart: 25, of which 11 were waited for; matrix products, arithmetic and copies ran while one was open for 13% of the time, Pallas kernels for 0%

profile of v3, /device:TPU:161, one launch (start us, length us, event | category | flops | bytes accessed | tf_op | source)
XLA Modules:
  0.0 207.5 jit_solution(17943205671571099553)
XLA Ops:
  6.5 2.1 collective-permute-start.7
  8.6 2.0 collective-permute-start.6
  11.9 5.8 %collective-permute-start.4 = (bf16[192,768]{1,0:T(8,128)(2,1)}, bf16[192,768]{1,0:T(8,128)(2,1)S(1)}, u32[]{:S(2)}, u32[]{:S(2)}) collective-permute-start(bf16[192,768]{1,0:T(8,128)(2,1)} %bitcast.184), channel_id=1, source_target_pairs={{0,12},{8,20},{16,28},{24,36},{32,44},{40,52},{48,60},{56,68},{64,... | collective-permute-start | bytes 884744 | tf_op jit(solution)/shard_map/ppermute | solution.py:16
  17.7 6.3 %collective-permute-start.3 = (bf16[192,768]{1,0:T(8,128)(2,1)}, bf16[192,768]{1,0:T(8,128)(2,1)S(1)}, u32[]{:S(2)}, u32[]{:S(2)}) collective-permute-start(bf16[192,768]{1,0:T(8,128)(2,1)} %bitcast.185), channel_id=1, source_target_pairs={{0,8},{4,12},{8,16},{12,20},{16,24},{20,28},{24,32},{28,36},{32,40... | collective-permute-start | bytes 884744 | tf_op jit(solution)/shard_map/ppermute | solution.py:16
  33.0 1.9 collective-permute-start.2
  35.7 4.4 %collective-permute-start.13 = (bf16[192,768]{1,0:T(8,128)(2,1)S(1)}, bf16[192,768]{1,0:T(8,128)(2,1)}, u32[]{:S(2)}, u32[]{:S(2)}) collective-permute-start(bf16[192,768]{1,0:T(8,128)(2,1)S(1)} %bitcast.187), channel_id=1, source_target_pairs={{4,0},{8,4},{12,8},{16,12},{20,16},{24,20},{28,24},{32,28},{36,32}... | collective-permute-start | bytes 884744 | tf_op jit(solution)/shard_map/ppermute | solution.py:16
  41.7 5.3 %collective-permute-start.12 = (bf16[192,768]{1,0:T(8,128)(2,1)S(1)}, bf16[192,768]{1,0:T(8,128)(2,1)}, u32[]{:S(2)}, u32[]{:S(2)}) collective-permute-start(bf16[192,768]{1,0:T(8,128)(2,1)S(1)} %bitcast.188), channel_id=1, source_target_pairs={{8,0},{12,4},{16,8},{20,12},{24,16},{28,20},{32,24},{36,28},{40,32... | collective-permute-start | bytes 884744 | tf_op jit(solution)/shard_map/ppermute | solution.py:16
  49.9 7.3 %collective-permute-start.10 = (bf16[192,768]{1,0:T(8,128)(2,1)S(1)}, bf16[192,768]{1,0:T(8,128)(2,1)}, u32[]{:S(2)}, u32[]{:S(2)}) collective-permute-start(bf16[192,768]{1,0:T(8,128)(2,1)S(1)} %bitcast.190), channel_id=1, source_target_pairs={{0,12},{8,20},{16,28},{24,36},{32,44},{40,52},{48,60},{56,68},{64,... | collective-permute-start | bytes 884744 | tf_op jit(solution)/shard_map/ppermute | solution.py:16
  57.9 1.9 collective-permute-start.8
  62.7 20.1 %all-gather.3.cloned.1.call-done = bf16[1,768,768]{1,2,0:T(8,128)(2,1)} async-done(((bf16[1,768,96]{1,2,0:T(8,128)(2,1)}), bf16[1,768,768]{1,2,0:T(8,128)(2,1)}) %all-gather.3.cloned.1.call-update) | async-done | bytes 1179664 | tf_op jit(solution)/shard_map/all_gather | solution.py:143
  85.4 1.4 fusion.96
  87.3 2.1 %collective-permute-start.9 = (bf16[192,768]{1,0:T(8,128)(2,1)S(1)}, bf16[192,768]{1,0:T(8,128)(2,1)S(1)}, u32[]{:S(2)}, u32[]{:S(2)}) collective-permute-start(bf16[192,768]{1,0:T(8,128)(2,1)S(1)} %bitcast.192), channel_id=1, source_target_pairs={{0,8},{4,12},{8,16},{12,20},{16,24},{20,28},{24,32},{28,36},{32,40... | collective-permute-start | bytes 884744 | tf_op jit(solution)/shard_map/ppermute | solution.py:16
  90.8 1.4 fusion.43
  92.7 1.4 fusion.101
  97.8 7.0 %collective-permute-done.9 = bf16[192,768]{1,0:T(8,128)(2,1)S(1)} collective-permute-done((bf16[192,768]{1,0:T(8,128)(2,1)S(1)}, bf16[192,768]{1,0:T(8,128)(2,1)S(1)}, u32[]{:S(2)}, u32[]{:S(2)}) %collective-permute-start.9) | collective-permute-done | bytes 294944 | tf_op jit(solution)/shard_map/ppermute | solution.py:16
  105.4 1.9 collective-permute-start.16
  107.3 1.9 collective-permute-start.15
  109.3 3.4 %collective-permute-start.14 = (bf16[192,768]{1,0:T(8,128)(2,1)S(1)}, bf16[192,768]{1,0:T(8,128)(2,1)S(1)}, u32[]{:S(2)}, u32[]{:S(2)}) collective-permute-start(bf16[192,768]{1,0:T(8,128)(2,1)S(1)} %bitcast.179), channel_id=1, source_target_pairs={{0,32},{32,64},{64,96},{96,0},{1,33},{33,65},{65,97},{97,1},{2,34}... | collective-permute-start | bytes 884744 | tf_op jit(solution)/shard_map/ppermute | solution.py:167
  113.2 1.8 collective-permute-done.16
  115.6 2.3 %collective-permute-done.15 = bf16[192,768]{1,0:T(8,128)(2,1)S(1)} collective-permute-done((bf16[192,768]{1,0:T(8,128)(2,1)S(1)}, bf16[192,768]{1,0:T(8,128)(2,1)S(1)}, u32[]{:S(2)}, u32[]{:S(2)}) %collective-permute-start.15) | collective-permute-done | bytes 294944 | tf_op jit(solution)/shard_map/ppermute | solution.py:167
  118.5 7.5 %collective-permute-done.14 = bf16[192,768]{1,0:T(8,128)(2,1)S(1)} collective-permute-done((bf16[192,768]{1,0:T(8,128)(2,1)S(1)}, bf16[192,768]{1,0:T(8,128)(2,1)S(1)}, u32[]{:S(2)}, u32[]{:S(2)}) %collective-permute-start.14) | collective-permute-done | bytes 294944 | tf_op jit(solution)/shard_map/ppermute | solution.py:167
  127.5 1.4 collective-permute-start.20
  130.4 8.8 %collective-permute-done.20 = bf16[192,768]{1,0:T(8,128)(2,1)S(1)} collective-permute-done((bf16[192,768]{1,0:T(8,128)(2,1)S(1)}, bf16[192,768]{1,0:T(8,128)(2,1)S(1)}, u32[]{:S(2)}, u32[]{:S(2)}) %collective-permute-start.20) | collective-permute-done | bytes 294944 | tf_op jit(solution)/shard_map/ppermute | solution.py:195
  139.2 5.1 %collective-permute-done.18 = bf16[192,768]{1,0:T(8,128)(2,1)S(1)} collective-permute-done((bf16[192,768]{1,0:T(8,128)(2,1)S(1)}, bf16[192,768]{1,0:T(8,128)(2,1)S(1)}, u32[]{:S(2)}, u32[]{:S(2)}) %collective-permute-start.18) | collective-permute-done | bytes 294944 | tf_op jit(solution)/shard_map/ppermute | solution.py:189
  144.4 3.1 %collective-permute-start.21 = (bf16[192,768]{1,0:T(8,128)(2,1)S(1)}, bf16[192,768]{1,0:T(8,128)(2,1)S(1)}, u32[]{:S(2)}, u32[]{:S(2)}) collective-permute-start(bf16[192,768]{1,0:T(8,128)(2,1)S(1)} %get-tuple-element.10), channel_id=1, source_target_pairs={{3,2},{2,1},{7,6},{6,5},{11,10},{10,9},{15,14},{14,13},{19,18},{18... | collective-permute-start | bytes 884744 | tf_op jit(solution)/shard_map/ppermute | solution.py:195
  147.5 1.9 collective-permute-start
  149.5 2.2 %collective-permute-start.19 = (bf16[192,768]{1,0:T(8,128)(2,1)S(1)}, bf16[192,768]{1,0:T(8,128)(2,1)S(1)}, u32[]{:S(2)}, u32[]{:S(2)}) collective-permute-start(bf16[192,768]{1,0:T(8,128)(2,1)S(1)} %get-tuple-element.9), channel_id=1, source_target_pairs={{0,1},{1,2},{2,3},{4,5},{5,6},{6,7},{8,9},{9,10},{10,11},{12,13},{... | collective-permute-start | bytes 884744 | tf_op jit(solution)/shard_map/ppermute | solution.py:189
  152.5 2.8 %collective-permute-start.22 = (bf16[192,768]{1,0:T(8,128)(2,1)S(1)}, bf16[192,768]{1,0:T(8,128)(2,1)S(1)}, u32[]{:S(2)}, u32[]{:S(2)}) collective-permute-start(bf16[192,768]{1,0:T(8,128)(2,1)S(1)} %fusion.34), channel_id=1, source_target_pairs={{3,2},{2,1},{1,0},{7,6},{6,5},{5,4},{11,10},{10,9},{9,8},{15,14},{... | collective-permute-start | bytes 884744 | tf_op jit(solution)/shard_map/ppermute | solution.py:195
  155.4 3.5 %collective-permute-start.1 = (f32[768]{0:T(1024)S(1)}, f32[768]{0:T(1024)S(1)}, u32[]{:S(2)}, u32[]{:S(2)}) collective-permute-start(f32[768]{0:T(1024)S(1)} %reduce.7), channel_id=1, source_target_pairs={{0,0},{1,32},{2,64},{3,96},{32,1},{33,33},{34,65},{35,97},{64,2},{... | collective-permute-start | bytes 9224 | tf_op jit(solution)/shard_map/ppermute | solution.py:203
  158.9 11.3 %collective-permute-done.1 = f32[768]{0:T(1024)S(1)} collective-permute-done((f32[768]{0:T(1024)S(1)}, f32[768]{0:T(1024)S(1)}, u32[]{:S(2)}, u32[]{:S(2)}) %collective-permute-start.1) | collective-permute-done | bytes 3104 | tf_op jit(solution)/shard_map/ppermute | solution.py:203
  170.4 18.0 %collective-permute-start.23 = (bf16[192,768]{1,0:T(8,128)(2,1)S(1)}, bf16[192,768]{1,0:T(8,128)(2,1)S(1)}, u32[]{:S(2)}, u32[]{:S(2)}) collective-permute-start(bf16[192,768]{1,0:T(8,128)(2,1)S(1)} %fusion.40), channel_id=1, source_target_pairs={{0,128},{1,160},{2,192},{3,224},{32,129},{33,161},{34,193},{35,225... | collective-permute-start | bytes 884744 | tf_op jit(solution)/shard_map/ppermute | solution.py:208
  188.5 11.4 %collective-permute-done.23 = bf16[192,768]{1,0:T(8,128)(2,1)S(1)} collective-permute-done((bf16[192,768]{1,0:T(8,128)(2,1)S(1)}, bf16[192,768]{1,0:T(8,128)(2,1)S(1)}, u32[]{:S(2)}, u32[]{:S(2)}) %collective-permute-start.23) | collective-permute-done | bytes 294944 | tf_op jit(solution)/shard_map/ppermute | solution.py:208
  (96 shorter events, 30.4 us)
Async XLA Ops:
  6.5 76.2 %all-gather.3.cloned.1.call-start = ((), (), s32[]{:S(2)}) async-start(), calls=%async_computation | async-start | bytes 1327104 | tf_op jit(solution)/shard_map/all_gather | solution.py:143
  6.5 26.4 %collective-permute-start.7 = (bf16[192,768]{1,0:T(8,128)(2,1)}, bf16[192,768]{1,0:T(8,128)(2,1)S(1)}, u32[]{:S(2)}, u32[]{:S(2)}) collective-permute-start(bf16[192,768]{1,0:T(8,128)(2,1)} %bitcast.181), channel_id=1, source_target_pairs={{4,0},{8,4},{12,8},{16,12},{20,16},{24,20},{28,24},{32,28},{36,32}... | collective-permute-start | bytes 884744 | tf_op jit(solution)/shard_map/ppermute | solution.py:16
  8.6 27.1 %collective-permute-start.6 = (bf16[192,768]{1,0:T(8,128)(2,1)}, bf16[192,768]{1,0:T(8,128)(2,1)}, u32[]{:S(2)}, u32[]{:S(2)}) collective-permute-start(bf16[192,768]{1,0:T(8,128)(2,1)} %bitcast.182), channel_id=1, source_target_pairs={{8,0},{12,4},{16,8},{20,12},{24,16},{28,20},{32,24},{36,28},{40,32... | collective-permute-start | bytes 884744 | tf_op jit(solution)/shard_map/ppermute | solution.py:16
  10.6 31.1 %collective-permute-start.5 = (bf16[192,768]{1,0:T(8,128)(2,1)}, bf16[192,768]{1,0:T(8,128)(2,1)S(1)}, u32[]{:S(2)}, u32[]{:S(2)}) collective-permute-start(bf16[192,768]{1,0:T(8,128)(2,1)} %bitcast.183), channel_id=1, source_target_pairs={{12,0},{20,8},{28,16},{36,24},{44,32},{52,40},{60,48},{68,56},{76,... | collective-permute-start | bytes 884744 | tf_op jit(solution)/shard_map/ppermute | solution.py:16
  11.9 36.0 %collective-permute-start.4 = (bf16[192,768]{1,0:T(8,128)(2,1)}, bf16[192,768]{1,0:T(8,128)(2,1)S(1)}, u32[]{:S(2)}, u32[]{:S(2)}) collective-permute-start(bf16[192,768]{1,0:T(8,128)(2,1)} %bitcast.184), channel_id=1, source_target_pairs={{0,12},{8,20},{16,28},{24,36},{32,44},{40,52},{48,60},{56,68},{64,... | collective-permute-start | bytes 884744 | tf_op jit(solution)/shard_map/ppermute | solution.py:16
  17.7 32.2 %collective-permute-start.3 = (bf16[192,768]{1,0:T(8,128)(2,1)}, bf16[192,768]{1,0:T(8,128)(2,1)S(1)}, u32[]{:S(2)}, u32[]{:S(2)}) collective-permute-start(bf16[192,768]{1,0:T(8,128)(2,1)} %bitcast.185), channel_id=1, source_target_pairs={{0,8},{4,12},{8,16},{12,20},{16,24},{20,28},{24,32},{28,36},{32,40... | collective-permute-start | bytes 884744 | tf_op jit(solution)/shard_map/ppermute | solution.py:16
  24.1 3.3 %copy-start.5 = (s32[16,27]{1,0:T(8,128)S(1)}, s32[16,27]{1,0:T(8,128)}, u32[]{:S(2)}) copy-start(s32[16,27]{1,0:T(8,128)} %param.13) | copy-start | bytes 5188
  25.4 2.7 %copy-start.2 = (bf16[1,192,768]{2,1,0:T(8,128)(2,1)S(1)}, bf16[1,192,768]{2,1,0:T(8,128)(2,1)}, u32[]{:S(2)}) copy-start(bf16[1,192,768]{2,1,0:T(8,128)(2,1)} %param.9) | copy-start | bytes 884740
  26.8 6.2 %copy-start.1 = (bf16[1,192,768]{2,1,0:T(8,128)(2,1)S(1)}, bf16[1,192,768]{2,1,0:T(8,128)(2,1)}, u32[]{:S(2)}) copy-start(bf16[1,192,768]{2,1,0:T(8,128)(2,1)} %param.8) | copy-start | bytes 884740
  33.0 1.9 copy-start.3
  33.0 24.9 %collective-permute-start.2 = (bf16[192,768]{1,0:T(8,128)(2,1)S(1)}, bf16[192,768]{1,0:T(8,128)(2,1)}, u32[]{:S(2)}, u32[]{:S(2)}) collective-permute-start(bf16[192,768]{1,0:T(8,128)(2,1)S(1)} %bitcast.186), channel_id=1, source_target_pairs={{0,4},{4,8},{8,12},{12,16},{16,20},{20,24},{24,28},{28,32},{32,36}... | collective-permute-start | bytes 884744 | tf_op jit(solution)/shard_map/ppermute | solution.py:16
  35.7 51.6 %collective-permute-start.13 = (bf16[192,768]{1,0:T(8,128)(2,1)S(1)}, bf16[192,768]{1,0:T(8,128)(2,1)}, u32[]{:S(2)}, u32[]{:S(2)}) collective-permute-start(bf16[192,768]{1,0:T(8,128)(2,1)S(1)} %bitcast.187), channel_id=1, source_target_pairs={{4,0},{8,4},{12,8},{16,12},{20,16},{24,20},{28,24},{32,28},{36,32}... | collective-permute-start | bytes 884744 | tf_op jit(solution)/shard_map/ppermute | solution.py:16
  41.7 49.1 %collective-permute-start.12 = (bf16[192,768]{1,0:T(8,128)(2,1)S(1)}, bf16[192,768]{1,0:T(8,128)(2,1)}, u32[]{:S(2)}, u32[]{:S(2)}) collective-permute-start(bf16[192,768]{1,0:T(8,128)(2,1)S(1)} %bitcast.188), channel_id=1, source_target_pairs={{8,0},{12,4},{16,8},{20,12},{24,16},{28,20},{32,24},{36,28},{40,32... | collective-permute-start | bytes 884744 | tf_op jit(solution)/shard_map/ppermute | solution.py:16
  47.9 46.2 %collective-permute-start.11 = (bf16[192,768]{1,0:T(8,128)(2,1)S(1)}, bf16[192,768]{1,0:T(8,128)(2,1)}, u32[]{:S(2)}, u32[]{:S(2)}) collective-permute-start(bf16[192,768]{1,0:T(8,128)(2,1)S(1)} %bitcast.189), channel_id=1, source_target_pairs={{12,0},{20,8},{28,16},{36,24},{44,32},{52,40},{60,48},{68,56},{76,... | collective-permute-start | bytes 884744 | tf_op jit(solution)/shard_map/ppermute | solution.py:16
  49.9 45.6 %collective-permute-start.10 = (bf16[192,768]{1,0:T(8,128)(2,1)S(1)}, bf16[192,768]{1,0:T(8,128)(2,1)}, u32[]{:S(2)}, u32[]{:S(2)}) collective-permute-start(bf16[192,768]{1,0:T(8,128)(2,1)S(1)} %bitcast.190), channel_id=1, source_target_pairs={{0,12},{8,20},{16,28},{24,36},{32,44},{40,52},{48,60},{56,68},{64,... | collective-permute-start | bytes 884744 | tf_op jit(solution)/shard_map/ppermute | solution.py:16
  57.9 39.5 %collective-permute-start.8 = (bf16[192,768]{1,0:T(8,128)(2,1)S(1)}, bf16[192,768]{1,0:T(8,128)(2,1)S(1)}, u32[]{:S(2)}, u32[]{:S(2)}) collective-permute-start(bf16[192,768]{1,0:T(8,128)(2,1)S(1)} %bitcast.191), channel_id=1, source_target_pairs={{0,4},{4,8},{8,12},{12,16},{16,20},{20,24},{24,28},{28,32},{32,36}... | collective-permute-start | bytes 884744 | tf_op jit(solution)/shard_map/ppermute | solution.py:16
  87.3 17.5 %collective-permute-start.9 = (bf16[192,768]{1,0:T(8,128)(2,1)S(1)}, bf16[192,768]{1,0:T(8,128)(2,1)S(1)}, u32[]{:S(2)}, u32[]{:S(2)}) collective-permute-start(bf16[192,768]{1,0:T(8,128)(2,1)S(1)} %bitcast.192), channel_id=1, source_target_pairs={{0,8},{4,12},{8,16},{12,20},{16,24},{20,28},{24,32},{28,36},{32,40... | collective-permute-start | bytes 884744 | tf_op jit(solution)/shard_map/ppermute | solution.py:16
  104.8 7.8 %copy-start = (bf16[1,768,768]{1,2,0:T(8,128)(2,1)S(1)}, bf16[1,768,768]{1,2,0:T(8,128)(2,1)}, u32[]{:S(2)}) copy-start(bf16[1,768,768]{1,2,0:T(8,128)(2,1)} %all-gather.3.cloned.1.call-done) | copy-start | bytes 3538948
  105.4 9.7 %collective-permute-start.16 = (bf16[192,768]{1,0:T(8,128)(2,1)S(1)}, bf16[192,768]{1,0:T(8,128)(2,1)S(1)}, u32[]{:S(2)}, u32[]{:S(2)}) collective-permute-start(bf16[192,768]{1,0:T(8,128)(2,1)S(1)} %bitcast.177), channel_id=1, source_target_pairs={{0,96},{32,0},{64,32},{96,64},{1,97},{33,1},{65,33},{97,65},{2,98}... | collective-permute-start | bytes 884744 | tf_op jit(solution)/shard_map/ppermute | solution.py:167
  107.3 10.6 %collective-permute-start.15 = (bf16[192,768]{1,0:T(8,128)(2,1)S(1)}, bf16[192,768]{1,0:T(8,128)(2,1)S(1)}, u32[]{:S(2)}, u32[]{:S(2)}) collective-permute-start(bf16[192,768]{1,0:T(8,128)(2,1)S(1)} %bitcast.178), channel_id=1, source_target_pairs={{0,64},{32,96},{64,0},{96,32},{1,65},{33,97},{65,1},{97,33},{2,66}... | collective-permute-start | bytes 884744 | tf_op jit(solution)/shard_map/ppermute | solution.py:167
  109.3 16.7 %collective-permute-start.14 = (bf16[192,768]{1,0:T(8,128)(2,1)S(1)}, bf16[192,768]{1,0:T(8,128)(2,1)S(1)}, u32[]{:S(2)}, u32[]{:S(2)}) collective-permute-start(bf16[192,768]{1,0:T(8,128)(2,1)S(1)} %bitcast.179), channel_id=1, source_target_pairs={{0,32},{32,64},{64,96},{96,0},{1,33},{33,65},{65,97},{97,1},{2,34}... | collective-permute-start | bytes 884744 | tf_op jit(solution)/shard_map/ppermute | solution.py:167
  126.7 2.2 %collective-permute-start.17 = (bf16[192,768]{1,0:T(8,128)(2,1)S(1)}, bf16[192,768]{1,0:T(8,128)(2,1)S(1)}, u32[]{:S(2)}, u32[]{:S(2)}) collective-permute-start(bf16[192,768]{1,0:T(8,128)(2,1)S(1)} %get-tuple-element.11), channel_id=1, source_target_pairs={{0,1},{4,5},{8,9},{12,13},{16,17},{20,21},{24,25},{28,29},{32,33},... | collective-permute-start | bytes 884744 | tf_op jit(solution)/shard_map/ppermute | solution.py:189
  127.5 20.0 %copy-start.7 = (bf16[1,192,768]{2,1,0:T(8,128)(2,1)S(1)}, bf16[1,192,768]{2,1,0:T(8,128)(2,1)}, u32[]{:S(2)}) copy-start(bf16[1,192,768]{2,1,0:T(8,128)(2,1)} %param.10) | copy-start | bytes 884740
  127.5 11.7 %collective-permute-start.20 = (bf16[192,768]{1,0:T(8,128)(2,1)S(1)}, bf16[192,768]{1,0:T(8,128)(2,1)S(1)}, u32[]{:S(2)}, u32[]{:S(2)}) collective-permute-start(bf16[192,768]{1,0:T(8,128)(2,1)S(1)} %get-tuple-element.12), channel_id=1, source_target_pairs={{3,2},{7,6},{11,10},{15,14},{19,18},{23,22},{27,26},{31,30},{35,34... | collective-permute-start | bytes 884744 | tf_op jit(solution)/shard_map/ppermute | solution.py:195
  129.0 15.3 %collective-permute-start.18 = (bf16[192,768]{1,0:T(8,128)(2,1)S(1)}, bf16[192,768]{1,0:T(8,128)(2,1)S(1)}, u32[]{:S(2)}, u32[]{:S(2)}) collective-permute-start(bf16[192,768]{1,0:T(8,128)(2,1)S(1)} %fusion.35), channel_id=1, source_target_pairs={{0,1},{1,2},{4,5},{5,6},{8,9},{9,10},{12,13},{13,14},{16,17},{17,1... | collective-permute-start | bytes 884744 | tf_op jit(solution)/shard_map/ppermute | solution.py:189
  130.4 25.0 %copy-start.6 = (f32[1,768]{1,0:T(1,128)S(1)}, f32[1,768]{1,0:T(1,128)}, u32[]{:S(2)}) copy-start(f32[1,768]{1,0:T(1,128)} %param.12) | copy-start | bytes 9220
  144.4 8.1 %collective-permute-start.21 = (bf16[192,768]{1,0:T(8,128)(2,1)S(1)}, bf16[192,768]{1,0:T(8,128)(2,1)S(1)}, u32[]{:S(2)}, u32[]{:S(2)}) collective-permute-start(bf16[192,768]{1,0:T(8,128)(2,1)S(1)} %get-tuple-element.10), channel_id=1, source_target_pairs={{3,2},{2,1},{7,6},{6,5},{11,10},{10,9},{15,14},{14,13},{19,18},{18... | collective-permute-start | bytes 884744 | tf_op jit(solution)/shard_map/ppermute | solution.py:195
  147.5 22.7 %collective-permute-start = (bf16[192,768]{1,0:T(8,128)(2,1)S(1)}, bf16[192,768]{1,0:T(8,128)(2,1)S(1)}, u32[]{:S(2)}, u32[]{:S(2)}) collective-permute-start(bf16[192,768]{1,0:T(8,128)(2,1)S(1)} %bitcast.193), channel_id=1, source_target_pairs={{0,0},{1,32},{2,64},{3,96},{32,1},{33,33},{34,65},{35,97},{64,2},{... | collective-permute-start | bytes 884744 | tf_op jit(solution)/shard_map/ppermute | solution.py:202
  149.5 20.8 %collective-permute-start.19 = (bf16[192,768]{1,0:T(8,128)(2,1)S(1)}, bf16[192,768]{1,0:T(8,128)(2,1)S(1)}, u32[]{:S(2)}, u32[]{:S(2)}) collective-permute-start(bf16[192,768]{1,0:T(8,128)(2,1)S(1)} %get-tuple-element.9), channel_id=1, source_target_pairs={{0,1},{1,2},{2,3},{4,5},{5,6},{6,7},{8,9},{9,10},{10,11},{12,13},{... | collective-permute-start | bytes 884744 | tf_op jit(solution)/shard_map/ppermute | solution.py:189
  152.5 17.7 %collective-permute-start.22 = (bf16[192,768]{1,0:T(8,128)(2,1)S(1)}, bf16[192,768]{1,0:T(8,128)(2,1)S(1)}, u32[]{:S(2)}, u32[]{:S(2)}) collective-permute-start(bf16[192,768]{1,0:T(8,128)(2,1)S(1)} %fusion.34), channel_id=1, source_target_pairs={{3,2},{2,1},{1,0},{7,6},{6,5},{5,4},{11,10},{10,9},{9,8},{15,14},{... | collective-permute-start | bytes 884744 | tf_op jit(solution)/shard_map/ppermute | solution.py:195
  155.4 14.9 %collective-permute-start.1 = (f32[768]{0:T(1024)S(1)}, f32[768]{0:T(1024)S(1)}, u32[]{:S(2)}, u32[]{:S(2)}) collective-permute-start(f32[768]{0:T(1024)S(1)} %reduce.7), channel_id=1, source_target_pairs={{0,0},{1,32},{2,64},{3,96},{32,1},{33,33},{34,65},{35,97},{64,2},{... | collective-permute-start | bytes 9224 | tf_op jit(solution)/shard_map/ppermute | solution.py:203
  170.4 29.5 %collective-permute-start.23 = (bf16[192,768]{1,0:T(8,128)(2,1)S(1)}, bf16[192,768]{1,0:T(8,128)(2,1)S(1)}, u32[]{:S(2)}, u32[]{:S(2)}) collective-permute-start(bf16[192,768]{1,0:T(8,128)(2,1)S(1)} %fusion.40), channel_id=1, source_target_pairs={{0,128},{1,160},{2,192},{3,224},{32,129},{33,161},{34,193},{35,225... | collective-permute-start | bytes 884744 | tf_op jit(solution)/shard_map/ppermute | solution.py:208
  (1 other events, 1.0 us)
Sparse Core Ops, SparseCore 0:
  24.2 58.5 all-gather.2

commit v4 on v1

--- a/solution.py
+++ b/solution.py
@@ -140,6 +140,8 @@
     query_float = query_parts.astype(jnp.float32)
     query_lengths = jnp.sqrt(jnp.sum(query_float * query_float, axis=2))
     row_bound = query_lengths * jnp.repeat(bound_tiles, tile_rows, axis=0) * score_scale
+    weight_block = lax.all_gather(out_weight[0], "sy", axis=1, tiled=True)
+    weight_block, row_bound = lax.optimization_barrier((weight_block, row_bound))
     running = (
         jnp.zeros((row_count, head_count, HD), jnp.float32),
         jnp.zeros((head_count, row_count), jnp.float32),
@@ -161,12 +163,18 @@
     attended = (
         (weighted / summed.T[:, :, None]).astype(jnp.bfloat16).reshape(row_count, feature_count)
     )
-    token_block = lax.all_gather(attended, "sx", axis=0, tiled=True)
-    weight_block = lax.all_gather(out_weight[0], "sy", axis=1, tiled=True)
-    group_term = jnp.dot(token_block, weight_block, preferred_element_type=jnp.float32)
-    mixed = lax.psum_scatter(
-        group_term.astype(jnp.bfloat16), "head", scatter_dimension=0, tiled=True
-    ).astype(jnp.float32)
+    spread = jnp.broadcast_to(attended[None], (x_count,) + attended.shape)
+    token_parts = lax.all_to_all(spread, "sx", 0, 0)
+    terms = jnp.stack(
+        [
+            jnp.dot(token_parts[j], weight_block, preferred_element_type=jnp.float32).astype(
+                jnp.bfloat16
+            )
+            for j in range(x_count)
+        ]
+    )
+    arrived = lax.all_to_all(terms, "head", 0, 0)
+    mixed = jnp.sum(arrived.astype(jnp.float32), axis=0)
     swap = linear_pairs((x_count, head_groups), lambda a, b: (b, a))
     stream_block = lax.ppermute(stream[0], ("sx", "head"), swap)
     gate_block = lax.ppermute(gate_scale[0], ("sx", "head"), swap)

time: 243 us -> 203 us (0.84)
  the two profiles are of different devices: /device:TPU:6 before, /device:TPU:100 now
where the time goes in v4:
time: 203 us; the launch traced here: 202 us
  waiting for transfers between devices  69.8 us (34%)
  starting transfers between devices  63.3 us (31%)
  blocking collectives  21.2 us (10%)
  between operations  17.9 us (9%)
  matrix products  14.8 us (7%)
  local copies, waits for them, and re-layouts  9.76 us (5%)
  other arithmetic  5.28 us (3%)
    ppermute x12, starting transfers between devices, shifted(): return lax.ppermute(block, axis, route)  47.4 us
    all_to_all x1, waiting for transfers between devices, on_device(): arrived = lax.all_to_all(terms, 'head', 0, 0)  26.4 us
    all_to_all x1, blocking collectives, on_device(): token_parts = lax.all_to_all(spread, 'sx', 0, 0)  21.2 us
    all_gather x1, waiting for transfers between devices, on_device(): weight_block = lax.all_gather(out_weight[0], 'sy', axis=1, tiled=True)  13.2 us
    ppermute x1, waiting for transfers between devices, on_device(): gate_block = lax.ppermute(gate_scale[0], ('sx', 'head'), swap)  12.9 us
    ppermute x1, waiting for transfers between devices, on_device(): handed = lax.ppermute(updated, ('section', 'sx', 'head'), hand)  12.1 us
    all_to_all x1, starting transfers between devices, on_device(): arrived = lax.all_to_all(terms, 'head', 0, 0)  7.24 us
    dot_general x7, matrix products, attend(): jnp.einsum('hqk,khd->qhd', weights.astype(jnp.bfloat16), slab_values, pre...  6.69 us
  transfers between devices with their start and end apart: 17, of which 5 were waited for; matrix products, arithmetic and copies ran while one was open for 12% of the time, Pallas kernels for 0%

profile of v4, /device:TPU:100, one launch (start us, length us, event | category | flops | bytes accessed | tf_op | source)
XLA Modules:
  0.0 202.0 jit_solution(3575425609159530500)
XLA Ops:
  6.5 2.3 %collective-permute-start.7 = (bf16[192,768]{1,0:T(8,128)(2,1)}, bf16[192,768]{1,0:T(8,128)(2,1)S(1)}, u32[]{:S(2)}, u32[]{:S(2)}) collective-permute-start(bf16[192,768]{1,0:T(8,128)(2,1)} %bitcast.168), channel_id=1, source_target_pairs={{4,0},{8,4},{12,8},{16,12},{20,16},{24,20},{28,24},{32,28},{36,32}... | collective-permute-start | bytes 884744 | tf_op jit(solution)/shard_map/ppermute | solution.py:16
  8.9 2.2 %collective-permute-start.6 = (bf16[192,768]{1,0:T(8,128)(2,1)}, bf16[192,768]{1,0:T(8,128)(2,1)}, u32[]{:S(2)}, u32[]{:S(2)}) collective-permute-start(bf16[192,768]{1,0:T(8,128)(2,1)} %bitcast.169), channel_id=1, source_target_pairs={{8,0},{12,4},{16,8},{20,12},{24,16},{28,20},{32,24},{36,28},{40,32... | collective-permute-start | bytes 884744 | tf_op jit(solution)/shard_map/ppermute | solution.py:16
  11.1 1.3 collective-permute-start.5
  12.4 6.4 %collective-permute-start.4 = (bf16[192,768]{1,0:T(8,128)(2,1)}, bf16[192,768]{1,0:T(8,128)(2,1)S(1)}, u32[]{:S(2)}, u32[]{:S(2)}) collective-permute-start(bf16[192,768]{1,0:T(8,128)(2,1)} %bitcast.171), channel_id=1, source_target_pairs={{0,12},{8,20},{16,28},{24,36},{32,44},{40,52},{48,60},{56,68},{64,... | collective-permute-start | bytes 884744 | tf_op jit(solution)/shard_map/ppermute | solution.py:16
  18.8 6.6 %collective-permute-start.3 = (bf16[192,768]{1,0:T(8,128)(2,1)}, bf16[192,768]{1,0:T(8,128)(2,1)S(1)}, u32[]{:S(2)}, u32[]{:S(2)}) collective-permute-start(bf16[192,768]{1,0:T(8,128)(2,1)} %bitcast.172), channel_id=1, source_target_pairs={{0,8},{4,12},{8,16},{12,20},{16,24},{20,28},{24,32},{28,36},{32,40... | collective-permute-start | bytes 884744 | tf_op jit(solution)/shard_map/ppermute | solution.py:16
  25.5 1.3 reshape_squeeze.11
  26.8 1.4 reshape_squeeze.10
  34.4 1.9 collective-permute-start.2
  37.0 5.1 %collective-permute-start.13 = (bf16[192,768]{1,0:T(8,128)(2,1)S(1)}, bf16[192,768]{1,0:T(8,128)(2,1)}, u32[]{:S(2)}, u32[]{:S(2)}) collective-permute-start(bf16[192,768]{1,0:T(8,128)(2,1)S(1)} %bitcast.174), channel_id=1, source_target_pairs={{4,0},{8,4},{12,8},{16,12},{20,16},{24,20},{28,24},{32,28},{36,32}... | collective-permute-start | bytes 884744 | tf_op jit(solution)/shard_map/ppermute | solution.py:16
  42.1 1.3 reshape.181
  43.7 5.4 %collective-permute-start.12 = (bf16[192,768]{1,0:T(8,128)(2,1)S(1)}, bf16[192,768]{1,0:T(8,128)(2,1)}, u32[]{:S(2)}, u32[]{:S(2)}) collective-permute-start(bf16[192,768]{1,0:T(8,128)(2,1)S(1)} %bitcast.175), channel_id=1, source_target_pairs={{8,0},{12,4},{16,8},{20,12},{24,16},{28,20},{32,24},{36,28},{40,32... | collective-permute-start | bytes 884744 | tf_op jit(solution)/shard_map/ppermute | solution.py:16
  50.0 1.3 collective-permute-start.11
  52.0 7.8 %collective-permute-start.10 = (bf16[192,768]{1,0:T(8,128)(2,1)S(1)}, bf16[192,768]{1,0:T(8,128)(2,1)}, u32[]{:S(2)}, u32[]{:S(2)}) collective-permute-start(bf16[192,768]{1,0:T(8,128)(2,1)S(1)} %bitcast.177), channel_id=1, source_target_pairs={{0,12},{8,20},{16,28},{24,36},{32,44},{40,52},{48,60},{56,68},{64,... | collective-permute-start | bytes 884744 | tf_op jit(solution)/shard_map/ppermute | solution.py:16
  60.5 1.9 collective-permute-start.8
  62.5 1.3 reshape.177
  65.3 13.2 %all-gather.3.cloned.1.call-done = bf16[1,768,768]{1,2,0:T(8,128)(2,1)} async-done(((bf16[1,768,96]{1,2,0:T(8,128)(2,1)}), bf16[1,768,768]{1,2,0:T(8,128)(2,1)}) %all-gather.3.cloned.1.call-update) | async-done | bytes 1179664 | tf_op jit(solution)/shard_map/all_gather | solution.py:143
  81.1 1.4 fusion.88
  83.1 5.0 %collective-permute-start.9 = (bf16[192,768]{1,0:T(8,128)(2,1)S(1)}, bf16[192,768]{1,0:T(8,128)(2,1)S(1)}, u32[]{:S(2)}, u32[]{:S(2)}) collective-permute-start(bf16[192,768]{1,0:T(8,128)(2,1)S(1)} %bitcast.179), channel_id=1, source_target_pairs={{0,8},{4,12},{8,16},{12,20},{16,24},{20,28},{24,32},{28,36},{32,40... | collective-permute-start | bytes 884744 | tf_op jit(solution)/shard_map/ppermute | solution.py:16
  88.1 1.4 fusion.33
  89.5 1.4 fusion.35
  91.3 1.4 fusion.93
  92.8 1.4 fusion.37
  94.1 1.4 fusion.39
  96.4 5.3 %collective-permute-done.9 = bf16[192,768]{1,0:T(8,128)(2,1)S(1)} collective-permute-done((bf16[192,768]{1,0:T(8,128)(2,1)S(1)}, bf16[192,768]{1,0:T(8,128)(2,1)S(1)}, u32[]{:S(2)}, u32[]{:S(2)}) %collective-permute-start.9) | collective-permute-done | bytes 294944 | tf_op jit(solution)/shard_map/ppermute | solution.py:16
  102.3 21.2 %all_to_all.10 = bf16[4,192,768]{2,1,0:T(8,128)(2,1)S(1)} all-to-all(bf16[4,192,768]{2,1,0:T(8,128)(2,1)S(1)} %broadcast_in_dim.198), channel_id=1, replica_groups=mesh['section'=4,'sx'=4,'sy'=8,'head'=4] {'sx'}, dimensions={0} | all-to-all | bytes 2359296 | tf_op jit(solution)/shard_map/all_to_all | solution.py:167
  126.9 7.2 %all-to-all-start.1 = ((bf16[4,192,768]{2,1,0:T(8,128)(2,1)}), bf16[4,192,768]{2,1,0:T(8,128)(2,1)S(1)}, u32[]{:S(2)}, u32[]{:S(2)}) async-start(bf16[4,192,768]{2,1,0:T(8,128)(2,1)} %pad_maximum_fusion), calls=%async_computation.1 | async-start | bytes 2359296 | tf_op jit(solution)/shard_map/all_to_all | solution.py:176
  134.1 4.6 %collective-permute-start = (bf16[192,768]{1,0:T(8,128)(2,1)S(1)}, bf16[192,768]{1,0:T(8,128)(2,1)S(1)}, u32[]{:S(2)}, u32[]{:S(2)}) collective-permute-start(bf16[192,768]{1,0:T(8,128)(2,1)S(1)} %bitcast.180), channel_id=1, source_target_pairs={{0,0},{1,32},{2,64},{3,96},{32,1},{33,33},{34,65},{35,97},{64,2},{... | collective-permute-start | bytes 884744 | tf_op jit(solution)/shard_map/ppermute | solution.py:179
  138.8 2.1 %collective-permute-start.1 = (f32[768]{0:T(1024)S(1)}, f32[768]{0:T(1024)S(1)}, u32[]{:S(2)}, u32[]{:S(2)}) collective-permute-start(f32[768]{0:T(1024)S(1)} %reduce.7), channel_id=1, source_target_pairs={{0,0},{1,32},{2,64},{3,96},{32,1},{33,33},{34,65},{35,97},{64,2},{... | collective-permute-start | bytes 9224 | tf_op jit(solution)/shard_map/ppermute | solution.py:180
  140.9 26.4 %all-to-all-done.1 = bf16[4,192,768]{2,1,0:T(8,128)(2,1)S(1)} async-done(((bf16[4,192,768]{2,1,0:T(8,128)(2,1)}), bf16[4,192,768]{2,1,0:T(8,128)(2,1)S(1)}, u32[]{:S(2)}, u32[]{:S(2)}) %all-to-all-start.1) | async-done | bytes 1179680 | tf_op jit(solution)/shard_map/all_to_all | solution.py:176
  167.4 12.9 %collective-permute-done.1 = f32[768]{0:T(1024)S(1)} collective-permute-done((f32[768]{0:T(1024)S(1)}, f32[768]{0:T(1024)S(1)}, u32[]{:S(2)}, u32[]{:S(2)}) %collective-permute-start.1) | collective-permute-done | bytes 3104 | tf_op jit(solution)/shard_map/ppermute | solution.py:180
  180.4 1.9 collective-permute-start.14
  182.3 12.1 %collective-permute-done.14 = bf16[192,768]{1,0:T(8,128)(2,1)S(1)} collective-permute-done((bf16[192,768]{1,0:T(8,128)(2,1)S(1)}, bf16[192,768]{1,0:T(8,128)(2,1)S(1)}, u32[]{:S(2)}, u32[]{:S(2)}) %collective-permute-start.14) | collective-permute-done | bytes 294944 | tf_op jit(solution)/shard_map/ppermute | solution.py:185
  (79 shorter events, 16.3 us)
Async XLA Ops:
  6.5 71.9 %all-gather.3.cloned.1.call-start = ((), (), s32[]{:S(2)}) async-start(), calls=%async_computation.2 | async-start | bytes 1327104 | tf_op jit(solution)/shard_map/all_gather | solution.py:143
  6.5 27.8 %collective-permute-start.7 = (bf16[192,768]{1,0:T(8,128)(2,1)}, bf16[192,768]{1,0:T(8,128)(2,1)S(1)}, u32[]{:S(2)}, u32[]{:S(2)}) collective-permute-start(bf16[192,768]{1,0:T(8,128)(2,1)} %bitcast.168), channel_id=1, source_target_pairs={{4,0},{8,4},{12,8},{16,12},{20,16},{24,20},{28,24},{32,28},{36,32}... | collective-permute-start | bytes 884744 | tf_op jit(solution)/shard_map/ppermute | solution.py:16
  8.9 28.1 %collective-permute-start.6 = (bf16[192,768]{1,0:T(8,128)(2,1)}, bf16[192,768]{1,0:T(8,128)(2,1)}, u32[]{:S(2)}, u32[]{:S(2)}) collective-permute-start(bf16[192,768]{1,0:T(8,128)(2,1)} %bitcast.169), channel_id=1, source_target_pairs={{8,0},{12,4},{16,8},{20,12},{24,16},{28,20},{32,24},{36,28},{40,32... | collective-permute-start | bytes 884744 | tf_op jit(solution)/shard_map/ppermute | solution.py:16
  11.1 32.5 %collective-permute-start.5 = (bf16[192,768]{1,0:T(8,128)(2,1)}, bf16[192,768]{1,0:T(8,128)(2,1)S(1)}, u32[]{:S(2)}, u32[]{:S(2)}) collective-permute-start(bf16[192,768]{1,0:T(8,128)(2,1)} %bitcast.170), channel_id=1, source_target_pairs={{12,0},{20,8},{28,16},{36,24},{44,32},{52,40},{60,48},{68,56},{76,... | collective-permute-start | bytes 884744 | tf_op jit(solution)/shard_map/ppermute | solution.py:16
  12.4 37.5 %collective-permute-start.4 = (bf16[192,768]{1,0:T(8,128)(2,1)}, bf16[192,768]{1,0:T(8,128)(2,1)S(1)}, u32[]{:S(2)}, u32[]{:S(2)}) collective-permute-start(bf16[192,768]{1,0:T(8,128)(2,1)} %bitcast.171), channel_id=1, source_target_pairs={{0,12},{8,20},{16,28},{24,36},{32,44},{40,52},{48,60},{56,68},{64,... | collective-permute-start | bytes 884744 | tf_op jit(solution)/shard_map/ppermute | solution.py:16
  18.8 33.2 %collective-permute-start.3 = (bf16[192,768]{1,0:T(8,128)(2,1)}, bf16[192,768]{1,0:T(8,128)(2,1)S(1)}, u32[]{:S(2)}, u32[]{:S(2)}) collective-permute-start(bf16[192,768]{1,0:T(8,128)(2,1)} %bitcast.172), channel_id=1, source_target_pairs={{0,8},{4,12},{8,16},{12,20},{16,24},{20,28},{24,32},{28,36},{32,40... | collective-permute-start | bytes 884744 | tf_op jit(solution)/shard_map/ppermute | solution.py:16
  25.5 3.3 %copy-start.5 = (s32[16,27]{1,0:T(8,128)S(1)}, s32[16,27]{1,0:T(8,128)}, u32[]{:S(2)}) copy-start(s32[16,27]{1,0:T(8,128)} %param.13) | copy-start | bytes 5188
  26.8 2.7 %copy-start.2 = (bf16[1,192,768]{2,1,0:T(8,128)(2,1)S(1)}, bf16[1,192,768]{2,1,0:T(8,128)(2,1)}, u32[]{:S(2)}) copy-start(bf16[1,192,768]{2,1,0:T(8,128)(2,1)} %param.9) | copy-start | bytes 884740
  28.2 6.2 %copy-start.1 = (bf16[1,192,768]{2,1,0:T(8,128)(2,1)S(1)}, bf16[1,192,768]{2,1,0:T(8,128)(2,1)}, u32[]{:S(2)}) copy-start(bf16[1,192,768]{2,1,0:T(8,128)(2,1)} %param.8) | copy-start | bytes 884740
  34.4 1.9 copy-start.3
  34.4 26.2 %collective-permute-start.2 = (bf16[192,768]{1,0:T(8,128)(2,1)S(1)}, bf16[192,768]{1,0:T(8,128)(2,1)}, u32[]{:S(2)}, u32[]{:S(2)}) collective-permute-start(bf16[192,768]{1,0:T(8,128)(2,1)S(1)} %bitcast.173), channel_id=1, source_target_pairs={{0,4},{4,8},{8,12},{12,16},{16,20},{20,24},{24,28},{28,32},{32,36}... | collective-permute-start | bytes 884744 | tf_op jit(solution)/shard_map/ppermute | solution.py:16
  37.0 46.1 %collective-permute-start.13 = (bf16[192,768]{1,0:T(8,128)(2,1)S(1)}, bf16[192,768]{1,0:T(8,128)(2,1)}, u32[]{:S(2)}, u32[]{:S(2)}) collective-permute-start(bf16[192,768]{1,0:T(8,128)(2,1)S(1)} %bitcast.174), channel_id=1, source_target_pairs={{4,0},{8,4},{12,8},{16,12},{20,16},{24,20},{28,24},{32,28},{36,32}... | collective-permute-start | bytes 884744 | tf_op jit(solution)/shard_map/ppermute | solution.py:16
  43.7 45.7 %collective-permute-start.12 = (bf16[192,768]{1,0:T(8,128)(2,1)S(1)}, bf16[192,768]{1,0:T(8,128)(2,1)}, u32[]{:S(2)}, u32[]{:S(2)}) collective-permute-start(bf16[192,768]{1,0:T(8,128)(2,1)S(1)} %bitcast.175), channel_id=1, source_target_pairs={{8,0},{12,4},{16,8},{20,12},{24,16},{28,20},{32,24},{36,28},{40,32... | collective-permute-start | bytes 884744 | tf_op jit(solution)/shard_map/ppermute | solution.py:16
  50.0 42.8 %collective-permute-start.11 = (bf16[192,768]{1,0:T(8,128)(2,1)S(1)}, bf16[192,768]{1,0:T(8,128)(2,1)}, u32[]{:S(2)}, u32[]{:S(2)}) collective-permute-start(bf16[192,768]{1,0:T(8,128)(2,1)S(1)} %bitcast.176), channel_id=1, source_target_pairs={{12,0},{20,8},{28,16},{36,24},{44,32},{52,40},{60,48},{68,56},{76,... | collective-permute-start | bytes 884744 | tf_op jit(solution)/shard_map/ppermute | solution.py:16
  52.0 42.1 %collective-permute-start.10 = (bf16[192,768]{1,0:T(8,128)(2,1)S(1)}, bf16[192,768]{1,0:T(8,128)(2,1)}, u32[]{:S(2)}, u32[]{:S(2)}) collective-permute-start(bf16[192,768]{1,0:T(8,128)(2,1)S(1)} %bitcast.177), channel_id=1, source_target_pairs={{0,12},{8,20},{16,28},{24,36},{32,44},{40,52},{48,60},{56,68},{64,... | collective-permute-start | bytes 884744 | tf_op jit(solution)/shard_map/ppermute | solution.py:16
  60.5 35.5 %collective-permute-start.8 = (bf16[192,768]{1,0:T(8,128)(2,1)S(1)}, bf16[192,768]{1,0:T(8,128)(2,1)S(1)}, u32[]{:S(2)}, u32[]{:S(2)}) collective-permute-start(bf16[192,768]{1,0:T(8,128)(2,1)S(1)} %bitcast.178), channel_id=1, source_target_pairs={{0,4},{4,8},{8,12},{12,16},{16,20},{20,24},{24,28},{28,32},{32,36}... | collective-permute-start | bytes 884744 | tf_op jit(solution)/shard_map/ppermute | solution.py:16
  79.7 1.0 copy-start.4
  83.1 18.6 %collective-permute-start.9 = (bf16[192,768]{1,0:T(8,128)(2,1)S(1)}, bf16[192,768]{1,0:T(8,128)(2,1)S(1)}, u32[]{:S(2)}, u32[]{:S(2)}) collective-permute-start(bf16[192,768]{1,0:T(8,128)(2,1)S(1)} %bitcast.179), channel_id=1, source_target_pairs={{0,8},{4,12},{8,16},{12,20},{16,24},{20,28},{24,32},{28,36},{32,40... | collective-permute-start | bytes 884744 | tf_op jit(solution)/shard_map/ppermute | solution.py:16
  102.3 21.2 %copy-start = (bf16[1,768,768]{1,2,0:T(8,128)(2,1)S(1)}, bf16[1,768,768]{1,2,0:T(8,128)(2,1)}, u32[]{:S(2)}) copy-start(bf16[1,768,768]{1,2,0:T(8,128)(2,1)} %all-gather.3.cloned.1.call-done) | copy-start | bytes 3538948
  126.9 7.3 %copy-start.7 = (bf16[1,192,768]{2,1,0:T(8,128)(2,1)S(1)}, bf16[1,192,768]{2,1,0:T(8,128)(2,1)}, u32[]{:S(2)}) copy-start(bf16[1,192,768]{2,1,0:T(8,128)(2,1)} %param.10) | copy-start | bytes 884740
  126.9 11.9 %copy-start.6 = (f32[1,768]{1,0:T(1,128)S(1)}, f32[1,768]{1,0:T(1,128)}, u32[]{:S(2)}) copy-start(f32[1,768]{1,0:T(1,128)} %param.12) | copy-start | bytes 9220
  126.9 40.4 %all-to-all-start.1 = ((bf16[4,192,768]{2,1,0:T(8,128)(2,1)}), bf16[4,192,768]{2,1,0:T(8,128)(2,1)S(1)}, u32[]{:S(2)}, u32[]{:S(2)}) async-start(bf16[4,192,768]{2,1,0:T(8,128)(2,1)} %pad_maximum_fusion), calls=%async_computation.1 | async-start | bytes 2359296 | tf_op jit(solution)/shard_map/all_to_all | solution.py:176
  134.1 46.2 %collective-permute-start = (bf16[192,768]{1,0:T(8,128)(2,1)S(1)}, bf16[192,768]{1,0:T(8,128)(2,1)S(1)}, u32[]{:S(2)}, u32[]{:S(2)}) collective-permute-start(bf16[192,768]{1,0:T(8,128)(2,1)S(1)} %bitcast.180), channel_id=1, source_target_pairs={{0,0},{1,32},{2,64},{3,96},{32,1},{33,33},{34,65},{35,97},{64,2},{... | collective-permute-start | bytes 884744 | tf_op jit(solution)/shard_map/ppermute | solution.py:179
  138.8 41.5 %collective-permute-start.1 = (f32[768]{0:T(1024)S(1)}, f32[768]{0:T(1024)S(1)}, u32[]{:S(2)}, u32[]{:S(2)}) collective-permute-start(f32[768]{0:T(1024)S(1)} %reduce.7), channel_id=1, source_target_pairs={{0,0},{1,32},{2,64},{3,96},{32,1},{33,33},{34,65},{35,97},{64,2},{... | collective-permute-start | bytes 9224 | tf_op jit(solution)/shard_map/ppermute | solution.py:180
  180.4 14.0 %collective-permute-start.14 = (bf16[192,768]{1,0:T(8,128)(2,1)S(1)}, bf16[192,768]{1,0:T(8,128)(2,1)S(1)}, u32[]{:S(2)}, u32[]{:S(2)}) collective-permute-start(bf16[192,768]{1,0:T(8,128)(2,1)S(1)} %add_convert_fusion), channel_id=1, source_target_pairs={{0,128},{1,160},{2,192},{3,224},{32,129},{33,161},{34,193},{35,225... | collective-permute-start | bytes 884744 | tf_op jit(solution)/shard_map/ppermute | solution.py:185
Sparse Core Ops, SparseCore 0:
  25.6 52.8 all-gather.2

commit v5 on v4

--- a/solution.py
+++ b/solution.py
@@ -111,57 +111,85 @@
     x_index = lax.axis_index("sx")
     y_index = lax.axis_index("sy")
     position = x_index * y_count + y_index
+    parity = position % 2
     temporal = position // 2
     allowed = jnp.any(
         windows[:, :, None] == jnp.arange(tile_count, dtype=jnp.int32)[None, None, :], axis=1
     )
-    nearby = lax.dynamic_slice_in_dim(allowed, temporal * spatial_count, spatial_count, 0)
-    always = jnp.array(True)
-    slabs = [(own_keys, own_values, temporal, always)]
-    reach = min(3, seq_count - 1)
-    offsets = list(range(1, reach + 1)) + list(range(-reach, 0))
-    for offset in offsets:
-        moved_keys, moved_values = shifted(
-            (own_keys, own_values), ("sx", "sy"), seq_count, offset, needs(offset)
-        )
-        source = position - offset
-        in_range = (source >= 0) & (source < seq_count)
-        slabs.append((moved_keys, moved_values, source // 2, in_range))
-    keeps = [
-        slab_keep(nearby, slab_entry[2], slab_entry[3], spatial_count, temporal_count)
-        for slab_entry in slabs
-    ]
-    bound_tiles = jnp.zeros((spatial_count, head_count), jnp.float32)
-    for slab_entry, keep in zip(slabs, keeps):
-        maxima = tile_maxima(slab_entry[0], head_count, spatial_count)
-        candidate = jnp.where(keep[:, :, None], maxima[None, :, :], 0.0)
-        bound_tiles = jnp.maximum(bound_tiles, jnp.max(candidate, axis=1))
-    query_parts = split_heads(queries, head_count)
+    row_allowed = lax.dynamic_index_in_dim(allowed, temporal, 0, keepdims=False)
+    seq = ("sx", "sy")
+    half = feature_count // 2
+    own_heads = head_count // 2
+    tile_len = 2 * row_count
+    partner = [(i, i ^ 1) for i in range(seq_count)]
+
+    def partner_half(block):
+        return lax.dynamic_slice_in_dim(block, (1 - parity) * half, half, 1)
+
+    def own_half(block):
+        return lax.dynamic_slice_in_dim(block, parity * half, half, 1)
+
+    sent = lax.ppermute(
+        (partner_half(queries), partner_half(own_keys), partner_half(own_values)), seq, partner
+    )
+
+    def whole_tile(mine, theirs):
+        return jnp.where(
+            parity == 0,
+            jnp.concatenate([mine, theirs], axis=0),
+            jnp.concatenate([theirs, mine], axis=0),
+        )
+
+    tile_q = whole_tile(own_half(queries), sent[0])
+    tile_k = whole_tile(own_half(own_keys), sent[1])
+    tile_v = whole_tile(own_half(own_values), sent[2])
+    before = lax.ppermute((tile_k, tile_v), seq, [(i, i + 2) for i in range(seq_count - 2)])
+    after = lax.ppermute((tile_k, tile_v), seq, [(i, i - 2) for i in range(2, seq_count)])
+    key_tiles = [before, (tile_k, tile_v), after]
+    keeps = []
+    for step in (-1, 0, 1):
+        near = temporal + step
+        in_range = (near >= 0) & (near < temporal_count)
+        listed = lax.dynamic_index_in_dim(
+            row_allowed, jnp.clip(near, 0, temporal_count - 1), 0, keepdims=False
+        )
+        keeps.append(in_range & listed)
+    bound = jnp.zeros((own_heads,), jnp.float32)
+    for (keys, _), keep in zip(key_tiles, keeps):
+        key_float = keys.reshape(tile_len, own_heads, HD).astype(jnp.float32)
+        key_lengths = jnp.sqrt(jnp.sum(key_float * key_float, axis=2))
+        bound = jnp.maximum(bound, jnp.where(keep, jnp.max(key_lengths, axis=0), 0.0))
+    query_parts = tile_q.reshape(tile_len, own_heads, HD)
     query_float = query_parts.astype(jnp.float32)
     query_lengths = jnp.sqrt(jnp.sum(query_float * query_float, axis=2))
-    row_bound = query_lengths * jnp.repeat(bound_tiles, tile_rows, axis=0) * score_scale
+    row_bound = query_lengths * bound[None, :] * score_scale
     weight_block = lax.all_gather(out_weight[0], "sy", axis=1, tiled=True)
     weight_block, row_bound = lax.optimization_barrier((weight_block, row_bound))
-    running = (
-        jnp.zeros((row_count, head_count, HD), jnp.float32),
-        jnp.zeros((head_count, row_count), jnp.float32),
-    )
-    for slab_entry, keep in zip(slabs, keeps):
-        step_fn = partial(
-            attend,
-            slab_entry=slab_entry,
-            keep=keep,
-            query_parts=query_parts,
-            row_bound=row_bound,
-            head_count=head_count,
-            spatial_count=spatial_count,
-            tile_rows=tile_rows,
-            score_scale=score_scale,
-        )
-        running = step_fn(running)
-    weighted, summed = running
-    attended = (
-        (weighted / summed.T[:, :, None]).astype(jnp.bfloat16).reshape(row_count, feature_count)
+    weighted = jnp.zeros((tile_len, own_heads, HD), jnp.float32)
+    summed = jnp.zeros((own_heads, tile_len), jnp.float32)
+    for (keys, values), keep in zip(key_tiles, keeps):
+        key_parts = keys.reshape(tile_len, own_heads, HD)
+        value_parts = values.reshape(tile_len, own_heads, HD)
+        scores = (
+            jnp.einsum("qhd,khd->hqk", query_parts, key_parts, preferred_element_type=jnp.float32)
+            * score_scale
+        )
+        weights = jnp.where(keep, jnp.exp(scores - row_bound.T[:, :, None]), 0.0)
+        summed = summed + jnp.sum(weights, axis=2)
+        weighted = weighted + jnp.einsum(
+            "hqk,khd->qhd",
+            weights.astype(jnp.bfloat16),
+            value_parts,
+            preferred_element_type=jnp.float32,
+        )
+    tile_out = (weighted / summed.T[:, :, None]).astype(jnp.bfloat16).reshape(tile_len, half)
+    mine_rows = lax.dynamic_slice_in_dim(tile_out, parity * row_count, row_count, 0)
+    their_rows = lax.dynamic_slice_in_dim(tile_out, (1 - parity) * row_count, row_count, 0)
+    back = lax.ppermute(their_rows, seq, partner)
+    attended = jnp.where(
+        parity == 0,
+        jnp.concatenate([mine_rows, back], axis=1),
+        jnp.concatenate([back, mine_rows], axis=1),
     )
     spread = jnp.broadcast_to(attended[None], (x_count,) + attended.shape)
     token_parts = lax.all_to_all(spread, "sx", 0, 0)

time: 203 us -> 176 us (0.87)
  the two profiles are of different devices: /device:TPU:100 before, /device:TPU:92 now
where the time goes in v5:
time: 176 us
  waiting for transfers between devices  83.8 us (48%)
  starting transfers between devices  43.5 us (25%)
  blocking collectives  15.9 us (9%)
  between operations  15.7 us (9%)
  local copies, waits for them, and re-layouts  6.18 us (4%)
  other arithmetic  5.5 us (3%)
  matrix products  5.21 us (3%)
    all_to_all x1, waiting for transfers between devices, on_device(): arrived = lax.all_to_all(terms, 'head', 0, 0)  25.6 us
    ppermute x2, waiting for transfers between devices, on_device(): lax.ppermute((tile_k, tile_v), seq, [(i, i - 2) for i in range(2, seq_cou...  18.5 us
    all_to_all x1, blocking collectives, on_device(): token_parts = lax.all_to_all(spread, 'sx', 0, 0)  15.9 us
    ppermute x1, waiting for transfers between devices, on_device(): handed = lax.ppermute(updated, ('section', 'sx', 'head'), hand)  12.6 us
    ppermute x1, waiting for transfers between devices, on_device(): gate_block = lax.ppermute(gate_scale[0], ('sx', 'head'), swap)  12.4 us
    ppermute x2, starting transfers between devices, on_device(): lax.ppermute((tile_k, tile_v), seq, [(i, i + 2) for i in range(seq_count...  10.2 us
    all_to_all x1, starting transfers between devices, on_device(): arrived = lax.all_to_all(terms, 'head', 0, 0)  8.79 us
    ppermute x2, waiting for transfers between devices, on_device(): lax.ppermute((tile_k, tile_v), seq, [(i, i + 2) for i in range(seq_count...  8.62 us
  transfers between devices with their start and end apart: 13, of which 7 were waited for; matrix products, arithmetic and copies ran while one was open for 5% of the time, Pallas kernels for 0%

profile of v5, /device:TPU:92, one launch (start us, length us, event | category | flops | bytes accessed | tf_op | source)
XLA Modules:
  0.0 175.7 jit_solution(4404449519243086594)
XLA Ops:
  6.5 0.7 all-gather.3.cloned.1.call-update
  7.3 1.0 dynamic-slice_bitcast_fusion.1
  8.3 2.4 %collective-permute-start.4 = (bf16[192,384]{1,0:T(8,128)(2,1)S(1)}, bf16[192,384]{1,0:T(8,128)(2,1)S(1)}, u32[]{:S(2)}, u32[]{:S(2)}) collective-permute-start(bf16[192,384]{1,0:T(8,128)(2,1)S(1)} %get-tuple-element.19), channel_id=1, source_target_pairs={{0,4},{4,0},{8,12},{12,8},{16,20},{20,16},{24,28},{28,24},{32,36},... | collective-permute-start | bytes 442376 | tf_op jit(solution)/shard_map/ppermute | solution.py:132
  10.7 1.0 constant_dynamic-slice_fusion.2
  11.7 3.5 %collective-permute-start.5 = (bf16[192,384]{1,0:T(8,128)(2,1)S(1)}, bf16[192,384]{1,0:T(8,128)(2,1)S(1)}, u32[]{:S(2)}, u32[]{:S(2)}) collective-permute-start(bf16[192,384]{1,0:T(8,128)(2,1)S(1)} %get-tuple-element.18), channel_id=1, source_target_pairs={{0,4},{4,0},{8,12},{12,8},{16,20},{20,16},{24,28},{28,24},{32,36},... | collective-permute-start | bytes 442376 | tf_op jit(solution)/shard_map/ppermute | solution.py:132
  15.3 2.4 %collective-permute-start.2 = (bf16[192,384]{1,0:T(8,128)(2,1)S(1)}, bf16[192,384]{1,0:T(8,128)(2,1)S(1)}, u32[]{:S(2)}, u32[]{:S(2)}) collective-permute-start(bf16[192,384]{1,0:T(8,128)(2,1)S(1)} %get-tuple-element.16), channel_id=1, source_target_pairs={{0,4},{4,0},{8,12},{12,8},{16,20},{20,16},{24,28},{28,24},{32,36},... | collective-permute-start | bytes 442376 | tf_op jit(solution)/shard_map/ppermute | solution.py:132
  18.2 0.7 fusion.22
  20.8 0.8 maximum_select_fusion.5
  21.6 5.7 %collective-permute-start.6 = (bf16[384,384]{1,0:T(8,128)(2,1)}, bf16[384,384]{1,0:T(8,128)(2,1)S(1)}, u32[]{:S(2)}, u32[]{:S(2)}) collective-permute-start(bf16[384,384]{1,0:T(8,128)(2,1)} %maximum_select_fusion.5), channel_id=1, source_target_pairs={{0,8},{4,12},{8,16},{12,20},{16,24},{20,28},{24,32},{28,36},{32,40... | collective-permute-start | bytes 884744 | tf_op jit(solution)/shard_map/ppermute | solution.py:146
  27.3 1.9 %collective-permute-start.7 = (bf16[384,384]{1,0:T(8,128)(2,1)}, bf16[384,384]{1,0:T(8,128)(2,1)S(1)}, u32[]{:S(2)}, u32[]{:S(2)}) collective-permute-start(bf16[384,384]{1,0:T(8,128)(2,1)} %maximum_select_fusion.5), channel_id=1, source_target_pairs={{8,0},{12,4},{16,8},{20,12},{24,16},{28,20},{32,24},{36,28},{40,32... | collective-permute-start | bytes 884744 | tf_op jit(solution)/shard_map/ppermute | solution.py:147
  29.2 0.8 maximum_select_fusion.4
  30.0 3.5 %collective-permute-start.8 = (bf16[384,384]{1,0:T(8,128)(2,1)}, bf16[384,384]{1,0:T(8,128)(2,1)}, u32[]{:S(2)}, u32[]{:S(2)}) collective-permute-start(bf16[384,384]{1,0:T(8,128)(2,1)} %maximum_select_fusion.4), channel_id=1, source_target_pairs={{8,0},{12,4},{16,8},{20,12},{24,16},{28,20},{32,24},{36,28},{40,32... | collective-permute-start | bytes 884744 | tf_op jit(solution)/shard_map/ppermute | solution.py:147
  33.5 4.5 %collective-permute-start.3 = (bf16[384,384]{1,0:T(8,128)(2,1)}, bf16[384,384]{1,0:T(8,128)(2,1)S(1)}, u32[]{:S(2)}, u32[]{:S(2)}) collective-permute-start(bf16[384,384]{1,0:T(8,128)(2,1)} %maximum_select_fusion.4), channel_id=1, source_target_pairs={{0,8},{4,12},{8,16},{12,20},{16,24},{20,28},{24,32},{28,36},{32,40... | collective-permute-start | bytes 884744 | tf_op jit(solution)/shard_map/ppermute | solution.py:146
  39.8 8.6 %collective-permute-done.6 = bf16[384,384]{1,0:T(8,128)(2,1)S(1)} collective-permute-done((bf16[384,384]{1,0:T(8,128)(2,1)}, bf16[384,384]{1,0:T(8,128)(2,1)S(1)}, u32[]{:S(2)}, u32[]{:S(2)}) %collective-permute-start.6) | collective-permute-done | bytes 294944 | tf_op jit(solution)/shard_map/ppermute | solution.py:146
  48.6 3.3 %collective-permute-done.7 = bf16[384,384]{1,0:T(8,128)(2,1)S(1)} collective-permute-done((bf16[384,384]{1,0:T(8,128)(2,1)}, bf16[384,384]{1,0:T(8,128)(2,1)S(1)}, u32[]{:S(2)}, u32[]{:S(2)}) %collective-permute-start.7) | collective-permute-done | bytes 294944 | tf_op jit(solution)/shard_map/ppermute | solution.py:147
  52.1 15.2 %collective-permute-done.8 = bf16[384,384]{1,0:T(8,128)(2,1)} collective-permute-done((bf16[384,384]{1,0:T(8,128)(2,1)}, bf16[384,384]{1,0:T(8,128)(2,1)}, u32[]{:S(2)}, u32[]{:S(2)}) %collective-permute-start.8) | collective-permute-done | bytes 294944 | tf_op jit(solution)/shard_map/ppermute | solution.py:147
  67.3 1.2 copy.89
  69.4 0.7 fusion.23
  70.0 0.6 fusion.24
  70.7 0.6 fusion.25
  72.6 2.3 %collective-permute-start.9 = (bf16[192,384]{0,1:T(8,128)(2,1)S(1)}, bf16[192,384]{0,1:T(8,128)(2,1)S(1)}, u32[]{:S(2)}, u32[]{:S(2)}) collective-permute-start(bf16[192,384]{0,1:T(8,128)(2,1)S(1)} %get-tuple-element.14), channel_id=1, source_target_pairs={{0,4},{4,0},{8,12},{12,8},{16,20},{20,16},{24,28},{28,24},{32,36},... | collective-permute-start | bytes 442376 | tf_op jit(solution)/shard_map/ppermute | solution.py:188
  74.9 5.3 %collective-permute-done.9 = bf16[192,384]{0,1:T(8,128)(2,1)S(1)} collective-permute-done((bf16[192,384]{0,1:T(8,128)(2,1)S(1)}, bf16[192,384]{0,1:T(8,128)(2,1)S(1)}, u32[]{:S(2)}, u32[]{:S(2)}) %collective-permute-start.9) | collective-permute-done | bytes 147488 | tf_op jit(solution)/shard_map/ppermute | solution.py:188
  80.5 15.9 %all_to_all.10 = bf16[4,192,768]{2,1,0:T(8,128)(2,1)S(1)} all-to-all(bf16[4,192,768]{2,1,0:T(8,128)(2,1)S(1)} %broadcast_in_dim.31), channel_id=1, replica_groups=mesh['section'=4,'sx'=4,'sy'=8,'head'=4] {'sx'}, dimensions={0} | all-to-all | bytes 2359296 | tf_op jit(solution)/shard_map/all_to_all | solution.py:195
  98.6 1.2 pad_maximum_fusion
  99.8 8.8 %all-to-all-start.1 = ((bf16[4,192,768]{2,1,0:T(8,128)(2,1)}), bf16[4,192,768]{2,1,0:T(8,128)(2,1)S(1)}, u32[]{:S(2)}, u32[]{:S(2)}) async-start(bf16[4,192,768]{2,1,0:T(8,128)(2,1)} %pad_maximum_fusion), calls=%async_computation.1 | async-start | bytes 2359296 | tf_op jit(solution)/shard_map/all_to_all | solution.py:204
  108.6 4.6 %collective-permute-start = (bf16[192,768]{1,0:T(8,128)(2,1)S(1)}, bf16[192,768]{1,0:T(8,128)(2,1)S(1)}, u32[]{:S(2)}, u32[]{:S(2)}) collective-permute-start(bf16[192,768]{1,0:T(8,128)(2,1)S(1)} %bitcast.74), channel_id=1, source_target_pairs={{0,0},{1,32},{2,64},{3,96},{32,1},{33,33},{34,65},{35,97},{64,2},{... | collective-permute-start | bytes 884744 | tf_op jit(solution)/shard_map/ppermute | solution.py:207
  113.2 2.1 %collective-permute-start.1 = (f32[768]{0:T(1024)S(1)}, f32[768]{0:T(1024)S(1)}, u32[]{:S(2)}, u32[]{:S(2)}) collective-permute-start(f32[768]{0:T(1024)S(1)} %reduce), channel_id=1, source_target_pairs={{0,0},{1,32},{2,64},{3,96},{32,1},{33,33},{34,65},{35,97},{64,2},{... | collective-permute-start | bytes 9224 | tf_op jit(solution)/shard_map/ppermute | solution.py:208
  115.4 25.6 %all-to-all-done.1 = bf16[4,192,768]{2,1,0:T(8,128)(2,1)S(1)} async-done(((bf16[4,192,768]{2,1,0:T(8,128)(2,1)}), bf16[4,192,768]{2,1,0:T(8,128)(2,1)S(1)}, u32[]{:S(2)}, u32[]{:S(2)}) %all-to-all-start.1) | async-done | bytes 1179680 | tf_op jit(solution)/shard_map/all_to_all | solution.py:204
  141.2 12.4 %collective-permute-done.1 = f32[768]{0:T(1024)S(1)} collective-permute-done((f32[768]{0:T(1024)S(1)}, f32[768]{0:T(1024)S(1)}, u32[]{:S(2)}, u32[]{:S(2)}) %collective-permute-start.1) | collective-permute-done | bytes 3104 | tf_op jit(solution)/shard_map/ppermute | solution.py:208
  153.7 1.9 %collective-permute-start.10 = (bf16[192,768]{1,0:T(8,128)(2,1)S(1)}, bf16[192,768]{1,0:T(8,128)(2,1)S(1)}, u32[]{:S(2)}, u32[]{:S(2)}) collective-permute-start(bf16[192,768]{1,0:T(8,128)(2,1)S(1)} %add_convert_fusion), channel_id=1, source_target_pairs={{0,128},{1,160},{2,192},{3,224},{32,129},{33,161},{34,193},{35,225... | collective-permute-start | bytes 884744 | tf_op jit(solution)/shard_map/ppermute | solution.py:213
  155.6 12.6 %collective-permute-done.10 = bf16[192,768]{1,0:T(8,128)(2,1)S(1)} collective-permute-done((bf16[192,768]{1,0:T(8,128)(2,1)S(1)}, bf16[192,768]{1,0:T(8,128)(2,1)S(1)}, u32[]{:S(2)}, u32[]{:S(2)}) %collective-permute-start.10) | collective-permute-done | bytes 294944 | tf_op jit(solution)/shard_map/ppermute | solution.py:213
  168.2 0.7 copy.118
  (54 shorter events, 7.7 us)
Async XLA Ops:
  6.5 8.7 %copy-start.1 = (bf16[1,192,768]{2,1,0:T(8,128)(2,1)S(1)}, bf16[1,192,768]{2,1,0:T(8,128)(2,1)}, u32[]{:S(2)}) copy-start(bf16[1,192,768]{2,1,0:T(8,128)(2,1)} %param.9) | copy-start | bytes 884740
  6.5 11.1 %copy-start.2 = (s32[16,27]{1,0:T(8,128)S(1)}, s32[16,27]{1,0:T(8,128)}, u32[]{:S(2)}) copy-start(s32[16,27]{1,0:T(8,128)} %param.13) | copy-start | bytes 5188
  6.5 62.7 %all-gather.3.cloned.1.call-start = ((), (), s32[]{:S(2)}) async-start(), calls=%async_computation.2 | async-start | bytes 1327104 | tf_op jit(solution)/shard_map/all_gather | solution.py:166
  8.3 30.4 %collective-permute-start.4 = (bf16[192,384]{1,0:T(8,128)(2,1)S(1)}, bf16[192,384]{1,0:T(8,128)(2,1)S(1)}, u32[]{:S(2)}, u32[]{:S(2)}) collective-permute-start(bf16[192,384]{1,0:T(8,128)(2,1)S(1)} %get-tuple-element.19), channel_id=1, source_target_pairs={{0,4},{4,0},{8,12},{12,8},{16,20},{20,16},{24,28},{28,24},{32,36},... | collective-permute-start | bytes 442376 | tf_op jit(solution)/shard_map/ppermute | solution.py:132
  11.7 9.1 %collective-permute-start.5 = (bf16[192,384]{1,0:T(8,128)(2,1)S(1)}, bf16[192,384]{1,0:T(8,128)(2,1)S(1)}, u32[]{:S(2)}, u32[]{:S(2)}) collective-permute-start(bf16[192,384]{1,0:T(8,128)(2,1)S(1)} %get-tuple-element.18), channel_id=1, source_target_pairs={{0,4},{4,0},{8,12},{12,8},{16,20},{20,16},{24,28},{28,24},{32,36},... | collective-permute-start | bytes 442376 | tf_op jit(solution)/shard_map/ppermute | solution.py:132
  15.3 14.0 %collective-permute-start.2 = (bf16[192,384]{1,0:T(8,128)(2,1)S(1)}, bf16[192,384]{1,0:T(8,128)(2,1)S(1)}, u32[]{:S(2)}, u32[]{:S(2)}) collective-permute-start(bf16[192,384]{1,0:T(8,128)(2,1)S(1)} %get-tuple-element.16), channel_id=1, source_target_pairs={{0,4},{4,0},{8,12},{12,8},{16,20},{20,16},{24,28},{28,24},{32,36},... | collective-permute-start | bytes 442376 | tf_op jit(solution)/shard_map/ppermute | solution.py:132
  21.6 26.8 %collective-permute-start.6 = (bf16[384,384]{1,0:T(8,128)(2,1)}, bf16[384,384]{1,0:T(8,128)(2,1)S(1)}, u32[]{:S(2)}, u32[]{:S(2)}) collective-permute-start(bf16[384,384]{1,0:T(8,128)(2,1)} %maximum_select_fusion.5), channel_id=1, source_target_pairs={{0,8},{4,12},{8,16},{12,20},{16,24},{20,28},{24,32},{28,36},{32,40... | collective-permute-start | bytes 884744 | tf_op jit(solution)/shard_map/ppermute | solution.py:146
  27.3 24.6 %collective-permute-start.7 = (bf16[384,384]{1,0:T(8,128)(2,1)}, bf16[384,384]{1,0:T(8,128)(2,1)S(1)}, u32[]{:S(2)}, u32[]{:S(2)}) collective-permute-start(bf16[384,384]{1,0:T(8,128)(2,1)} %maximum_select_fusion.5), channel_id=1, source_target_pairs={{8,0},{12,4},{16,8},{20,12},{24,16},{28,20},{32,24},{36,28},{40,32... | collective-permute-start | bytes 884744 | tf_op jit(solution)/shard_map/ppermute | solution.py:147
  30.0 37.3 %collective-permute-start.8 = (bf16[384,384]{1,0:T(8,128)(2,1)}, bf16[384,384]{1,0:T(8,128)(2,1)}, u32[]{:S(2)}, u32[]{:S(2)}) collective-permute-start(bf16[384,384]{1,0:T(8,128)(2,1)} %maximum_select_fusion.4), channel_id=1, source_target_pairs={{8,0},{12,4},{16,8},{20,12},{24,16},{28,20},{32,24},{36,28},{40,32... | collective-permute-start | bytes 884744 | tf_op jit(solution)/shard_map/ppermute | solution.py:147
  33.5 35.0 %collective-permute-start.3 = (bf16[384,384]{1,0:T(8,128)(2,1)}, bf16[384,384]{1,0:T(8,128)(2,1)S(1)}, u32[]{:S(2)}, u32[]{:S(2)}) collective-permute-start(bf16[384,384]{1,0:T(8,128)(2,1)} %maximum_select_fusion.4), channel_id=1, source_target_pairs={{0,8},{4,12},{8,16},{12,20},{16,24},{20,28},{24,32},{28,36},{32,40... | collective-permute-start | bytes 884744 | tf_op jit(solution)/shard_map/ppermute | solution.py:146
  72.6 7.6 %collective-permute-start.9 = (bf16[192,384]{0,1:T(8,128)(2,1)S(1)}, bf16[192,384]{0,1:T(8,128)(2,1)S(1)}, u32[]{:S(2)}, u32[]{:S(2)}) collective-permute-start(bf16[192,384]{0,1:T(8,128)(2,1)S(1)} %get-tuple-element.14), channel_id=1, source_target_pairs={{0,4},{4,0},{8,12},{12,8},{16,20},{20,16},{24,28},{28,24},{32,36},... | collective-permute-start | bytes 442376 | tf_op jit(solution)/shard_map/ppermute | solution.py:188
  80.5 15.9 %copy-start = (bf16[1,768,768]{1,2,0:T(8,128)(2,1)S(1)}, bf16[1,768,768]{1,2,0:T(8,128)(2,1)}, u32[]{:S(2)}) copy-start(bf16[1,768,768]{1,2,0:T(8,128)(2,1)} %all-gather.3.cloned.1.call-done) | copy-start | bytes 3538948
  99.8 8.8 %copy-start.4 = (bf16[1,192,768]{2,1,0:T(8,128)(2,1)S(1)}, bf16[1,192,768]{2,1,0:T(8,128)(2,1)}, u32[]{:S(2)}) copy-start(bf16[1,192,768]{2,1,0:T(8,128)(2,1)} %param.10) | copy-start | bytes 884740
  99.8 13.4 %copy-start.3 = (f32[1,768]{1,0:T(1,128)S(1)}, f32[1,768]{1,0:T(1,128)}, u32[]{:S(2)}) copy-start(f32[1,768]{1,0:T(1,128)} %param.12) | copy-start | bytes 9220
  99.8 41.2 %all-to-all-start.1 = ((bf16[4,192,768]{2,1,0:T(8,128)(2,1)}), bf16[4,192,768]{2,1,0:T(8,128)(2,1)S(1)}, u32[]{:S(2)}, u32[]{:S(2)}) async-start(bf16[4,192,768]{2,1,0:T(8,128)(2,1)} %pad_maximum_fusion), calls=%async_computation.1 | async-start | bytes 2359296 | tf_op jit(solution)/shard_map/all_to_all | solution.py:204
  108.6 45.0 %collective-permute-start = (bf16[192,768]{1,0:T(8,128)(2,1)S(1)}, bf16[192,768]{1,0:T(8,128)(2,1)S(1)}, u32[]{:S(2)}, u32[]{:S(2)}) collective-permute-start(bf16[192,768]{1,0:T(8,128)(2,1)S(1)} %bitcast.74), channel_id=1, source_target_pairs={{0,0},{1,32},{2,64},{3,96},{32,1},{33,33},{34,65},{35,97},{64,2},{... | collective-permute-start | bytes 884744 | tf_op jit(solution)/shard_map/ppermute | solution.py:207
  113.2 40.3 %collective-permute-start.1 = (f32[768]{0:T(1024)S(1)}, f32[768]{0:T(1024)S(1)}, u32[]{:S(2)}, u32[]{:S(2)}) collective-permute-start(f32[768]{0:T(1024)S(1)} %reduce), channel_id=1, source_target_pairs={{0,0},{1,32},{2,64},{3,96},{32,1},{33,33},{34,65},{35,97},{64,2},{... | collective-permute-start | bytes 9224 | tf_op jit(solution)/shard_map/ppermute | solution.py:208
  153.7 14.5 %collective-permute-start.10 = (bf16[192,768]{1,0:T(8,128)(2,1)S(1)}, bf16[192,768]{1,0:T(8,128)(2,1)S(1)}, u32[]{:S(2)}, u32[]{:S(2)}) collective-permute-start(bf16[192,768]{1,0:T(8,128)(2,1)S(1)} %add_convert_fusion), channel_id=1, source_target_pairs={{0,128},{1,160},{2,192},{3,224},{32,129},{33,161},{34,193},{35,225... | collective-permute-start | bytes 884744 | tf_op jit(solution)/shard_map/ppermute | solution.py:213
Sparse Core Ops, SparseCore 0:
  9.4 54.2 all-gather.2

commit v6 on v5

--- a/solution.py
+++ b/solution.py
@@ -191,16 +191,26 @@
         jnp.concatenate([mine_rows, back], axis=1),
         jnp.concatenate([back, mine_rows], axis=1),
     )
-    spread = jnp.broadcast_to(attended[None], (x_count,) + attended.shape)
-    token_parts = lax.all_to_all(spread, "sx", 0, 0)
-    terms = jnp.stack(
+    up_ring = [(i, (i + 1) % x_count) for i in range(x_count)]
+    down_ring = [(i, (i - 1) % x_count) for i in range(x_count)]
+    from_below = lax.ppermute(attended, "sx", up_ring)
+    from_above = lax.ppermute(attended, "sx", down_ring)
+    middle = row_count // 2
+    far = jnp.concatenate(
         [
-            jnp.dot(token_parts[j], weight_block, preferred_element_type=jnp.float32).astype(
-                jnp.bfloat16
-            )
-            for j in range(x_count)
+            lax.ppermute(from_below[:middle], "sx", up_ring),
+            lax.ppermute(from_above[middle:], "sx", down_ring),
+        ],
+        axis=0,
+    )
+    relative = [attended, from_below, far, from_above]
+    relative_terms = jnp.stack(
+        [
+            jnp.dot(part, weight_block, preferred_element_type=jnp.float32).astype(jnp.bfloat16)
+            for part in relative
         ]
     )
+    terms = jnp.take(relative_terms, (x_index - jnp.arange(x_count)) % x_count, axis=0)
     arrived = lax.all_to_all(terms, "head", 0, 0)
     mixed = jnp.sum(arrived.astype(jnp.float32), axis=0)
     swap = linear_pairs((x_count, head_groups), lambda a, b: (b, a))

time: 176 us -> 182 us (1.034)
  the two profiles are of different devices: /device:TPU:92 before, /device:TPU:20 now
where the time goes in v6:
time: 182 us
  waiting for transfers between devices  91 us (50%)
  starting transfers between devices  57.1 us (31%)
  between operations  15.8 us (9%)
  local copies, waits for them, and re-layouts  6.71 us (4%)
  other arithmetic  5.72 us (3%)
  matrix products  5.4 us (3%)
    ppermute x2, waiting for transfers between devices, on_device(): lax.ppermute((tile_k, tile_v), seq, [(i, i - 2) for i in range(2, seq_cou...  28.3 us
    ppermute x1, waiting for transfers between devices, on_device(): gate_block = lax.ppermute(gate_scale[0], ('sx', 'head'), swap)  22.8 us
    all_to_all x1, waiting for transfers between devices, on_device(): arrived = lax.all_to_all(terms, 'head', 0, 0)  14.2 us
    ppermute x1, waiting for transfers between devices, on_device(): handed = lax.ppermute(updated, ('section', 'sx', 'head'), hand)  10.6 us
    ppermute x1, starting transfers between devices, on_device(): stream_block = lax.ppermute(stream[0], ('sx', 'head'), swap)  9.75 us
    ppermute x3, starting transfers between devices, on_device(): lax.ppermute((partner_half(queries), partner_half(own_keys), partner_half...  9.32 us
    ppermute x2, starting transfers between devices, on_device(): lax.ppermute((tile_k, tile_v), seq, [(i, i + 2) for i in range(seq_count...  8.39 us
    ppermute x2, starting transfers between devices, on_device(): lax.ppermute((tile_k, tile_v), seq, [(i, i - 2) for i in range(2, seq_cou...  6.28 us
  transfers between devices with their start and end apart: 17, of which 8 were waited for; matrix products, arithmetic and copies ran while one was open for 6% of the time, Pallas kernels for 0%

profile of v6, /device:TPU:20, one launch (start us, length us, event | category | flops | bytes accessed | tf_op | source)
XLA Modules:
  0.0 181.7 jit_solution(3058848575924749339)
XLA Ops:
  6.5 0.7 all-gather.3.cloned.1.call-update
  7.3 1.0 constant_dynamic-slice_fusion.4
  8.3 3.5 %collective-permute-start.2 = (bf16[192,384]{1,0:T(8,128)(2,1)S(1)}, bf16[192,384]{1,0:T(8,128)(2,1)S(1)}, u32[]{:S(2)}, u32[]{:S(2)}) collective-permute-start(bf16[192,384]{1,0:T(8,128)(2,1)S(1)} %get-tuple-element.20), channel_id=1, source_target_pairs={{0,4},{4,0},{8,12},{12,8},{16,20},{20,16},{24,28},{28,24},{32,36},... | collective-permute-start | bytes 442376 | tf_op jit(solution)/shard_map/ppermute | solution.py:132
  11.8 1.0 constant_dynamic-slice_fusion.2
  12.8 2.4 %collective-permute-start.5 = (bf16[192,384]{1,0:T(8,128)(2,1)S(1)}, bf16[192,384]{1,0:T(8,128)(2,1)S(1)}, u32[]{:S(2)}, u32[]{:S(2)}) collective-permute-start(bf16[192,384]{1,0:T(8,128)(2,1)S(1)} %get-tuple-element.18), channel_id=1, source_target_pairs={{0,4},{4,0},{8,12},{12,8},{16,20},{20,16},{24,28},{28,24},{32,36},... | collective-permute-start | bytes 442376 | tf_op jit(solution)/shard_map/ppermute | solution.py:132
  15.3 3.5 %collective-permute-start.4 = (bf16[192,384]{1,0:T(8,128)(2,1)S(1)}, bf16[192,384]{1,0:T(8,128)(2,1)S(1)}, u32[]{:S(2)}, u32[]{:S(2)}) collective-permute-start(bf16[192,384]{1,0:T(8,128)(2,1)S(1)} %get-tuple-element.15), channel_id=1, source_target_pairs={{0,4},{4,0},{8,12},{12,8},{16,20},{20,16},{24,28},{28,24},{32,36},... | collective-permute-start | bytes 442376 | tf_op jit(solution)/shard_map/ppermute | solution.py:132
  21.9 0.8 maximum_select_fusion.5
  22.7 4.8 %collective-permute-start.6 = (bf16[384,384]{1,0:T(8,128)(2,1)}, bf16[384,384]{1,0:T(8,128)(2,1)S(1)}, u32[]{:S(2)}, u32[]{:S(2)}) collective-permute-start(bf16[384,384]{1,0:T(8,128)(2,1)} %maximum_select_fusion.5), channel_id=1, source_target_pairs={{0,8},{4,12},{8,16},{12,20},{16,24},{20,28},{24,32},{28,36},{32,40... | collective-permute-start | bytes 884744 | tf_op jit(solution)/shard_map/ppermute | solution.py:146
  27.5 1.9 %collective-permute-start.7 = (bf16[384,384]{1,0:T(8,128)(2,1)}, bf16[384,384]{1,0:T(8,128)(2,1)S(1)}, u32[]{:S(2)}, u32[]{:S(2)}) collective-permute-start(bf16[384,384]{1,0:T(8,128)(2,1)} %maximum_select_fusion.5), channel_id=1, source_target_pairs={{8,0},{12,4},{16,8},{20,12},{24,16},{28,20},{32,24},{36,28},{40,32... | collective-permute-start | bytes 884744 | tf_op jit(solution)/shard_map/ppermute | solution.py:147
  29.5 0.8 maximum_select_fusion.4
  30.3 4.3 %collective-permute-start.8 = (bf16[384,384]{1,0:T(8,128)(2,1)}, bf16[384,384]{1,0:T(8,128)(2,1)}, u32[]{:S(2)}, u32[]{:S(2)}) collective-permute-start(bf16[384,384]{1,0:T(8,128)(2,1)} %maximum_select_fusion.4), channel_id=1, source_target_pairs={{8,0},{12,4},{16,8},{20,12},{24,16},{28,20},{32,24},{36,28},{40,32... | collective-permute-start | bytes 884744 | tf_op jit(solution)/shard_map/ppermute | solution.py:147
  34.6 3.6 %collective-permute-start.3 = (bf16[384,384]{1,0:T(8,128)(2,1)}, bf16[384,384]{1,0:T(8,128)(2,1)S(1)}, u32[]{:S(2)}, u32[]{:S(2)}) collective-permute-start(bf16[384,384]{1,0:T(8,128)(2,1)} %maximum_select_fusion.4), channel_id=1, source_target_pairs={{0,8},{4,12},{8,16},{12,20},{16,24},{20,28},{24,32},{28,36},{32,40... | collective-permute-start | bytes 884744 | tf_op jit(solution)/shard_map/ppermute | solution.py:146
  40.0 28.3 %collective-permute-done.8 = bf16[384,384]{1,0:T(8,128)(2,1)} collective-permute-done((bf16[384,384]{1,0:T(8,128)(2,1)}, bf16[384,384]{1,0:T(8,128)(2,1)}, u32[]{:S(2)}, u32[]{:S(2)}) %collective-permute-start.8) | collective-permute-done | bytes 294944 | tf_op jit(solution)/shard_map/ppermute | solution.py:147
  68.3 1.2 copy.84
  74.1 2.1 %collective-permute-start.9 = (bf16[192,384]{0,1:T(8,128)(2,1)S(1)}, bf16[192,384]{0,1:T(8,128)(2,1)S(1)}, u32[]{:S(2)}, u32[]{:S(2)}) collective-permute-start(bf16[192,384]{0,1:T(8,128)(2,1)S(1)} %get-tuple-element.14), channel_id=1, source_target_pairs={{0,4},{4,0},{8,12},{12,8},{16,20},{20,16},{24,28},{28,24},{32,36},... | collective-permute-start | bytes 442376 | tf_op jit(solution)/shard_map/ppermute | solution.py:188
  76.2 6.2 %collective-permute-done.9 = bf16[192,384]{0,1:T(8,128)(2,1)S(1)} collective-permute-done((bf16[192,384]{0,1:T(8,128)(2,1)S(1)}, bf16[192,384]{0,1:T(8,128)(2,1)S(1)}, u32[]{:S(2)}, u32[]{:S(2)}) %collective-permute-start.9) | collective-permute-done | bytes 147488 | tf_op jit(solution)/shard_map/ppermute | solution.py:188
  82.5 2.5 %collective-permute-start.12 = (bf16[192,768]{0,1:T(8,128)(2,1)S(1)}, bf16[192,768]{0,1:T(8,128)(2,1)S(1)}, u32[]{:S(2)}, u32[]{:S(2)}) collective-permute-start(bf16[192,768]{0,1:T(8,128)(2,1)S(1)} %maximum_select_fusion.3), channel_id=1, source_target_pairs={{0,96},{32,0},{64,32},{96,64},{1,97},{33,1},{65,33},{97,65},{2,98}... | collective-permute-start | bytes 884744 | tf_op jit(solution)/shard_map/ppermute | solution.py:197
  85.0 3.4 %collective-permute-start.10 = (bf16[192,768]{0,1:T(8,128)(2,1)S(1)}, bf16[192,768]{0,1:T(8,128)(2,1)S(1)}, u32[]{:S(2)}, u32[]{:S(2)}) collective-permute-start(bf16[192,768]{0,1:T(8,128)(2,1)S(1)} %maximum_select_fusion.3), channel_id=1, source_target_pairs={{0,32},{32,64},{64,96},{96,0},{1,33},{33,65},{65,97},{97,1},{2,34}... | collective-permute-start | bytes 884744 | tf_op jit(solution)/shard_map/ppermute | solution.py:196
  88.9 5.0 %collective-permute-done.12 = bf16[192,768]{0,1:T(8,128)(2,1)S(1)} collective-permute-done((bf16[192,768]{0,1:T(8,128)(2,1)S(1)}, bf16[192,768]{0,1:T(8,128)(2,1)S(1)}, u32[]{:S(2)}, u32[]{:S(2)}) %collective-permute-start.12) | collective-permute-done | bytes 294944 | tf_op jit(solution)/shard_map/ppermute | solution.py:197
  94.1 2.5 %collective-permute-start.13 = (bf16[96,768]{0,1:T(8,128)(2,1)S(1)}, bf16[96,768]{0,1:T(8,128)(2,1)S(1)}, u32[]{:S(2)}, u32[]{:S(2)}) collective-permute-start(bf16[96,768]{0,1:T(8,128)(2,1)S(1)} %slice.11), channel_id=1, source_target_pairs={{0,96},{32,0},{64,32},{96,64},{1,97},{33,1},{65,33},{97,65},{2,98}... | collective-permute-start | bytes 442376 | tf_op jit(solution)/shard_map/ppermute | solution.py:202
  96.6 3.4 %collective-permute-start.11 = (bf16[96,768]{0,1:T(8,128)(2,1)S(1)}, bf16[96,768]{0,1:T(8,128)(2,1)S(1)}, u32[]{:S(2)}, u32[]{:S(2)}) collective-permute-start(bf16[96,768]{0,1:T(8,128)(2,1)S(1)} %slice.10), channel_id=1, source_target_pairs={{0,32},{32,64},{64,96},{96,0},{1,33},{33,65},{65,97},{97,1},{2,34}... | collective-permute-start | bytes 442376 | tf_op jit(solution)/shard_map/ppermute | solution.py:201
  101.7 2.5 %collective-permute-done.11 = bf16[96,768]{0,1:T(8,128)(2,1)S(1)} collective-permute-done((bf16[96,768]{0,1:T(8,128)(2,1)S(1)}, bf16[96,768]{0,1:T(8,128)(2,1)S(1)}, u32[]{:S(2)}, u32[]{:S(2)}) %collective-permute-start.11) | collective-permute-done | bytes 147488 | tf_op jit(solution)/shard_map/ppermute | solution.py:201
  104.2 0.7 fusion.6
  105.7 1.2 broadcast_select_fusion
  106.9 5.8 %all-to-all-start = ((bf16[4,192,768]{2,1,0:T(8,128)(2,1)}), bf16[4,192,768]{2,1,0:T(8,128)(2,1)S(1)}, u32[]{:S(2)}, u32[]{:S(2)}) async-start(bf16[4,192,768]{2,1,0:T(8,128)(2,1)} %broadcast_select_fusion), calls=%async_computation | async-start | bytes 2359296 | tf_op jit(solution)/shard_map/all_to_all | solution.py:214
  112.7 9.8 %collective-permute-start = (bf16[192,768]{1,0:T(8,128)(2,1)S(1)}, bf16[192,768]{1,0:T(8,128)(2,1)S(1)}, u32[]{:S(2)}, u32[]{:S(2)}) collective-permute-start(bf16[192,768]{1,0:T(8,128)(2,1)S(1)} %bitcast.67), channel_id=1, source_target_pairs={{0,0},{1,32},{2,64},{3,96},{32,1},{33,33},{34,65},{35,97},{64,2},{... | collective-permute-start | bytes 884744 | tf_op jit(solution)/shard_map/ppermute | solution.py:217
  122.5 1.9 %collective-permute-start.1 = (f32[768]{0:T(1024)S(1)}, f32[768]{0:T(1024)S(1)}, u32[]{:S(2)}, u32[]{:S(2)}) collective-permute-start(f32[768]{0:T(1024)S(1)} %reduce), channel_id=1, source_target_pairs={{0,0},{1,32},{2,64},{3,96},{32,1},{33,33},{34,65},{35,97},{64,2},{... | collective-permute-start | bytes 9224 | tf_op jit(solution)/shard_map/ppermute | solution.py:218
  124.4 14.2 %all-to-all-done = bf16[4,192,768]{2,1,0:T(8,128)(2,1)S(1)} async-done(((bf16[4,192,768]{2,1,0:T(8,128)(2,1)}), bf16[4,192,768]{2,1,0:T(8,128)(2,1)S(1)}, u32[]{:S(2)}, u32[]{:S(2)}) %all-to-all-start) | async-done | bytes 1179680 | tf_op jit(solution)/shard_map/all_to_all | solution.py:214
  138.7 22.8 %collective-permute-done.1 = f32[768]{0:T(1024)S(1)} collective-permute-done((f32[768]{0:T(1024)S(1)}, f32[768]{0:T(1024)S(1)}, u32[]{:S(2)}, u32[]{:S(2)}) %collective-permute-start.1) | collective-permute-done | bytes 3104 | tf_op jit(solution)/shard_map/ppermute | solution.py:218
  161.6 1.9 %collective-permute-start.14 = (bf16[192,768]{1,0:T(8,128)(2,1)S(1)}, bf16[192,768]{1,0:T(8,128)(2,1)S(1)}, u32[]{:S(2)}, u32[]{:S(2)}) collective-permute-start(bf16[192,768]{1,0:T(8,128)(2,1)S(1)} %add_convert_fusion), channel_id=1, source_target_pairs={{0,128},{1,160},{2,192},{3,224},{32,129},{33,161},{34,193},{35,225... | collective-permute-start | bytes 884744 | tf_op jit(solution)/shard_map/ppermute | solution.py:223
  163.6 10.6 %collective-permute-done.14 = bf16[192,768]{1,0:T(8,128)(2,1)S(1)} collective-permute-done((bf16[192,768]{1,0:T(8,128)(2,1)S(1)}, bf16[192,768]{1,0:T(8,128)(2,1)S(1)}, u32[]{:S(2)}, u32[]{:S(2)}) %collective-permute-start.14) | collective-permute-done | bytes 294944 | tf_op jit(solution)/shard_map/ppermute | solution.py:223
  174.2 0.7 copy.112
  (66 shorter events, 11.0 us)
Async XLA Ops:
  6.5 8.7 %copy-start.1 = (bf16[1,192,768]{2,1,0:T(8,128)(2,1)S(1)}, bf16[1,192,768]{2,1,0:T(8,128)(2,1)}, u32[]{:S(2)}) copy-start(bf16[1,192,768]{2,1,0:T(8,128)(2,1)} %param.7) | copy-start | bytes 884740
  6.5 12.2 %copy-start.2 = (s32[16,27]{1,0:T(8,128)S(1)}, s32[16,27]{1,0:T(8,128)}, u32[]{:S(2)}) copy-start(s32[16,27]{1,0:T(8,128)} %param.13) | copy-start | bytes 5188
  6.5 64.2 %all-gather.3.cloned.1.call-start = ((), (), s32[]{:S(2)}) async-start(), calls=%async_computation.1 | async-start | bytes 1327104 | tf_op jit(solution)/shard_map/all_gather | solution.py:166
  8.3 21.2 %collective-permute-start.2 = (bf16[192,384]{1,0:T(8,128)(2,1)S(1)}, bf16[192,384]{1,0:T(8,128)(2,1)S(1)}, u32[]{:S(2)}, u32[]{:S(2)}) collective-permute-start(bf16[192,384]{1,0:T(8,128)(2,1)S(1)} %get-tuple-element.20), channel_id=1, source_target_pairs={{0,4},{4,0},{8,12},{12,8},{16,20},{20,16},{24,28},{28,24},{32,36},... | collective-permute-start | bytes 442376 | tf_op jit(solution)/shard_map/ppermute | solution.py:132
  12.8 9.1 %collective-permute-start.5 = (bf16[192,384]{1,0:T(8,128)(2,1)S(1)}, bf16[192,384]{1,0:T(8,128)(2,1)S(1)}, u32[]{:S(2)}, u32[]{:S(2)}) collective-permute-start(bf16[192,384]{1,0:T(8,128)(2,1)S(1)} %get-tuple-element.18), channel_id=1, source_target_pairs={{0,4},{4,0},{8,12},{12,8},{16,20},{20,16},{24,28},{28,24},{32,36},... | collective-permute-start | bytes 442376 | tf_op jit(solution)/shard_map/ppermute | solution.py:132
  15.3 23.7 %collective-permute-start.4 = (bf16[192,384]{1,0:T(8,128)(2,1)S(1)}, bf16[192,384]{1,0:T(8,128)(2,1)S(1)}, u32[]{:S(2)}, u32[]{:S(2)}) collective-permute-start(bf16[192,384]{1,0:T(8,128)(2,1)S(1)} %get-tuple-element.15), channel_id=1, source_target_pairs={{0,4},{4,0},{8,12},{12,8},{16,20},{20,16},{24,28},{28,24},{32,36},... | collective-permute-start | bytes 442376 | tf_op jit(solution)/shard_map/ppermute | solution.py:132
  22.7 46.8 %collective-permute-start.6 = (bf16[384,384]{1,0:T(8,128)(2,1)}, bf16[384,384]{1,0:T(8,128)(2,1)S(1)}, u32[]{:S(2)}, u32[]{:S(2)}) collective-permute-start(bf16[384,384]{1,0:T(8,128)(2,1)} %maximum_select_fusion.5), channel_id=1, source_target_pairs={{0,8},{4,12},{8,16},{12,20},{16,24},{20,28},{24,32},{28,36},{32,40... | collective-permute-start | bytes 884744 | tf_op jit(solution)/shard_map/ppermute | solution.py:146
  27.5 42.2 %collective-permute-start.7 = (bf16[384,384]{1,0:T(8,128)(2,1)}, bf16[384,384]{1,0:T(8,128)(2,1)S(1)}, u32[]{:S(2)}, u32[]{:S(2)}) collective-permute-start(bf16[384,384]{1,0:T(8,128)(2,1)} %maximum_select_fusion.5), channel_id=1, source_target_pairs={{8,0},{12,4},{16,8},{20,12},{24,16},{28,20},{32,24},{36,28},{40,32... | collective-permute-start | bytes 884744 | tf_op jit(solution)/shard_map/ppermute | solution.py:147
  30.3 38.0 %collective-permute-start.8 = (bf16[384,384]{1,0:T(8,128)(2,1)}, bf16[384,384]{1,0:T(8,128)(2,1)}, u32[]{:S(2)}, u32[]{:S(2)}) collective-permute-start(bf16[384,384]{1,0:T(8,128)(2,1)} %maximum_select_fusion.4), channel_id=1, source_target_pairs={{8,0},{12,4},{16,8},{20,12},{24,16},{28,20},{32,24},{36,28},{40,32... | collective-permute-start | bytes 884744 | tf_op jit(solution)/shard_map/ppermute | solution.py:147
  34.6 35.3 %collective-permute-start.3 = (bf16[384,384]{1,0:T(8,128)(2,1)}, bf16[384,384]{1,0:T(8,128)(2,1)S(1)}, u32[]{:S(2)}, u32[]{:S(2)}) collective-permute-start(bf16[384,384]{1,0:T(8,128)(2,1)} %maximum_select_fusion.4), channel_id=1, source_target_pairs={{0,8},{4,12},{8,16},{12,20},{16,24},{20,28},{24,32},{28,36},{32,40... | collective-permute-start | bytes 884744 | tf_op jit(solution)/shard_map/ppermute | solution.py:146
  73.9 14.5 %copy-start = (bf16[1,768,768]{1,2,0:T(8,128)(2,1)S(1)}, bf16[1,768,768]{1,2,0:T(8,128)(2,1)}, u32[]{:S(2)}) copy-start(bf16[1,768,768]{1,2,0:T(8,128)(2,1)} %all-gather.3.cloned.1.call-done) | copy-start | bytes 3538948
  74.1 8.3 %collective-permute-start.9 = (bf16[192,384]{0,1:T(8,128)(2,1)S(1)}, bf16[192,384]{0,1:T(8,128)(2,1)S(1)}, u32[]{:S(2)}, u32[]{:S(2)}) collective-permute-start(bf16[192,384]{0,1:T(8,128)(2,1)S(1)} %get-tuple-element.14), channel_id=1, source_target_pairs={{0,4},{4,0},{8,12},{12,8},{16,20},{20,16},{24,28},{28,24},{32,36},... | collective-permute-start | bytes 442376 | tf_op jit(solution)/shard_map/ppermute | solution.py:188
  82.5 11.5 %collective-permute-start.12 = (bf16[192,768]{0,1:T(8,128)(2,1)S(1)}, bf16[192,768]{0,1:T(8,128)(2,1)S(1)}, u32[]{:S(2)}, u32[]{:S(2)}) collective-permute-start(bf16[192,768]{0,1:T(8,128)(2,1)S(1)} %maximum_select_fusion.3), channel_id=1, source_target_pairs={{0,96},{32,0},{64,32},{96,64},{1,97},{33,1},{65,33},{97,65},{2,98}... | collective-permute-start | bytes 884744 | tf_op jit(solution)/shard_map/ppermute | solution.py:197
  85.0 11.6 %collective-permute-start.10 = (bf16[192,768]{0,1:T(8,128)(2,1)S(1)}, bf16[192,768]{0,1:T(8,128)(2,1)S(1)}, u32[]{:S(2)}, u32[]{:S(2)}) collective-permute-start(bf16[192,768]{0,1:T(8,128)(2,1)S(1)} %maximum_select_fusion.3), channel_id=1, source_target_pairs={{0,32},{32,64},{64,96},{96,0},{1,33},{33,65},{65,97},{97,1},{2,34}... | collective-permute-start | bytes 884744 | tf_op jit(solution)/shard_map/ppermute | solution.py:196
  94.1 7.6 %collective-permute-start.13 = (bf16[96,768]{0,1:T(8,128)(2,1)S(1)}, bf16[96,768]{0,1:T(8,128)(2,1)S(1)}, u32[]{:S(2)}, u32[]{:S(2)}) collective-permute-start(bf16[96,768]{0,1:T(8,128)(2,1)S(1)} %slice.11), channel_id=1, source_target_pairs={{0,96},{32,0},{64,32},{96,64},{1,97},{33,1},{65,33},{97,65},{2,98}... | collective-permute-start | bytes 442376 | tf_op jit(solution)/shard_map/ppermute | solution.py:202
  96.6 7.6 %collective-permute-start.11 = (bf16[96,768]{0,1:T(8,128)(2,1)S(1)}, bf16[96,768]{0,1:T(8,128)(2,1)S(1)}, u32[]{:S(2)}, u32[]{:S(2)}) collective-permute-start(bf16[96,768]{0,1:T(8,128)(2,1)S(1)} %slice.10), channel_id=1, source_target_pairs={{0,32},{32,64},{64,96},{96,0},{1,33},{33,65},{65,97},{97,1},{2,34}... | collective-permute-start | bytes 442376 | tf_op jit(solution)/shard_map/ppermute | solution.py:201
  106.9 5.8 %copy-start.4 = (bf16[1,192,768]{2,1,0:T(8,128)(2,1)S(1)}, bf16[1,192,768]{2,1,0:T(8,128)(2,1)}, u32[]{:S(2)}) copy-start(bf16[1,192,768]{2,1,0:T(8,128)(2,1)} %param.10) | copy-start | bytes 884740
  106.9 15.5 %copy-start.3 = (f32[1,768]{1,0:T(1,128)S(1)}, f32[1,768]{1,0:T(1,128)}, u32[]{:S(2)}) copy-start(f32[1,768]{1,0:T(1,128)} %param.12) | copy-start | bytes 9220
  106.9 31.7 %all-to-all-start = ((bf16[4,192,768]{2,1,0:T(8,128)(2,1)}), bf16[4,192,768]{2,1,0:T(8,128)(2,1)S(1)}, u32[]{:S(2)}, u32[]{:S(2)}) async-start(bf16[4,192,768]{2,1,0:T(8,128)(2,1)} %broadcast_select_fusion), calls=%async_computation | async-start | bytes 2359296 | tf_op jit(solution)/shard_map/all_to_all | solution.py:214
  112.7 48.9 %collective-permute-start = (bf16[192,768]{1,0:T(8,128)(2,1)S(1)}, bf16[192,768]{1,0:T(8,128)(2,1)S(1)}, u32[]{:S(2)}, u32[]{:S(2)}) collective-permute-start(bf16[192,768]{1,0:T(8,128)(2,1)S(1)} %bitcast.67), channel_id=1, source_target_pairs={{0,0},{1,32},{2,64},{3,96},{32,1},{33,33},{34,65},{35,97},{64,2},{... | collective-permute-start | bytes 884744 | tf_op jit(solution)/shard_map/ppermute | solution.py:217
  122.5 39.1 %collective-permute-start.1 = (f32[768]{0:T(1024)S(1)}, f32[768]{0:T(1024)S(1)}, u32[]{:S(2)}, u32[]{:S(2)}) collective-permute-start(f32[768]{0:T(1024)S(1)} %reduce), channel_id=1, source_target_pairs={{0,0},{1,32},{2,64},{3,96},{32,1},{33,33},{34,65},{35,97},{64,2},{... | collective-permute-start | bytes 9224 | tf_op jit(solution)/shard_map/ppermute | solution.py:218
  161.6 12.6 %collective-permute-start.14 = (bf16[192,768]{1,0:T(8,128)(2,1)S(1)}, bf16[192,768]{1,0:T(8,128)(2,1)S(1)}, u32[]{:S(2)}, u32[]{:S(2)}) collective-permute-start(bf16[192,768]{1,0:T(8,128)(2,1)S(1)} %add_convert_fusion), channel_id=1, source_target_pairs={{0,128},{1,160},{2,192},{3,224},{32,129},{33,161},{34,193},{35,225... | collective-permute-start | bytes 884744 | tf_op jit(solution)/shard_map/ppermute | solution.py:223
Sparse Core Ops, SparseCore 0:
  9.4 54.7 all-gather.2

commit v7 on v5

--- a/solution.py
+++ b/solution.py
@@ -129,9 +129,14 @@
     def own_half(block):
         return lax.dynamic_slice_in_dim(block, parity * half, half, 1)
 
-    sent = lax.ppermute(
-        (partner_half(queries), partner_half(own_keys), partner_half(own_values)), seq, partner
-    )
+    swapped = lax.ppermute(
+        jnp.concatenate(
+            [partner_half(queries), partner_half(own_keys), partner_half(own_values)], axis=1
+        ),
+        seq,
+        partner,
+    )
+    sent = [swapped[:, part * half:(part + 1) * half] for part in range(3)]
 
     def whole_tile(mine, theirs):
         return jnp.where(
@@ -143,8 +148,34 @@
     tile_q = whole_tile(own_half(queries), sent[0])
     tile_k = whole_tile(own_half(own_keys), sent[1])
     tile_v = whole_tile(own_half(own_values), sent[2])
-    before = lax.ppermute((tile_k, tile_v), seq, [(i, i + 2) for i in range(seq_count - 2)])
-    after = lax.ppermute((tile_k, tile_v), seq, [(i, i - 2) for i in range(2, seq_count)])
+    halves = [
+        jnp.concatenate(
+            [own_keys[:, r * half:(r + 1) * half], own_values[:, r * half:(r + 1) * half]],
+            axis=1,
+        )
+        for r in range(2)
+    ]
+    near_slabs = {}
+    for offset in (-2, -1, 2, 3):
+        arrived = []
+        for r in range(2):
+            route = [
+                (2 * t + offset, 2 * t + r)
+                for t in range(seq_count // 2)
+                if 0 <= 2 * t + offset < seq_count
+            ]
+            arrived.append(lax.ppermute(halves[r], seq, route))
+        near_slabs[offset] = jnp.where(parity == 0, arrived[0], arrived[1])
+
+    def near_tile(first, second):
+        keys = jnp.concatenate([near_slabs[first][:, :half], near_slabs[second][:, :half]], 0)
+        values = jnp.concatenate(
+            [near_slabs[first][:, half:], near_slabs[second][:, half:]], 0
+        )
+        return keys, values
+
+    before = near_tile(-2, -1)
+    after = near_tile(2, 3)
     key_tiles = [before, (tile_k, tile_v), after]
     keeps = []
     for step in (-1, 0, 1):

time: 176 us -> 193 us (1.097)
  the two profiles are of different devices: /device:TPU:92 before, /device:TPU:68 now
where the time goes in v7:
time: 193 us
  waiting for transfers between devices  85.9 us (45%)
  starting transfers between devices  57.1 us (30%)
  blocking collectives  16.7 us (9%)
  between operations  15.9 us (8%)
  other arithmetic  6.84 us (4%)
  matrix products  5.21 us (3%)
  local copies, waits for them, and re-layouts  4.92 us (3%)
    ppermute x8, starting transfers between devices, on_device(): arrived.append(lax.ppermute(halves[r], seq, route))  37.7 us
    ppermute x8, waiting for transfers between devices, on_device(): arrived.append(lax.ppermute(halves[r], seq, route))  30.4 us
    all_to_all x1, waiting for transfers between devices, on_device(): arrived = lax.all_to_all(terms, 'head', 0, 0)  25.5 us
    all_to_all x1, blocking collectives, on_device(): token_parts = lax.all_to_all(spread, 'sx', 0, 0)  16.7 us
    ppermute x1, waiting for transfers between devices, on_device(): gate_block = lax.ppermute(gate_scale[0], ('sx', 'head'), swap)  12.4 us
    ppermute x1, waiting for transfers between devices, on_device(): handed = lax.ppermute(updated, ('section', 'sx', 'head'), hand)  11.8 us
    all_to_all x1, starting transfers between devices, on_device(): arrived = lax.all_to_all(terms, 'head', 0, 0)  6.99 us
    ppermute x1, waiting for transfers between devices, on_device(): back = lax.ppermute(their_rows, seq, partner)  5.75 us
  transfers between devices with their start and end apart: 15, of which 7 were waited for; matrix products, arithmetic and copies ran while one was open for 4% of the time, Pallas kernels for 0%

profile of v7, /device:TPU:68, one launch (start us, length us, event | category | flops | bytes accessed | tf_op | source)
XLA Modules:
  0.0 192.6 jit_solution(9850678097858322305)
XLA Ops:
  6.5 1.1 copy.72
  7.7 1.1 copy.73
  9.0 1.4 collective-permute-start.4
  10.4 4.5 %collective-permute-start.2 = (bf16[192,768]{0,1:T(8,128)(2,1)S(1)}, bf16[192,768]{0,1:T(8,128)(2,1)S(1)}, u32[]{:S(2)}, u32[]{:S(2)}) collective-permute-start(bf16[192,768]{0,1:T(8,128)(2,1)S(1)} %pad_maximum_fusion.2), channel_id=1, source_target_pairs={{0,8},{8,16},{16,24},{24,32},{32,40},{40,48},{48,56},{56,64},{64,7... | collective-permute-start | bytes 884744 | tf_op jit(solution)/shard_map/ppermute | solution.py:167
  15.0 1.4 collective-permute-start.5
  16.4 7.9 %collective-permute-start.3 = (bf16[192,768]{0,1:T(8,128)(2,1)S(1)}, bf16[192,768]{0,1:T(8,128)(2,1)}, u32[]{:S(2)}, u32[]{:S(2)}) collective-permute-start(bf16[192,768]{0,1:T(8,128)(2,1)S(1)} %pad_maximum_fusion.3), channel_id=1, source_target_pairs={{0,12},{8,20},{16,28},{24,36},{32,44},{40,52},{48,60},{56,68},{64,... | collective-permute-start | bytes 884744 | tf_op jit(solution)/shard_map/ppermute | solution.py:167
  24.3 1.3 collective-permute-start.9
  26.4 0.7 fusion.27
  29.1 5.5 %collective-permute-done.4 = bf16[192,768]{0,1:T(8,128)(2,1)} collective-permute-done((bf16[192,768]{0,1:T(8,128)(2,1)S(1)}, bf16[192,768]{0,1:T(8,128)(2,1)}, u32[]{:S(2)}, u32[]{:S(2)}) %collective-permute-start.4) | collective-permute-done | bytes 294944 | tf_op jit(solution)/shard_map/ppermute | solution.py:167
  34.6 0.7 collective-permute-start.10
  35.3 11.5 %collective-permute-start.7 = (bf16[192,768]{0,1:T(8,128)(2,1)S(1)}, bf16[192,768]{0,1:T(8,128)(2,1)S(1)}, u32[]{:S(2)}, u32[]{:S(2)}) collective-permute-start(bf16[192,768]{0,1:T(8,128)(2,1)S(1)} %pad_maximum_fusion.2), channel_id=1, source_target_pairs={{8,0},{16,8},{24,16},{32,24},{40,32},{48,40},{56,48},{64,56},{72,6... | collective-permute-start | bytes 884744 | tf_op jit(solution)/shard_map/ppermute | solution.py:167
  46.8 1.1 broadcast_select_fusion.2
  47.9 8.9 %collective-permute-start.8 = (bf16[192,768]{0,1:T(8,128)(2,1)S(1)}, bf16[192,768]{0,1:T(8,128)(2,1)S(1)}, u32[]{:S(2)}, u32[]{:S(2)}) collective-permute-start(bf16[192,768]{0,1:T(8,128)(2,1)S(1)} %pad_maximum_fusion.3), channel_id=1, source_target_pairs={{8,4},{16,12},{24,20},{32,28},{40,36},{48,44},{56,52},{64,60},{72,... | collective-permute-start | bytes 884744 | tf_op jit(solution)/shard_map/ppermute | solution.py:167
  56.8 1.9 collective-permute-start.6
  58.8 1.1 broadcast_select_fusion
  60.0 15.2 %collective-permute-done.7 = bf16[192,768]{0,1:T(8,128)(2,1)S(1)} collective-permute-done((bf16[192,768]{0,1:T(8,128)(2,1)S(1)}, bf16[192,768]{0,1:T(8,128)(2,1)S(1)}, u32[]{:S(2)}, u32[]{:S(2)}) %collective-permute-start.7) | collective-permute-done | bytes 294944 | tf_op jit(solution)/shard_map/ppermute | solution.py:167
  75.1 9.7 %collective-permute-done.8 = bf16[192,768]{0,1:T(8,128)(2,1)S(1)} collective-permute-done((bf16[192,768]{0,1:T(8,128)(2,1)S(1)}, bf16[192,768]{0,1:T(8,128)(2,1)S(1)}, u32[]{:S(2)}, u32[]{:S(2)}) %collective-permute-start.8) | collective-permute-done | bytes 294944 | tf_op jit(solution)/shard_map/ppermute | solution.py:167
  88.0 0.7 fusion.29
  88.7 0.6 fusion.28
  89.3 0.6 fusion.30
  91.3 1.9 collective-permute-start.11
  93.2 5.7 %collective-permute-done.11 = bf16[192,384]{0,1:T(8,128)(2,1)S(1)} collective-permute-done((bf16[192,384]{0,1:T(8,128)(2,1)S(1)}, bf16[192,384]{0,1:T(8,128)(2,1)S(1)}, u32[]{:S(2)}, u32[]{:S(2)}) %collective-permute-start.11) | collective-permute-done | bytes 147488 | tf_op jit(solution)/shard_map/ppermute | solution.py:219
  99.3 16.7 %all_to_all.10 = bf16[4,192,768]{2,1,0:T(8,128)(2,1)S(1)} all-to-all(bf16[4,192,768]{2,1,0:T(8,128)(2,1)S(1)} %broadcast_in_dim.31), channel_id=1, replica_groups=mesh['section'=4,'sx'=4,'sy'=8,'head'=4] {'sx'}, dimensions={0} | all-to-all | bytes 2359296 | tf_op jit(solution)/shard_map/all_to_all | solution.py:226
  118.3 1.2 pad_maximum_fusion
  119.4 7.0 %all-to-all-start.1 = ((bf16[4,192,768]{2,1,0:T(8,128)(2,1)}), bf16[4,192,768]{2,1,0:T(8,128)(2,1)S(1)}, u32[]{:S(2)}, u32[]{:S(2)}) async-start(bf16[4,192,768]{2,1,0:T(8,128)(2,1)} %pad_maximum_fusion), calls=%async_computation.1 | async-start | bytes 2359296 | tf_op jit(solution)/shard_map/all_to_all | solution.py:235
  126.4 4.6 %collective-permute-start = (bf16[192,768]{1,0:T(8,128)(2,1)S(1)}, bf16[192,768]{1,0:T(8,128)(2,1)S(1)}, u32[]{:S(2)}, u32[]{:S(2)}) collective-permute-start(bf16[192,768]{1,0:T(8,128)(2,1)S(1)} %bitcast.74), channel_id=1, source_target_pairs={{0,0},{1,32},{2,64},{3,96},{32,1},{33,33},{34,65},{35,97},{64,2},{... | collective-permute-start | bytes 884744 | tf_op jit(solution)/shard_map/ppermute | solution.py:238
  131.1 2.1 %collective-permute-start.1 = (f32[768]{0:T(1024)S(1)}, f32[768]{0:T(1024)S(1)}, u32[]{:S(2)}, u32[]{:S(2)}) collective-permute-start(f32[768]{0:T(1024)S(1)} %reduce), channel_id=1, source_target_pairs={{0,0},{1,32},{2,64},{3,96},{32,1},{33,33},{34,65},{35,97},{64,2},{... | collective-permute-start | bytes 9224 | tf_op jit(solution)/shard_map/ppermute | solution.py:239
  133.2 25.5 %all-to-all-done.1 = bf16[4,192,768]{2,1,0:T(8,128)(2,1)S(1)} async-done(((bf16[4,192,768]{2,1,0:T(8,128)(2,1)}), bf16[4,192,768]{2,1,0:T(8,128)(2,1)S(1)}, u32[]{:S(2)}, u32[]{:S(2)}) %all-to-all-start.1) | async-done | bytes 1179680 | tf_op jit(solution)/shard_map/all_to_all | solution.py:235
  158.9 12.4 %collective-permute-done.1 = f32[768]{0:T(1024)S(1)} collective-permute-done((f32[768]{0:T(1024)S(1)}, f32[768]{0:T(1024)S(1)}, u32[]{:S(2)}, u32[]{:S(2)}) %collective-permute-start.1) | collective-permute-done | bytes 3104 | tf_op jit(solution)/shard_map/ppermute | solution.py:239
  171.4 1.9 collective-permute-start.12
  173.3 11.8 %collective-permute-done.12 = bf16[192,768]{1,0:T(8,128)(2,1)S(1)} collective-permute-done((bf16[192,768]{1,0:T(8,128)(2,1)S(1)}, bf16[192,768]{1,0:T(8,128)(2,1)S(1)}, u32[]{:S(2)}, u32[]{:S(2)}) %collective-permute-start.12) | collective-permute-done | bytes 294944 | tf_op jit(solution)/shard_map/ppermute | solution.py:244
  185.1 0.7 copy.111
  (75 shorter events, 8.2 us)
Async XLA Ops:
  6.5 81.4 %all-gather.3.cloned.1.call-start = ((), (), s32[]{:S(2)}) async-start(), calls=%async_computation.2 | async-start | bytes 1327104 | tf_op jit(solution)/shard_map/all_gather | solution.py:197
  8.9 16.8 %copy-start.1 = (bf16[1,192,768]{2,1,0:T(8,128)(2,1)S(1)}, bf16[1,192,768]{2,1,0:T(8,128)(2,1)}, u32[]{:S(2)}) copy-start(bf16[1,192,768]{2,1,0:T(8,128)(2,1)} %param.8) | copy-start | bytes 884740
  8.9 16.9 %copy-start.2 = (bf16[1,192,768]{2,1,0:T(8,128)(2,1)S(1)}, bf16[1,192,768]{2,1,0:T(8,128)(2,1)}, u32[]{:S(2)}) copy-start(bf16[1,192,768]{2,1,0:T(8,128)(2,1)} %param.9) | copy-start | bytes 884740
  8.9 16.8 %copy-start.3 = (bf16[1,192,768]{2,1,0:T(8,128)(2,1)S(1)}, bf16[1,192,768]{2,1,0:T(8,128)(2,1)}, u32[]{:S(2)}) copy-start(bf16[1,192,768]{2,1,0:T(8,128)(2,1)} %param.7) | copy-start | bytes 884740
  9.0 25.6 %collective-permute-start.4 = (bf16[192,768]{0,1:T(8,128)(2,1)S(1)}, bf16[192,768]{0,1:T(8,128)(2,1)}, u32[]{:S(2)}, u32[]{:S(2)}) collective-permute-start(bf16[192,768]{0,1:T(8,128)(2,1)S(1)} %pad_maximum_fusion.2), channel_id=1, source_target_pairs={{4,8},{12,16},{20,24},{28,32},{36,40},{44,48},{52,56},{60,64},{68,... | collective-permute-start | bytes 884744 | tf_op jit(solution)/shard_map/ppermute | solution.py:167
  10.4 37.5 %collective-permute-start.2 = (bf16[192,768]{0,1:T(8,128)(2,1)S(1)}, bf16[192,768]{0,1:T(8,128)(2,1)S(1)}, u32[]{:S(2)}, u32[]{:S(2)}) collective-permute-start(bf16[192,768]{0,1:T(8,128)(2,1)S(1)} %pad_maximum_fusion.2), channel_id=1, source_target_pairs={{0,8},{8,16},{16,24},{24,32},{32,40},{40,48},{48,56},{56,64},{64,7... | collective-permute-start | bytes 884744 | tf_op jit(solution)/shard_map/ppermute | solution.py:167
  15.0 10.9 %copy-start.4 = (s32[16,27]{1,0:T(8,128)S(1)}, s32[16,27]{1,0:T(8,128)}, u32[]{:S(2)}) copy-start(s32[16,27]{1,0:T(8,128)} %param.13) | copy-start | bytes 5188
  15.0 20.3 %collective-permute-start.5 = (bf16[192,768]{0,1:T(8,128)(2,1)S(1)}, bf16[192,768]{0,1:T(8,128)(2,1)}, u32[]{:S(2)}, u32[]{:S(2)}) collective-permute-start(bf16[192,768]{0,1:T(8,128)(2,1)S(1)} %pad_maximum_fusion.3), channel_id=1, source_target_pairs={{4,12},{12,20},{20,28},{28,36},{36,44},{44,52},{52,60},{60,68},{68... | collective-permute-start | bytes 884744 | tf_op jit(solution)/shard_map/ppermute | solution.py:167
  16.4 40.4 %collective-permute-start.3 = (bf16[192,768]{0,1:T(8,128)(2,1)S(1)}, bf16[192,768]{0,1:T(8,128)(2,1)}, u32[]{:S(2)}, u32[]{:S(2)}) collective-permute-start(bf16[192,768]{0,1:T(8,128)(2,1)S(1)} %pad_maximum_fusion.3), channel_id=1, source_target_pairs={{0,12},{8,20},{16,28},{24,36},{32,44},{40,52},{48,60},{56,68},{64,... | collective-permute-start | bytes 884744 | tf_op jit(solution)/shard_map/ppermute | solution.py:167
  24.3 34.5 %collective-permute-start.9 = (bf16[192,768]{0,1:T(8,128)(2,1)S(1)}, bf16[192,768]{0,1:T(8,128)(2,1)}, u32[]{:S(2)}, u32[]{:S(2)}) collective-permute-start(bf16[192,768]{0,1:T(8,128)(2,1)S(1)} %pad_maximum_fusion.2), channel_id=1, source_target_pairs={{12,0},{20,8},{28,16},{36,24},{44,32},{52,40},{60,48},{68,56},{76,... | collective-permute-start | bytes 884744 | tf_op jit(solution)/shard_map/ppermute | solution.py:167
  34.6 24.3 %collective-permute-start.10 = (bf16[192,768]{0,1:T(8,128)(2,1)S(1)}, bf16[192,768]{0,1:T(8,128)(2,1)S(1)}, u32[]{:S(2)}, u32[]{:S(2)}) collective-permute-start(bf16[192,768]{0,1:T(8,128)(2,1)S(1)} %pad_maximum_fusion.3), channel_id=1, source_target_pairs={{12,4},{20,12},{28,20},{36,28},{44,36},{52,44},{60,52},{68,60},{76... | collective-permute-start | bytes 884744 | tf_op jit(solution)/shard_map/ppermute | solution.py:167
  35.3 39.9 %collective-permute-start.7 = (bf16[192,768]{0,1:T(8,128)(2,1)S(1)}, bf16[192,768]{0,1:T(8,128)(2,1)S(1)}, u32[]{:S(2)}, u32[]{:S(2)}) collective-permute-start(bf16[192,768]{0,1:T(8,128)(2,1)S(1)} %pad_maximum_fusion.2), channel_id=1, source_target_pairs={{8,0},{16,8},{24,16},{32,24},{40,32},{48,40},{56,48},{64,56},{72,6... | collective-permute-start | bytes 884744 | tf_op jit(solution)/shard_map/ppermute | solution.py:167
  47.9 37.0 %collective-permute-start.8 = (bf16[192,768]{0,1:T(8,128)(2,1)S(1)}, bf16[192,768]{0,1:T(8,128)(2,1)S(1)}, u32[]{:S(2)}, u32[]{:S(2)}) collective-permute-start(bf16[192,768]{0,1:T(8,128)(2,1)S(1)} %pad_maximum_fusion.3), channel_id=1, source_target_pairs={{8,4},{16,12},{24,20},{32,28},{40,36},{48,44},{56,52},{64,60},{72,... | collective-permute-start | bytes 884744 | tf_op jit(solution)/shard_map/ppermute | solution.py:167
  56.8 29.1 %collective-permute-start.6 = (bf16[192,1152]{1,0:T(8,128)(2,1)S(1)}, bf16[192,1152]{1,0:T(8,128)(2,1)S(1)}, u32[]{:S(2)}, u32[]{:S(2)}) collective-permute-start(bf16[192,1152]{1,0:T(8,128)(2,1)S(1)} %pad_maximum_fusion.1), channel_id=1, source_target_pairs={{0,4},{4,0},{8,12},{12,8},{16,20},{20,16},{24,28},{28,24},{32,36},... | collective-permute-start | bytes 1327112 | tf_op jit(solution)/shard_map/ppermute | solution.py:132
  91.3 7.7 %collective-permute-start.11 = (bf16[192,384]{0,1:T(8,128)(2,1)S(1)}, bf16[192,384]{0,1:T(8,128)(2,1)S(1)}, u32[]{:S(2)}, u32[]{:S(2)}) collective-permute-start(bf16[192,384]{0,1:T(8,128)(2,1)S(1)} %get-tuple-element.29), channel_id=1, source_target_pairs={{0,4},{4,0},{8,12},{12,8},{16,20},{20,16},{24,28},{28,24},{32,36},... | collective-permute-start | bytes 442376 | tf_op jit(solution)/shard_map/ppermute | solution.py:219
  99.3 16.7 %copy-start = (bf16[1,768,768]{1,2,0:T(8,128)(2,1)S(1)}, bf16[1,768,768]{1,2,0:T(8,128)(2,1)}, u32[]{:S(2)}) copy-start(bf16[1,768,768]{1,2,0:T(8,128)(2,1)} %all-gather.3.cloned.1.call-done) | copy-start | bytes 3538948
  119.4 7.0 %copy-start.6 = (bf16[1,192,768]{2,1,0:T(8,128)(2,1)S(1)}, bf16[1,192,768]{2,1,0:T(8,128)(2,1)}, u32[]{:S(2)}) copy-start(bf16[1,192,768]{2,1,0:T(8,128)(2,1)} %param.10) | copy-start | bytes 884740
  119.4 11.6 %copy-start.5 = (f32[1,768]{1,0:T(1,128)S(1)}, f32[1,768]{1,0:T(1,128)}, u32[]{:S(2)}) copy-start(f32[1,768]{1,0:T(1,128)} %param.12) | copy-start | bytes 9220
  119.4 39.3 %all-to-all-start.1 = ((bf16[4,192,768]{2,1,0:T(8,128)(2,1)}), bf16[4,192,768]{2,1,0:T(8,128)(2,1)S(1)}, u32[]{:S(2)}, u32[]{:S(2)}) async-start(bf16[4,192,768]{2,1,0:T(8,128)(2,1)} %pad_maximum_fusion), calls=%async_computation.1 | async-start | bytes 2359296 | tf_op jit(solution)/shard_map/all_to_all | solution.py:235
  126.4 44.9 %collective-permute-start = (bf16[192,768]{1,0:T(8,128)(2,1)S(1)}, bf16[192,768]{1,0:T(8,128)(2,1)S(1)}, u32[]{:S(2)}, u32[]{:S(2)}) collective-permute-start(bf16[192,768]{1,0:T(8,128)(2,1)S(1)} %bitcast.74), channel_id=1, source_target_pairs={{0,0},{1,32},{2,64},{3,96},{32,1},{33,33},{34,65},{35,97},{64,2},{... | collective-permute-start | bytes 884744 | tf_op jit(solution)/shard_map/ppermute | solution.py:238
  131.1 40.2 %collective-permute-start.1 = (f32[768]{0:T(1024)S(1)}, f32[768]{0:T(1024)S(1)}, u32[]{:S(2)}, u32[]{:S(2)}) collective-permute-start(f32[768]{0:T(1024)S(1)} %reduce), channel_id=1, source_target_pairs={{0,0},{1,32},{2,64},{3,96},{32,1},{33,33},{34,65},{35,97},{64,2},{... | collective-permute-start | bytes 9224 | tf_op jit(solution)/shard_map/ppermute | solution.py:239
  171.4 13.7 %collective-permute-start.12 = (bf16[192,768]{1,0:T(8,128)(2,1)S(1)}, bf16[192,768]{1,0:T(8,128)(2,1)S(1)}, u32[]{:S(2)}, u32[]{:S(2)}) collective-permute-start(bf16[192,768]{1,0:T(8,128)(2,1)S(1)} %add_convert_fusion), channel_id=1, source_target_pairs={{0,128},{1,160},{2,192},{3,224},{32,129},{33,161},{34,193},{35,225... | collective-permute-start | bytes 884744 | tf_op jit(solution)/shard_map/ppermute | solution.py:244
Sparse Core Ops, SparseCore 0:
  25.8 57.0 all-gather.2

commit v8 on v5

--- a/solution.py
+++ b/solution.py
@@ -103,12 +103,13 @@
     tile_count = windows.shape[0]
     temporal_count = tile_count // spatial_count
     score_scale = 1.0 / math.sqrt(HD)
-    x_count = lax.axis_size("sx")
+    x_count = lax.axis_size("sxhi") * lax.axis_size("sxlo")
     y_count = lax.axis_size("sy")
     head_groups = lax.axis_size("head")
     sections = lax.axis_size("section")
     seq_count = x_count * y_count
-    x_index = lax.axis_index("sx")
+    pair_index = lax.axis_index("sxlo")
+    x_index = lax.axis_index("sxhi") * lax.axis_size("sxlo") + pair_index
     y_index = lax.axis_index("sy")
     position = x_index * y_count + y_index
     parity = position % 2
@@ -117,7 +118,7 @@
         windows[:, :, None] == jnp.arange(tile_count, dtype=jnp.int32)[None, None, :], axis=1
     )
     row_allowed = lax.dynamic_index_in_dim(allowed, temporal, 0, keepdims=False)
-    seq = ("sx", "sy")
+    seq = ("sxhi", "sxlo", "sy")
     half = feature_count // 2
     own_heads = head_count // 2
     tile_len = 2 * row_count
@@ -163,7 +164,7 @@
     query_float = query_parts.astype(jnp.float32)
     query_lengths = jnp.sqrt(jnp.sum(query_float * query_float, axis=2))
     row_bound = query_lengths * bound[None, :] * score_scale
-    weight_block = lax.all_gather(out_weight[0], "sy", axis=1, tiled=True)
+    weight_block = lax.all_gather(out_weight[0], ("sxhi", "sy"), axis=1, tiled=True)
     weight_block, row_bound = lax.optimization_barrier((weight_block, row_bound))
     weighted = jnp.zeros((tile_len, own_heads, HD), jnp.float32)
     summed = jnp.zeros((own_heads, tile_len), jnp.float32)
@@ -191,26 +192,31 @@
         jnp.concatenate([mine_rows, back], axis=1),
         jnp.concatenate([back, mine_rows], axis=1),
     )
-    spread = jnp.broadcast_to(attended[None], (x_count,) + attended.shape)
-    token_parts = lax.all_to_all(spread, "sx", 0, 0)
+    other = lax.ppermute(attended, "sxlo", [(0, 1), (1, 0)])
+    slab_of = [jnp.where(pair_index == a, attended, other) for a in range(2)]
+    columns = weight_block.shape[1] // 2
     terms = jnp.stack(
         [
-            jnp.dot(token_parts[j], weight_block, preferred_element_type=jnp.float32).astype(
-                jnp.bfloat16
-            )
-            for j in range(x_count)
+            jnp.dot(
+                slab_of[a],
+                weight_block[:, b * columns:(b + 1) * columns],
+                preferred_element_type=jnp.float32,
+            ).astype(jnp.bfloat16)
+            for a in range(2)
+            for b in range(2)
         ]
     )
     arrived = lax.all_to_all(terms, "head", 0, 0)
     mixed = jnp.sum(arrived.astype(jnp.float32), axis=0)
-    swap = linear_pairs((x_count, head_groups), lambda a, b: (b, a))
-    stream_block = lax.ppermute(stream[0], ("sx", "head"), swap)
-    gate_block = lax.ppermute(gate_scale[0], ("sx", "head"), swap)
+    fetch = linear_pairs((2, head_groups), lambda a, c: (c % 2, 2 * a + c // 2))
+    stream_block = lax.ppermute(stream[0], ("sxlo", "head"), fetch)
+    gate_block = lax.ppermute(gate_scale[0], ("sxlo", "head"), fetch)
     updated = (stream_block.astype(jnp.float32) + gate_block[None, :] * mixed).astype(jnp.bfloat16)
     hand = linear_pairs(
-        (sections, x_count, head_groups), lambda s, a, b: ((s + 1) % sections, b, a)
-    )
-    handed = lax.ppermute(updated, ("section", "sx", "head"), hand)
+        (sections, 2, head_groups),
+        lambda s, l, g: ((s + 1) % sections, g // 2, l + 2 * (g % 2)),
+    )
+    handed = lax.ppermute(updated, ("section", "sxlo", "head"), hand)
     return handed[None]
 
 
@@ -218,10 +224,10 @@
     sections, seq_count, head_count = mesh.devices.shape
     x_count = 4 if seq_count % 4 == 0 else 1
     split_mesh = Mesh(
-        mesh.devices.reshape(sections, x_count, seq_count // x_count, head_count),
-        ("section", "sx", "sy", "head"),
-    )
-    seq = ("sx", "sy")
+        mesh.devices.reshape(sections, x_count // 2, 2, seq_count // x_count, head_count),
+        ("section", "sxhi", "sxlo", "sy", "head"),
+    )
+    seq = ("sxhi", "sxlo", "sy")
     in_specs = (
         P("section", seq, "head"),
         P("section", seq, "head"),

time: 176 us -> 203 us (1.15)
  the two profiles are of different devices: /device:TPU:92 before, /device:TPU:64 now
where the time goes in v8:
time: 203 us; the launch traced here: 202 us
  waiting for transfers between devices  126 us (62%)
  starting transfers between devices  43.3 us (21%)
  between operations  15.7 us (8%)
  local copies, waits for them, and re-layouts  6.88 us (3%)
  other arithmetic  5.5 us (3%)
  matrix products  5.31 us (3%)
    all_gather x1, waiting for transfers between devices, on_device(): lax.all_gather(out_weight[0], ('sxhi', 'sy'), axis=1, tiled=True)  53.5 us
    ppermute x2, waiting for transfers between devices, on_device(): lax.ppermute((tile_k, tile_v), seq, [(i, i - 2) for i in range(2, seq_cou...  22.4 us
    all_to_all x1, waiting for transfers between devices, on_device(): arrived = lax.all_to_all(terms, 'head', 0, 0)  17.8 us
    ppermute x1, waiting for transfers between devices, on_device(): handed = lax.ppermute(updated, ('section', 'sxlo', 'head'), hand)  11.2 us
    ppermute x2, starting transfers between devices, on_device(): lax.ppermute((tile_k, tile_v), seq, [(i, i + 2) for i in range(seq_count...  10.6 us
    ppermute x3, starting transfers between devices, on_device(): lax.ppermute((partner_half(queries), partner_half(own_keys), partner_half...  9.33 us
    ppermute x1, waiting for transfers between devices, on_device(): gate_block = lax.ppermute(gate_scale[0], ('sxlo', 'head'), fetch)  8.5 us
    ppermute x1, waiting for transfers between devices, on_device(): other = lax.ppermute(attended, 'sxlo', [(0, 1), (1, 0)])  7.18 us
  transfers between devices with their start and end apart: 14, of which 8 were waited for; matrix products, arithmetic and copies ran while one was open for 5% of the time, Pallas kernels for 0%

profile of v8, /device:TPU:64, one launch (start us, length us, event | category | flops | bytes accessed | tf_op | source)
XLA Modules:
  0.0 202.4 jit_solution(2265600152553854689)
XLA Ops:
  6.5 0.7 all-gather.3.cloned.1.call-update
  7.3 1.0 dynamic-slice_bitcast_fusion.1
  8.3 3.5 %collective-permute-start.4 = (bf16[192,384]{1,0:T(8,128)(2,1)S(1)}, bf16[192,384]{1,0:T(8,128)(2,1)S(1)}, u32[]{:S(2)}, u32[]{:S(2)}) collective-permute-start(bf16[192,384]{1,0:T(8,128)(2,1)S(1)} %get-tuple-element.19), channel_id=1, source_target_pairs={{0,4},{4,0},{8,12},{12,8},{16,20},{20,16},{24,28},{28,24},{32,36},... | collective-permute-start | bytes 442376 | tf_op jit(solution)/shard_map/ppermute | solution.py:133
  11.8 1.0 constant_dynamic-slice_fusion.2
  12.8 2.4 %collective-permute-start.5 = (bf16[192,384]{1,0:T(8,128)(2,1)S(1)}, bf16[192,384]{1,0:T(8,128)(2,1)S(1)}, u32[]{:S(2)}, u32[]{:S(2)}) collective-permute-start(bf16[192,384]{1,0:T(8,128)(2,1)S(1)} %get-tuple-element.18), channel_id=1, source_target_pairs={{0,4},{4,0},{8,12},{12,8},{16,20},{20,16},{24,28},{28,24},{32,36},... | collective-permute-start | bytes 442376 | tf_op jit(solution)/shard_map/ppermute | solution.py:133
  15.2 1.0 constant_dynamic-slice_fusion.4
  16.2 3.5 %collective-permute-start.2 = (bf16[192,384]{1,0:T(8,128)(2,1)S(1)}, bf16[192,384]{1,0:T(8,128)(2,1)S(1)}, u32[]{:S(2)}, u32[]{:S(2)}) collective-permute-start(bf16[192,384]{1,0:T(8,128)(2,1)S(1)} %get-tuple-element.16), channel_id=1, source_target_pairs={{0,4},{4,0},{8,12},{12,8},{16,20},{20,16},{24,28},{28,24},{32,36},... | collective-permute-start | bytes 442376 | tf_op jit(solution)/shard_map/ppermute | solution.py:133
  22.8 0.8 maximum_select_fusion.5
  23.6 4.5 %collective-permute-start.6 = (bf16[384,384]{1,0:T(8,128)(2,1)}, bf16[384,384]{1,0:T(8,128)(2,1)S(1)}, u32[]{:S(2)}, u32[]{:S(2)}) collective-permute-start(bf16[384,384]{1,0:T(8,128)(2,1)} %maximum_select_fusion.5), channel_id=1, source_target_pairs={{0,8},{4,12},{8,16},{12,20},{16,24},{20,28},{24,32},{28,36},{32,40... | collective-permute-start | bytes 884744 | tf_op jit(solution)/shard_map/ppermute | solution.py:147
  28.1 1.3 collective-permute-start.7
  29.4 0.8 maximum_select_fusion.4
  30.2 1.3 collective-permute-start.8
  31.5 6.1 %collective-permute-start.3 = (bf16[384,384]{1,0:T(8,128)(2,1)}, bf16[384,384]{1,0:T(8,128)(2,1)S(1)}, u32[]{:S(2)}, u32[]{:S(2)}) collective-permute-start(bf16[384,384]{1,0:T(8,128)(2,1)} %maximum_select_fusion.4), channel_id=1, source_target_pairs={{0,8},{4,12},{8,16},{12,20},{16,24},{20,28},{24,32},{28,36},{32,40... | collective-permute-start | bytes 884744 | tf_op jit(solution)/shard_map/ppermute | solution.py:147
  39.6 16.1 %collective-permute-done.7 = bf16[384,384]{1,0:T(8,128)(2,1)S(1)} collective-permute-done((bf16[384,384]{1,0:T(8,128)(2,1)}, bf16[384,384]{1,0:T(8,128)(2,1)S(1)}, u32[]{:S(2)}, u32[]{:S(2)}) %collective-permute-start.7) | collective-permute-done | bytes 294944 | tf_op jit(solution)/shard_map/ppermute | solution.py:148
  55.9 6.3 %collective-permute-done.8 = bf16[384,384]{1,0:T(8,128)(2,1)} collective-permute-done((bf16[384,384]{1,0:T(8,128)(2,1)}, bf16[384,384]{1,0:T(8,128)(2,1)}, u32[]{:S(2)}, u32[]{:S(2)}) %collective-permute-start.8) | collective-permute-done | bytes 294944 | tf_op jit(solution)/shard_map/ppermute | solution.py:148
  62.2 1.2 copy.84
  64.2 53.5 %all-gather.3.cloned.1.call-done = bf16[1,768,1536]{1,2,0:T(8,128)(2,1)} async-done(((bf16[1,768,96]{1,2,0:T(8,128)(2,1)}), bf16[1,768,1536]{1,2,0:T(8,128)(2,1)}) %all-gather.3.cloned.1.call-update) | async-done | bytes 2359312 | tf_op jit(solution)/shard_map/all_gather | solution.py:167
  117.7 0.7 fusion.27
  118.4 0.6 fusion.28
  121.0 3.2 %collective-permute-start.9 = (bf16[192,384]{0,1:T(8,128)(2,1)S(1)}, bf16[192,384]{0,1:T(8,128)(2,1)S(1)}, u32[]{:S(2)}, u32[]{:S(2)}) collective-permute-start(bf16[192,384]{0,1:T(8,128)(2,1)S(1)} %get-tuple-element.14), channel_id=1, source_target_pairs={{0,4},{4,0},{8,12},{12,8},{16,20},{20,16},{24,28},{28,24},{32,36},... | collective-permute-start | bytes 442376 | tf_op jit(solution)/shard_map/ppermute | solution.py:189
  124.1 4.5 %collective-permute-done.9 = bf16[192,384]{0,1:T(8,128)(2,1)S(1)} collective-permute-done((bf16[192,384]{0,1:T(8,128)(2,1)S(1)}, bf16[192,384]{0,1:T(8,128)(2,1)S(1)}, u32[]{:S(2)}, u32[]{:S(2)}) %collective-permute-start.9) | collective-permute-done | bytes 147488 | tf_op jit(solution)/shard_map/ppermute | solution.py:189
  128.8 2.5 %collective-permute-start.10 = (bf16[192,768]{0,1:T(8,128)(2,1)S(1)}, bf16[192,768]{0,1:T(8,128)(2,1)S(1)}, u32[]{:S(2)}, u32[]{:S(2)}) collective-permute-start(bf16[192,768]{0,1:T(8,128)(2,1)S(1)} %maximum_select_fusion.3), channel_id=1, source_target_pairs={{0,32},{32,0},{1,33},{33,1},{2,34},{34,2},{3,35},{35,3},{4,36},{36... | collective-permute-start | bytes 884744 | tf_op jit(solution)/shard_map/ppermute | solution.py:195
  131.3 7.2 %collective-permute-done.10 = bf16[192,768]{0,1:T(8,128)(2,1)S(1)} collective-permute-done((bf16[192,768]{0,1:T(8,128)(2,1)S(1)}, bf16[192,768]{0,1:T(8,128)(2,1)S(1)}, u32[]{:S(2)}, u32[]{:S(2)}) %collective-permute-start.10) | collective-permute-done | bytes 294944 | tf_op jit(solution)/shard_map/ppermute | solution.py:195
  140.8 1.2 pad_maximum_fusion
  142.0 5.6 %all-to-all-start = ((bf16[4,192,768]{2,1,0:T(8,128)(2,1)}), bf16[4,192,768]{2,1,0:T(8,128)(2,1)S(1)}, u32[]{:S(2)}, u32[]{:S(2)}) async-start(bf16[4,192,768]{2,1,0:T(8,128)(2,1)} %pad_maximum_fusion), calls=%async_computation | async-start | bytes 2359296 | tf_op jit(solution)/shard_map/all_to_all | solution.py:209
  147.5 1.9 collective-permute-start
  149.5 5.7 %collective-permute-start.1 = (f32[768]{0:T(1024)S(1)}, f32[768]{0:T(1024)S(1)}, u32[]{:S(2)}, u32[]{:S(2)}) collective-permute-start(f32[768]{0:T(1024)S(1)} %reduce), channel_id=1, source_target_pairs={{0,0},{1,32},{2,1},{3,33},{32,2},{33,34},{34,3},{35,35},{4,4},{5,3... | collective-permute-start | bytes 9224 | tf_op jit(solution)/shard_map/ppermute | solution.py:213
  155.2 17.8 %all-to-all-done = bf16[4,192,768]{2,1,0:T(8,128)(2,1)S(1)} async-done(((bf16[4,192,768]{2,1,0:T(8,128)(2,1)}), bf16[4,192,768]{2,1,0:T(8,128)(2,1)S(1)}, u32[]{:S(2)}, u32[]{:S(2)}) %all-to-all-start) | async-done | bytes 1179680 | tf_op jit(solution)/shard_map/all_to_all | solution.py:209
  173.2 8.5 %collective-permute-done.1 = f32[768]{0:T(1024)S(1)} collective-permute-done((f32[768]{0:T(1024)S(1)}, f32[768]{0:T(1024)S(1)}, u32[]{:S(2)}, u32[]{:S(2)}) %collective-permute-start.1) | collective-permute-done | bytes 3104 | tf_op jit(solution)/shard_map/ppermute | solution.py:213
  181.8 1.9 collective-permute-start.11
  183.7 11.2 %collective-permute-done.11 = bf16[192,768]{1,0:T(8,128)(2,1)S(1)} collective-permute-done((bf16[192,768]{1,0:T(8,128)(2,1)S(1)}, bf16[192,768]{1,0:T(8,128)(2,1)S(1)}, u32[]{:S(2)}, u32[]{:S(2)}) %collective-permute-start.11) | collective-permute-done | bytes 294944 | tf_op jit(solution)/shard_map/ppermute | solution.py:219
  194.9 0.7 copy.112
  (51 shorter events, 8.7 us)
Async XLA Ops:
  6.5 13.2 %copy-start = (s32[16,27]{1,0:T(8,128)S(1)}, s32[16,27]{1,0:T(8,128)}, u32[]{:S(2)}) copy-start(s32[16,27]{1,0:T(8,128)} %param.13) | copy-start | bytes 5188
  6.5 111.1 %all-gather.3.cloned.1.call-start = ((), (), s32[]{:S(2)}) async-start(), calls=%async_computation.1 | async-start | bytes 2506752 | tf_op jit(solution)/shard_map/all_gather | solution.py:167
  8.3 30.0 %collective-permute-start.4 = (bf16[192,384]{1,0:T(8,128)(2,1)S(1)}, bf16[192,384]{1,0:T(8,128)(2,1)S(1)}, u32[]{:S(2)}, u32[]{:S(2)}) collective-permute-start(bf16[192,384]{1,0:T(8,128)(2,1)S(1)} %get-tuple-element.19), channel_id=1, source_target_pairs={{0,4},{4,0},{8,12},{12,8},{16,20},{20,16},{24,28},{28,24},{32,36},... | collective-permute-start | bytes 442376 | tf_op jit(solution)/shard_map/ppermute | solution.py:133
  12.8 10.0 %collective-permute-start.5 = (bf16[192,384]{1,0:T(8,128)(2,1)S(1)}, bf16[192,384]{1,0:T(8,128)(2,1)S(1)}, u32[]{:S(2)}, u32[]{:S(2)}) collective-permute-start(bf16[192,384]{1,0:T(8,128)(2,1)S(1)} %get-tuple-element.18), channel_id=1, source_target_pairs={{0,4},{4,0},{8,12},{12,8},{16,20},{20,16},{24,28},{28,24},{32,36},... | collective-permute-start | bytes 442376 | tf_op jit(solution)/shard_map/ppermute | solution.py:133
  16.2 13.2 %collective-permute-start.2 = (bf16[192,384]{1,0:T(8,128)(2,1)S(1)}, bf16[192,384]{1,0:T(8,128)(2,1)S(1)}, u32[]{:S(2)}, u32[]{:S(2)}) collective-permute-start(bf16[192,384]{1,0:T(8,128)(2,1)S(1)} %get-tuple-element.16), channel_id=1, source_target_pairs={{0,4},{4,0},{8,12},{12,8},{16,20},{20,16},{24,28},{28,24},{32,36},... | collective-permute-start | bytes 442376 | tf_op jit(solution)/shard_map/ppermute | solution.py:133
  23.6 15.8 %collective-permute-start.6 = (bf16[384,384]{1,0:T(8,128)(2,1)}, bf16[384,384]{1,0:T(8,128)(2,1)S(1)}, u32[]{:S(2)}, u32[]{:S(2)}) collective-permute-start(bf16[384,384]{1,0:T(8,128)(2,1)} %maximum_select_fusion.5), channel_id=1, source_target_pairs={{0,8},{4,12},{8,16},{12,20},{16,24},{20,28},{24,32},{28,36},{32,40... | collective-permute-start | bytes 884744 | tf_op jit(solution)/shard_map/ppermute | solution.py:147
  28.1 27.6 %collective-permute-start.7 = (bf16[384,384]{1,0:T(8,128)(2,1)}, bf16[384,384]{1,0:T(8,128)(2,1)S(1)}, u32[]{:S(2)}, u32[]{:S(2)}) collective-permute-start(bf16[384,384]{1,0:T(8,128)(2,1)} %maximum_select_fusion.5), channel_id=1, source_target_pairs={{8,0},{12,4},{16,8},{20,12},{24,16},{28,20},{32,24},{36,28},{40,32... | collective-permute-start | bytes 884744 | tf_op jit(solution)/shard_map/ppermute | solution.py:148
  30.2 32.0 %collective-permute-start.8 = (bf16[384,384]{1,0:T(8,128)(2,1)}, bf16[384,384]{1,0:T(8,128)(2,1)}, u32[]{:S(2)}, u32[]{:S(2)}) collective-permute-start(bf16[384,384]{1,0:T(8,128)(2,1)} %maximum_select_fusion.4), channel_id=1, source_target_pairs={{8,0},{12,4},{16,8},{20,12},{24,16},{28,20},{32,24},{36,28},{40,32... | collective-permute-start | bytes 884744 | tf_op jit(solution)/shard_map/ppermute | solution.py:148
  31.5 31.9 %collective-permute-start.3 = (bf16[384,384]{1,0:T(8,128)(2,1)}, bf16[384,384]{1,0:T(8,128)(2,1)S(1)}, u32[]{:S(2)}, u32[]{:S(2)}) collective-permute-start(bf16[384,384]{1,0:T(8,128)(2,1)} %maximum_select_fusion.4), channel_id=1, source_target_pairs={{0,8},{4,12},{8,16},{12,20},{16,24},{20,28},{24,32},{28,36},{32,40... | collective-permute-start | bytes 884744 | tf_op jit(solution)/shard_map/ppermute | solution.py:147
  120.4 18.1 %copy-start.2 = (bf16[1,768,1536]{1,2,0:T(8,128)(2,1)S(1)}, bf16[1,768,1536]{1,2,0:T(8,128)(2,1)}, u32[]{:S(2)}) copy-start(bf16[1,768,1536]{1,2,0:T(8,128)(2,1)} %all-gather.3.cloned.1.call-done) | copy-start | bytes 7077892
  121.0 7.7 %collective-permute-start.9 = (bf16[192,384]{0,1:T(8,128)(2,1)S(1)}, bf16[192,384]{0,1:T(8,128)(2,1)S(1)}, u32[]{:S(2)}, u32[]{:S(2)}) collective-permute-start(bf16[192,384]{0,1:T(8,128)(2,1)S(1)} %get-tuple-element.14), channel_id=1, source_target_pairs={{0,4},{4,0},{8,12},{12,8},{16,20},{20,16},{24,28},{28,24},{32,36},... | collective-permute-start | bytes 442376 | tf_op jit(solution)/shard_map/ppermute | solution.py:189
  128.8 9.7 %collective-permute-start.10 = (bf16[192,768]{0,1:T(8,128)(2,1)S(1)}, bf16[192,768]{0,1:T(8,128)(2,1)S(1)}, u32[]{:S(2)}, u32[]{:S(2)}) collective-permute-start(bf16[192,768]{0,1:T(8,128)(2,1)S(1)} %maximum_select_fusion.3), channel_id=1, source_target_pairs={{0,32},{32,0},{1,33},{33,1},{2,34},{34,2},{3,35},{35,3},{4,36},{36... | collective-permute-start | bytes 884744 | tf_op jit(solution)/shard_map/ppermute | solution.py:195
  141.9 5.6 %copy-start.3 = (bf16[1,192,768]{2,1,0:T(8,128)(2,1)S(1)}, bf16[1,192,768]{2,1,0:T(8,128)(2,1)}, u32[]{:S(2)}) copy-start(bf16[1,192,768]{2,1,0:T(8,128)(2,1)} %param.10) | copy-start | bytes 884740
  142.0 7.5 %copy-start.1 = (f32[1,768]{1,0:T(1,128)S(1)}, f32[1,768]{1,0:T(1,128)}, u32[]{:S(2)}) copy-start(f32[1,768]{1,0:T(1,128)} %param.12) | copy-start | bytes 9220
  142.0 31.1 %all-to-all-start = ((bf16[4,192,768]{2,1,0:T(8,128)(2,1)}), bf16[4,192,768]{2,1,0:T(8,128)(2,1)S(1)}, u32[]{:S(2)}, u32[]{:S(2)}) async-start(bf16[4,192,768]{2,1,0:T(8,128)(2,1)} %pad_maximum_fusion), calls=%async_computation | async-start | bytes 2359296 | tf_op jit(solution)/shard_map/all_to_all | solution.py:209
  147.5 34.1 %collective-permute-start = (bf16[192,768]{1,0:T(8,128)(2,1)S(1)}, bf16[192,768]{1,0:T(8,128)(2,1)S(1)}, u32[]{:S(2)}, u32[]{:S(2)}) collective-permute-start(bf16[192,768]{1,0:T(8,128)(2,1)S(1)} %bitcast.58), channel_id=1, source_target_pairs={{0,0},{1,32},{2,1},{3,33},{32,2},{33,34},{34,3},{35,35},{4,4},{5,3... | collective-permute-start | bytes 884744 | tf_op jit(solution)/shard_map/ppermute | solution.py:212
  149.5 32.2 %collective-permute-start.1 = (f32[768]{0:T(1024)S(1)}, f32[768]{0:T(1024)S(1)}, u32[]{:S(2)}, u32[]{:S(2)}) collective-permute-start(f32[768]{0:T(1024)S(1)} %reduce), channel_id=1, source_target_pairs={{0,0},{1,32},{2,1},{3,33},{32,2},{33,34},{34,3},{35,35},{4,4},{5,3... | collective-permute-start | bytes 9224 | tf_op jit(solution)/shard_map/ppermute | solution.py:213
  181.8 13.1 %collective-permute-start.11 = (bf16[192,768]{1,0:T(8,128)(2,1)S(1)}, bf16[192,768]{1,0:T(8,128)(2,1)S(1)}, u32[]{:S(2)}, u32[]{:S(2)}) collective-permute-start(bf16[192,768]{1,0:T(8,128)(2,1)S(1)} %add_convert_fusion), channel_id=1, source_target_pairs={{0,128},{1,130},{2,160},{3,162},{32,129},{33,131},{34,161},{35,163... | collective-permute-start | bytes 884744 | tf_op jit(solution)/shard_map/ppermute | solution.py:219
Sparse Core Ops, SparseCore 0:
  10.5 107.0 all-gather.2

commit v9 on v5

--- a/solution.py
+++ b/solution.py
@@ -191,26 +191,34 @@
         jnp.concatenate([mine_rows, back], axis=1),
         jnp.concatenate([back, mine_rows], axis=1),
     )
-    spread = jnp.broadcast_to(attended[None], (x_count,) + attended.shape)
-    token_parts = lax.all_to_all(spread, "sx", 0, 0)
-    terms = jnp.stack(
-        [
-            jnp.dot(token_parts[j], weight_block, preferred_element_type=jnp.float32).astype(
-                jnp.bfloat16
-            )
-            for j in range(x_count)
-        ]
-    )
-    arrived = lax.all_to_all(terms, "head", 0, 0)
-    mixed = jnp.sum(arrived.astype(jnp.float32), axis=0)
     swap = linear_pairs((x_count, head_groups), lambda a, b: (b, a))
     stream_block = lax.ppermute(stream[0], ("sx", "head"), swap)
     gate_block = lax.ppermute(gate_scale[0], ("sx", "head"), swap)
-    updated = (stream_block.astype(jnp.float32) + gate_block[None, :] * mixed).astype(jnp.bfloat16)
     hand = linear_pairs(
         (sections, x_count, head_groups), lambda s, a, b: ((s + 1) % sections, b, a)
     )
-    handed = lax.ppermute(updated, ("section", "sx", "head"), hand)
+    chunk_rows = row_count // 2
+    handed_chunks = []
+    for chunk in range(2):
+        rows = slice(chunk * chunk_rows, (chunk + 1) * chunk_rows)
+        piece = attended[rows]
+        spread = jnp.broadcast_to(piece[None], (x_count,) + piece.shape)
+        token_parts = lax.all_to_all(spread, "sx", 0, 0)
+        terms = jnp.stack(
+            [
+                jnp.dot(
+                    token_parts[j], weight_block, preferred_element_type=jnp.float32
+                ).astype(jnp.bfloat16)
+                for j in range(x_count)
+            ]
+        )
+        arrived = lax.all_to_all(terms, "head", 0, 0)
+        mixed = jnp.sum(arrived.astype(jnp.float32), axis=0)
+        updated = (
+            stream_block[rows].astype(jnp.float32) + gate_block[None, :] * mixed
+        ).astype(jnp.bfloat16)
+        handed_chunks.append(lax.ppermute(updated, ("section", "sx", "head"), hand))
+    handed = jnp.concatenate(handed_chunks, axis=0)
     return handed[None]
 
 

time: 176 us -> 187 us (1.062)
  the two profiles are of different devices: /device:TPU:92 before, /device:TPU:127 now
where the time goes in v9:
time: 187 us; the launch traced here: 186 us
  starting transfers between devices  78.1 us (42%)
  waiting for transfers between devices  70.6 us (38%)
  between operations  15.8 us (8%)
  local copies, waits for them, and re-layouts  7.42 us (4%)
  matrix products  7.02 us (4%)
  other arithmetic  6.84 us (4%)
    ppermute x2, starting transfers between devices, on_device(): handed_chunks.append(lax.ppermute(updated, ('section', 'sx', 'head'), hand))  22.7 us
    ppermute x2, waiting for transfers between devices, on_device(): lax.ppermute((tile_k, tile_v), seq, [(i, i + 2) for i in range(seq_count...  16.5 us
    all_to_all x2, waiting for transfers between devices, on_device(): arrived = lax.all_to_all(terms, 'head', 0, 0)  14.7 us
    all_to_all x2, starting transfers between devices, on_device(): arrived = lax.all_to_all(terms, 'head', 0, 0)  14.4 us
    ppermute x2, starting transfers between devices, on_device(): lax.ppermute((tile_k, tile_v), seq, [(i, i - 2) for i in range(2, seq_cou...  10.6 us
    all_to_all x2, starting transfers between devices, on_device(): token_parts = lax.all_to_all(spread, 'sx', 0, 0)  9.09 us
    ppermute x2, waiting for transfers between devices, on_device(): handed_chunks.append(lax.ppermute(updated, ('section', 'sx', 'head'), hand))  8.66 us
    ppermute x3, starting transfers between devices, on_device(): lax.ppermute((partner_half(queries), partner_half(own_keys), partner_half...  8.25 us
  transfers between devices with their start and end apart: 17, of which 12 were waited for; matrix products, arithmetic and copies ran while one was open for 8% of the time, Pallas kernels for 0%

profile of v9, /device:TPU:127, one launch (start us, length us, event | category | flops | bytes accessed | tf_op | source)
XLA Modules:
  0.0 185.8 jit_solution(13195040477741958044)
XLA Ops:
  7.3 1.0 dynamic-slice_bitcast_fusion.1
  8.3 3.0 %collective-permute-start.4 = (bf16[192,384]{1,0:T(8,128)(2,1)S(1)}, bf16[192,384]{1,0:T(8,128)(2,1)S(1)}, u32[]{:S(2)}, u32[]{:S(2)}) collective-permute-start(bf16[192,384]{1,0:T(8,128)(2,1)S(1)} %get-tuple-element.23), channel_id=1, source_target_pairs={{0,4},{4,0},{8,12},{12,8},{16,20},{20,16},{24,28},{28,24},{32,36},... | collective-permute-start | bytes 442376 | tf_op jit(solution)/shard_map/ppermute | solution.py:132
  11.3 1.0 constant_dynamic-slice_fusion.2
  12.3 2.3 %collective-permute-start.5 = (bf16[192,384]{1,0:T(8,128)(2,1)S(1)}, bf16[192,384]{1,0:T(8,128)(2,1)S(1)}, u32[]{:S(2)}, u32[]{:S(2)}) collective-permute-start(bf16[192,384]{1,0:T(8,128)(2,1)S(1)} %get-tuple-element.22), channel_id=1, source_target_pairs={{0,4},{4,0},{8,12},{12,8},{16,20},{20,16},{24,28},{28,24},{32,36},... | collective-permute-start | bytes 442376 | tf_op jit(solution)/shard_map/ppermute | solution.py:132
  14.7 3.0 %collective-permute-start.2 = (bf16[192,384]{1,0:T(8,128)(2,1)S(1)}, bf16[192,384]{1,0:T(8,128)(2,1)S(1)}, u32[]{:S(2)}, u32[]{:S(2)}) collective-permute-start(bf16[192,384]{1,0:T(8,128)(2,1)S(1)} %get-tuple-element.20), channel_id=1, source_target_pairs={{0,4},{4,0},{8,12},{12,8},{16,20},{20,16},{24,28},{28,24},{32,36},... | collective-permute-start | bytes 442376 | tf_op jit(solution)/shard_map/ppermute | solution.py:132
  21.7 1.3 collective-permute-start.6
  22.9 4.9 %collective-permute-start.7 = (bf16[384,384]{1,0:T(8,128)(2,1)}, bf16[384,384]{1,0:T(8,128)(2,1)S(1)}, u32[]{:S(2)}, u32[]{:S(2)}) collective-permute-start(bf16[384,384]{1,0:T(8,128)(2,1)} %maximum_select_fusion.5), channel_id=1, source_target_pairs={{8,0},{12,4},{16,8},{20,12},{24,16},{28,20},{32,24},{36,28},{40,32... | collective-permute-start | bytes 884744 | tf_op jit(solution)/shard_map/ppermute | solution.py:147
  28.7 5.7 %collective-permute-start.8 = (bf16[384,384]{1,0:T(8,128)(2,1)}, bf16[384,384]{1,0:T(8,128)(2,1)}, u32[]{:S(2)}, u32[]{:S(2)}) collective-permute-start(bf16[384,384]{1,0:T(8,128)(2,1)} %maximum_select_fusion.4), channel_id=1, source_target_pairs={{8,0},{12,4},{16,8},{20,12},{24,16},{28,20},{32,24},{36,28},{40,32... | collective-permute-start | bytes 884744 | tf_op jit(solution)/shard_map/ppermute | solution.py:147
  34.3 1.3 collective-permute-start.3
  37.4 14.7 %collective-permute-done.6 = bf16[384,384]{1,0:T(8,128)(2,1)S(1)} collective-permute-done((bf16[384,384]{1,0:T(8,128)(2,1)}, bf16[384,384]{1,0:T(8,128)(2,1)S(1)}, u32[]{:S(2)}, u32[]{:S(2)}) %collective-permute-start.6) | collective-permute-done | bytes 294944 | tf_op jit(solution)/shard_map/ppermute | solution.py:146
  52.5 6.7 %collective-permute-done.8 = bf16[384,384]{1,0:T(8,128)(2,1)} collective-permute-done((bf16[384,384]{1,0:T(8,128)(2,1)}, bf16[384,384]{1,0:T(8,128)(2,1)}, u32[]{:S(2)}, u32[]{:S(2)}) %collective-permute-start.8) | collective-permute-done | bytes 294944 | tf_op jit(solution)/shard_map/ppermute | solution.py:147
  59.2 1.2 copy.94
  60.4 1.8 collective-permute-done.3
  63.0 3.2 %all-gather.3.cloned.1.call-done = bf16[1,768,768]{1,2,0:T(8,128)(2,1)} async-done(((bf16[1,768,96]{1,2,0:T(8,128)(2,1)}), bf16[1,768,768]{1,2,0:T(8,128)(2,1)}) %all-gather.3.cloned.1.call-update) | async-done | bytes 1179664 | tf_op jit(solution)/shard_map/all_gather | solution.py:166
  69.5 1.9 %collective-permute-start.9 = (bf16[192,384]{0,1:T(8,128)(2,1)S(1)}, bf16[192,384]{0,1:T(8,128)(2,1)S(1)}, u32[]{:S(2)}, u32[]{:S(2)}) collective-permute-start(bf16[192,384]{0,1:T(8,128)(2,1)S(1)} %get-tuple-element.18), channel_id=1, source_target_pairs={{0,4},{4,0},{8,12},{12,8},{16,20},{20,16},{24,28},{28,24},{32,36},... | collective-permute-start | bytes 442376 | tf_op jit(solution)/shard_map/ppermute | solution.py:188
  71.4 5.9 %collective-permute-done.9 = bf16[192,384]{0,1:T(8,128)(2,1)S(1)} collective-permute-done((bf16[192,384]{0,1:T(8,128)(2,1)S(1)}, bf16[192,384]{0,1:T(8,128)(2,1)S(1)}, u32[]{:S(2)}, u32[]{:S(2)}) %collective-permute-start.9) | collective-permute-done | bytes 147488 | tf_op jit(solution)/shard_map/ppermute | solution.py:188
  77.7 0.9 broadcast_in_dim.20
  78.5 3.9 %all-to-all-start = ((bf16[4,96,768]{2,1,0:T(8,128)(2,1)}), bf16[4,96,768]{2,1,0:T(8,128)(2,1)S(1)}, u32[]{:S(2)}, u32[]{:S(2)}) async-start(bf16[4,96,768]{2,1,0:T(8,128)(2,1)} %broadcast_in_dim.20), calls=%async_computation | async-start | bytes 1179648 | tf_op jit(solution)/shard_map/all_to_all | solution.py:206
  82.6 5.5 %all-to-all-done = bf16[4,96,768]{2,1,0:T(8,128)(2,1)S(1)} async-done(((bf16[4,96,768]{2,1,0:T(8,128)(2,1)}), bf16[4,96,768]{2,1,0:T(8,128)(2,1)S(1)}, u32[]{:S(2)}, u32[]{:S(2)}) %all-to-all-start) | async-done | bytes 589856 | tf_op jit(solution)/shard_map/all_to_all | solution.py:206
  89.0 5.1 %all-to-all-start.2 = ((bf16[4,96,768]{2,1,0:T(8,128)(2,1)}), bf16[4,96,768]{2,1,0:T(8,128)(2,1)S(1)}, u32[]{:S(2)}, u32[]{:S(2)}) async-start(bf16[4,96,768]{2,1,0:T(8,128)(2,1)} %broadcast_in_dim.21), calls=%async_computation.2 | async-start | bytes 1179648 | tf_op jit(solution)/shard_map/all_to_all | solution.py:206
  97.1 2.6 %all-to-all-done.2 = bf16[4,96,768]{2,1,0:T(8,128)(2,1)S(1)} async-done(((bf16[4,96,768]{2,1,0:T(8,128)(2,1)}), bf16[4,96,768]{2,1,0:T(8,128)(2,1)S(1)}, u32[]{:S(2)}, u32[]{:S(2)}) %all-to-all-start.2) | async-done | bytes 589856 | tf_op jit(solution)/shard_map/all_to_all | solution.py:206
  99.6 6.5 %all-to-all-start.1 = ((bf16[4,96,768]{2,1,0:T(8,128)(2,1)}), bf16[4,96,768]{2,1,0:T(8,128)(2,1)S(1)}, u32[]{:S(2)}, u32[]{:S(2)}) async-start(bf16[4,96,768]{2,1,0:T(8,128)(2,1)} %pad_maximum_fusion), calls=%async_computation.1 | async-start | bytes 1179648 | tf_op jit(solution)/shard_map/all_to_all | solution.py:215
  109.1 5.2 %all-to-all-done.1 = bf16[4,96,768]{2,1,0:T(8,128)(2,1)S(1)} async-done(((bf16[4,96,768]{2,1,0:T(8,128)(2,1)}), bf16[4,96,768]{2,1,0:T(8,128)(2,1)S(1)}, u32[]{:S(2)}, u32[]{:S(2)}) %all-to-all-start.1) | async-done | bytes 589856 | tf_op jit(solution)/shard_map/all_to_all | solution.py:215
  114.3 7.9 %all-to-all-start.3 = ((bf16[4,96,768]{2,1,0:T(8,128)(2,1)}), bf16[4,96,768]{2,1,0:T(8,128)(2,1)S(1)}, u32[]{:S(2)}, u32[]{:S(2)}) async-start(bf16[4,96,768]{2,1,0:T(8,128)(2,1)} %pad_maximum_fusion.1), calls=%async_computation.3 | async-start | bytes 1179648 | tf_op jit(solution)/shard_map/all_to_all | solution.py:215
  122.2 5.4 %collective-permute-start = (bf16[192,768]{1,0:T(8,128)(2,1)S(1)}, bf16[192,768]{1,0:T(8,128)(2,1)S(1)}, u32[]{:S(2)}, u32[]{:S(2)}) collective-permute-start(bf16[192,768]{1,0:T(8,128)(2,1)S(1)} %bitcast.102), channel_id=1, source_target_pairs={{0,0},{1,32},{2,64},{3,96},{32,1},{33,33},{34,65},{35,97},{64,2},{... | collective-permute-start | bytes 884744 | tf_op jit(solution)/shard_map/ppermute | solution.py:195
  127.7 3.1 %collective-permute-start.1 = (f32[768]{0:T(1024)S(1)}, f32[768]{0:T(1024)S(1)}, u32[]{:S(2)}, u32[]{:S(2)}) collective-permute-start(f32[768]{0:T(1024)S(1)} %reduce), channel_id=1, source_target_pairs={{0,0},{1,32},{2,64},{3,96},{32,1},{33,33},{34,65},{35,97},{64,2},{... | collective-permute-start | bytes 9224 | tf_op jit(solution)/shard_map/ppermute | solution.py:196
  130.9 9.5 %all-to-all-done.3 = bf16[4,96,768]{2,1,0:T(8,128)(2,1)S(1)} async-done(((bf16[4,96,768]{2,1,0:T(8,128)(2,1)}), bf16[4,96,768]{2,1,0:T(8,128)(2,1)S(1)}, u32[]{:S(2)}, u32[]{:S(2)}) %all-to-all-start.3) | async-done | bytes 589856 | tf_op jit(solution)/shard_map/all_to_all | solution.py:215
  140.5 6.2 %collective-permute-done.1 = f32[768]{0:T(1024)S(1)} collective-permute-done((f32[768]{0:T(1024)S(1)}, f32[768]{0:T(1024)S(1)}, u32[]{:S(2)}, u32[]{:S(2)}) %collective-permute-start.1) | collective-permute-done | bytes 3104 | tf_op jit(solution)/shard_map/ppermute | solution.py:196
  146.8 20.8 %collective-permute-start.11 = (bf16[96,768]{1,0:T(8,128)(2,1)S(1)}, bf16[96,768]{1,0:T(8,128)(2,1)S(1)}, u32[]{:S(2)}, u32[]{:S(2)}) collective-permute-start(bf16[96,768]{1,0:T(8,128)(2,1)S(1)} %get-tuple-element.16), channel_id=1, source_target_pairs={{0,128},{1,160},{2,192},{3,224},{32,129},{33,161},{34,193},{35,225... | collective-permute-start | bytes 442376 | tf_op jit(solution)/shard_map/ppermute | solution.py:220
  167.6 1.9 %collective-permute-start.10 = (bf16[96,768]{1,0:T(8,128)(2,1)S(1)}, bf16[96,768]{1,0:T(8,128)(2,1)S(1)}, u32[]{:S(2)}, u32[]{:S(2)}) collective-permute-start(bf16[96,768]{1,0:T(8,128)(2,1)S(1)} %get-tuple-element.15), channel_id=1, source_target_pairs={{0,128},{1,160},{2,192},{3,224},{32,129},{33,161},{34,193},{35,225... | collective-permute-start | bytes 442376 | tf_op jit(solution)/shard_map/ppermute | solution.py:220
  169.5 3.3 %collective-permute-done.11 = bf16[96,768]{1,0:T(8,128)(2,1)S(1)} collective-permute-done((bf16[96,768]{1,0:T(8,128)(2,1)S(1)}, bf16[96,768]{1,0:T(8,128)(2,1)S(1)}, u32[]{:S(2)}, u32[]{:S(2)}) %collective-permute-start.11) | collective-permute-done | bytes 147488 | tf_op jit(solution)/shard_map/ppermute | solution.py:220
  172.8 5.4 %collective-permute-done.10 = bf16[96,768]{1,0:T(8,128)(2,1)S(1)} collective-permute-done((bf16[96,768]{1,0:T(8,128)(2,1)S(1)}, bf16[96,768]{1,0:T(8,128)(2,1)S(1)}, u32[]{:S(2)}, u32[]{:S(2)}) %collective-permute-start.10) | collective-permute-done | bytes 147488 | tf_op jit(solution)/shard_map/ppermute | solution.py:220
  (70 shorter events, 17.9 us)
Async XLA Ops:
  6.5 8.1 %copy-start.1 = (bf16[1,192,768]{2,1,0:T(8,128)(2,1)S(1)}, bf16[1,192,768]{2,1,0:T(8,128)(2,1)}, u32[]{:S(2)}) copy-start(bf16[1,192,768]{2,1,0:T(8,128)(2,1)} %param.9) | copy-start | bytes 884740
  6.5 11.1 %copy-start.2 = (s32[16,27]{1,0:T(8,128)S(1)}, s32[16,27]{1,0:T(8,128)}, u32[]{:S(2)}) copy-start(s32[16,27]{1,0:T(8,128)} %param.13) | copy-start | bytes 5188
  6.5 59.6 %all-gather.3.cloned.1.call-start = ((), (), s32[]{:S(2)}) async-start(), calls=%async_computation.4 | async-start | bytes 1327104 | tf_op jit(solution)/shard_map/all_gather | solution.py:166
  8.3 28.1 %collective-permute-start.4 = (bf16[192,384]{1,0:T(8,128)(2,1)S(1)}, bf16[192,384]{1,0:T(8,128)(2,1)S(1)}, u32[]{:S(2)}, u32[]{:S(2)}) collective-permute-start(bf16[192,384]{1,0:T(8,128)(2,1)S(1)} %get-tuple-element.23), channel_id=1, source_target_pairs={{0,4},{4,0},{8,12},{12,8},{16,20},{20,16},{24,28},{28,24},{32,36},... | collective-permute-start | bytes 442376 | tf_op jit(solution)/shard_map/ppermute | solution.py:132
  12.3 8.5 %collective-permute-start.5 = (bf16[192,384]{1,0:T(8,128)(2,1)S(1)}, bf16[192,384]{1,0:T(8,128)(2,1)S(1)}, u32[]{:S(2)}, u32[]{:S(2)}) collective-permute-start(bf16[192,384]{1,0:T(8,128)(2,1)S(1)} %get-tuple-element.22), channel_id=1, source_target_pairs={{0,4},{4,0},{8,12},{12,8},{16,20},{20,16},{24,28},{28,24},{32,36},... | collective-permute-start | bytes 442376 | tf_op jit(solution)/shard_map/ppermute | solution.py:132
  14.7 13.2 %collective-permute-start.2 = (bf16[192,384]{1,0:T(8,128)(2,1)S(1)}, bf16[192,384]{1,0:T(8,128)(2,1)S(1)}, u32[]{:S(2)}, u32[]{:S(2)}) collective-permute-start(bf16[192,384]{1,0:T(8,128)(2,1)S(1)} %get-tuple-element.20), channel_id=1, source_target_pairs={{0,4},{4,0},{8,12},{12,8},{16,20},{20,16},{24,28},{28,24},{32,36},... | collective-permute-start | bytes 442376 | tf_op jit(solution)/shard_map/ppermute | solution.py:132
  21.7 30.4 %collective-permute-start.6 = (bf16[384,384]{1,0:T(8,128)(2,1)}, bf16[384,384]{1,0:T(8,128)(2,1)S(1)}, u32[]{:S(2)}, u32[]{:S(2)}) collective-permute-start(bf16[384,384]{1,0:T(8,128)(2,1)} %maximum_select_fusion.5), channel_id=1, source_target_pairs={{0,8},{4,12},{8,16},{12,20},{16,24},{20,28},{24,32},{28,36},{32,40... | collective-permute-start | bytes 884744 | tf_op jit(solution)/shard_map/ppermute | solution.py:146
  22.9 29.3 %collective-permute-start.7 = (bf16[384,384]{1,0:T(8,128)(2,1)}, bf16[384,384]{1,0:T(8,128)(2,1)S(1)}, u32[]{:S(2)}, u32[]{:S(2)}) collective-permute-start(bf16[384,384]{1,0:T(8,128)(2,1)} %maximum_select_fusion.5), channel_id=1, source_target_pairs={{8,0},{12,4},{16,8},{20,12},{24,16},{28,20},{32,24},{36,28},{40,32... | collective-permute-start | bytes 884744 | tf_op jit(solution)/shard_map/ppermute | solution.py:147
  28.7 30.5 %collective-permute-start.8 = (bf16[384,384]{1,0:T(8,128)(2,1)}, bf16[384,384]{1,0:T(8,128)(2,1)}, u32[]{:S(2)}, u32[]{:S(2)}) collective-permute-start(bf16[384,384]{1,0:T(8,128)(2,1)} %maximum_select_fusion.4), channel_id=1, source_target_pairs={{8,0},{12,4},{16,8},{20,12},{24,16},{28,20},{32,24},{36,28},{40,32... | collective-permute-start | bytes 884744 | tf_op jit(solution)/shard_map/ppermute | solution.py:147
  34.3 27.9 %collective-permute-start.3 = (bf16[384,384]{1,0:T(8,128)(2,1)}, bf16[384,384]{1,0:T(8,128)(2,1)S(1)}, u32[]{:S(2)}, u32[]{:S(2)}) collective-permute-start(bf16[384,384]{1,0:T(8,128)(2,1)} %maximum_select_fusion.4), channel_id=1, source_target_pairs={{0,8},{4,12},{8,16},{12,20},{16,24},{20,28},{24,32},{28,36},{32,40... | collective-permute-start | bytes 884744 | tf_op jit(solution)/shard_map/ppermute | solution.py:146
  69.5 7.8 %collective-permute-start.9 = (bf16[192,384]{0,1:T(8,128)(2,1)S(1)}, bf16[192,384]{0,1:T(8,128)(2,1)S(1)}, u32[]{:S(2)}, u32[]{:S(2)}) collective-permute-start(bf16[192,384]{0,1:T(8,128)(2,1)S(1)} %get-tuple-element.18), channel_id=1, source_target_pairs={{0,4},{4,0},{8,12},{12,8},{16,20},{20,16},{24,28},{28,24},{32,36},... | collective-permute-start | bytes 442376 | tf_op jit(solution)/shard_map/ppermute | solution.py:188
  78.5 9.5 %all-to-all-start = ((bf16[4,96,768]{2,1,0:T(8,128)(2,1)}), bf16[4,96,768]{2,1,0:T(8,128)(2,1)S(1)}, u32[]{:S(2)}, u32[]{:S(2)}) async-start(bf16[4,96,768]{2,1,0:T(8,128)(2,1)} %broadcast_in_dim.20), calls=%async_computation | async-start | bytes 1179648 | tf_op jit(solution)/shard_map/all_to_all | solution.py:206
  82.5 11.6 %copy-start = (bf16[1,768,768]{1,2,0:T(8,128)(2,1)S(1)}, bf16[1,768,768]{1,2,0:T(8,128)(2,1)}, u32[]{:S(2)}) copy-start(bf16[1,768,768]{1,2,0:T(8,128)(2,1)} %all-gather.3.cloned.1.call-done) | copy-start | bytes 3538948
  89.0 10.7 %all-to-all-start.2 = ((bf16[4,96,768]{2,1,0:T(8,128)(2,1)}), bf16[4,96,768]{2,1,0:T(8,128)(2,1)S(1)}, u32[]{:S(2)}, u32[]{:S(2)}) async-start(bf16[4,96,768]{2,1,0:T(8,128)(2,1)} %broadcast_in_dim.21), calls=%async_computation.2 | async-start | bytes 1179648 | tf_op jit(solution)/shard_map/all_to_all | solution.py:206
  99.6 14.7 %all-to-all-start.1 = ((bf16[4,96,768]{2,1,0:T(8,128)(2,1)}), bf16[4,96,768]{2,1,0:T(8,128)(2,1)S(1)}, u32[]{:S(2)}, u32[]{:S(2)}) async-start(bf16[4,96,768]{2,1,0:T(8,128)(2,1)} %pad_maximum_fusion), calls=%async_computation.1 | async-start | bytes 1179648 | tf_op jit(solution)/shard_map/all_to_all | solution.py:215
  108.2 14.0 %copy-start.4 = (bf16[1,192,768]{2,1,0:T(8,128)(2,1)S(1)}, bf16[1,192,768]{2,1,0:T(8,128)(2,1)}, u32[]{:S(2)}) copy-start(bf16[1,192,768]{2,1,0:T(8,128)(2,1)} %param.10) | copy-start | bytes 884740
  108.2 19.4 %copy-start.3 = (f32[1,768]{1,0:T(1,128)S(1)}, f32[1,768]{1,0:T(1,128)}, u32[]{:S(2)}) copy-start(f32[1,768]{1,0:T(1,128)} %param.12) | copy-start | bytes 9220
  114.3 26.1 %all-to-all-start.3 = ((bf16[4,96,768]{2,1,0:T(8,128)(2,1)}), bf16[4,96,768]{2,1,0:T(8,128)(2,1)S(1)}, u32[]{:S(2)}, u32[]{:S(2)}) async-start(bf16[4,96,768]{2,1,0:T(8,128)(2,1)} %pad_maximum_fusion.1), calls=%async_computation.3 | async-start | bytes 1179648 | tf_op jit(solution)/shard_map/all_to_all | solution.py:215
  122.2 24.5 %collective-permute-start = (bf16[192,768]{1,0:T(8,128)(2,1)S(1)}, bf16[192,768]{1,0:T(8,128)(2,1)S(1)}, u32[]{:S(2)}, u32[]{:S(2)}) collective-permute-start(bf16[192,768]{1,0:T(8,128)(2,1)S(1)} %bitcast.102), channel_id=1, source_target_pairs={{0,0},{1,32},{2,64},{3,96},{32,1},{33,33},{34,65},{35,97},{64,2},{... | collective-permute-start | bytes 884744 | tf_op jit(solution)/shard_map/ppermute | solution.py:195
  127.7 19.1 %collective-permute-start.1 = (f32[768]{0:T(1024)S(1)}, f32[768]{0:T(1024)S(1)}, u32[]{:S(2)}, u32[]{:S(2)}) collective-permute-start(f32[768]{0:T(1024)S(1)} %reduce), channel_id=1, source_target_pairs={{0,0},{1,32},{2,64},{3,96},{32,1},{33,33},{34,65},{35,97},{64,2},{... | collective-permute-start | bytes 9224 | tf_op jit(solution)/shard_map/ppermute | solution.py:196
  146.8 26.0 %collective-permute-start.11 = (bf16[96,768]{1,0:T(8,128)(2,1)S(1)}, bf16[96,768]{1,0:T(8,128)(2,1)S(1)}, u32[]{:S(2)}, u32[]{:S(2)}) collective-permute-start(bf16[96,768]{1,0:T(8,128)(2,1)S(1)} %get-tuple-element.16), channel_id=1, source_target_pairs={{0,128},{1,160},{2,192},{3,224},{32,129},{33,161},{34,193},{35,225... | collective-permute-start | bytes 442376 | tf_op jit(solution)/shard_map/ppermute | solution.py:220
  167.6 10.6 %collective-permute-start.10 = (bf16[96,768]{1,0:T(8,128)(2,1)S(1)}, bf16[96,768]{1,0:T(8,128)(2,1)S(1)}, u32[]{:S(2)}, u32[]{:S(2)}) collective-permute-start(bf16[96,768]{1,0:T(8,128)(2,1)S(1)} %get-tuple-element.15), channel_id=1, source_target_pairs={{0,128},{1,160},{2,192},{3,224},{32,129},{33,161},{34,193},{35,225... | collective-permute-start | bytes 442376 | tf_op jit(solution)/shard_map/ppermute | solution.py:220
Sparse Core Ops, SparseCore 0:
  9.4 56.6 all-gather.2

commit v10 on v5

--- a/solution.py
+++ b/solution.py
@@ -201,8 +201,17 @@
             for j in range(x_count)
         ]
     )
-    arrived = lax.all_to_all(terms, "head", 0, 0)
-    mixed = jnp.sum(arrived.astype(jnp.float32), axis=0)
+    split = row_count // 2
+    offloaded = lax.psum_scatter(
+        terms[:, :split].reshape(head_groups * split, terms.shape[2]),
+        "head",
+        scatter_dimension=0,
+        tiled=True,
+    )
+    arrived = lax.all_to_all(terms[:, split:], "head", 0, 0)
+    mixed = jnp.concatenate(
+        [offloaded.astype(jnp.float32), jnp.sum(arrived.astype(jnp.float32), axis=0)], axis=0
+    )
     swap = linear_pairs((x_count, head_groups), lambda a, b: (b, a))
     stream_block = lax.ppermute(stream[0], ("sx", "head"), swap)
     gate_block = lax.ppermute(gate_scale[0], ("sx", "head"), swap)

time: 176 us -> 176 us (level)
  the two profiles are of different devices: /device:TPU:92 before, /device:TPU:28 now
where the time goes in v10:
time: 176 us
  waiting for transfers between devices  77.4 us (44%)
  starting transfers between devices  47.2 us (27%)
  blocking collectives  17.6 us (10%)
  between operations  15.8 us (9%)
  local copies, waits for them, and re-layouts  7.27 us (4%)
  other arithmetic  5.33 us (3%)
  matrix products  5.21 us (3%)
    ppermute x1, waiting for transfers between devices, on_device(): handed = lax.ppermute(updated, ('section', 'sx', 'head'), hand)  18.8 us
    all_to_all x1, blocking collectives, on_device(): token_parts = lax.all_to_all(spread, 'sx', 0, 0)  17.6 us
    ppermute x2, waiting for transfers between devices, on_device(): lax.ppermute((tile_k, tile_v), seq, [(i, i - 2) for i in range(2, seq_cou...  16.8 us
    reduce_scatter x1, waiting for transfers between devices, on_device(): lax.psum_scatter(terms[:, :split].reshape(head_groups * split, terms.shap...  15.8 us
    ppermute x2, starting transfers between devices, on_device(): lax.ppermute((tile_k, tile_v), seq, [(i, i + 2) for i in range(seq_count...  10.2 us
    ppermute x2, waiting for transfers between devices, on_device(): lax.ppermute((tile_k, tile_v), seq, [(i, i + 2) for i in range(seq_count...  8.44 us
    ppermute x3, starting transfers between devices, on_device(): lax.ppermute((partner_half(queries), partner_half(own_keys), partner_half...  8.19 us
    ppermute x1, waiting for transfers between devices, on_device(): gate_block = lax.ppermute(gate_scale[0], ('sx', 'head'), swap)  7.88 us
  transfers between devices with their start and end apart: 14, of which 8 were waited for; matrix products, arithmetic and copies ran while one was open for 6% of the time, Pallas kernels for 0%

profile of v10, /device:TPU:28, one launch (start us, length us, event | category | flops | bytes accessed | tf_op | source)
XLA Modules:
  0.0 175.7 jit_solution(9812134047514776214)
XLA Ops:
  6.5 0.7 all-gather.3.cloned.1.call-update
  7.3 1.0 dynamic-slice_bitcast_fusion.1
  8.4 2.4 %collective-permute-start.4 = (bf16[192,384]{1,0:T(8,128)(2,1)S(1)}, bf16[192,384]{1,0:T(8,128)(2,1)S(1)}, u32[]{:S(2)}, u32[]{:S(2)}) collective-permute-start(bf16[192,384]{1,0:T(8,128)(2,1)S(1)} %get-tuple-element.21), channel_id=1, source_target_pairs={{0,4},{4,0},{8,12},{12,8},{16,20},{20,16},{24,28},{28,24},{32,36},... | collective-permute-start | bytes 442376 | tf_op jit(solution)/shard_map/ppermute | solution.py:132
  10.7 1.0 constant_dynamic-slice_fusion.2
  11.7 3.5 %collective-permute-start.5 = (bf16[192,384]{1,0:T(8,128)(2,1)S(1)}, bf16[192,384]{1,0:T(8,128)(2,1)S(1)}, u32[]{:S(2)}, u32[]{:S(2)}) collective-permute-start(bf16[192,384]{1,0:T(8,128)(2,1)S(1)} %get-tuple-element.20), channel_id=1, source_target_pairs={{0,4},{4,0},{8,12},{12,8},{16,20},{20,16},{24,28},{28,24},{32,36},... | collective-permute-start | bytes 442376 | tf_op jit(solution)/shard_map/ppermute | solution.py:132
  15.3 2.4 %collective-permute-start.2 = (bf16[192,384]{1,0:T(8,128)(2,1)S(1)}, bf16[192,384]{1,0:T(8,128)(2,1)S(1)}, u32[]{:S(2)}, u32[]{:S(2)}) collective-permute-start(bf16[192,384]{1,0:T(8,128)(2,1)S(1)} %get-tuple-element.18), channel_id=1, source_target_pairs={{0,4},{4,0},{8,12},{12,8},{16,20},{20,16},{24,28},{28,24},{32,36},... | collective-permute-start | bytes 442376 | tf_op jit(solution)/shard_map/ppermute | solution.py:132
  18.3 0.7 fusion.25
  20.8 0.8 maximum_select_fusion.5
  21.6 5.7 %collective-permute-start.6 = (bf16[384,384]{1,0:T(8,128)(2,1)}, bf16[384,384]{1,0:T(8,128)(2,1)S(1)}, u32[]{:S(2)}, u32[]{:S(2)}) collective-permute-start(bf16[384,384]{1,0:T(8,128)(2,1)} %maximum_select_fusion.5), channel_id=1, source_target_pairs={{0,8},{4,12},{8,16},{12,20},{16,24},{20,28},{24,32},{28,36},{32,40... | collective-permute-start | bytes 884744 | tf_op jit(solution)/shard_map/ppermute | solution.py:146
  27.4 1.9 %collective-permute-start.7 = (bf16[384,384]{1,0:T(8,128)(2,1)}, bf16[384,384]{1,0:T(8,128)(2,1)S(1)}, u32[]{:S(2)}, u32[]{:S(2)}) collective-permute-start(bf16[384,384]{1,0:T(8,128)(2,1)} %maximum_select_fusion.5), channel_id=1, source_target_pairs={{8,0},{12,4},{16,8},{20,12},{24,16},{28,20},{32,24},{36,28},{40,32... | collective-permute-start | bytes 884744 | tf_op jit(solution)/shard_map/ppermute | solution.py:147
  29.3 0.8 maximum_select_fusion.4
  30.1 3.5 %collective-permute-start.8 = (bf16[384,384]{1,0:T(8,128)(2,1)}, bf16[384,384]{1,0:T(8,128)(2,1)}, u32[]{:S(2)}, u32[]{:S(2)}) collective-permute-start(bf16[384,384]{1,0:T(8,128)(2,1)} %maximum_select_fusion.4), channel_id=1, source_target_pairs={{8,0},{12,4},{16,8},{20,12},{24,16},{28,20},{32,24},{36,28},{40,32... | collective-permute-start | bytes 884744 | tf_op jit(solution)/shard_map/ppermute | solution.py:147
  33.6 4.5 %collective-permute-start.3 = (bf16[384,384]{1,0:T(8,128)(2,1)}, bf16[384,384]{1,0:T(8,128)(2,1)S(1)}, u32[]{:S(2)}, u32[]{:S(2)}) collective-permute-start(bf16[384,384]{1,0:T(8,128)(2,1)} %maximum_select_fusion.4), channel_id=1, source_target_pairs={{0,8},{4,12},{8,16},{12,20},{16,24},{20,28},{24,32},{28,36},{32,40... | collective-permute-start | bytes 884744 | tf_op jit(solution)/shard_map/ppermute | solution.py:146
  39.8 8.4 %collective-permute-done.6 = bf16[384,384]{1,0:T(8,128)(2,1)S(1)} collective-permute-done((bf16[384,384]{1,0:T(8,128)(2,1)}, bf16[384,384]{1,0:T(8,128)(2,1)S(1)}, u32[]{:S(2)}, u32[]{:S(2)}) %collective-permute-start.6) | collective-permute-done | bytes 294944 | tf_op jit(solution)/shard_map/ppermute | solution.py:146
  48.5 4.0 %collective-permute-done.7 = bf16[384,384]{1,0:T(8,128)(2,1)S(1)} collective-permute-done((bf16[384,384]{1,0:T(8,128)(2,1)}, bf16[384,384]{1,0:T(8,128)(2,1)S(1)}, u32[]{:S(2)}, u32[]{:S(2)}) %collective-permute-start.7) | collective-permute-done | bytes 294944 | tf_op jit(solution)/shard_map/ppermute | solution.py:147
  52.7 12.8 %collective-permute-done.8 = bf16[384,384]{1,0:T(8,128)(2,1)} collective-permute-done((bf16[384,384]{1,0:T(8,128)(2,1)}, bf16[384,384]{1,0:T(8,128)(2,1)}, u32[]{:S(2)}, u32[]{:S(2)}) %collective-permute-start.8) | collective-permute-done | bytes 294944 | tf_op jit(solution)/shard_map/ppermute | solution.py:147
  65.5 1.2 copy.89
  67.5 0.7 fusion.26
  70.8 5.2 %collective-permute-start.9 = (bf16[192,384]{0,1:T(8,128)(2,1)S(1)}, bf16[192,384]{0,1:T(8,128)(2,1)S(1)}, u32[]{:S(2)}, u32[]{:S(2)}) collective-permute-start(bf16[192,384]{0,1:T(8,128)(2,1)S(1)} %get-tuple-element.16), channel_id=1, source_target_pairs={{0,4},{4,0},{8,12},{12,8},{16,20},{20,16},{24,28},{28,24},{32,36},... | collective-permute-start | bytes 442376 | tf_op jit(solution)/shard_map/ppermute | solution.py:188
  76.0 4.6 %collective-permute-done.9 = bf16[192,384]{0,1:T(8,128)(2,1)S(1)} collective-permute-done((bf16[192,384]{0,1:T(8,128)(2,1)S(1)}, bf16[192,384]{0,1:T(8,128)(2,1)S(1)}, u32[]{:S(2)}, u32[]{:S(2)}) %collective-permute-start.9) | collective-permute-done | bytes 147488 | tf_op jit(solution)/shard_map/ppermute | solution.py:188
  80.9 17.6 %all_to_all.10 = bf16[4,192,768]{2,1,0:T(8,128)(2,1)S(1)} all-to-all(bf16[4,192,768]{2,1,0:T(8,128)(2,1)S(1)} %broadcast_in_dim.31), channel_id=1, replica_groups=mesh['section'=4,'sx'=4,'sy'=8,'head'=4] {'sx'}, dimensions={0} | all-to-all | bytes 2359296 | tf_op jit(solution)/shard_map/all_to_all | solution.py:195
  100.9 1.1 fusion.24
  102.0 7.1 %all-to-all-start.1 = ((bf16[4,96,768]{2,1,0:T(8,128)(2,1)}), bf16[4,96,768]{2,1,0:T(8,128)(2,1)S(1)}, u32[]{:S(2)}, u32[]{:S(2)}) async-start(bf16[4,96,768]{2,1,0:T(8,128)(2,1)} %get-tuple-element.14), calls=%async_computation.2 | async-start | bytes 1179648 | tf_op jit(solution)/shard_map/all_to_all | solution.py:211
  109.1 7.0 %collective-permute-start = (bf16[192,768]{1,0:T(8,128)(2,1)S(1)}, bf16[192,768]{1,0:T(8,128)(2,1)S(1)}, u32[]{:S(2)}, u32[]{:S(2)}) collective-permute-start(bf16[192,768]{1,0:T(8,128)(2,1)S(1)} %bitcast.76), channel_id=1, source_target_pairs={{0,0},{1,32},{2,64},{3,96},{32,1},{33,33},{34,65},{35,97},{64,2},{... | collective-permute-start | bytes 884744 | tf_op jit(solution)/shard_map/ppermute | solution.py:216
  116.1 2.2 %collective-permute-start.1 = (f32[768]{0:T(1024)S(1)}, f32[768]{0:T(1024)S(1)}, u32[]{:S(2)}, u32[]{:S(2)}) collective-permute-start(f32[768]{0:T(1024)S(1)} %reduce), channel_id=1, source_target_pairs={{0,0},{1,32},{2,64},{3,96},{32,1},{33,33},{34,65},{35,97},{64,2},{... | collective-permute-start | bytes 9224 | tf_op jit(solution)/shard_map/ppermute | solution.py:217
  118.3 4.3 %all-to-all-done.1 = bf16[4,96,768]{2,1,0:T(8,128)(2,1)S(1)} async-done(((bf16[4,96,768]{2,1,0:T(8,128)(2,1)}), bf16[4,96,768]{2,1,0:T(8,128)(2,1)S(1)}, u32[]{:S(2)}, u32[]{:S(2)}) %all-to-all-start.1) | async-done | bytes 589856 | tf_op jit(solution)/shard_map/all_to_all | solution.py:211
  122.7 15.8 %reduce-scatter.2.cloned.1.call-done = bf16[96,768]{1,0:T(8,128)(2,1)} async-done(((bf16[384,768]{1,0:T(8,128)(2,1)}), bf16[96,768]{1,0:T(8,128)(2,1)}) %reduce-scatter.2.cloned.1.call-update) | async-done | bytes 147472 | tf_op jit(solution)/shard_map/reduce_scatter | solution.py:205
  138.5 0.9 convert_element_type.61
  139.4 7.9 %collective-permute-done.1 = f32[768]{0:T(1024)S(1)} collective-permute-done((f32[768]{0:T(1024)S(1)}, f32[768]{0:T(1024)S(1)}, u32[]{:S(2)}, u32[]{:S(2)}) %collective-permute-start.1) | collective-permute-done | bytes 3104 | tf_op jit(solution)/shard_map/ppermute | solution.py:217
  147.4 1.9 %collective-permute-start.10 = (bf16[192,768]{1,0:T(8,128)(2,1)S(1)}, bf16[192,768]{1,0:T(8,128)(2,1)S(1)}, u32[]{:S(2)}, u32[]{:S(2)}) collective-permute-start(bf16[192,768]{1,0:T(8,128)(2,1)S(1)} %fusion.14), channel_id=1, source_target_pairs={{0,128},{1,160},{2,192},{3,224},{32,129},{33,161},{34,193},{35,225... | collective-permute-start | bytes 884744 | tf_op jit(solution)/shard_map/ppermute | solution.py:222
  149.3 18.8 %collective-permute-done.10 = bf16[192,768]{1,0:T(8,128)(2,1)S(1)} collective-permute-done((bf16[192,768]{1,0:T(8,128)(2,1)S(1)}, bf16[192,768]{1,0:T(8,128)(2,1)S(1)}, u32[]{:S(2)}, u32[]{:S(2)}) %collective-permute-start.10) | collective-permute-done | bytes 294944 | tf_op jit(solution)/shard_map/ppermute | solution.py:222
  168.1 0.7 copy.118
  (59 shorter events, 9.1 us)
Async XLA Ops:
  6.5 8.7 %copy-start.1 = (bf16[1,192,768]{2,1,0:T(8,128)(2,1)S(1)}, bf16[1,192,768]{2,1,0:T(8,128)(2,1)}, u32[]{:S(2)}) copy-start(bf16[1,192,768]{2,1,0:T(8,128)(2,1)} %param.9) | copy-start | bytes 884740
  6.5 11.1 %copy-start.2 = (s32[16,27]{1,0:T(8,128)S(1)}, s32[16,27]{1,0:T(8,128)}, u32[]{:S(2)}) copy-start(s32[16,27]{1,0:T(8,128)} %param.13) | copy-start | bytes 5188
  6.5 60.9 %all-gather.3.cloned.1.call-start = ((), (), s32[]{:S(2)}) async-start(), calls=%async_computation.4 | async-start | bytes 1327104 | tf_op jit(solution)/shard_map/all_gather | solution.py:166
  7.3 131.2 %reduce-scatter.2.cloned.1.call-start = ((), (), s32[]{:S(2)}) async-start(), calls=%async_computation.3 | async-start | bytes 737280 | tf_op jit(solution)/shard_map/reduce_scatter | solution.py:205
  8.4 30.4 %collective-permute-start.4 = (bf16[192,384]{1,0:T(8,128)(2,1)S(1)}, bf16[192,384]{1,0:T(8,128)(2,1)S(1)}, u32[]{:S(2)}, u32[]{:S(2)}) collective-permute-start(bf16[192,384]{1,0:T(8,128)(2,1)S(1)} %get-tuple-element.21), channel_id=1, source_target_pairs={{0,4},{4,0},{8,12},{12,8},{16,20},{20,16},{24,28},{28,24},{32,36},... | collective-permute-start | bytes 442376 | tf_op jit(solution)/shard_map/ppermute | solution.py:132
  11.7 9.1 %collective-permute-start.5 = (bf16[192,384]{1,0:T(8,128)(2,1)S(1)}, bf16[192,384]{1,0:T(8,128)(2,1)S(1)}, u32[]{:S(2)}, u32[]{:S(2)}) collective-permute-start(bf16[192,384]{1,0:T(8,128)(2,1)S(1)} %get-tuple-element.20), channel_id=1, source_target_pairs={{0,4},{4,0},{8,12},{12,8},{16,20},{20,16},{24,28},{28,24},{32,36},... | collective-permute-start | bytes 442376 | tf_op jit(solution)/shard_map/ppermute | solution.py:132
  15.3 14.0 %collective-permute-start.2 = (bf16[192,384]{1,0:T(8,128)(2,1)S(1)}, bf16[192,384]{1,0:T(8,128)(2,1)S(1)}, u32[]{:S(2)}, u32[]{:S(2)}) collective-permute-start(bf16[192,384]{1,0:T(8,128)(2,1)S(1)} %get-tuple-element.18), channel_id=1, source_target_pairs={{0,4},{4,0},{8,12},{12,8},{16,20},{20,16},{24,28},{28,24},{32,36},... | collective-permute-start | bytes 442376 | tf_op jit(solution)/shard_map/ppermute | solution.py:132
  21.6 26.6 %collective-permute-start.6 = (bf16[384,384]{1,0:T(8,128)(2,1)}, bf16[384,384]{1,0:T(8,128)(2,1)S(1)}, u32[]{:S(2)}, u32[]{:S(2)}) collective-permute-start(bf16[384,384]{1,0:T(8,128)(2,1)} %maximum_select_fusion.5), channel_id=1, source_target_pairs={{0,8},{4,12},{8,16},{12,20},{16,24},{20,28},{24,32},{28,36},{32,40... | collective-permute-start | bytes 884744 | tf_op jit(solution)/shard_map/ppermute | solution.py:146
  27.4 25.1 %collective-permute-start.7 = (bf16[384,384]{1,0:T(8,128)(2,1)}, bf16[384,384]{1,0:T(8,128)(2,1)S(1)}, u32[]{:S(2)}, u32[]{:S(2)}) collective-permute-start(bf16[384,384]{1,0:T(8,128)(2,1)} %maximum_select_fusion.5), channel_id=1, source_target_pairs={{8,0},{12,4},{16,8},{20,12},{24,16},{28,20},{32,24},{36,28},{40,32... | collective-permute-start | bytes 884744 | tf_op jit(solution)/shard_map/ppermute | solution.py:147
  30.1 35.4 %collective-permute-start.8 = (bf16[384,384]{1,0:T(8,128)(2,1)}, bf16[384,384]{1,0:T(8,128)(2,1)}, u32[]{:S(2)}, u32[]{:S(2)}) collective-permute-start(bf16[384,384]{1,0:T(8,128)(2,1)} %maximum_select_fusion.4), channel_id=1, source_target_pairs={{8,0},{12,4},{16,8},{20,12},{24,16},{28,20},{32,24},{36,28},{40,32... | collective-permute-start | bytes 884744 | tf_op jit(solution)/shard_map/ppermute | solution.py:147
  33.6 33.1 %collective-permute-start.3 = (bf16[384,384]{1,0:T(8,128)(2,1)}, bf16[384,384]{1,0:T(8,128)(2,1)S(1)}, u32[]{:S(2)}, u32[]{:S(2)}) collective-permute-start(bf16[384,384]{1,0:T(8,128)(2,1)} %maximum_select_fusion.4), channel_id=1, source_target_pairs={{0,8},{4,12},{8,16},{12,20},{16,24},{20,28},{24,32},{28,36},{32,40... | collective-permute-start | bytes 884744 | tf_op jit(solution)/shard_map/ppermute | solution.py:146
  70.8 9.8 %collective-permute-start.9 = (bf16[192,384]{0,1:T(8,128)(2,1)S(1)}, bf16[192,384]{0,1:T(8,128)(2,1)S(1)}, u32[]{:S(2)}, u32[]{:S(2)}) collective-permute-start(bf16[192,384]{0,1:T(8,128)(2,1)S(1)} %get-tuple-element.16), channel_id=1, source_target_pairs={{0,4},{4,0},{8,12},{12,8},{16,20},{20,16},{24,28},{28,24},{32,36},... | collective-permute-start | bytes 442376 | tf_op jit(solution)/shard_map/ppermute | solution.py:188
  80.9 17.6 %copy-start = (bf16[1,768,768]{1,2,0:T(8,128)(2,1)S(1)}, bf16[1,768,768]{1,2,0:T(8,128)(2,1)}, u32[]{:S(2)}) copy-start(bf16[1,768,768]{1,2,0:T(8,128)(2,1)} %all-gather.3.cloned.1.call-done) | copy-start | bytes 3538948
  101.9 7.2 %copy-start.4 = (bf16[1,192,768]{2,1,0:T(8,128)(2,1)S(1)}, bf16[1,192,768]{2,1,0:T(8,128)(2,1)}, u32[]{:S(2)}) copy-start(bf16[1,192,768]{2,1,0:T(8,128)(2,1)} %param.10) | copy-start | bytes 884740
  101.9 14.2 %copy-start.3 = (f32[1,768]{1,0:T(1,128)S(1)}, f32[1,768]{1,0:T(1,128)}, u32[]{:S(2)}) copy-start(f32[1,768]{1,0:T(1,128)} %param.12) | copy-start | bytes 9220
  102.0 20.6 %all-to-all-start.1 = ((bf16[4,96,768]{2,1,0:T(8,128)(2,1)}), bf16[4,96,768]{2,1,0:T(8,128)(2,1)S(1)}, u32[]{:S(2)}, u32[]{:S(2)}) async-start(bf16[4,96,768]{2,1,0:T(8,128)(2,1)} %get-tuple-element.14), calls=%async_computation.2 | async-start | bytes 1179648 | tf_op jit(solution)/shard_map/all_to_all | solution.py:211
  109.1 38.2 %collective-permute-start = (bf16[192,768]{1,0:T(8,128)(2,1)S(1)}, bf16[192,768]{1,0:T(8,128)(2,1)S(1)}, u32[]{:S(2)}, u32[]{:S(2)}) collective-permute-start(bf16[192,768]{1,0:T(8,128)(2,1)S(1)} %bitcast.76), channel_id=1, source_target_pairs={{0,0},{1,32},{2,64},{3,96},{32,1},{33,33},{34,65},{35,97},{64,2},{... | collective-permute-start | bytes 884744 | tf_op jit(solution)/shard_map/ppermute | solution.py:216
  116.1 31.2 %collective-permute-start.1 = (f32[768]{0:T(1024)S(1)}, f32[768]{0:T(1024)S(1)}, u32[]{:S(2)}, u32[]{:S(2)}) collective-permute-start(f32[768]{0:T(1024)S(1)} %reduce), channel_id=1, source_target_pairs={{0,0},{1,32},{2,64},{3,96},{32,1},{33,33},{34,65},{35,97},{64,2},{... | collective-permute-start | bytes 9224 | tf_op jit(solution)/shard_map/ppermute | solution.py:217
  147.4 20.8 %collective-permute-start.10 = (bf16[192,768]{1,0:T(8,128)(2,1)S(1)}, bf16[192,768]{1,0:T(8,128)(2,1)S(1)}, u32[]{:S(2)}, u32[]{:S(2)}) collective-permute-start(bf16[192,768]{1,0:T(8,128)(2,1)S(1)} %fusion.14), channel_id=1, source_target_pairs={{0,128},{1,160},{2,192},{3,224},{32,129},{33,161},{34,193},{35,225... | collective-permute-start | bytes 884744 | tf_op jit(solution)/shard_map/ppermute | solution.py:222
Sparse Core Ops, SparseCore 0:
  9.4 55.7 all-gather.2
  102.1 36.3 reduce-scatter.1

commit v11 on v5

--- a/solution.py
+++ b/solution.py
@@ -201,8 +201,14 @@
             for j in range(x_count)
         ]
     )
-    arrived = lax.all_to_all(terms, "head", 0, 0)
-    mixed = jnp.sum(arrived.astype(jnp.float32), axis=0)
+    group_index = lax.axis_index("head")
+    mixed = lax.dynamic_index_in_dim(terms, group_index, 0, keepdims=False).astype(jnp.float32)
+    for shift in range(1, head_groups):
+        outgoing = lax.dynamic_index_in_dim(
+            terms, (group_index + shift) % head_groups, 0, keepdims=False
+        )
+        route = [(g, (g + shift) % head_groups) for g in range(head_groups)]
+        mixed = mixed + lax.ppermute(outgoing, "head", route).astype(jnp.float32)
     swap = linear_pairs((x_count, head_groups), lambda a, b: (b, a))
     stream_block = lax.ppermute(stream[0], ("sx", "head"), swap)
     gate_block = lax.ppermute(gate_scale[0], ("sx", "head"), swap)

time: 176 us -> 174 us (0.989)
  the two profiles are of different devices: /device:TPU:92 before, /device:TPU:6 now
where the time goes in v11:
time: 174 us; the launch traced here: 172 us
  waiting for transfers between devices  72.1 us (41%)
  starting transfers between devices  66.8 us (38%)
  between operations  15.8 us (9%)
  local copies, waits for them, and re-layouts  7.25 us (4%)
  matrix products  5.2 us (3%)
  other arithmetic  4.48 us (3%)
    ppermute x2, waiting for transfers between devices, on_device(): lax.ppermute((tile_k, tile_v), seq, [(i, i - 2) for i in range(2, seq_cou...  19.7 us
    ppermute x1, waiting for transfers between devices, on_device(): handed = lax.ppermute(updated, ('section', 'sx', 'head'), hand)  18.9 us
    ppermute x3, starting transfers between devices, on_device(): mixed = mixed + lax.ppermute(outgoing, 'head', route).astype(jnp.float32)  16.8 us
    all_to_all x1, waiting for transfers between devices, on_device(): token_parts = lax.all_to_all(spread, 'sx', 0, 0)  11.5 us
    ppermute x3, starting transfers between devices, on_device(): lax.ppermute((partner_half(queries), partner_half(own_keys), partner_half...  9.33 us
    ppermute x1, waiting for transfers between devices, on_device(): gate_block = lax.ppermute(gate_scale[0], ('sx', 'head'), swap)  8.81 us
    ppermute x2, starting transfers between devices, on_device(): lax.ppermute((tile_k, tile_v), seq, [(i, i + 2) for i in range(seq_count...  7.81 us
    ppermute x2, starting transfers between devices, on_device(): lax.ppermute((tile_k, tile_v), seq, [(i, i - 2) for i in range(2, seq_cou...  7.76 us
  transfers between devices with their start and end apart: 16, of which 9 were waited for; matrix products, arithmetic and copies ran while one was open for 7% of the time, Pallas kernels for 0%

profile of v11, /device:TPU:6, one launch (start us, length us, event | category | flops | bytes accessed | tf_op | source)
XLA Modules:
  0.0 171.6 jit_solution(4092226790564080851)
XLA Ops:
  6.5 0.7 all-gather.3.cloned.1.call-update
  7.3 1.0 dynamic-slice_bitcast_fusion.4
  8.3 3.5 %collective-permute-start.4 = (bf16[192,384]{1,0:T(8,128)(2,1)S(1)}, bf16[192,384]{1,0:T(8,128)(2,1)S(1)}, u32[]{:S(2)}, u32[]{:S(2)}) collective-permute-start(bf16[192,384]{1,0:T(8,128)(2,1)S(1)} %get-tuple-element.22), channel_id=1, source_target_pairs={{0,4},{4,0},{8,12},{12,8},{16,20},{20,16},{24,28},{28,24},{32,36},... | collective-permute-start | bytes 442376 | tf_op jit(solution)/shard_map/ppermute | solution.py:132
  11.8 1.0 constant_dynamic-slice_fusion.2
  12.8 2.4 %collective-permute-start.5 = (bf16[192,384]{1,0:T(8,128)(2,1)S(1)}, bf16[192,384]{1,0:T(8,128)(2,1)S(1)}, u32[]{:S(2)}, u32[]{:S(2)}) collective-permute-start(bf16[192,384]{1,0:T(8,128)(2,1)S(1)} %get-tuple-element.21), channel_id=1, source_target_pairs={{0,4},{4,0},{8,12},{12,8},{16,20},{20,16},{24,28},{28,24},{32,36},... | collective-permute-start | bytes 442376 | tf_op jit(solution)/shard_map/ppermute | solution.py:132
  15.2 3.5 %collective-permute-start.2 = (bf16[192,384]{1,0:T(8,128)(2,1)S(1)}, bf16[192,384]{1,0:T(8,128)(2,1)S(1)}, u32[]{:S(2)}, u32[]{:S(2)}) collective-permute-start(bf16[192,384]{1,0:T(8,128)(2,1)S(1)} %get-tuple-element.19), channel_id=1, source_target_pairs={{0,4},{4,0},{8,12},{12,8},{16,20},{20,16},{24,28},{28,24},{32,36},... | collective-permute-start | bytes 442376 | tf_op jit(solution)/shard_map/ppermute | solution.py:132
  21.9 0.8 maximum_select_fusion.5
  22.7 4.5 %collective-permute-start.6 = (bf16[384,384]{1,0:T(8,128)(2,1)}, bf16[384,384]{1,0:T(8,128)(2,1)S(1)}, u32[]{:S(2)}, u32[]{:S(2)}) collective-permute-start(bf16[384,384]{1,0:T(8,128)(2,1)} %maximum_select_fusion.5), channel_id=1, source_target_pairs={{0,8},{4,12},{8,16},{12,20},{16,24},{20,28},{24,32},{28,36},{32,40... | collective-permute-start | bytes 884744 | tf_op jit(solution)/shard_map/ppermute | solution.py:146
  27.2 4.4 %collective-permute-start.7 = (bf16[384,384]{1,0:T(8,128)(2,1)}, bf16[384,384]{1,0:T(8,128)(2,1)S(1)}, u32[]{:S(2)}, u32[]{:S(2)}) collective-permute-start(bf16[384,384]{1,0:T(8,128)(2,1)} %maximum_select_fusion.5), channel_id=1, source_target_pairs={{8,0},{12,4},{16,8},{20,12},{24,16},{28,20},{32,24},{36,28},{40,32... | collective-permute-start | bytes 884744 | tf_op jit(solution)/shard_map/ppermute | solution.py:147
  31.6 0.8 maximum_select_fusion.4
  32.4 3.4 %collective-permute-start.8 = (bf16[384,384]{1,0:T(8,128)(2,1)}, bf16[384,384]{1,0:T(8,128)(2,1)}, u32[]{:S(2)}, u32[]{:S(2)}) collective-permute-start(bf16[384,384]{1,0:T(8,128)(2,1)} %maximum_select_fusion.4), channel_id=1, source_target_pairs={{8,0},{12,4},{16,8},{20,12},{24,16},{28,20},{32,24},{36,28},{40,32... | collective-permute-start | bytes 884744 | tf_op jit(solution)/shard_map/ppermute | solution.py:147
  35.8 3.3 %collective-permute-start.3 = (bf16[384,384]{1,0:T(8,128)(2,1)}, bf16[384,384]{1,0:T(8,128)(2,1)S(1)}, u32[]{:S(2)}, u32[]{:S(2)}) collective-permute-start(bf16[384,384]{1,0:T(8,128)(2,1)} %maximum_select_fusion.4), channel_id=1, source_target_pairs={{0,8},{4,12},{8,16},{12,20},{16,24},{20,28},{24,32},{28,36},{32,40... | collective-permute-start | bytes 884744 | tf_op jit(solution)/shard_map/ppermute | solution.py:146
  40.9 4.8 %collective-permute-done.6 = bf16[384,384]{1,0:T(8,128)(2,1)S(1)} collective-permute-done((bf16[384,384]{1,0:T(8,128)(2,1)}, bf16[384,384]{1,0:T(8,128)(2,1)S(1)}, u32[]{:S(2)}, u32[]{:S(2)}) %collective-permute-start.6) | collective-permute-done | bytes 294944 | tf_op jit(solution)/shard_map/ppermute | solution.py:146
  45.9 3.1 %collective-permute-done.7 = bf16[384,384]{1,0:T(8,128)(2,1)S(1)} collective-permute-done((bf16[384,384]{1,0:T(8,128)(2,1)}, bf16[384,384]{1,0:T(8,128)(2,1)S(1)}, u32[]{:S(2)}, u32[]{:S(2)}) %collective-permute-start.7) | collective-permute-done | bytes 294944 | tf_op jit(solution)/shard_map/ppermute | solution.py:147
  49.2 16.6 %collective-permute-done.8 = bf16[384,384]{1,0:T(8,128)(2,1)} collective-permute-done((bf16[384,384]{1,0:T(8,128)(2,1)}, bf16[384,384]{1,0:T(8,128)(2,1)}, u32[]{:S(2)}, u32[]{:S(2)}) %collective-permute-start.8) | collective-permute-done | bytes 294944 | tf_op jit(solution)/shard_map/ppermute | solution.py:147
  65.8 1.2 copy.89
  67.7 1.2 all-gather.3.cloned.1.call-done
  72.2 3.4 %collective-permute-start.9 = (bf16[192,384]{0,1:T(8,128)(2,1)S(1)}, bf16[192,384]{0,1:T(8,128)(2,1)S(1)}, u32[]{:S(2)}, u32[]{:S(2)}) collective-permute-start(bf16[192,384]{0,1:T(8,128)(2,1)S(1)} %get-tuple-element.17), channel_id=1, source_target_pairs={{0,4},{4,0},{8,12},{12,8},{16,20},{20,16},{24,28},{28,24},{32,36},... | collective-permute-start | bytes 442376 | tf_op jit(solution)/shard_map/ppermute | solution.py:188
  75.5 4.2 %collective-permute-done.9 = bf16[192,384]{0,1:T(8,128)(2,1)S(1)} collective-permute-done((bf16[192,384]{0,1:T(8,128)(2,1)S(1)}, bf16[192,384]{0,1:T(8,128)(2,1)S(1)}, u32[]{:S(2)}, u32[]{:S(2)}) %collective-permute-start.9) | collective-permute-done | bytes 147488 | tf_op jit(solution)/shard_map/ppermute | solution.py:188
  80.1 1.1 broadcast_in_dim.31
  81.2 5.6 %all-to-all-start = ((bf16[4,192,768]{2,1,0:T(8,128)(2,1)}), bf16[4,192,768]{2,1,0:T(8,128)(2,1)S(1)}, u32[]{:S(2)}, u32[]{:S(2)}) async-start(bf16[4,192,768]{2,1,0:T(8,128)(2,1)} %broadcast_in_dim.31), calls=%async_computation | async-start | bytes 2359296 | tf_op jit(solution)/shard_map/all_to_all | solution.py:195
  86.8 6.5 %collective-permute-start = (bf16[192,768]{1,0:T(8,128)(2,1)S(1)}, bf16[192,768]{1,0:T(8,128)(2,1)S(1)}, u32[]{:S(2)}, u32[]{:S(2)}) collective-permute-start(bf16[192,768]{1,0:T(8,128)(2,1)S(1)} %bitcast.83), channel_id=1, source_target_pairs={{0,0},{1,32},{2,64},{3,96},{32,1},{33,33},{34,65},{35,97},{64,2},{... | collective-permute-start | bytes 884744 | tf_op jit(solution)/shard_map/ppermute | solution.py:213
  93.4 11.5 %all-to-all-done = bf16[4,192,768]{2,1,0:T(8,128)(2,1)S(1)} async-done(((bf16[4,192,768]{2,1,0:T(8,128)(2,1)}), bf16[4,192,768]{2,1,0:T(8,128)(2,1)S(1)}, u32[]{:S(2)}, u32[]{:S(2)}) %all-to-all-start) | async-done | bytes 1179680 | tf_op jit(solution)/shard_map/all_to_all | solution.py:195
  107.4 12.4 %collective-permute-start.12 = (bf16[192,768]{1,0:T(8,128)(2,1)S(1)}, bf16[192,768]{1,0:T(8,128)(2,1)S(1)}, u32[]{:S(2)}, u32[]{:S(2)}) collective-permute-start(bf16[192,768]{1,0:T(8,128)(2,1)S(1)} %get-tuple-element.14), channel_id=1, source_target_pairs={{0,3},{1,0},{2,1},{3,2},{4,7},{5,4},{6,5},{7,6},{8,11},{9,8},{10,9... | collective-permute-start | bytes 884744 | tf_op jit(solution)/shard_map/ppermute | solution.py:211
  119.8 1.9 %collective-permute-start.11 = (bf16[192,768]{1,0:T(8,128)(2,1)S(1)}, bf16[192,768]{1,0:T(8,128)(2,1)S(1)}, u32[]{:S(2)}, u32[]{:S(2)}) collective-permute-start(bf16[192,768]{1,0:T(8,128)(2,1)S(1)} %get-tuple-element.15), channel_id=1, source_target_pairs={{0,2},{1,3},{2,0},{3,1},{4,6},{5,7},{6,4},{7,5},{8,10},{9,11},{10,... | collective-permute-start | bytes 884744 | tf_op jit(solution)/shard_map/ppermute | solution.py:211
  121.8 2.5 %collective-permute-start.10 = (bf16[192,768]{1,0:T(8,128)(2,1)S(1)}, bf16[192,768]{1,0:T(8,128)(2,1)S(1)}, u32[]{:S(2)}, u32[]{:S(2)}) collective-permute-start(bf16[192,768]{1,0:T(8,128)(2,1)S(1)} %get-tuple-element.13), channel_id=1, source_target_pairs={{0,1},{1,2},{2,3},{3,0},{4,5},{5,6},{6,7},{7,4},{8,9},{9,10},{10,1... | collective-permute-start | bytes 884744 | tf_op jit(solution)/shard_map/ppermute | solution.py:211
  124.3 7.6 %collective-permute-start.1 = (f32[768]{0:T(1024)S(1)}, f32[768]{0:T(1024)S(1)}, u32[]{:S(2)}, u32[]{:S(2)}) collective-permute-start(f32[768]{0:T(1024)S(1)} %reduce), channel_id=1, source_target_pairs={{0,0},{1,32},{2,64},{3,96},{32,1},{33,33},{34,65},{35,97},{64,2},{... | collective-permute-start | bytes 9224 | tf_op jit(solution)/shard_map/ppermute | solution.py:214
  131.9 8.8 %collective-permute-done.1 = f32[768]{0:T(1024)S(1)} collective-permute-done((f32[768]{0:T(1024)S(1)}, f32[768]{0:T(1024)S(1)}, u32[]{:S(2)}, u32[]{:S(2)}) %collective-permute-start.1) | collective-permute-done | bytes 3104 | tf_op jit(solution)/shard_map/ppermute | solution.py:214
  140.7 2.3 %collective-permute-done.11 = bf16[192,768]{1,0:T(8,128)(2,1)S(1)} collective-permute-done((bf16[192,768]{1,0:T(8,128)(2,1)S(1)}, bf16[192,768]{1,0:T(8,128)(2,1)S(1)}, u32[]{:S(2)}, u32[]{:S(2)}) %collective-permute-start.11) | collective-permute-done | bytes 294944 | tf_op jit(solution)/shard_map/ppermute | solution.py:211
  143.2 1.9 %collective-permute-start.13 = (bf16[192,768]{1,0:T(8,128)(2,1)S(1)}, bf16[192,768]{1,0:T(8,128)(2,1)S(1)}, u32[]{:S(2)}, u32[]{:S(2)}) collective-permute-start(bf16[192,768]{1,0:T(8,128)(2,1)S(1)} %fusion.17), channel_id=1, source_target_pairs={{0,128},{1,160},{2,192},{3,224},{32,129},{33,161},{34,193},{35,225... | collective-permute-start | bytes 884744 | tf_op jit(solution)/shard_map/ppermute | solution.py:219
  145.2 18.9 %collective-permute-done.13 = bf16[192,768]{1,0:T(8,128)(2,1)S(1)} collective-permute-done((bf16[192,768]{1,0:T(8,128)(2,1)S(1)}, bf16[192,768]{1,0:T(8,128)(2,1)S(1)}, u32[]{:S(2)}, u32[]{:S(2)}) %collective-permute-start.13) | collective-permute-done | bytes 294944 | tf_op jit(solution)/shard_map/ppermute | solution.py:219
  164.1 0.7 copy.118
  (59 shorter events, 10.3 us)
Async XLA Ops:
  6.5 8.7 %copy-start.1 = (bf16[1,192,768]{2,1,0:T(8,128)(2,1)S(1)}, bf16[1,192,768]{2,1,0:T(8,128)(2,1)}, u32[]{:S(2)}) copy-start(bf16[1,192,768]{2,1,0:T(8,128)(2,1)} %param.9) | copy-start | bytes 884740
  6.5 12.2 %copy-start.2 = (s32[16,27]{1,0:T(8,128)S(1)}, s32[16,27]{1,0:T(8,128)}, u32[]{:S(2)}) copy-start(s32[16,27]{1,0:T(8,128)} %param.13) | copy-start | bytes 5188
  6.5 62.3 %all-gather.3.cloned.1.call-start = ((), (), s32[]{:S(2)}) async-start(), calls=%async_computation.1 | async-start | bytes 1327104 | tf_op jit(solution)/shard_map/all_gather | solution.py:166
  8.3 31.6 %collective-permute-start.4 = (bf16[192,384]{1,0:T(8,128)(2,1)S(1)}, bf16[192,384]{1,0:T(8,128)(2,1)S(1)}, u32[]{:S(2)}, u32[]{:S(2)}) collective-permute-start(bf16[192,384]{1,0:T(8,128)(2,1)S(1)} %get-tuple-element.22), channel_id=1, source_target_pairs={{0,4},{4,0},{8,12},{12,8},{16,20},{20,16},{24,28},{28,24},{32,36},... | collective-permute-start | bytes 442376 | tf_op jit(solution)/shard_map/ppermute | solution.py:132
  12.8 9.1 %collective-permute-start.5 = (bf16[192,384]{1,0:T(8,128)(2,1)S(1)}, bf16[192,384]{1,0:T(8,128)(2,1)S(1)}, u32[]{:S(2)}, u32[]{:S(2)}) collective-permute-start(bf16[192,384]{1,0:T(8,128)(2,1)S(1)} %get-tuple-element.21), channel_id=1, source_target_pairs={{0,4},{4,0},{8,12},{12,8},{16,20},{20,16},{24,28},{28,24},{32,36},... | collective-permute-start | bytes 442376 | tf_op jit(solution)/shard_map/ppermute | solution.py:132
  15.2 16.3 %collective-permute-start.2 = (bf16[192,384]{1,0:T(8,128)(2,1)S(1)}, bf16[192,384]{1,0:T(8,128)(2,1)S(1)}, u32[]{:S(2)}, u32[]{:S(2)}) collective-permute-start(bf16[192,384]{1,0:T(8,128)(2,1)S(1)} %get-tuple-element.19), channel_id=1, source_target_pairs={{0,4},{4,0},{8,12},{12,8},{16,20},{20,16},{24,28},{28,24},{32,36},... | collective-permute-start | bytes 442376 | tf_op jit(solution)/shard_map/ppermute | solution.py:132
  22.7 22.9 %collective-permute-start.6 = (bf16[384,384]{1,0:T(8,128)(2,1)}, bf16[384,384]{1,0:T(8,128)(2,1)S(1)}, u32[]{:S(2)}, u32[]{:S(2)}) collective-permute-start(bf16[384,384]{1,0:T(8,128)(2,1)} %maximum_select_fusion.5), channel_id=1, source_target_pairs={{0,8},{4,12},{8,16},{12,20},{16,24},{20,28},{24,32},{28,36},{32,40... | collective-permute-start | bytes 884744 | tf_op jit(solution)/shard_map/ppermute | solution.py:146
  27.2 21.8 %collective-permute-start.7 = (bf16[384,384]{1,0:T(8,128)(2,1)}, bf16[384,384]{1,0:T(8,128)(2,1)S(1)}, u32[]{:S(2)}, u32[]{:S(2)}) collective-permute-start(bf16[384,384]{1,0:T(8,128)(2,1)} %maximum_select_fusion.5), channel_id=1, source_target_pairs={{8,0},{12,4},{16,8},{20,12},{24,16},{28,20},{32,24},{36,28},{40,32... | collective-permute-start | bytes 884744 | tf_op jit(solution)/shard_map/ppermute | solution.py:147
  32.4 33.4 %collective-permute-start.8 = (bf16[384,384]{1,0:T(8,128)(2,1)}, bf16[384,384]{1,0:T(8,128)(2,1)}, u32[]{:S(2)}, u32[]{:S(2)}) collective-permute-start(bf16[384,384]{1,0:T(8,128)(2,1)} %maximum_select_fusion.4), channel_id=1, source_target_pairs={{8,0},{12,4},{16,8},{20,12},{24,16},{28,20},{32,24},{36,28},{40,32... | collective-permute-start | bytes 884744 | tf_op jit(solution)/shard_map/ppermute | solution.py:147
  35.8 31.1 %collective-permute-start.3 = (bf16[384,384]{1,0:T(8,128)(2,1)}, bf16[384,384]{1,0:T(8,128)(2,1)S(1)}, u32[]{:S(2)}, u32[]{:S(2)}) collective-permute-start(bf16[384,384]{1,0:T(8,128)(2,1)} %maximum_select_fusion.4), channel_id=1, source_target_pairs={{0,8},{4,12},{8,16},{12,20},{16,24},{20,28},{24,32},{28,36},{32,40... | collective-permute-start | bytes 884744 | tf_op jit(solution)/shard_map/ppermute | solution.py:146
  72.2 7.6 %collective-permute-start.9 = (bf16[192,384]{0,1:T(8,128)(2,1)S(1)}, bf16[192,384]{0,1:T(8,128)(2,1)S(1)}, u32[]{:S(2)}, u32[]{:S(2)}) collective-permute-start(bf16[192,384]{0,1:T(8,128)(2,1)S(1)} %get-tuple-element.17), channel_id=1, source_target_pairs={{0,4},{4,0},{8,12},{12,8},{16,20},{20,16},{24,28},{28,24},{32,36},... | collective-permute-start | bytes 442376 | tf_op jit(solution)/shard_map/ppermute | solution.py:188
  81.2 5.7 %copy-start.4 = (bf16[1,192,768]{2,1,0:T(8,128)(2,1)S(1)}, bf16[1,192,768]{2,1,0:T(8,128)(2,1)}, u32[]{:S(2)}) copy-start(bf16[1,192,768]{2,1,0:T(8,128)(2,1)} %param.10) | copy-start | bytes 884740
  81.2 23.7 %copy-start = (bf16[1,768,768]{1,2,0:T(8,128)(2,1)S(1)}, bf16[1,768,768]{1,2,0:T(8,128)(2,1)}, u32[]{:S(2)}) copy-start(bf16[1,768,768]{1,2,0:T(8,128)(2,1)} %all-gather.3.cloned.1.call-done) | copy-start | bytes 3538948
  81.2 23.7 %all-to-all-start = ((bf16[4,192,768]{2,1,0:T(8,128)(2,1)}), bf16[4,192,768]{2,1,0:T(8,128)(2,1)S(1)}, u32[]{:S(2)}, u32[]{:S(2)}) async-start(bf16[4,192,768]{2,1,0:T(8,128)(2,1)} %broadcast_in_dim.31), calls=%async_computation | async-start | bytes 2359296 | tf_op jit(solution)/shard_map/all_to_all | solution.py:195
  86.8 53.9 %collective-permute-start = (bf16[192,768]{1,0:T(8,128)(2,1)S(1)}, bf16[192,768]{1,0:T(8,128)(2,1)S(1)}, u32[]{:S(2)}, u32[]{:S(2)}) collective-permute-start(bf16[192,768]{1,0:T(8,128)(2,1)S(1)} %bitcast.83), channel_id=1, source_target_pairs={{0,0},{1,32},{2,64},{3,96},{32,1},{33,33},{34,65},{35,97},{64,2},{... | collective-permute-start | bytes 884744 | tf_op jit(solution)/shard_map/ppermute | solution.py:213
  107.3 17.0 %copy-start.3 = (f32[1,768]{1,0:T(1,128)S(1)}, f32[1,768]{1,0:T(1,128)}, u32[]{:S(2)}) copy-start(f32[1,768]{1,0:T(1,128)} %param.12) | copy-start | bytes 9220
  107.4 33.3 %collective-permute-start.12 = (bf16[192,768]{1,0:T(8,128)(2,1)S(1)}, bf16[192,768]{1,0:T(8,128)(2,1)S(1)}, u32[]{:S(2)}, u32[]{:S(2)}) collective-permute-start(bf16[192,768]{1,0:T(8,128)(2,1)S(1)} %get-tuple-element.14), channel_id=1, source_target_pairs={{0,3},{1,0},{2,1},{3,2},{4,7},{5,4},{6,5},{7,6},{8,11},{9,8},{10,9... | collective-permute-start | bytes 884744 | tf_op jit(solution)/shard_map/ppermute | solution.py:211
  119.8 23.2 %collective-permute-start.11 = (bf16[192,768]{1,0:T(8,128)(2,1)S(1)}, bf16[192,768]{1,0:T(8,128)(2,1)S(1)}, u32[]{:S(2)}, u32[]{:S(2)}) collective-permute-start(bf16[192,768]{1,0:T(8,128)(2,1)S(1)} %get-tuple-element.15), channel_id=1, source_target_pairs={{0,2},{1,3},{2,0},{3,1},{4,6},{5,7},{6,4},{7,5},{8,10},{9,11},{10,... | collective-permute-start | bytes 884744 | tf_op jit(solution)/shard_map/ppermute | solution.py:211
  121.8 21.3 %collective-permute-start.10 = (bf16[192,768]{1,0:T(8,128)(2,1)S(1)}, bf16[192,768]{1,0:T(8,128)(2,1)S(1)}, u32[]{:S(2)}, u32[]{:S(2)}) collective-permute-start(bf16[192,768]{1,0:T(8,128)(2,1)S(1)} %get-tuple-element.13), channel_id=1, source_target_pairs={{0,1},{1,2},{2,3},{3,0},{4,5},{5,6},{6,7},{7,4},{8,9},{9,10},{10,1... | collective-permute-start | bytes 884744 | tf_op jit(solution)/shard_map/ppermute | solution.py:211
  124.3 16.4 %collective-permute-start.1 = (f32[768]{0:T(1024)S(1)}, f32[768]{0:T(1024)S(1)}, u32[]{:S(2)}, u32[]{:S(2)}) collective-permute-start(f32[768]{0:T(1024)S(1)} %reduce), channel_id=1, source_target_pairs={{0,0},{1,32},{2,64},{3,96},{32,1},{33,33},{34,65},{35,97},{64,2},{... | collective-permute-start | bytes 9224 | tf_op jit(solution)/shard_map/ppermute | solution.py:214
  143.2 20.8 %collective-permute-start.13 = (bf16[192,768]{1,0:T(8,128)(2,1)S(1)}, bf16[192,768]{1,0:T(8,128)(2,1)S(1)}, u32[]{:S(2)}, u32[]{:S(2)}) collective-permute-start(bf16[192,768]{1,0:T(8,128)(2,1)S(1)} %fusion.17), channel_id=1, source_target_pairs={{0,128},{1,160},{2,192},{3,224},{32,129},{33,161},{34,193},{35,225... | collective-permute-start | bytes 884744 | tf_op jit(solution)/shard_map/ppermute | solution.py:219
Sparse Core Ops, SparseCore 0:
  9.4 59.3 all-gather.2

commit v12 on v11

--- a/solution.py
+++ b/solution.py
@@ -191,22 +191,24 @@
         jnp.concatenate([mine_rows, back], axis=1),
         jnp.concatenate([back, mine_rows], axis=1),
     )
-    spread = jnp.broadcast_to(attended[None], (x_count,) + attended.shape)
-    token_parts = lax.all_to_all(spread, "sx", 0, 0)
+    token_parts = [attended] + [
+        lax.ppermute(attended, "sx", [(i, (i + d) % x_count) for i in range(x_count)])
+        for d in range(1, x_count)
+    ]
     terms = jnp.stack(
         [
-            jnp.dot(token_parts[j], weight_block, preferred_element_type=jnp.float32).astype(
-                jnp.bfloat16
-            )
-            for j in range(x_count)
+            jnp.dot(part, weight_block, preferred_element_type=jnp.float32).astype(jnp.bfloat16)
+            for part in token_parts
         ]
     )
+
+    def term_for(slab_x):
+        return lax.dynamic_index_in_dim(terms, (x_index - slab_x) % x_count, 0, keepdims=False)
+
     group_index = lax.axis_index("head")
-    mixed = lax.dynamic_index_in_dim(terms, group_index, 0, keepdims=False).astype(jnp.float32)
+    mixed = term_for(group_index).astype(jnp.float32)
     for shift in range(1, head_groups):
-        outgoing = lax.dynamic_index_in_dim(
-            terms, (group_index + shift) % head_groups, 0, keepdims=False
-        )
+        outgoing = term_for((group_index + shift) % head_groups)
         route = [(g, (g + shift) % head_groups) for g in range(head_groups)]
         mixed = mixed + lax.ppermute(outgoing, "head", route).astype(jnp.float32)
     swap = linear_pairs((x_count, head_groups), lambda a, b: (b, a))

time: 174 us -> 177 us (1.017)
  waiting for transfers between devices: 72.1 us -> 75.1 us
  starting transfers between devices: 66.8 us -> 69.2 us
    all_to_all x1 -> x0, waiting for transfers between devices: 11.5 us -> none  [on_device(): token_parts = lax.all_to_all(spread, 'sx', 0, 0)]
    ppermute x0 -> x3, waiting for transfers between devices: none -> 9.38 us  [on_device(): lax.ppermute(attended, 'sx', [(i, (i + d) % x_count) for i in range(x_cou...]
    ppermute x0 -> x3, starting transfers between devices: none -> 9.21 us  [on_device(): lax.ppermute(attended, 'sx', [(i, (i + d) % x_count) for i in range(x_cou...]
    ppermute x3, waiting for transfers between devices: 2.3 us -> 8.49 us  [on_device(): mixed = mixed + lax.ppermute(outgoing, 'head', route).astype(jnp.float32)]
    ppermute x1, starting transfers between devices: 7.61 us -> 1.92 us  [on_device(): gate_block = lax.ppermute(gate_scale[0], ('sx', 'head'), swap)]
    all_to_all x1 -> x0, starting transfers between devices: 5.65 us -> none  [on_device(): token_parts = lax.all_to_all(spread, 'sx', 0, 0)]
    ppermute x2, waiting for transfers between devices: 19.7 us -> 25 us  [on_device(): lax.ppermute((tile_k, tile_v), seq, [(i, i - 2) for i in range(2, seq_cou...]
    ppermute x2, waiting for transfers between devices: 4.76 us -> 0.01 us  [on_device(): lax.ppermute((tile_k, tile_v), seq, [(i, i + 2) for i in range(seq_count...]
  transfers between devices with their start and end apart: 16 -> 18, of which waited for: 9 -> 7; matrix products, arithmetic and copies ran while one was open for 7% -> 6% of each run, Pallas kernels for 0% -> 0%
where the time goes in v12:
time: 177 us; the launch traced here: 176 us
  waiting for transfers between devices  75.1 us (42%)
  starting transfers between devices  69.2 us (39%)
  between operations  15.9 us (9%)
  local copies, waits for them, and re-layouts  6 us (3%)
  matrix products  5.19 us (3%)
  other arithmetic  4.48 us (3%)
    ppermute x2, waiting for transfers between devices, on_device(): lax.ppermute((tile_k, tile_v), seq, [(i, i - 2) for i in range(2, seq_cou...  25 us
    ppermute x3, starting transfers between devices, on_device(): mixed = mixed + lax.ppermute(outgoing, 'head', route).astype(jnp.float32)  19.8 us
    ppermute x1, waiting for transfers between devices, on_device(): handed = lax.ppermute(updated, ('section', 'sx', 'head'), hand)  17.1 us
    ppermute x1, waiting for transfers between devices, on_device(): gate_block = lax.ppermute(gate_scale[0], ('sx', 'head'), swap)  9.8 us
    ppermute x3, waiting for transfers between devices, on_device(): lax.ppermute(attended, 'sx', [(i, (i + d) % x_count) for i in range(x_cou...  9.38 us
    ppermute x3, starting transfers between devices, on_device(): lax.ppermute((partner_half(queries), partner_half(own_keys), partner_half...  9.32 us
    ppermute x3, starting transfers between devices, on_device(): lax.ppermute(attended, 'sx', [(i, (i + d) % x_count) for i in range(x_cou...  9.21 us
    ppermute x3, waiting for transfers between devices, on_device(): mixed = mixed + lax.ppermute(outgoing, 'head', route).astype(jnp.float32)  8.49 us
  transfers between devices with their start and end apart: 18, of which 7 were waited for; matrix products, arithmetic and copies ran while one was open for 6% of the time, Pallas kernels for 0%

profile of v12, /device:TPU:6, one launch (start us, length us, event | category | flops | bytes accessed | tf_op | source)
XLA Modules:
  0.0 175.9 jit_solution(10033550952028836720)
XLA Ops:
  6.5 0.7 all-gather.3.cloned.1.call-update
  7.3 1.0 constant_dynamic-slice_fusion.4
  8.3 3.5 %collective-permute-start.2 = (bf16[192,384]{1,0:T(8,128)(2,1)S(1)}, bf16[192,384]{1,0:T(8,128)(2,1)S(1)}, u32[]{:S(2)}, u32[]{:S(2)}) collective-permute-start(bf16[192,384]{1,0:T(8,128)(2,1)S(1)} %get-tuple-element.23), channel_id=1, source_target_pairs={{0,4},{4,0},{8,12},{12,8},{16,20},{20,16},{24,28},{28,24},{32,36},... | collective-permute-start | bytes 442376 | tf_op jit(solution)/shard_map/ppermute | solution.py:132
  11.8 1.0 constant_dynamic-slice_fusion.2
  12.8 2.4 %collective-permute-start.5 = (bf16[192,384]{1,0:T(8,128)(2,1)S(1)}, bf16[192,384]{1,0:T(8,128)(2,1)S(1)}, u32[]{:S(2)}, u32[]{:S(2)}) collective-permute-start(bf16[192,384]{1,0:T(8,128)(2,1)S(1)} %get-tuple-element.21), channel_id=1, source_target_pairs={{0,4},{4,0},{8,12},{12,8},{16,20},{20,16},{24,28},{28,24},{32,36},... | collective-permute-start | bytes 442376 | tf_op jit(solution)/shard_map/ppermute | solution.py:132
  15.3 3.5 %collective-permute-start.4 = (bf16[192,384]{1,0:T(8,128)(2,1)S(1)}, bf16[192,384]{1,0:T(8,128)(2,1)S(1)}, u32[]{:S(2)}, u32[]{:S(2)}) collective-permute-start(bf16[192,384]{1,0:T(8,128)(2,1)S(1)} %get-tuple-element.18), channel_id=1, source_target_pairs={{0,4},{4,0},{8,12},{12,8},{16,20},{20,16},{24,28},{28,24},{32,36},... | collective-permute-start | bytes 442376 | tf_op jit(solution)/shard_map/ppermute | solution.py:132
  21.9 0.8 maximum_select_fusion.5
  22.7 4.5 %collective-permute-start.6 = (bf16[384,384]{1,0:T(8,128)(2,1)}, bf16[384,384]{1,0:T(8,128)(2,1)S(1)}, u32[]{:S(2)}, u32[]{:S(2)}) collective-permute-start(bf16[384,384]{1,0:T(8,128)(2,1)} %maximum_select_fusion.5), channel_id=1, source_target_pairs={{0,8},{4,12},{8,16},{12,20},{16,24},{20,28},{24,32},{28,36},{32,40... | collective-permute-start | bytes 884744 | tf_op jit(solution)/shard_map/ppermute | solution.py:146
  27.2 4.4 %collective-permute-start.7 = (bf16[384,384]{1,0:T(8,128)(2,1)}, bf16[384,384]{1,0:T(8,128)(2,1)S(1)}, u32[]{:S(2)}, u32[]{:S(2)}) collective-permute-start(bf16[384,384]{1,0:T(8,128)(2,1)} %maximum_select_fusion.5), channel_id=1, source_target_pairs={{8,0},{12,4},{16,8},{20,12},{24,16},{28,20},{32,24},{36,28},{40,32... | collective-permute-start | bytes 884744 | tf_op jit(solution)/shard_map/ppermute | solution.py:147
  31.6 0.8 maximum_select_fusion.4
  32.4 3.4 %collective-permute-start.8 = (bf16[384,384]{1,0:T(8,128)(2,1)}, bf16[384,384]{1,0:T(8,128)(2,1)}, u32[]{:S(2)}, u32[]{:S(2)}) collective-permute-start(bf16[384,384]{1,0:T(8,128)(2,1)} %maximum_select_fusion.4), channel_id=1, source_target_pairs={{8,0},{12,4},{16,8},{20,12},{24,16},{28,20},{32,24},{36,28},{40,32... | collective-permute-start | bytes 884744 | tf_op jit(solution)/shard_map/ppermute | solution.py:147
  35.8 3.3 %collective-permute-start.3 = (bf16[384,384]{1,0:T(8,128)(2,1)}, bf16[384,384]{1,0:T(8,128)(2,1)S(1)}, u32[]{:S(2)}, u32[]{:S(2)}) collective-permute-start(bf16[384,384]{1,0:T(8,128)(2,1)} %maximum_select_fusion.4), channel_id=1, source_target_pairs={{0,8},{4,12},{8,16},{12,20},{16,24},{20,28},{24,32},{28,36},{32,40... | collective-permute-start | bytes 884744 | tf_op jit(solution)/shard_map/ppermute | solution.py:146
  40.9 25.0 %collective-permute-done.8 = bf16[384,384]{1,0:T(8,128)(2,1)} collective-permute-done((bf16[384,384]{1,0:T(8,128)(2,1)}, bf16[384,384]{1,0:T(8,128)(2,1)}, u32[]{:S(2)}, u32[]{:S(2)}) %collective-permute-start.8) | collective-permute-done | bytes 294944 | tf_op jit(solution)/shard_map/ppermute | solution.py:147
  65.9 1.2 copy.84
  68.6 0.7 fusion.28
  69.3 0.6 fusion.29
  71.8 3.6 %collective-permute-start.9 = (bf16[192,384]{0,1:T(8,128)(2,1)S(1)}, bf16[192,384]{0,1:T(8,128)(2,1)S(1)}, u32[]{:S(2)}, u32[]{:S(2)}) collective-permute-start(bf16[192,384]{0,1:T(8,128)(2,1)S(1)} %get-tuple-element.17), channel_id=1, source_target_pairs={{0,4},{4,0},{8,12},{12,8},{16,20},{20,16},{24,28},{28,24},{32,36},... | collective-permute-start | bytes 442376 | tf_op jit(solution)/shard_map/ppermute | solution.py:188
  75.4 4.4 %collective-permute-done.9 = bf16[192,384]{0,1:T(8,128)(2,1)S(1)} collective-permute-done((bf16[192,384]{0,1:T(8,128)(2,1)S(1)}, bf16[192,384]{0,1:T(8,128)(2,1)S(1)}, u32[]{:S(2)}, u32[]{:S(2)}) %collective-permute-start.9) | collective-permute-done | bytes 147488 | tf_op jit(solution)/shard_map/ppermute | solution.py:188
  80.0 4.0 %collective-permute-start.12 = (bf16[192,768]{0,1:T(8,128)(2,1)S(1)}, bf16[192,768]{0,1:T(8,128)(2,1)S(1)}, u32[]{:S(2)}, u32[]{:S(2)}) collective-permute-start(bf16[192,768]{0,1:T(8,128)(2,1)S(1)} %maximum_select_fusion.3), channel_id=1, source_target_pairs={{0,96},{32,0},{64,32},{96,64},{1,97},{33,1},{65,33},{97,65},{2,98}... | collective-permute-start | bytes 884744 | tf_op jit(solution)/shard_map/ppermute | solution.py:195
  84.0 7.8 %collective-permute-start = (bf16[192,768]{1,0:T(8,128)(2,1)S(1)}, bf16[192,768]{1,0:T(8,128)(2,1)S(1)}, u32[]{:S(2)}, u32[]{:S(2)}) collective-permute-start(bf16[192,768]{1,0:T(8,128)(2,1)S(1)} %bitcast.75), channel_id=1, source_target_pairs={{0,0},{1,32},{2,64},{3,96},{32,1},{33,33},{34,65},{35,97},{64,2},{... | collective-permute-start | bytes 884744 | tf_op jit(solution)/shard_map/ppermute | solution.py:215
  91.9 1.9 %collective-permute-start.11 = (bf16[192,768]{0,1:T(8,128)(2,1)S(1)}, bf16[192,768]{0,1:T(8,128)(2,1)S(1)}, u32[]{:S(2)}, u32[]{:S(2)}) collective-permute-start(bf16[192,768]{0,1:T(8,128)(2,1)S(1)} %maximum_select_fusion.3), channel_id=1, source_target_pairs={{0,64},{32,96},{64,0},{96,32},{1,65},{33,97},{65,1},{97,33},{2,66}... | collective-permute-start | bytes 884744 | tf_op jit(solution)/shard_map/ppermute | solution.py:195
  93.9 3.3 %collective-permute-start.10 = (bf16[192,768]{0,1:T(8,128)(2,1)S(1)}, bf16[192,768]{0,1:T(8,128)(2,1)S(1)}, u32[]{:S(2)}, u32[]{:S(2)}) collective-permute-start(bf16[192,768]{0,1:T(8,128)(2,1)S(1)} %maximum_select_fusion.3), channel_id=1, source_target_pairs={{0,32},{32,64},{64,96},{96,0},{1,33},{33,65},{65,97},{97,1},{2,34}... | collective-permute-start | bytes 884744 | tf_op jit(solution)/shard_map/ppermute | solution.py:195
  97.7 9.4 %collective-permute-done.12 = bf16[192,768]{0,1:T(8,128)(2,1)S(1)} collective-permute-done((bf16[192,768]{0,1:T(8,128)(2,1)S(1)}, bf16[192,768]{0,1:T(8,128)(2,1)S(1)}, u32[]{:S(2)}, u32[]{:S(2)}) %collective-permute-start.12) | collective-permute-done | bytes 294944 | tf_op jit(solution)/shard_map/ppermute | solution.py:195
  109.0 10.9 %collective-permute-start.15 = (bf16[192,768]{1,0:T(8,128)(2,1)S(1)}, bf16[192,768]{1,0:T(8,128)(2,1)S(1)}, u32[]{:S(2)}, u32[]{:S(2)}) collective-permute-start(bf16[192,768]{1,0:T(8,128)(2,1)S(1)} %get-tuple-element.14), channel_id=1, source_target_pairs={{0,3},{1,0},{2,1},{3,2},{4,7},{5,4},{6,5},{7,6},{8,11},{9,8},{10,9... | collective-permute-start | bytes 884744 | tf_op jit(solution)/shard_map/ppermute | solution.py:213
  119.9 4.9 %collective-permute-start.14 = (bf16[192,768]{1,0:T(8,128)(2,1)S(1)}, bf16[192,768]{1,0:T(8,128)(2,1)S(1)}, u32[]{:S(2)}, u32[]{:S(2)}) collective-permute-start(bf16[192,768]{1,0:T(8,128)(2,1)S(1)} %get-tuple-element.15), channel_id=1, source_target_pairs={{0,2},{1,3},{2,0},{3,1},{4,6},{5,7},{6,4},{7,5},{8,10},{9,11},{10,... | collective-permute-start | bytes 884744 | tf_op jit(solution)/shard_map/ppermute | solution.py:213
  124.9 3.9 %collective-permute-start.13 = (bf16[192,768]{1,0:T(8,128)(2,1)S(1)}, bf16[192,768]{1,0:T(8,128)(2,1)S(1)}, u32[]{:S(2)}, u32[]{:S(2)}) collective-permute-start(bf16[192,768]{1,0:T(8,128)(2,1)S(1)} %get-tuple-element.13), channel_id=1, source_target_pairs={{0,1},{1,2},{2,3},{3,0},{4,5},{5,6},{6,7},{7,4},{8,9},{9,10},{10,1... | collective-permute-start | bytes 884744 | tf_op jit(solution)/shard_map/ppermute | solution.py:213
  128.9 1.9 %collective-permute-start.1 = (f32[768]{0:T(1024)S(1)}, f32[768]{0:T(1024)S(1)}, u32[]{:S(2)}, u32[]{:S(2)}) collective-permute-start(f32[768]{0:T(1024)S(1)} %reduce), channel_id=1, source_target_pairs={{0,0},{1,32},{2,64},{3,96},{32,1},{33,33},{34,65},{35,97},{64,2},{... | collective-permute-start | bytes 9224 | tf_op jit(solution)/shard_map/ppermute | solution.py:216
  130.8 9.8 %collective-permute-done.1 = f32[768]{0:T(1024)S(1)} collective-permute-done((f32[768]{0:T(1024)S(1)}, f32[768]{0:T(1024)S(1)}, u32[]{:S(2)}, u32[]{:S(2)}) %collective-permute-start.1) | collective-permute-done | bytes 3104 | tf_op jit(solution)/shard_map/ppermute | solution.py:216
  140.6 8.5 %collective-permute-done.14 = bf16[192,768]{1,0:T(8,128)(2,1)S(1)} collective-permute-done((bf16[192,768]{1,0:T(8,128)(2,1)S(1)}, bf16[192,768]{1,0:T(8,128)(2,1)S(1)}, u32[]{:S(2)}, u32[]{:S(2)}) %collective-permute-start.14) | collective-permute-done | bytes 294944 | tf_op jit(solution)/shard_map/ppermute | solution.py:213
  149.3 1.9 %collective-permute-start.16 = (bf16[192,768]{1,0:T(8,128)(2,1)S(1)}, bf16[192,768]{1,0:T(8,128)(2,1)S(1)}, u32[]{:S(2)}, u32[]{:S(2)}) collective-permute-start(bf16[192,768]{1,0:T(8,128)(2,1)S(1)} %fusion.17), channel_id=1, source_target_pairs={{0,128},{1,160},{2,192},{3,224},{32,129},{33,161},{34,193},{35,225... | collective-permute-start | bytes 884744 | tf_op jit(solution)/shard_map/ppermute | solution.py:221
  151.2 17.1 %collective-permute-done.16 = bf16[192,768]{1,0:T(8,128)(2,1)S(1)} collective-permute-done((bf16[192,768]{1,0:T(8,128)(2,1)S(1)}, bf16[192,768]{1,0:T(8,128)(2,1)S(1)}, u32[]{:S(2)}, u32[]{:S(2)}) %collective-permute-start.16) | collective-permute-done | bytes 294944 | tf_op jit(solution)/shard_map/ppermute | solution.py:221
  168.3 0.7 copy.112
  (61 shorter events, 9.1 us)
Async XLA Ops:
  6.5 8.7 %copy-start.1 = (bf16[1,192,768]{2,1,0:T(8,128)(2,1)S(1)}, bf16[1,192,768]{2,1,0:T(8,128)(2,1)}, u32[]{:S(2)}) copy-start(bf16[1,192,768]{2,1,0:T(8,128)(2,1)} %param.7) | copy-start | bytes 884740
  6.5 12.2 %copy-start.2 = (s32[16,27]{1,0:T(8,128)S(1)}, s32[16,27]{1,0:T(8,128)}, u32[]{:S(2)}) copy-start(s32[16,27]{1,0:T(8,128)} %param.13) | copy-start | bytes 5188
  6.5 62.0 %all-gather.3.cloned.1.call-start = ((), (), s32[]{:S(2)}) async-start(), calls=%async_computation | async-start | bytes 1327104 | tf_op jit(solution)/shard_map/all_gather | solution.py:166
  8.3 23.3 %collective-permute-start.2 = (bf16[192,384]{1,0:T(8,128)(2,1)S(1)}, bf16[192,384]{1,0:T(8,128)(2,1)S(1)}, u32[]{:S(2)}, u32[]{:S(2)}) collective-permute-start(bf16[192,384]{1,0:T(8,128)(2,1)S(1)} %get-tuple-element.23), channel_id=1, source_target_pairs={{0,4},{4,0},{8,12},{12,8},{16,20},{20,16},{24,28},{28,24},{32,36},... | collective-permute-start | bytes 442376 | tf_op jit(solution)/shard_map/ppermute | solution.py:132
  12.8 9.1 %collective-permute-start.5 = (bf16[192,384]{1,0:T(8,128)(2,1)S(1)}, bf16[192,384]{1,0:T(8,128)(2,1)S(1)}, u32[]{:S(2)}, u32[]{:S(2)}) collective-permute-start(bf16[192,384]{1,0:T(8,128)(2,1)S(1)} %get-tuple-element.21), channel_id=1, source_target_pairs={{0,4},{4,0},{8,12},{12,8},{16,20},{20,16},{24,28},{28,24},{32,36},... | collective-permute-start | bytes 442376 | tf_op jit(solution)/shard_map/ppermute | solution.py:132
  15.3 24.6 %collective-permute-start.4 = (bf16[192,384]{1,0:T(8,128)(2,1)S(1)}, bf16[192,384]{1,0:T(8,128)(2,1)S(1)}, u32[]{:S(2)}, u32[]{:S(2)}) collective-permute-start(bf16[192,384]{1,0:T(8,128)(2,1)S(1)} %get-tuple-element.18), channel_id=1, source_target_pairs={{0,4},{4,0},{8,12},{12,8},{16,20},{20,16},{24,28},{28,24},{32,36},... | collective-permute-start | bytes 442376 | tf_op jit(solution)/shard_map/ppermute | solution.py:132
  22.7 44.4 %collective-permute-start.6 = (bf16[384,384]{1,0:T(8,128)(2,1)}, bf16[384,384]{1,0:T(8,128)(2,1)S(1)}, u32[]{:S(2)}, u32[]{:S(2)}) collective-permute-start(bf16[384,384]{1,0:T(8,128)(2,1)} %maximum_select_fusion.5), channel_id=1, source_target_pairs={{0,8},{4,12},{8,16},{12,20},{16,24},{20,28},{24,32},{28,36},{32,40... | collective-permute-start | bytes 884744 | tf_op jit(solution)/shard_map/ppermute | solution.py:146
  27.2 40.1 %collective-permute-start.7 = (bf16[384,384]{1,0:T(8,128)(2,1)}, bf16[384,384]{1,0:T(8,128)(2,1)S(1)}, u32[]{:S(2)}, u32[]{:S(2)}) collective-permute-start(bf16[384,384]{1,0:T(8,128)(2,1)} %maximum_select_fusion.5), channel_id=1, source_target_pairs={{8,0},{12,4},{16,8},{20,12},{24,16},{28,20},{32,24},{36,28},{40,32... | collective-permute-start | bytes 884744 | tf_op jit(solution)/shard_map/ppermute | solution.py:147
  32.4 33.5 %collective-permute-start.8 = (bf16[384,384]{1,0:T(8,128)(2,1)}, bf16[384,384]{1,0:T(8,128)(2,1)}, u32[]{:S(2)}, u32[]{:S(2)}) collective-permute-start(bf16[384,384]{1,0:T(8,128)(2,1)} %maximum_select_fusion.4), channel_id=1, source_target_pairs={{8,0},{12,4},{16,8},{20,12},{24,16},{28,20},{32,24},{36,28},{40,32... | collective-permute-start | bytes 884744 | tf_op jit(solution)/shard_map/ppermute | solution.py:147
  35.8 31.8 %collective-permute-start.3 = (bf16[384,384]{1,0:T(8,128)(2,1)}, bf16[384,384]{1,0:T(8,128)(2,1)S(1)}, u32[]{:S(2)}, u32[]{:S(2)}) collective-permute-start(bf16[384,384]{1,0:T(8,128)(2,1)} %maximum_select_fusion.4), channel_id=1, source_target_pairs={{0,8},{4,12},{8,16},{12,20},{16,24},{20,28},{24,32},{28,36},{32,40... | collective-permute-start | bytes 884744 | tf_op jit(solution)/shard_map/ppermute | solution.py:146
  71.6 12.4 %copy-start.4 = (bf16[1,192,768]{2,1,0:T(8,128)(2,1)S(1)}, bf16[1,192,768]{2,1,0:T(8,128)(2,1)}, u32[]{:S(2)}) copy-start(bf16[1,192,768]{2,1,0:T(8,128)(2,1)} %param.10) | copy-start | bytes 884740
  71.6 25.5 %copy-start = (bf16[1,768,768]{1,2,0:T(8,128)(2,1)S(1)}, bf16[1,768,768]{1,2,0:T(8,128)(2,1)}, u32[]{:S(2)}) copy-start(bf16[1,768,768]{1,2,0:T(8,128)(2,1)} %all-gather.3.cloned.1.call-done) | copy-start | bytes 3538948
  71.8 8.0 %collective-permute-start.9 = (bf16[192,384]{0,1:T(8,128)(2,1)S(1)}, bf16[192,384]{0,1:T(8,128)(2,1)S(1)}, u32[]{:S(2)}, u32[]{:S(2)}) collective-permute-start(bf16[192,384]{0,1:T(8,128)(2,1)S(1)} %get-tuple-element.17), channel_id=1, source_target_pairs={{0,4},{4,0},{8,12},{12,8},{16,20},{20,16},{24,28},{28,24},{32,36},... | collective-permute-start | bytes 442376 | tf_op jit(solution)/shard_map/ppermute | solution.py:188
  80.0 27.1 %collective-permute-start.12 = (bf16[192,768]{0,1:T(8,128)(2,1)S(1)}, bf16[192,768]{0,1:T(8,128)(2,1)S(1)}, u32[]{:S(2)}, u32[]{:S(2)}) collective-permute-start(bf16[192,768]{0,1:T(8,128)(2,1)S(1)} %maximum_select_fusion.3), channel_id=1, source_target_pairs={{0,96},{32,0},{64,32},{96,64},{1,97},{33,1},{65,33},{97,65},{2,98}... | collective-permute-start | bytes 884744 | tf_op jit(solution)/shard_map/ppermute | solution.py:195
  84.0 56.6 %collective-permute-start = (bf16[192,768]{1,0:T(8,128)(2,1)S(1)}, bf16[192,768]{1,0:T(8,128)(2,1)S(1)}, u32[]{:S(2)}, u32[]{:S(2)}) collective-permute-start(bf16[192,768]{1,0:T(8,128)(2,1)S(1)} %bitcast.75), channel_id=1, source_target_pairs={{0,0},{1,32},{2,64},{3,96},{32,1},{33,33},{34,65},{35,97},{64,2},{... | collective-permute-start | bytes 884744 | tf_op jit(solution)/shard_map/ppermute | solution.py:215
  91.9 15.7 %collective-permute-start.11 = (bf16[192,768]{0,1:T(8,128)(2,1)S(1)}, bf16[192,768]{0,1:T(8,128)(2,1)S(1)}, u32[]{:S(2)}, u32[]{:S(2)}) collective-permute-start(bf16[192,768]{0,1:T(8,128)(2,1)S(1)} %maximum_select_fusion.3), channel_id=1, source_target_pairs={{0,64},{32,96},{64,0},{96,32},{1,65},{33,97},{65,1},{97,33},{2,66}... | collective-permute-start | bytes 884744 | tf_op jit(solution)/shard_map/ppermute | solution.py:195
  93.9 14.3 %collective-permute-start.10 = (bf16[192,768]{0,1:T(8,128)(2,1)S(1)}, bf16[192,768]{0,1:T(8,128)(2,1)S(1)}, u32[]{:S(2)}, u32[]{:S(2)}) collective-permute-start(bf16[192,768]{0,1:T(8,128)(2,1)S(1)} %maximum_select_fusion.3), channel_id=1, source_target_pairs={{0,32},{32,64},{64,96},{96,0},{1,33},{33,65},{65,97},{97,1},{2,34}... | collective-permute-start | bytes 884744 | tf_op jit(solution)/shard_map/ppermute | solution.py:195
  108.9 19.9 %copy-start.3 = (f32[1,768]{1,0:T(1,128)S(1)}, f32[1,768]{1,0:T(1,128)}, u32[]{:S(2)}) copy-start(f32[1,768]{1,0:T(1,128)} %param.12) | copy-start | bytes 9220
  109.0 31.6 %collective-permute-start.15 = (bf16[192,768]{1,0:T(8,128)(2,1)S(1)}, bf16[192,768]{1,0:T(8,128)(2,1)S(1)}, u32[]{:S(2)}, u32[]{:S(2)}) collective-permute-start(bf16[192,768]{1,0:T(8,128)(2,1)S(1)} %get-tuple-element.14), channel_id=1, source_target_pairs={{0,3},{1,0},{2,1},{3,2},{4,7},{5,4},{6,5},{7,6},{8,11},{9,8},{10,9... | collective-permute-start | bytes 884744 | tf_op jit(solution)/shard_map/ppermute | solution.py:213
  119.9 29.2 %collective-permute-start.14 = (bf16[192,768]{1,0:T(8,128)(2,1)S(1)}, bf16[192,768]{1,0:T(8,128)(2,1)S(1)}, u32[]{:S(2)}, u32[]{:S(2)}) collective-permute-start(bf16[192,768]{1,0:T(8,128)(2,1)S(1)} %get-tuple-element.15), channel_id=1, source_target_pairs={{0,2},{1,3},{2,0},{3,1},{4,6},{5,7},{6,4},{7,5},{8,10},{9,11},{10,... | collective-permute-start | bytes 884744 | tf_op jit(solution)/shard_map/ppermute | solution.py:213
  124.9 24.2 %collective-permute-start.13 = (bf16[192,768]{1,0:T(8,128)(2,1)S(1)}, bf16[192,768]{1,0:T(8,128)(2,1)S(1)}, u32[]{:S(2)}, u32[]{:S(2)}) collective-permute-start(bf16[192,768]{1,0:T(8,128)(2,1)S(1)} %get-tuple-element.13), channel_id=1, source_target_pairs={{0,1},{1,2},{2,3},{3,0},{4,5},{5,6},{6,7},{7,4},{8,9},{9,10},{10,1... | collective-permute-start | bytes 884744 | tf_op jit(solution)/shard_map/ppermute | solution.py:213
  128.9 11.7 %collective-permute-start.1 = (f32[768]{0:T(1024)S(1)}, f32[768]{0:T(1024)S(1)}, u32[]{:S(2)}, u32[]{:S(2)}) collective-permute-start(f32[768]{0:T(1024)S(1)} %reduce), channel_id=1, source_target_pairs={{0,0},{1,32},{2,64},{3,96},{32,1},{33,33},{34,65},{35,97},{64,2},{... | collective-permute-start | bytes 9224 | tf_op jit(solution)/shard_map/ppermute | solution.py:216
  149.3 19.0 %collective-permute-start.16 = (bf16[192,768]{1,0:T(8,128)(2,1)S(1)}, bf16[192,768]{1,0:T(8,128)(2,1)S(1)}, u32[]{:S(2)}, u32[]{:S(2)}) collective-permute-start(bf16[192,768]{1,0:T(8,128)(2,1)S(1)} %fusion.17), channel_id=1, source_target_pairs={{0,128},{1,160},{2,192},{3,224},{32,129},{33,161},{34,193},{35,225... | collective-permute-start | bytes 884744 | tf_op jit(solution)/shard_map/ppermute | solution.py:221
Sparse Core Ops, SparseCore 0:
  9.4 59.0 all-gather.2

commit v13 on v11

--- a/solution.py
+++ b/solution.py
@@ -164,7 +164,12 @@
     query_lengths = jnp.sqrt(jnp.sum(query_float * query_float, axis=2))
     row_bound = query_lengths * bound[None, :] * score_scale
     weight_block = lax.all_gather(out_weight[0], "sy", axis=1, tiled=True)
-    weight_block, row_bound = lax.optimization_barrier((weight_block, row_bound))
+    swap = linear_pairs((x_count, head_groups), lambda a, b: (b, a))
+    stream_block = lax.ppermute(stream[0], ("sx", "head"), swap)
+    gate_block = lax.ppermute(gate_scale[0], ("sx", "head"), swap)
+    weight_block, row_bound, stream_block, gate_block = lax.optimization_barrier(
+        (weight_block, row_bound, stream_block, gate_block)
+    )
     weighted = jnp.zeros((tile_len, own_heads, HD), jnp.float32)
     summed = jnp.zeros((own_heads, tile_len), jnp.float32)
     for (keys, values), keep in zip(key_tiles, keeps):
@@ -209,9 +214,6 @@
         )
         route = [(g, (g + shift) % head_groups) for g in range(head_groups)]
         mixed = mixed + lax.ppermute(outgoing, "head", route).astype(jnp.float32)
-    swap = linear_pairs((x_count, head_groups), lambda a, b: (b, a))
-    stream_block = lax.ppermute(stream[0], ("sx", "head"), swap)
-    gate_block = lax.ppermute(gate_scale[0], ("sx", "head"), swap)
     updated = (stream_block.astype(jnp.float32) + gate_block[None, :] * mixed).astype(jnp.bfloat16)
     hand = linear_pairs(
         (sections, x_count, head_groups), lambda s, a, b: ((s + 1) % sections, b, a)

time: 174 us -> 169 us (0.971)
  the two profiles are of different devices: /device:TPU:6 before, /device:TPU:169 now
where the time goes in v13:
time: 169 us; the launch traced here: 168 us
  waiting for transfers between devices  77.9 us (46%)
  starting transfers between devices  57 us (34%)
  between operations  15.8 us (9%)
  local copies, waits for them, and re-layouts  6.34 us (4%)
  other arithmetic  5.43 us (3%)
  matrix products  5.21 us (3%)
    ppermute x3, waiting for transfers between devices, on_device(): mixed = mixed + lax.ppermute(outgoing, 'head', route).astype(jnp.float32)  22.6 us
    ppermute x2, waiting for transfers between devices, on_device(): lax.ppermute((tile_k, tile_v), seq, [(i, i + 2) for i in range(seq_count...  22.3 us
    ppermute x1, waiting for transfers between devices, on_device(): handed = lax.ppermute(updated, ('section', 'sx', 'head'), hand)  16.3 us
    ppermute x3, starting transfers between devices, on_device(): mixed = mixed + lax.ppermute(outgoing, 'head', route).astype(jnp.float32)  15.2 us
    all_to_all x1, waiting for transfers between devices, on_device(): token_parts = lax.all_to_all(spread, 'sx', 0, 0)  13 us
    ppermute x3, starting transfers between devices, on_device(): lax.ppermute((partner_half(queries), partner_half(own_keys), partner_half...  8.25 us
    ppermute x2, starting transfers between devices, on_device(): lax.ppermute((tile_k, tile_v), seq, [(i, i - 2) for i in range(2, seq_cou...  6.89 us
    ppermute x1, starting transfers between devices, on_device(): gate_block = lax.ppermute(gate_scale[0], ('sx', 'head'), swap)  5.75 us
  transfers between devices with their start and end apart: 16, of which 7 were waited for; matrix products, arithmetic and copies ran while one was open for 5% of the time, Pallas kernels for 0%

profile of v13, /device:TPU:169, one launch (start us, length us, event | category | flops | bytes accessed | tf_op | source)
XLA Modules:
  0.0 167.8 jit_solution(13465936966010004379)
XLA Ops:
  6.5 0.7 all-gather.3.cloned.1.call-update
  7.3 1.0 dynamic-slice_bitcast_fusion.5
  8.3 3.0 %collective-permute-start = (bf16[192,384]{1,0:T(8,128)(2,1)S(1)}, bf16[192,384]{1,0:T(8,128)(2,1)S(1)}, u32[]{:S(2)}, u32[]{:S(2)}) collective-permute-start(bf16[192,384]{1,0:T(8,128)(2,1)S(1)} %get-tuple-element.26), channel_id=1, source_target_pairs={{0,4},{4,0},{8,12},{12,8},{16,20},{20,16},{24,28},{28,24},{32,36},... | collective-permute-start | bytes 442376 | tf_op jit(solution)/shard_map/ppermute | solution.py:132
  11.3 1.0 constant_dynamic-slice_fusion.3
  12.3 2.3 %collective-permute-start.1 = (bf16[192,384]{1,0:T(8,128)(2,1)S(1)}, bf16[192,384]{1,0:T(8,128)(2,1)S(1)}, u32[]{:S(2)}, u32[]{:S(2)}) collective-permute-start(bf16[192,384]{1,0:T(8,128)(2,1)S(1)} %get-tuple-element.25), channel_id=1, source_target_pairs={{0,4},{4,0},{8,12},{12,8},{16,20},{20,16},{24,28},{28,24},{32,36},... | collective-permute-start | bytes 442376 | tf_op jit(solution)/shard_map/ppermute | solution.py:132
  14.6 2.8 %collective-permute-start.4 = (bf16[192,768]{1,0:T(8,128)(2,1)}, bf16[192,768]{1,0:T(8,128)(2,1)}, u32[]{:S(2)}, u32[]{:S(2)}) collective-permute-start(bf16[192,768]{1,0:T(8,128)(2,1)} %bitcast.9), channel_id=1, source_target_pairs={{0,0},{1,32},{2,64},{3,96},{32,1},{33,33},{34,65},{35,97},{64,2},{... | collective-permute-start | bytes 884744 | tf_op jit(solution)/shard_map/ppermute | solution.py:168
  17.5 5.8 %collective-permute-start.5 = (f32[768]{0:T(1024)S(1)}, f32[768]{0:T(1024)S(1)}, u32[]{:S(2)}, u32[]{:S(2)}) collective-permute-start(f32[768]{0:T(1024)S(1)} %reduce), channel_id=1, source_target_pairs={{0,0},{1,32},{2,64},{3,96},{32,1},{33,33},{34,65},{35,97},{64,2},{... | collective-permute-start | bytes 9224 | tf_op jit(solution)/shard_map/ppermute | solution.py:169
  23.3 3.0 %collective-permute-start.6 = (bf16[192,384]{1,0:T(8,128)(2,1)S(1)}, bf16[192,384]{1,0:T(8,128)(2,1)S(1)}, u32[]{:S(2)}, u32[]{:S(2)}) collective-permute-start(bf16[192,384]{1,0:T(8,128)(2,1)S(1)} %get-tuple-element.23), channel_id=1, source_target_pairs={{0,4},{4,0},{8,12},{12,8},{16,20},{20,16},{24,28},{28,24},{32,36},... | collective-permute-start | bytes 442376 | tf_op jit(solution)/shard_map/ppermute | solution.py:132
  26.9 0.7 fusion.27
  29.5 0.8 maximum_select_fusion.4
  30.3 2.4 %collective-permute-start.2 = (bf16[384,384]{1,0:T(8,128)(2,1)}, bf16[384,384]{1,0:T(8,128)(2,1)S(1)}, u32[]{:S(2)}, u32[]{:S(2)}) collective-permute-start(bf16[384,384]{1,0:T(8,128)(2,1)} %maximum_select_fusion.4), channel_id=1, source_target_pairs={{0,8},{4,12},{8,16},{12,20},{16,24},{20,28},{24,32},{28,36},{32,40... | collective-permute-start | bytes 884744 | tf_op jit(solution)/shard_map/ppermute | solution.py:146
  33.3 5.0 %collective-permute-start.3 = (bf16[384,384]{1,0:T(8,128)(2,1)}, bf16[384,384]{1,0:T(8,128)(2,1)S(1)}, u32[]{:S(2)}, u32[]{:S(2)}) collective-permute-start(bf16[384,384]{1,0:T(8,128)(2,1)} %maximum_select_fusion.4), channel_id=1, source_target_pairs={{8,0},{12,4},{16,8},{20,12},{24,16},{28,20},{32,24},{36,28},{40,32... | collective-permute-start | bytes 884744 | tf_op jit(solution)/shard_map/ppermute | solution.py:147
  38.3 0.8 maximum_select_fusion.5
  39.3 1.9 %collective-permute-start.8 = (bf16[384,384]{1,0:T(8,128)(2,1)}, bf16[384,384]{1,0:T(8,128)(2,1)S(1)}, u32[]{:S(2)}, u32[]{:S(2)}) collective-permute-start(bf16[384,384]{1,0:T(8,128)(2,1)} %maximum_select_fusion.5), channel_id=1, source_target_pairs={{8,0},{12,4},{16,8},{20,12},{24,16},{28,20},{32,24},{36,28},{40,32... | collective-permute-start | bytes 884744 | tf_op jit(solution)/shard_map/ppermute | solution.py:147
  42.2 10.4 %collective-permute-done.2 = bf16[384,384]{1,0:T(8,128)(2,1)S(1)} collective-permute-done((bf16[384,384]{1,0:T(8,128)(2,1)}, bf16[384,384]{1,0:T(8,128)(2,1)S(1)}, u32[]{:S(2)}, u32[]{:S(2)}) %collective-permute-start.2) | collective-permute-done | bytes 294944 | tf_op jit(solution)/shard_map/ppermute | solution.py:146
  52.6 2.7 %collective-permute-start.7 = (bf16[384,384]{1,0:T(8,128)(2,1)}, bf16[384,384]{1,0:T(8,128)(2,1)S(1)}, u32[]{:S(2)}, u32[]{:S(2)}) collective-permute-start(bf16[384,384]{1,0:T(8,128)(2,1)} %maximum_select_fusion.5), channel_id=1, source_target_pairs={{0,8},{4,12},{8,16},{12,20},{16,24},{20,28},{24,32},{28,36},{32,40... | collective-permute-start | bytes 884744 | tf_op jit(solution)/shard_map/ppermute | solution.py:146
  56.5 11.9 %collective-permute-done.7 = bf16[384,384]{1,0:T(8,128)(2,1)S(1)} collective-permute-done((bf16[384,384]{1,0:T(8,128)(2,1)}, bf16[384,384]{1,0:T(8,128)(2,1)S(1)}, u32[]{:S(2)}, u32[]{:S(2)}) %collective-permute-start.7) | collective-permute-done | bytes 294944 | tf_op jit(solution)/shard_map/ppermute | solution.py:146
  68.8 0.7 fusion.28
  72.0 4.6 %collective-permute-start.9 = (bf16[192,384]{0,1:T(8,128)(2,1)S(1)}, bf16[192,384]{0,1:T(8,128)(2,1)S(1)}, u32[]{:S(2)}, u32[]{:S(2)}) collective-permute-start(bf16[192,384]{0,1:T(8,128)(2,1)S(1)} %get-tuple-element.21), channel_id=1, source_target_pairs={{0,4},{4,0},{8,12},{12,8},{16,20},{20,16},{24,28},{28,24},{32,36},... | collective-permute-start | bytes 442376 | tf_op jit(solution)/shard_map/ppermute | solution.py:193
  76.6 3.0 %collective-permute-done.9 = bf16[192,384]{0,1:T(8,128)(2,1)S(1)} collective-permute-done((bf16[192,384]{0,1:T(8,128)(2,1)S(1)}, bf16[192,384]{0,1:T(8,128)(2,1)S(1)}, u32[]{:S(2)}, u32[]{:S(2)}) %collective-permute-start.9) | collective-permute-done | bytes 147488 | tf_op jit(solution)/shard_map/ppermute | solution.py:193
  79.9 1.1 broadcast_in_dim.31
  81.1 3.7 %all-to-all-start = ((bf16[4,192,768]{2,1,0:T(8,128)(2,1)}), bf16[4,192,768]{2,1,0:T(8,128)(2,1)S(1)}, u32[]{:S(2)}, u32[]{:S(2)}) async-start(bf16[4,192,768]{2,1,0:T(8,128)(2,1)} %broadcast_in_dim.31), calls=%async_computation | async-start | bytes 2359296 | tf_op jit(solution)/shard_map/all_to_all | solution.py:200
  84.8 13.0 %all-to-all-done = bf16[4,192,768]{2,1,0:T(8,128)(2,1)S(1)} async-done(((bf16[4,192,768]{2,1,0:T(8,128)(2,1)}), bf16[4,192,768]{2,1,0:T(8,128)(2,1)S(1)}, u32[]{:S(2)}, u32[]{:S(2)}) %all-to-all-start) | async-done | bytes 1179680 | tf_op jit(solution)/shard_map/all_to_all | solution.py:200
  100.2 3.2 %collective-permute-start.12 = (bf16[192,768]{1,0:T(8,128)(2,1)S(1)}, bf16[192,768]{1,0:T(8,128)(2,1)S(1)}, u32[]{:S(2)}, u32[]{:S(2)}) collective-permute-start(bf16[192,768]{1,0:T(8,128)(2,1)S(1)} %get-tuple-element.18), channel_id=1, source_target_pairs={{0,3},{1,0},{2,1},{3,2},{4,7},{5,4},{6,5},{7,6},{8,11},{9,8},{10,9... | collective-permute-start | bytes 884744 | tf_op jit(solution)/shard_map/ppermute | solution.py:216
  103.4 10.1 %collective-permute-start.11 = (bf16[192,768]{1,0:T(8,128)(2,1)S(1)}, bf16[192,768]{1,0:T(8,128)(2,1)S(1)}, u32[]{:S(2)}, u32[]{:S(2)}) collective-permute-start(bf16[192,768]{1,0:T(8,128)(2,1)S(1)} %get-tuple-element.19), channel_id=1, source_target_pairs={{0,2},{1,3},{2,0},{3,1},{4,6},{5,7},{6,4},{7,5},{8,10},{9,11},{10,... | collective-permute-start | bytes 884744 | tf_op jit(solution)/shard_map/ppermute | solution.py:216
  113.5 1.9 %collective-permute-start.10 = (bf16[192,768]{1,0:T(8,128)(2,1)S(1)}, bf16[192,768]{1,0:T(8,128)(2,1)S(1)}, u32[]{:S(2)}, u32[]{:S(2)}) collective-permute-start(bf16[192,768]{1,0:T(8,128)(2,1)S(1)} %get-tuple-element.17), channel_id=1, source_target_pairs={{0,1},{1,2},{2,3},{3,0},{4,5},{5,6},{6,7},{7,4},{8,9},{9,10},{10,1... | collective-permute-start | bytes 884744 | tf_op jit(solution)/shard_map/ppermute | solution.py:216
  115.4 15.7 %collective-permute-done.11 = bf16[192,768]{1,0:T(8,128)(2,1)S(1)} collective-permute-done((bf16[192,768]{1,0:T(8,128)(2,1)S(1)}, bf16[192,768]{1,0:T(8,128)(2,1)S(1)}, u32[]{:S(2)}, u32[]{:S(2)}) %collective-permute-start.11) | collective-permute-done | bytes 294944 | tf_op jit(solution)/shard_map/ppermute | solution.py:216
  131.1 6.9 %collective-permute-done.10 = bf16[192,768]{1,0:T(8,128)(2,1)S(1)} collective-permute-done((bf16[192,768]{1,0:T(8,128)(2,1)S(1)}, bf16[192,768]{1,0:T(8,128)(2,1)S(1)}, u32[]{:S(2)}, u32[]{:S(2)}) %collective-permute-start.10) | collective-permute-done | bytes 294944 | tf_op jit(solution)/shard_map/ppermute | solution.py:216
  138.0 1.2 fusion.17
  139.2 4.8 %collective-permute-start.13 = (bf16[192,768]{1,0:T(8,128)(2,1)S(1)}, bf16[192,768]{1,0:T(8,128)(2,1)S(1)}, u32[]{:S(2)}, u32[]{:S(2)}) collective-permute-start(bf16[192,768]{1,0:T(8,128)(2,1)S(1)} %fusion.17), channel_id=1, source_target_pairs={{0,128},{1,160},{2,192},{3,224},{32,129},{33,161},{34,193},{35,225... | collective-permute-start | bytes 884744 | tf_op jit(solution)/shard_map/ppermute | solution.py:221
  143.9 16.3 %collective-permute-done.13 = bf16[192,768]{1,0:T(8,128)(2,1)S(1)} collective-permute-done((bf16[192,768]{1,0:T(8,128)(2,1)S(1)}, bf16[192,768]{1,0:T(8,128)(2,1)S(1)}, u32[]{:S(2)}, u32[]{:S(2)}) %collective-permute-start.13) | collective-permute-done | bytes 294944 | tf_op jit(solution)/shard_map/ppermute | solution.py:221
  160.2 0.7 copy.118
  (57 shorter events, 9.1 us)
Async XLA Ops:
  6.5 11.0 %copy-start.3 = (f32[1,768]{1,0:T(1,128)S(1)}, f32[1,768]{1,0:T(1,128)}, u32[]{:S(2)}) copy-start(f32[1,768]{1,0:T(1,128)} %param.12) | copy-start | bytes 9220
  6.5 16.7 %copy-start.1 = (bf16[1,192,768]{2,1,0:T(8,128)(2,1)S(1)}, bf16[1,192,768]{2,1,0:T(8,128)(2,1)}, u32[]{:S(2)}) copy-start(bf16[1,192,768]{2,1,0:T(8,128)(2,1)} %param.9) | copy-start | bytes 884740
  6.5 62.1 %all-gather.3.cloned.1.call-start = ((), (), s32[]{:S(2)}) async-start(), calls=%async_computation.1 | async-start | bytes 1327104 | tf_op jit(solution)/shard_map/all_gather | solution.py:166
  8.3 18.3 %copy-start.2 = (s32[16,27]{1,0:T(8,128)S(1)}, s32[16,27]{1,0:T(8,128)}, u32[]{:S(2)}) copy-start(s32[16,27]{1,0:T(8,128)} %param.13) | copy-start | bytes 5188
  8.3 30.9 %collective-permute-start = (bf16[192,384]{1,0:T(8,128)(2,1)S(1)}, bf16[192,384]{1,0:T(8,128)(2,1)S(1)}, u32[]{:S(2)}, u32[]{:S(2)}) collective-permute-start(bf16[192,384]{1,0:T(8,128)(2,1)S(1)} %get-tuple-element.26), channel_id=1, source_target_pairs={{0,4},{4,0},{8,12},{12,8},{16,20},{20,16},{24,28},{28,24},{32,36},... | collective-permute-start | bytes 442376 | tf_op jit(solution)/shard_map/ppermute | solution.py:132
  12.3 17.2 %collective-permute-start.1 = (bf16[192,384]{1,0:T(8,128)(2,1)S(1)}, bf16[192,384]{1,0:T(8,128)(2,1)S(1)}, u32[]{:S(2)}, u32[]{:S(2)}) collective-permute-start(bf16[192,384]{1,0:T(8,128)(2,1)S(1)} %get-tuple-element.25), channel_id=1, source_target_pairs={{0,4},{4,0},{8,12},{12,8},{16,20},{20,16},{24,28},{28,24},{32,36},... | collective-permute-start | bytes 442376 | tf_op jit(solution)/shard_map/ppermute | solution.py:132
  14.6 54.0 %collective-permute-start.4 = (bf16[192,768]{1,0:T(8,128)(2,1)}, bf16[192,768]{1,0:T(8,128)(2,1)}, u32[]{:S(2)}, u32[]{:S(2)}) collective-permute-start(bf16[192,768]{1,0:T(8,128)(2,1)} %bitcast.9), channel_id=1, source_target_pairs={{0,0},{1,32},{2,64},{3,96},{32,1},{33,33},{34,65},{35,97},{64,2},{... | collective-permute-start | bytes 884744 | tf_op jit(solution)/shard_map/ppermute | solution.py:168
  17.5 51.1 %collective-permute-start.5 = (f32[768]{0:T(1024)S(1)}, f32[768]{0:T(1024)S(1)}, u32[]{:S(2)}, u32[]{:S(2)}) collective-permute-start(f32[768]{0:T(1024)S(1)} %reduce), channel_id=1, source_target_pairs={{0,0},{1,32},{2,64},{3,96},{32,1},{33,33},{34,65},{35,97},{64,2},{... | collective-permute-start | bytes 9224 | tf_op jit(solution)/shard_map/ppermute | solution.py:169
  23.3 10.0 %collective-permute-start.6 = (bf16[192,384]{1,0:T(8,128)(2,1)S(1)}, bf16[192,384]{1,0:T(8,128)(2,1)S(1)}, u32[]{:S(2)}, u32[]{:S(2)}) collective-permute-start(bf16[192,384]{1,0:T(8,128)(2,1)S(1)} %get-tuple-element.23), channel_id=1, source_target_pairs={{0,4},{4,0},{8,12},{12,8},{16,20},{20,16},{24,28},{28,24},{32,36},... | collective-permute-start | bytes 442376 | tf_op jit(solution)/shard_map/ppermute | solution.py:132
  30.3 22.3 %collective-permute-start.2 = (bf16[384,384]{1,0:T(8,128)(2,1)}, bf16[384,384]{1,0:T(8,128)(2,1)S(1)}, u32[]{:S(2)}, u32[]{:S(2)}) collective-permute-start(bf16[384,384]{1,0:T(8,128)(2,1)} %maximum_select_fusion.4), channel_id=1, source_target_pairs={{0,8},{4,12},{8,16},{12,20},{16,24},{20,28},{24,32},{28,36},{32,40... | collective-permute-start | bytes 884744 | tf_op jit(solution)/shard_map/ppermute | solution.py:146
  33.3 22.2 %collective-permute-start.3 = (bf16[384,384]{1,0:T(8,128)(2,1)}, bf16[384,384]{1,0:T(8,128)(2,1)S(1)}, u32[]{:S(2)}, u32[]{:S(2)}) collective-permute-start(bf16[384,384]{1,0:T(8,128)(2,1)} %maximum_select_fusion.4), channel_id=1, source_target_pairs={{8,0},{12,4},{16,8},{20,12},{24,16},{28,20},{32,24},{36,28},{40,32... | collective-permute-start | bytes 884744 | tf_op jit(solution)/shard_map/ppermute | solution.py:147
  39.3 17.0 %collective-permute-start.8 = (bf16[384,384]{1,0:T(8,128)(2,1)}, bf16[384,384]{1,0:T(8,128)(2,1)S(1)}, u32[]{:S(2)}, u32[]{:S(2)}) collective-permute-start(bf16[384,384]{1,0:T(8,128)(2,1)} %maximum_select_fusion.5), channel_id=1, source_target_pairs={{8,0},{12,4},{16,8},{20,12},{24,16},{28,20},{32,24},{36,28},{40,32... | collective-permute-start | bytes 884744 | tf_op jit(solution)/shard_map/ppermute | solution.py:147
  52.6 15.8 %collective-permute-start.7 = (bf16[384,384]{1,0:T(8,128)(2,1)}, bf16[384,384]{1,0:T(8,128)(2,1)S(1)}, u32[]{:S(2)}, u32[]{:S(2)}) collective-permute-start(bf16[384,384]{1,0:T(8,128)(2,1)} %maximum_select_fusion.5), channel_id=1, source_target_pairs={{0,8},{4,12},{8,16},{12,20},{16,24},{20,28},{24,32},{28,36},{32,40... | collective-permute-start | bytes 884744 | tf_op jit(solution)/shard_map/ppermute | solution.py:146
  72.0 7.7 %collective-permute-start.9 = (bf16[192,384]{0,1:T(8,128)(2,1)S(1)}, bf16[192,384]{0,1:T(8,128)(2,1)S(1)}, u32[]{:S(2)}, u32[]{:S(2)}) collective-permute-start(bf16[192,384]{0,1:T(8,128)(2,1)S(1)} %get-tuple-element.21), channel_id=1, source_target_pairs={{0,4},{4,0},{8,12},{12,8},{16,20},{20,16},{24,28},{28,24},{32,36},... | collective-permute-start | bytes 442376 | tf_op jit(solution)/shard_map/ppermute | solution.py:193
  81.1 16.7 %copy-start = (bf16[1,768,768]{1,2,0:T(8,128)(2,1)S(1)}, bf16[1,768,768]{1,2,0:T(8,128)(2,1)}, u32[]{:S(2)}) copy-start(bf16[1,768,768]{1,2,0:T(8,128)(2,1)} %all-gather.3.cloned.1.call-done) | copy-start | bytes 3538948
  81.1 16.7 %all-to-all-start = ((bf16[4,192,768]{2,1,0:T(8,128)(2,1)}), bf16[4,192,768]{2,1,0:T(8,128)(2,1)S(1)}, u32[]{:S(2)}, u32[]{:S(2)}) async-start(bf16[4,192,768]{2,1,0:T(8,128)(2,1)} %broadcast_in_dim.31), calls=%async_computation | async-start | bytes 2359296 | tf_op jit(solution)/shard_map/all_to_all | solution.py:200
  100.2 15.2 %collective-permute-start.12 = (bf16[192,768]{1,0:T(8,128)(2,1)S(1)}, bf16[192,768]{1,0:T(8,128)(2,1)S(1)}, u32[]{:S(2)}, u32[]{:S(2)}) collective-permute-start(bf16[192,768]{1,0:T(8,128)(2,1)S(1)} %get-tuple-element.18), channel_id=1, source_target_pairs={{0,3},{1,0},{2,1},{3,2},{4,7},{5,4},{6,5},{7,6},{8,11},{9,8},{10,9... | collective-permute-start | bytes 884744 | tf_op jit(solution)/shard_map/ppermute | solution.py:216
  103.4 27.7 %collective-permute-start.11 = (bf16[192,768]{1,0:T(8,128)(2,1)S(1)}, bf16[192,768]{1,0:T(8,128)(2,1)S(1)}, u32[]{:S(2)}, u32[]{:S(2)}) collective-permute-start(bf16[192,768]{1,0:T(8,128)(2,1)S(1)} %get-tuple-element.19), channel_id=1, source_target_pairs={{0,2},{1,3},{2,0},{3,1},{4,6},{5,7},{6,4},{7,5},{8,10},{9,11},{10,... | collective-permute-start | bytes 884744 | tf_op jit(solution)/shard_map/ppermute | solution.py:216
  113.5 24.5 %collective-permute-start.10 = (bf16[192,768]{1,0:T(8,128)(2,1)S(1)}, bf16[192,768]{1,0:T(8,128)(2,1)S(1)}, u32[]{:S(2)}, u32[]{:S(2)}) collective-permute-start(bf16[192,768]{1,0:T(8,128)(2,1)S(1)} %get-tuple-element.17), channel_id=1, source_target_pairs={{0,1},{1,2},{2,3},{3,0},{4,5},{5,6},{6,7},{7,4},{8,9},{9,10},{10,1... | collective-permute-start | bytes 884744 | tf_op jit(solution)/shard_map/ppermute | solution.py:216
  139.2 21.1 %collective-permute-start.13 = (bf16[192,768]{1,0:T(8,128)(2,1)S(1)}, bf16[192,768]{1,0:T(8,128)(2,1)S(1)}, u32[]{:S(2)}, u32[]{:S(2)}) collective-permute-start(bf16[192,768]{1,0:T(8,128)(2,1)S(1)} %fusion.17), channel_id=1, source_target_pairs={{0,128},{1,160},{2,192},{3,224},{32,129},{33,161},{34,193},{35,225... | collective-permute-start | bytes 884744 | tf_op jit(solution)/shard_map/ppermute | solution.py:221
Sparse Core Ops, SparseCore 0:
  9.4 53.1 all-gather.2

commit v14 on v13

--- a/solution.py
+++ b/solution.py
@@ -165,8 +165,9 @@
     row_bound = query_lengths * bound[None, :] * score_scale
     weight_block = lax.all_gather(out_weight[0], "sy", axis=1, tiled=True)
     swap = linear_pairs((x_count, head_groups), lambda a, b: (b, a))
-    stream_block = lax.ppermute(stream[0], ("sx", "head"), swap)
-    gate_block = lax.ppermute(gate_scale[0], ("sx", "head"), swap)
+    stream_in, gate_in, _ = lax.optimization_barrier((stream[0], gate_scale[0], tile_k))
+    stream_block = lax.ppermute(stream_in, ("sx", "head"), swap)
+    gate_block = lax.ppermute(gate_in, ("sx", "head"), swap)
     weight_block, row_bound, stream_block, gate_block = lax.optimization_barrier(
         (weight_block, row_bound, stream_block, gate_block)
     )

time: 169 us -> 163 us (0.964)
  the two profiles are of different devices: /device:TPU:169 before, /device:TPU:153 now
where the time goes in v14:
time: 163 us
  waiting for transfers between devices  83.6 us (51%)
  starting transfers between devices  46.2 us (28%)
  between operations  15.8 us (10%)
  local copies, waits for them, and re-layouts  6.36 us (4%)
  other arithmetic  5.45 us (3%)
  matrix products  5.25 us (3%)
    ppermute x3, waiting for transfers between devices, on_device(): mixed = mixed + lax.ppermute(outgoing, 'head', route).astype(jnp.float32)  22.5 us
    ppermute x1, waiting for transfers between devices, on_device(): handed = lax.ppermute(updated, ('section', 'sx', 'head'), hand)  17.9 us
    all_to_all x1, waiting for transfers between devices, on_device(): token_parts = lax.all_to_all(spread, 'sx', 0, 0)  14.5 us
    ppermute x2, starting transfers between devices, on_device(): lax.ppermute((tile_k, tile_v), seq, [(i, i + 2) for i in range(seq_count...  10.9 us
    ppermute x2, waiting for transfers between devices, on_device(): lax.ppermute((tile_k, tile_v), seq, [(i, i + 2) for i in range(seq_count...  10.1 us
    ppermute x3, starting transfers between devices, on_device(): mixed = mixed + lax.ppermute(outgoing, 'head', route).astype(jnp.float32)  9.98 us
    all_gather x1, waiting for transfers between devices, on_device(): weight_block = lax.all_gather(out_weight[0], 'sy', axis=1, tiled=True)  7.37 us
    ppermute x3, starting transfers between devices, on_device(): lax.ppermute((partner_half(queries), partner_half(own_keys), partner_half...  7.35 us
  transfers between devices with their start and end apart: 16, of which 9 were waited for; matrix products, arithmetic and copies ran while one was open for 5% of the time, Pallas kernels for 0%

profile of v14, /device:TPU:153, one launch (start us, length us, event | category | flops | bytes accessed | tf_op | source)
XLA Modules:
  0.0 162.6 jit_solution(8820100510145776718)
XLA Ops:
  6.5 0.7 all-gather.3.cloned.1.call-update
  7.3 1.0 dynamic-slice_bitcast_fusion.5
  8.3 2.1 %collective-permute-start = (bf16[192,384]{1,0:T(8,128)(2,1)S(1)}, bf16[192,384]{1,0:T(8,128)(2,1)S(1)}, u32[]{:S(2)}, u32[]{:S(2)}) collective-permute-start(bf16[192,384]{1,0:T(8,128)(2,1)S(1)} %get-tuple-element.30), channel_id=1, source_target_pairs={{0,4},{4,0},{8,12},{12,8},{16,20},{20,16},{24,28},{28,24},{32,36},... | collective-permute-start | bytes 442376 | tf_op jit(solution)/shard_map/ppermute | solution.py:132
  10.4 1.0 constant_dynamic-slice_fusion.3
  11.4 3.2 %collective-permute-start.1 = (bf16[192,384]{1,0:T(8,128)(2,1)S(1)}, bf16[192,384]{1,0:T(8,128)(2,1)S(1)}, u32[]{:S(2)}, u32[]{:S(2)}) collective-permute-start(bf16[192,384]{1,0:T(8,128)(2,1)S(1)} %get-tuple-element.29), channel_id=1, source_target_pairs={{0,4},{4,0},{8,12},{12,8},{16,20},{20,16},{24,28},{28,24},{32,36},... | collective-permute-start | bytes 442376 | tf_op jit(solution)/shard_map/ppermute | solution.py:132
  14.7 2.1 %collective-permute-start.6 = (bf16[192,384]{1,0:T(8,128)(2,1)S(1)}, bf16[192,384]{1,0:T(8,128)(2,1)S(1)}, u32[]{:S(2)}, u32[]{:S(2)}) collective-permute-start(bf16[192,384]{1,0:T(8,128)(2,1)S(1)} %get-tuple-element.27), channel_id=1, source_target_pairs={{0,4},{4,0},{8,12},{12,8},{16,20},{20,16},{24,28},{28,24},{32,36},... | collective-permute-start | bytes 442376 | tf_op jit(solution)/shard_map/ppermute | solution.py:132
  20.0 0.8 maximum_select_fusion.4
  20.8 5.4 %collective-permute-start.2 = (bf16[384,384]{1,0:T(8,128)(2,1)}, bf16[384,384]{1,0:T(8,128)(2,1)S(1)}, u32[]{:S(2)}, u32[]{:S(2)}) collective-permute-start(bf16[384,384]{1,0:T(8,128)(2,1)} %maximum_select_fusion.4), channel_id=1, source_target_pairs={{0,8},{4,12},{8,16},{12,20},{16,24},{20,28},{24,32},{28,36},{32,40... | collective-permute-start | bytes 884744 | tf_op jit(solution)/shard_map/ppermute | solution.py:146
  26.2 1.9 %collective-permute-start.3 = (bf16[384,384]{1,0:T(8,128)(2,1)}, bf16[384,384]{1,0:T(8,128)(2,1)S(1)}, u32[]{:S(2)}, u32[]{:S(2)}) collective-permute-start(bf16[384,384]{1,0:T(8,128)(2,1)} %maximum_select_fusion.4), channel_id=1, source_target_pairs={{8,0},{12,4},{16,8},{20,12},{24,16},{28,20},{32,24},{36,28},{40,32... | collective-permute-start | bytes 884744 | tf_op jit(solution)/shard_map/ppermute | solution.py:147
  28.2 0.8 maximum_select_fusion.5
  29.0 1.9 %collective-permute-start.8 = (bf16[384,384]{1,0:T(8,128)(2,1)}, bf16[384,384]{1,0:T(8,128)(2,1)S(1)}, u32[]{:S(2)}, u32[]{:S(2)}) collective-permute-start(bf16[384,384]{1,0:T(8,128)(2,1)} %maximum_select_fusion.5), channel_id=1, source_target_pairs={{8,0},{12,4},{16,8},{20,12},{24,16},{28,20},{32,24},{36,28},{40,32... | collective-permute-start | bytes 884744 | tf_op jit(solution)/shard_map/ppermute | solution.py:147
  30.9 5.5 %collective-permute-start.7 = (bf16[384,384]{1,0:T(8,128)(2,1)}, bf16[384,384]{1,0:T(8,128)(2,1)S(1)}, u32[]{:S(2)}, u32[]{:S(2)}) collective-permute-start(bf16[384,384]{1,0:T(8,128)(2,1)} %maximum_select_fusion.5), channel_id=1, source_target_pairs={{0,8},{4,12},{8,16},{12,20},{16,24},{20,28},{24,32},{28,36},{32,40... | collective-permute-start | bytes 884744 | tf_op jit(solution)/shard_map/ppermute | solution.py:146
  37.1 2.8 %collective-permute-start.4 = (bf16[192,768]{1,0:T(8,128)(2,1)}, bf16[192,768]{1,0:T(8,128)(2,1)}, u32[]{:S(2)}, u32[]{:S(2)}) collective-permute-start(bf16[192,768]{1,0:T(8,128)(2,1)} %bitcast.9), channel_id=1, source_target_pairs={{0,0},{1,32},{2,64},{3,96},{32,1},{33,33},{34,65},{35,97},{64,2},{... | collective-permute-start | bytes 884744 | tf_op jit(solution)/shard_map/ppermute | solution.py:169
  41.0 3.3 %collective-permute-done.2 = bf16[384,384]{1,0:T(8,128)(2,1)S(1)} collective-permute-done((bf16[384,384]{1,0:T(8,128)(2,1)}, bf16[384,384]{1,0:T(8,128)(2,1)S(1)}, u32[]{:S(2)}, u32[]{:S(2)}) %collective-permute-start.2) | collective-permute-done | bytes 294944 | tf_op jit(solution)/shard_map/ppermute | solution.py:146
  44.3 2.4 %collective-permute-start.5 = (f32[768]{0:T(1024)S(1)}, f32[768]{0:T(1024)S(1)}, u32[]{:S(2)}, u32[]{:S(2)}) collective-permute-start(f32[768]{0:T(1024)S(1)} %reduce), channel_id=1, source_target_pairs={{0,0},{1,32},{2,64},{3,96},{32,1},{33,33},{34,65},{35,97},{64,2},{... | collective-permute-start | bytes 9224 | tf_op jit(solution)/shard_map/ppermute | solution.py:170
  47.8 5.2 %collective-permute-done.8 = bf16[384,384]{1,0:T(8,128)(2,1)S(1)} collective-permute-done((bf16[384,384]{1,0:T(8,128)(2,1)}, bf16[384,384]{1,0:T(8,128)(2,1)S(1)}, u32[]{:S(2)}, u32[]{:S(2)}) %collective-permute-start.8) | collective-permute-done | bytes 294944 | tf_op jit(solution)/shard_map/ppermute | solution.py:147
  53.2 6.8 %collective-permute-done.7 = bf16[384,384]{1,0:T(8,128)(2,1)S(1)} collective-permute-done((bf16[384,384]{1,0:T(8,128)(2,1)}, bf16[384,384]{1,0:T(8,128)(2,1)S(1)}, u32[]{:S(2)}, u32[]{:S(2)}) %collective-permute-start.7) | collective-permute-done | bytes 294944 | tf_op jit(solution)/shard_map/ppermute | solution.py:146
  60.2 7.4 %all-gather.3.cloned.1.call-done = bf16[1,768,768]{1,2,0:T(8,128)(2,1)} async-done(((bf16[1,768,96]{1,2,0:T(8,128)(2,1)}), bf16[1,768,768]{1,2,0:T(8,128)(2,1)}) %all-gather.3.cloned.1.call-update) | async-done | bytes 1179664 | tf_op jit(solution)/shard_map/all_gather | solution.py:166
  71.0 1.9 %collective-permute-start.9 = (bf16[192,384]{0,1:T(8,128)(2,1)S(1)}, bf16[192,384]{0,1:T(8,128)(2,1)S(1)}, u32[]{:S(2)}, u32[]{:S(2)}) collective-permute-start(bf16[192,384]{0,1:T(8,128)(2,1)S(1)} %get-tuple-element.25), channel_id=1, source_target_pairs={{0,4},{4,0},{8,12},{12,8},{16,20},{20,16},{24,28},{28,24},{32,36},... | collective-permute-start | bytes 442376 | tf_op jit(solution)/shard_map/ppermute | solution.py:194
  72.9 5.2 %collective-permute-done.9 = bf16[192,384]{0,1:T(8,128)(2,1)S(1)} collective-permute-done((bf16[192,384]{0,1:T(8,128)(2,1)S(1)}, bf16[192,384]{0,1:T(8,128)(2,1)S(1)}, u32[]{:S(2)}, u32[]{:S(2)}) %collective-permute-start.9) | collective-permute-done | bytes 147488 | tf_op jit(solution)/shard_map/ppermute | solution.py:194
  78.4 1.1 broadcast_in_dim.31
  79.5 3.9 %all-to-all-start = ((bf16[4,192,768]{2,1,0:T(8,128)(2,1)}), bf16[4,192,768]{2,1,0:T(8,128)(2,1)S(1)}, u32[]{:S(2)}, u32[]{:S(2)}) async-start(bf16[4,192,768]{2,1,0:T(8,128)(2,1)} %broadcast_in_dim.31), calls=%async_computation | async-start | bytes 2359296 | tf_op jit(solution)/shard_map/all_to_all | solution.py:201
  83.4 14.5 %all-to-all-done = bf16[4,192,768]{2,1,0:T(8,128)(2,1)S(1)} async-done(((bf16[4,192,768]{2,1,0:T(8,128)(2,1)}), bf16[4,192,768]{2,1,0:T(8,128)(2,1)S(1)}, u32[]{:S(2)}, u32[]{:S(2)}) %all-to-all-start) | async-done | bytes 1179680 | tf_op jit(solution)/shard_map/all_to_all | solution.py:201
  100.3 1.9 %collective-permute-start.12 = (bf16[192,768]{1,0:T(8,128)(2,1)S(1)}, bf16[192,768]{1,0:T(8,128)(2,1)S(1)}, u32[]{:S(2)}, u32[]{:S(2)}) collective-permute-start(bf16[192,768]{1,0:T(8,128)(2,1)S(1)} %get-tuple-element.22), channel_id=1, source_target_pairs={{0,3},{1,0},{2,1},{3,2},{4,7},{5,4},{6,5},{7,6},{8,11},{9,8},{10,9... | collective-permute-start | bytes 884744 | tf_op jit(solution)/shard_map/ppermute | solution.py:217
  102.3 6.1 %collective-permute-start.11 = (bf16[192,768]{1,0:T(8,128)(2,1)S(1)}, bf16[192,768]{1,0:T(8,128)(2,1)S(1)}, u32[]{:S(2)}, u32[]{:S(2)}) collective-permute-start(bf16[192,768]{1,0:T(8,128)(2,1)S(1)} %get-tuple-element.23), channel_id=1, source_target_pairs={{0,2},{1,3},{2,0},{3,1},{4,6},{5,7},{6,4},{7,5},{8,10},{9,11},{10,... | collective-permute-start | bytes 884744 | tf_op jit(solution)/shard_map/ppermute | solution.py:217
  108.4 1.9 %collective-permute-start.10 = (bf16[192,768]{1,0:T(8,128)(2,1)S(1)}, bf16[192,768]{1,0:T(8,128)(2,1)S(1)}, u32[]{:S(2)}, u32[]{:S(2)}) collective-permute-start(bf16[192,768]{1,0:T(8,128)(2,1)S(1)} %get-tuple-element.21), channel_id=1, source_target_pairs={{0,1},{1,2},{2,3},{3,0},{4,5},{5,6},{6,7},{7,4},{8,9},{9,10},{10,1... | collective-permute-start | bytes 884744 | tf_op jit(solution)/shard_map/ppermute | solution.py:217
  110.3 16.5 %collective-permute-done.11 = bf16[192,768]{1,0:T(8,128)(2,1)S(1)} collective-permute-done((bf16[192,768]{1,0:T(8,128)(2,1)S(1)}, bf16[192,768]{1,0:T(8,128)(2,1)S(1)}, u32[]{:S(2)}, u32[]{:S(2)}) %collective-permute-start.11) | collective-permute-done | bytes 294944 | tf_op jit(solution)/shard_map/ppermute | solution.py:217
  126.9 6.0 %collective-permute-done.10 = bf16[192,768]{1,0:T(8,128)(2,1)S(1)} collective-permute-done((bf16[192,768]{1,0:T(8,128)(2,1)S(1)}, bf16[192,768]{1,0:T(8,128)(2,1)S(1)}, u32[]{:S(2)}, u32[]{:S(2)}) %collective-permute-start.10) | collective-permute-done | bytes 294944 | tf_op jit(solution)/shard_map/ppermute | solution.py:217
  132.9 1.2 fusion.17
  134.1 3.1 %collective-permute-start.13 = (bf16[192,768]{1,0:T(8,128)(2,1)S(1)}, bf16[192,768]{1,0:T(8,128)(2,1)S(1)}, u32[]{:S(2)}, u32[]{:S(2)}) collective-permute-start(bf16[192,768]{1,0:T(8,128)(2,1)S(1)} %fusion.17), channel_id=1, source_target_pairs={{0,128},{1,160},{2,192},{3,224},{32,129},{33,161},{34,193},{35,225... | collective-permute-start | bytes 884744 | tf_op jit(solution)/shard_map/ppermute | solution.py:222
  137.1 17.9 %collective-permute-done.13 = bf16[192,768]{1,0:T(8,128)(2,1)S(1)} collective-permute-done((bf16[192,768]{1,0:T(8,128)(2,1)S(1)}, bf16[192,768]{1,0:T(8,128)(2,1)S(1)}, u32[]{:S(2)}, u32[]{:S(2)}) %collective-permute-start.13) | collective-permute-done | bytes 294944 | tf_op jit(solution)/shard_map/ppermute | solution.py:222
  155.1 0.7 copy.118
  (57 shorter events, 10.4 us)
Async XLA Ops:
  6.5 8.1 %copy-start.1 = (bf16[1,192,768]{2,1,0:T(8,128)(2,1)S(1)}, bf16[1,192,768]{2,1,0:T(8,128)(2,1)}, u32[]{:S(2)}) copy-start(bf16[1,192,768]{2,1,0:T(8,128)(2,1)} %param.9) | copy-start | bytes 884740
  6.5 10.3 %copy-start.2 = (s32[16,27]{1,0:T(8,128)S(1)}, s32[16,27]{1,0:T(8,128)}, u32[]{:S(2)}) copy-start(s32[16,27]{1,0:T(8,128)} %param.13) | copy-start | bytes 5188
  6.5 61.1 %all-gather.3.cloned.1.call-start = ((), (), s32[]{:S(2)}) async-start(), calls=%async_computation.1 | async-start | bytes 1327104 | tf_op jit(solution)/shard_map/all_gather | solution.py:166
  8.3 11.6 %copy-start.3 = (f32[1,768]{1,0:T(1,128)S(1)}, f32[1,768]{1,0:T(1,128)}, u32[]{:S(2)}) copy-start(f32[1,768]{1,0:T(1,128)} %param.12) | copy-start | bytes 9220
  8.3 28.8 %collective-permute-start = (bf16[192,384]{1,0:T(8,128)(2,1)S(1)}, bf16[192,384]{1,0:T(8,128)(2,1)S(1)}, u32[]{:S(2)}, u32[]{:S(2)}) collective-permute-start(bf16[192,384]{1,0:T(8,128)(2,1)S(1)} %get-tuple-element.30), channel_id=1, source_target_pairs={{0,4},{4,0},{8,12},{12,8},{16,20},{20,16},{24,28},{28,24},{32,36},... | collective-permute-start | bytes 442376 | tf_op jit(solution)/shard_map/ppermute | solution.py:132
  11.4 8.6 %collective-permute-start.1 = (bf16[192,384]{1,0:T(8,128)(2,1)S(1)}, bf16[192,384]{1,0:T(8,128)(2,1)S(1)}, u32[]{:S(2)}, u32[]{:S(2)}) collective-permute-start(bf16[192,384]{1,0:T(8,128)(2,1)S(1)} %get-tuple-element.29), channel_id=1, source_target_pairs={{0,4},{4,0},{8,12},{12,8},{16,20},{20,16},{24,28},{28,24},{32,36},... | collective-permute-start | bytes 442376 | tf_op jit(solution)/shard_map/ppermute | solution.py:132
  14.7 13.5 %collective-permute-start.6 = (bf16[192,384]{1,0:T(8,128)(2,1)S(1)}, bf16[192,384]{1,0:T(8,128)(2,1)S(1)}, u32[]{:S(2)}, u32[]{:S(2)}) collective-permute-start(bf16[192,384]{1,0:T(8,128)(2,1)S(1)} %get-tuple-element.27), channel_id=1, source_target_pairs={{0,4},{4,0},{8,12},{12,8},{16,20},{20,16},{24,28},{28,24},{32,36},... | collective-permute-start | bytes 442376 | tf_op jit(solution)/shard_map/ppermute | solution.py:132
  20.8 23.5 %collective-permute-start.2 = (bf16[384,384]{1,0:T(8,128)(2,1)}, bf16[384,384]{1,0:T(8,128)(2,1)S(1)}, u32[]{:S(2)}, u32[]{:S(2)}) collective-permute-start(bf16[384,384]{1,0:T(8,128)(2,1)} %maximum_select_fusion.4), channel_id=1, source_target_pairs={{0,8},{4,12},{8,16},{12,20},{16,24},{20,28},{24,32},{28,36},{32,40... | collective-permute-start | bytes 884744 | tf_op jit(solution)/shard_map/ppermute | solution.py:146
  26.2 20.8 %collective-permute-start.3 = (bf16[384,384]{1,0:T(8,128)(2,1)}, bf16[384,384]{1,0:T(8,128)(2,1)S(1)}, u32[]{:S(2)}, u32[]{:S(2)}) collective-permute-start(bf16[384,384]{1,0:T(8,128)(2,1)} %maximum_select_fusion.4), channel_id=1, source_target_pairs={{8,0},{12,4},{16,8},{20,12},{24,16},{28,20},{32,24},{36,28},{40,32... | collective-permute-start | bytes 884744 | tf_op jit(solution)/shard_map/ppermute | solution.py:147
  29.0 24.0 %collective-permute-start.8 = (bf16[384,384]{1,0:T(8,128)(2,1)}, bf16[384,384]{1,0:T(8,128)(2,1)S(1)}, u32[]{:S(2)}, u32[]{:S(2)}) collective-permute-start(bf16[384,384]{1,0:T(8,128)(2,1)} %maximum_select_fusion.5), channel_id=1, source_target_pairs={{8,0},{12,4},{16,8},{20,12},{24,16},{28,20},{32,24},{36,28},{40,32... | collective-permute-start | bytes 884744 | tf_op jit(solution)/shard_map/ppermute | solution.py:147
  30.9 29.1 %collective-permute-start.7 = (bf16[384,384]{1,0:T(8,128)(2,1)}, bf16[384,384]{1,0:T(8,128)(2,1)S(1)}, u32[]{:S(2)}, u32[]{:S(2)}) collective-permute-start(bf16[384,384]{1,0:T(8,128)(2,1)} %maximum_select_fusion.5), channel_id=1, source_target_pairs={{0,8},{4,12},{8,16},{12,20},{16,24},{20,28},{24,32},{28,36},{32,40... | collective-permute-start | bytes 884744 | tf_op jit(solution)/shard_map/ppermute | solution.py:146
  37.1 23.1 %collective-permute-start.4 = (bf16[192,768]{1,0:T(8,128)(2,1)}, bf16[192,768]{1,0:T(8,128)(2,1)}, u32[]{:S(2)}, u32[]{:S(2)}) collective-permute-start(bf16[192,768]{1,0:T(8,128)(2,1)} %bitcast.9), channel_id=1, source_target_pairs={{0,0},{1,32},{2,64},{3,96},{32,1},{33,33},{34,65},{35,97},{64,2},{... | collective-permute-start | bytes 884744 | tf_op jit(solution)/shard_map/ppermute | solution.py:169
  44.3 15.9 %collective-permute-start.5 = (f32[768]{0:T(1024)S(1)}, f32[768]{0:T(1024)S(1)}, u32[]{:S(2)}, u32[]{:S(2)}) collective-permute-start(f32[768]{0:T(1024)S(1)} %reduce), channel_id=1, source_target_pairs={{0,0},{1,32},{2,64},{3,96},{32,1},{33,33},{34,65},{35,97},{64,2},{... | collective-permute-start | bytes 9224 | tf_op jit(solution)/shard_map/ppermute | solution.py:170
  71.0 7.1 %collective-permute-start.9 = (bf16[192,384]{0,1:T(8,128)(2,1)S(1)}, bf16[192,384]{0,1:T(8,128)(2,1)S(1)}, u32[]{:S(2)}, u32[]{:S(2)}) collective-permute-start(bf16[192,384]{0,1:T(8,128)(2,1)S(1)} %get-tuple-element.25), channel_id=1, source_target_pairs={{0,4},{4,0},{8,12},{12,8},{16,20},{20,16},{24,28},{28,24},{32,36},... | collective-permute-start | bytes 442376 | tf_op jit(solution)/shard_map/ppermute | solution.py:194
  79.5 18.4 %copy-start = (bf16[1,768,768]{1,2,0:T(8,128)(2,1)S(1)}, bf16[1,768,768]{1,2,0:T(8,128)(2,1)}, u32[]{:S(2)}) copy-start(bf16[1,768,768]{1,2,0:T(8,128)(2,1)} %all-gather.3.cloned.1.call-done) | copy-start | bytes 3538948
  79.5 18.4 %all-to-all-start = ((bf16[4,192,768]{2,1,0:T(8,128)(2,1)}), bf16[4,192,768]{2,1,0:T(8,128)(2,1)S(1)}, u32[]{:S(2)}, u32[]{:S(2)}) async-start(bf16[4,192,768]{2,1,0:T(8,128)(2,1)} %broadcast_in_dim.31), calls=%async_computation | async-start | bytes 2359296 | tf_op jit(solution)/shard_map/all_to_all | solution.py:201
  100.3 10.0 %collective-permute-start.12 = (bf16[192,768]{1,0:T(8,128)(2,1)S(1)}, bf16[192,768]{1,0:T(8,128)(2,1)S(1)}, u32[]{:S(2)}, u32[]{:S(2)}) collective-permute-start(bf16[192,768]{1,0:T(8,128)(2,1)S(1)} %get-tuple-element.22), channel_id=1, source_target_pairs={{0,3},{1,0},{2,1},{3,2},{4,7},{5,4},{6,5},{7,6},{8,11},{9,8},{10,9... | collective-permute-start | bytes 884744 | tf_op jit(solution)/shard_map/ppermute | solution.py:217
  102.3 24.6 %collective-permute-start.11 = (bf16[192,768]{1,0:T(8,128)(2,1)S(1)}, bf16[192,768]{1,0:T(8,128)(2,1)S(1)}, u32[]{:S(2)}, u32[]{:S(2)}) collective-permute-start(bf16[192,768]{1,0:T(8,128)(2,1)S(1)} %get-tuple-element.23), channel_id=1, source_target_pairs={{0,2},{1,3},{2,0},{3,1},{4,6},{5,7},{6,4},{7,5},{8,10},{9,11},{10,... | collective-permute-start | bytes 884744 | tf_op jit(solution)/shard_map/ppermute | solution.py:217
  108.4 24.5 %collective-permute-start.10 = (bf16[192,768]{1,0:T(8,128)(2,1)S(1)}, bf16[192,768]{1,0:T(8,128)(2,1)S(1)}, u32[]{:S(2)}, u32[]{:S(2)}) collective-permute-start(bf16[192,768]{1,0:T(8,128)(2,1)S(1)} %get-tuple-element.21), channel_id=1, source_target_pairs={{0,1},{1,2},{2,3},{3,0},{4,5},{5,6},{6,7},{7,4},{8,9},{9,10},{10,1... | collective-permute-start | bytes 884744 | tf_op jit(solution)/shard_map/ppermute | solution.py:217
  134.1 21.0 %collective-permute-start.13 = (bf16[192,768]{1,0:T(8,128)(2,1)S(1)}, bf16[192,768]{1,0:T(8,128)(2,1)S(1)}, u32[]{:S(2)}, u32[]{:S(2)}) collective-permute-start(bf16[192,768]{1,0:T(8,128)(2,1)S(1)} %fusion.17), channel_id=1, source_target_pairs={{0,128},{1,160},{2,192},{3,224},{32,129},{33,161},{34,193},{35,225... | collective-permute-start | bytes 884744 | tf_op jit(solution)/shard_map/ppermute | solution.py:222
Sparse Core Ops, SparseCore 0:
  9.4 58.1 all-gather.2

commit v15 on v14

--- a/solution.py
+++ b/solution.py
@@ -129,9 +129,14 @@
     def own_half(block):
         return lax.dynamic_slice_in_dim(block, parity * half, half, 1)
 
-    sent = lax.ppermute(
-        (partner_half(queries), partner_half(own_keys), partner_half(own_values)), seq, partner
-    )
+    swapped = lax.ppermute(
+        jnp.concatenate(
+            [partner_half(queries), partner_half(own_keys), partner_half(own_values)], axis=1
+        ),
+        seq,
+        partner,
+    )
+    sent = [swapped[:, part * half:(part + 1) * half] for part in range(3)]
 
     def whole_tile(mine, theirs):
         return jnp.where(
@@ -143,8 +148,12 @@
     tile_q = whole_tile(own_half(queries), sent[0])
     tile_k = whole_tile(own_half(own_keys), sent[1])
     tile_v = whole_tile(own_half(own_values), sent[2])
-    before = lax.ppermute((tile_k, tile_v), seq, [(i, i + 2) for i in range(seq_count - 2)])
-    after = lax.ppermute((tile_k, tile_v), seq, [(i, i - 2) for i in range(2, seq_count)])
+    tile_kv = jnp.concatenate([tile_k, tile_v], axis=1)
+    moved = [
+        lax.ppermute(tile_kv, seq, [(i, i + 2) for i in range(seq_count - 2)]),
+        lax.ppermute(tile_kv, seq, [(i, i - 2) for i in range(2, seq_count)]),
+    ]
+    before, after = [(block[:, :half], block[:, half:]) for block in moved]
     key_tiles = [before, (tile_k, tile_v), after]
     keeps = []
     for step in (-1, 0, 1):

time: 163 us -> 169 us (1.037)
  the two profiles are of different devices: /device:TPU:153 before, /device:TPU:145 now
where the time goes in v15:
time: 169 us; the launch traced here: 168 us
  waiting for transfers between devices  96.1 us (57%)
  starting transfers between devices  38.5 us (23%)
  between operations  15.8 us (9%)
  local copies, waits for them, and re-layouts  8.02 us (5%)
  matrix products  5.21 us (3%)
  other arithmetic  4.57 us (3%)
    ppermute x3, waiting for transfers between devices, on_device(): mixed = mixed + lax.ppermute(outgoing, 'head', route).astype(jnp.float32)  22.6 us
    ppermute x1, waiting for transfers between devices, on_device(): handed = lax.ppermute(updated, ('section', 'sx', 'head'), hand)  17.3 us
    ppermute x1, waiting for transfers between devices, on_device(): lax.ppermute(tile_kv, seq, [(i, i + 2) for i in range(seq_count - 2)])  17.3 us
    all_to_all x1, waiting for transfers between devices, on_device(): token_parts = lax.all_to_all(spread, 'sx', 0, 0)  14.6 us
    ppermute x3, starting transfers between devices, on_device(): mixed = mixed + lax.ppermute(outgoing, 'head', route).astype(jnp.float32)  10.1 us
    ppermute x1, waiting for transfers between devices, on_device(): lax.ppermute(jnp.concatenate([partner_half(queries), partner_half(own_key...  9.45 us
    ppermute x1, waiting for transfers between devices, on_device(): lax.ppermute(tile_kv, seq, [(i, i - 2) for i in range(2, seq_count)])  9.38 us
    ppermute x1, starting transfers between devices, on_device(): gate_block = lax.ppermute(gate_in, ('sx', 'head'), swap)  5.75 us
  transfers between devices with their start and end apart: 12, of which 8 were waited for; matrix products, arithmetic and copies ran while one was open for 4% of the time, Pallas kernels for 0%

profile of v15, /device:TPU:145, one launch (start us, length us, event | category | flops | bytes accessed | tf_op | source)
XLA Modules:
  0.0 168.2 jit_solution(7146867588152361601)
XLA Ops:
  6.5 1.0 constant_dynamic-slice_fusion.3
  7.6 1.2 dynamic-slice_bitcast_fusion.5
  8.8 3.2 %collective-permute-start = (bf16[192,1152]{1,0:T(8,128)(2,1)S(1)}, bf16[192,1152]{1,0:T(8,128)(2,1)S(1)}, u32[]{:S(2)}, u32[]{:S(2)}) collective-permute-start(bf16[192,1152]{1,0:T(8,128)(2,1)S(1)} %pad_maximum_fusion.2), channel_id=1, source_target_pairs={{0,4},{4,0},{8,12},{12,8},{16,20},{20,16},{24,28},{28,24},{32,36},... | collective-permute-start | bytes 1327112 | tf_op jit(solution)/shard_map/ppermute | solution.py:132
  12.3 9.4 %collective-permute-done = bf16[192,1152]{1,0:T(8,128)(2,1)S(1)} collective-permute-done((bf16[192,1152]{1,0:T(8,128)(2,1)S(1)}, bf16[192,1152]{1,0:T(8,128)(2,1)S(1)}, u32[]{:S(2)}, u32[]{:S(2)}) %collective-permute-start) | collective-permute-done | bytes 442400 | tf_op jit(solution)/shard_map/ppermute | solution.py:132
  22.0 5.4 %collective-permute-start.1 = (bf16[384,768]{1,0:T(8,128)(2,1)S(1)}, bf16[384,768]{1,0:T(8,128)(2,1)S(1)}, u32[]{:S(2)}, u32[]{:S(2)}) collective-permute-start(bf16[384,768]{1,0:T(8,128)(2,1)S(1)} %pad_maximum_fusion.1), channel_id=1, source_target_pairs={{0,8},{4,12},{8,16},{12,20},{16,24},{20,28},{24,32},{28,36},{32,40... | collective-permute-start | bytes 1769480 | tf_op jit(solution)/shard_map/ppermute | solution.py:153
  27.8 0.7 fusion.30
  30.5 1.9 %collective-permute-start.2 = (bf16[384,768]{1,0:T(8,128)(2,1)S(1)}, bf16[384,768]{1,0:T(8,128)(2,1)}, u32[]{:S(2)}, u32[]{:S(2)}) collective-permute-start(bf16[384,768]{1,0:T(8,128)(2,1)S(1)} %pad_maximum_fusion.1), channel_id=1, source_target_pairs={{8,0},{12,4},{16,8},{20,12},{24,16},{28,20},{32,24},{36,28},{40,32... | collective-permute-start | bytes 1769480 | tf_op jit(solution)/shard_map/ppermute | solution.py:154
  32.5 1.2 multiply_reduce_fusion
  33.8 2.9 %collective-permute-start.3 = (bf16[192,768]{1,0:T(8,128)(2,1)}, bf16[192,768]{1,0:T(8,128)(2,1)S(1)}, u32[]{:S(2)}, u32[]{:S(2)}) collective-permute-start(bf16[192,768]{1,0:T(8,128)(2,1)} %bitcast.11), channel_id=1, source_target_pairs={{0,0},{1,32},{2,64},{3,96},{32,1},{33,33},{34,65},{35,97},{64,2},{... | collective-permute-start | bytes 884744 | tf_op jit(solution)/shard_map/ppermute | solution.py:178
  36.7 5.7 %collective-permute-start.4 = (f32[768]{0:T(1024)S(1)}, f32[768]{0:T(1024)S(1)}, u32[]{:S(2)}, u32[]{:S(2)}) collective-permute-start(f32[768]{0:T(1024)S(1)} %reduce), channel_id=1, source_target_pairs={{0,0},{1,32},{2,64},{3,96},{32,1},{33,33},{34,65},{35,97},{64,2},{... | collective-permute-start | bytes 9224 | tf_op jit(solution)/shard_map/ppermute | solution.py:179
  42.6 1.2 multiply_reduce_fusion.1
  44.2 17.3 %collective-permute-done.1 = bf16[384,768]{1,0:T(8,128)(2,1)S(1)} collective-permute-done((bf16[384,768]{1,0:T(8,128)(2,1)S(1)}, bf16[384,768]{1,0:T(8,128)(2,1)S(1)}, u32[]{:S(2)}, u32[]{:S(2)}) %collective-permute-start.1) | collective-permute-done | bytes 589856 | tf_op jit(solution)/shard_map/ppermute | solution.py:153
  61.8 9.4 %collective-permute-done.2 = bf16[384,768]{1,0:T(8,128)(2,1)} collective-permute-done((bf16[384,768]{1,0:T(8,128)(2,1)S(1)}, bf16[384,768]{1,0:T(8,128)(2,1)}, u32[]{:S(2)}, u32[]{:S(2)}) %collective-permute-start.2) | collective-permute-done | bytes 589856 | tf_op jit(solution)/shard_map/ppermute | solution.py:154
  71.1 1.1 fusion.28
  73.6 0.7 fusion.31
  74.2 0.6 fusion.32
  75.2 0.6 fusion.33
  77.1 1.9 %collective-permute-start.5 = (bf16[192,384]{0,1:T(8,128)(2,1)S(1)}, bf16[192,384]{0,1:T(8,128)(2,1)S(1)}, u32[]{:S(2)}, u32[]{:S(2)}) collective-permute-start(bf16[192,384]{0,1:T(8,128)(2,1)S(1)} %get-tuple-element.32), channel_id=1, source_target_pairs={{0,4},{4,0},{8,12},{12,8},{16,20},{20,16},{24,28},{28,24},{32,36},... | collective-permute-start | bytes 442376 | tf_op jit(solution)/shard_map/ppermute | solution.py:203
  79.1 5.5 %collective-permute-done.5 = bf16[192,384]{0,1:T(8,128)(2,1)S(1)} collective-permute-done((bf16[192,384]{0,1:T(8,128)(2,1)S(1)}, bf16[192,384]{0,1:T(8,128)(2,1)S(1)}, u32[]{:S(2)}, u32[]{:S(2)}) %collective-permute-start.5) | collective-permute-done | bytes 147488 | tf_op jit(solution)/shard_map/ppermute | solution.py:203
  84.8 1.1 broadcast_in_dim.31
  85.9 3.7 %all-to-all-start = ((bf16[4,192,768]{2,1,0:T(8,128)(2,1)}), bf16[4,192,768]{2,1,0:T(8,128)(2,1)S(1)}, u32[]{:S(2)}, u32[]{:S(2)}) async-start(bf16[4,192,768]{2,1,0:T(8,128)(2,1)} %broadcast_in_dim.31), calls=%async_computation | async-start | bytes 2359296 | tf_op jit(solution)/shard_map/all_to_all | solution.py:210
  89.6 14.6 %all-to-all-done = bf16[4,192,768]{2,1,0:T(8,128)(2,1)S(1)} async-done(((bf16[4,192,768]{2,1,0:T(8,128)(2,1)}), bf16[4,192,768]{2,1,0:T(8,128)(2,1)S(1)}, u32[]{:S(2)}, u32[]{:S(2)}) %all-to-all-start) | async-done | bytes 1179680 | tf_op jit(solution)/shard_map/all_to_all | solution.py:210
  105.4 0.6 fusion.5
  105.9 0.6 fusion.4
  106.7 2.2 %collective-permute-start.8 = (bf16[192,768]{1,0:T(8,128)(2,1)S(1)}, bf16[192,768]{1,0:T(8,128)(2,1)S(1)}, u32[]{:S(2)}, u32[]{:S(2)}) collective-permute-start(bf16[192,768]{1,0:T(8,128)(2,1)S(1)} %get-tuple-element.22), channel_id=1, source_target_pairs={{0,3},{1,0},{2,1},{3,2},{4,7},{5,4},{6,5},{7,6},{8,11},{9,8},{10,9... | collective-permute-start | bytes 884744 | tf_op jit(solution)/shard_map/ppermute | solution.py:226
  108.9 6.0 %collective-permute-start.7 = (bf16[192,768]{1,0:T(8,128)(2,1)S(1)}, bf16[192,768]{1,0:T(8,128)(2,1)S(1)}, u32[]{:S(2)}, u32[]{:S(2)}) collective-permute-start(bf16[192,768]{1,0:T(8,128)(2,1)S(1)} %get-tuple-element.23), channel_id=1, source_target_pairs={{0,2},{1,3},{2,0},{3,1},{4,6},{5,7},{6,4},{7,5},{8,10},{9,11},{10,... | collective-permute-start | bytes 884744 | tf_op jit(solution)/shard_map/ppermute | solution.py:226
  114.9 1.9 %collective-permute-start.6 = (bf16[192,768]{1,0:T(8,128)(2,1)S(1)}, bf16[192,768]{1,0:T(8,128)(2,1)S(1)}, u32[]{:S(2)}, u32[]{:S(2)}) collective-permute-start(bf16[192,768]{1,0:T(8,128)(2,1)S(1)} %get-tuple-element.21), channel_id=1, source_target_pairs={{0,1},{1,2},{2,3},{3,0},{4,5},{5,6},{6,7},{7,4},{8,9},{9,10},{10,1... | collective-permute-start | bytes 884744 | tf_op jit(solution)/shard_map/ppermute | solution.py:226
  116.9 16.8 %collective-permute-done.7 = bf16[192,768]{1,0:T(8,128)(2,1)S(1)} collective-permute-done((bf16[192,768]{1,0:T(8,128)(2,1)S(1)}, bf16[192,768]{1,0:T(8,128)(2,1)S(1)}, u32[]{:S(2)}, u32[]{:S(2)}) %collective-permute-start.7) | collective-permute-done | bytes 294944 | tf_op jit(solution)/shard_map/ppermute | solution.py:226
  133.6 5.8 %collective-permute-done.6 = bf16[192,768]{1,0:T(8,128)(2,1)S(1)} collective-permute-done((bf16[192,768]{1,0:T(8,128)(2,1)S(1)}, bf16[192,768]{1,0:T(8,128)(2,1)S(1)}, u32[]{:S(2)}, u32[]{:S(2)}) %collective-permute-start.6) | collective-permute-done | bytes 294944 | tf_op jit(solution)/shard_map/ppermute | solution.py:226
  139.7 3.7 %collective-permute-start.9 = (bf16[192,768]{1,0:T(8,128)(2,1)S(1)}, bf16[192,768]{1,0:T(8,128)(2,1)S(1)}, u32[]{:S(2)}, u32[]{:S(2)}) collective-permute-start(bf16[192,768]{1,0:T(8,128)(2,1)S(1)} %fusion.17), channel_id=1, source_target_pairs={{0,128},{1,160},{2,192},{3,224},{32,129},{33,161},{34,193},{35,225... | collective-permute-start | bytes 884744 | tf_op jit(solution)/shard_map/ppermute | solution.py:231
  143.4 17.3 %collective-permute-done.9 = bf16[192,768]{1,0:T(8,128)(2,1)S(1)} collective-permute-done((bf16[192,768]{1,0:T(8,128)(2,1)S(1)}, bf16[192,768]{1,0:T(8,128)(2,1)S(1)}, u32[]{:S(2)}, u32[]{:S(2)}) %collective-permute-start.9) | collective-permute-done | bytes 294944 | tf_op jit(solution)/shard_map/ppermute | solution.py:231
  160.6 0.7 copy.118
  (56 shorter events, 6.6 us)
Async XLA Ops:
  6.5 66.9 %all-gather.3.cloned.1.call-start = ((), (), s32[]{:S(2)}) async-start(), calls=%async_computation.1 | async-start | bytes 1327104 | tf_op jit(solution)/shard_map/all_gather | solution.py:175
  8.8 12.9 %collective-permute-start = (bf16[192,1152]{1,0:T(8,128)(2,1)S(1)}, bf16[192,1152]{1,0:T(8,128)(2,1)S(1)}, u32[]{:S(2)}, u32[]{:S(2)}) collective-permute-start(bf16[192,1152]{1,0:T(8,128)(2,1)S(1)} %pad_maximum_fusion.2), channel_id=1, source_target_pairs={{0,4},{4,0},{8,12},{12,8},{16,20},{20,16},{24,28},{28,24},{32,36},... | collective-permute-start | bytes 1327112 | tf_op jit(solution)/shard_map/ppermute | solution.py:132
  21.8 5.7 %copy-start.3 = (s32[16,27]{1,0:T(8,128)S(1)}, s32[16,27]{1,0:T(8,128)}, u32[]{:S(2)}) copy-start(s32[16,27]{1,0:T(8,128)} %param.13) | copy-start | bytes 5188
  21.8 8.6 %copy-start.4 = (f32[1,768]{1,0:T(1,128)S(1)}, f32[1,768]{1,0:T(1,128)}, u32[]{:S(2)}) copy-start(f32[1,768]{1,0:T(1,128)} %param.12) | copy-start | bytes 9220
  22.0 39.4 %collective-permute-start.1 = (bf16[384,768]{1,0:T(8,128)(2,1)S(1)}, bf16[384,768]{1,0:T(8,128)(2,1)S(1)}, u32[]{:S(2)}, u32[]{:S(2)}) collective-permute-start(bf16[384,768]{1,0:T(8,128)(2,1)S(1)} %pad_maximum_fusion.1), channel_id=1, source_target_pairs={{0,8},{4,12},{8,16},{12,20},{16,24},{20,28},{24,32},{28,36},{32,40... | collective-permute-start | bytes 1769480 | tf_op jit(solution)/shard_map/ppermute | solution.py:153
  30.5 40.6 %collective-permute-start.2 = (bf16[384,768]{1,0:T(8,128)(2,1)S(1)}, bf16[384,768]{1,0:T(8,128)(2,1)}, u32[]{:S(2)}, u32[]{:S(2)}) collective-permute-start(bf16[384,768]{1,0:T(8,128)(2,1)S(1)} %pad_maximum_fusion.1), channel_id=1, source_target_pairs={{8,0},{12,4},{16,8},{20,12},{24,16},{28,20},{32,24},{36,28},{40,32... | collective-permute-start | bytes 1769480 | tf_op jit(solution)/shard_map/ppermute | solution.py:154
  33.8 39.6 %collective-permute-start.3 = (bf16[192,768]{1,0:T(8,128)(2,1)}, bf16[192,768]{1,0:T(8,128)(2,1)S(1)}, u32[]{:S(2)}, u32[]{:S(2)}) collective-permute-start(bf16[192,768]{1,0:T(8,128)(2,1)} %bitcast.11), channel_id=1, source_target_pairs={{0,0},{1,32},{2,64},{3,96},{32,1},{33,33},{34,65},{35,97},{64,2},{... | collective-permute-start | bytes 884744 | tf_op jit(solution)/shard_map/ppermute | solution.py:178
  36.7 36.7 %collective-permute-start.4 = (f32[768]{0:T(1024)S(1)}, f32[768]{0:T(1024)S(1)}, u32[]{:S(2)}, u32[]{:S(2)}) collective-permute-start(f32[768]{0:T(1024)S(1)} %reduce), channel_id=1, source_target_pairs={{0,0},{1,32},{2,64},{3,96},{32,1},{33,33},{34,65},{35,97},{64,2},{... | collective-permute-start | bytes 9224 | tf_op jit(solution)/shard_map/ppermute | solution.py:179
  72.5 1.1 copy-start.2
  74.2 1.0 copy-start.1
  77.1 7.4 %collective-permute-start.5 = (bf16[192,384]{0,1:T(8,128)(2,1)S(1)}, bf16[192,384]{0,1:T(8,128)(2,1)S(1)}, u32[]{:S(2)}, u32[]{:S(2)}) collective-permute-start(bf16[192,384]{0,1:T(8,128)(2,1)S(1)} %get-tuple-element.32), channel_id=1, source_target_pairs={{0,4},{4,0},{8,12},{12,8},{16,20},{20,16},{24,28},{28,24},{32,36},... | collective-permute-start | bytes 442376 | tf_op jit(solution)/shard_map/ppermute | solution.py:203
  85.9 18.3 %copy-start = (bf16[1,768,768]{1,2,0:T(8,128)(2,1)S(1)}, bf16[1,768,768]{1,2,0:T(8,128)(2,1)}, u32[]{:S(2)}) copy-start(bf16[1,768,768]{1,2,0:T(8,128)(2,1)} %all-gather.3.cloned.1.call-done) | copy-start | bytes 3538948
  85.9 18.3 %all-to-all-start = ((bf16[4,192,768]{2,1,0:T(8,128)(2,1)}), bf16[4,192,768]{2,1,0:T(8,128)(2,1)S(1)}, u32[]{:S(2)}, u32[]{:S(2)}) async-start(bf16[4,192,768]{2,1,0:T(8,128)(2,1)} %broadcast_in_dim.31), calls=%async_computation | async-start | bytes 2359296 | tf_op jit(solution)/shard_map/all_to_all | solution.py:210
  106.7 10.1 %collective-permute-start.8 = (bf16[192,768]{1,0:T(8,128)(2,1)S(1)}, bf16[192,768]{1,0:T(8,128)(2,1)S(1)}, u32[]{:S(2)}, u32[]{:S(2)}) collective-permute-start(bf16[192,768]{1,0:T(8,128)(2,1)S(1)} %get-tuple-element.22), channel_id=1, source_target_pairs={{0,3},{1,0},{2,1},{3,2},{4,7},{5,4},{6,5},{7,6},{8,11},{9,8},{10,9... | collective-permute-start | bytes 884744 | tf_op jit(solution)/shard_map/ppermute | solution.py:226
  108.9 24.7 %collective-permute-start.7 = (bf16[192,768]{1,0:T(8,128)(2,1)S(1)}, bf16[192,768]{1,0:T(8,128)(2,1)S(1)}, u32[]{:S(2)}, u32[]{:S(2)}) collective-permute-start(bf16[192,768]{1,0:T(8,128)(2,1)S(1)} %get-tuple-element.23), channel_id=1, source_target_pairs={{0,2},{1,3},{2,0},{3,1},{4,6},{5,7},{6,4},{7,5},{8,10},{9,11},{10,... | collective-permute-start | bytes 884744 | tf_op jit(solution)/shard_map/ppermute | solution.py:226
  114.9 24.5 %collective-permute-start.6 = (bf16[192,768]{1,0:T(8,128)(2,1)S(1)}, bf16[192,768]{1,0:T(8,128)(2,1)S(1)}, u32[]{:S(2)}, u32[]{:S(2)}) collective-permute-start(bf16[192,768]{1,0:T(8,128)(2,1)S(1)} %get-tuple-element.21), channel_id=1, source_target_pairs={{0,1},{1,2},{2,3},{3,0},{4,5},{5,6},{6,7},{7,4},{8,9},{9,10},{10,1... | collective-permute-start | bytes 884744 | tf_op jit(solution)/shard_map/ppermute | solution.py:226
  139.7 21.0 %collective-permute-start.9 = (bf16[192,768]{1,0:T(8,128)(2,1)S(1)}, bf16[192,768]{1,0:T(8,128)(2,1)S(1)}, u32[]{:S(2)}, u32[]{:S(2)}) collective-permute-start(bf16[192,768]{1,0:T(8,128)(2,1)S(1)} %fusion.17), channel_id=1, source_target_pairs={{0,128},{1,160},{2,192},{3,224},{32,129},{33,161},{34,193},{35,225... | collective-permute-start | bytes 884744 | tf_op jit(solution)/shard_map/ppermute | solution.py:231
Sparse Core Ops, SparseCore 0:
  12.2 56.8 all-gather.2

commit v16 on v14

--- a/solution.py
+++ b/solution.py
@@ -219,7 +219,15 @@
     hand = linear_pairs(
         (sections, x_count, head_groups), lambda s, a, b: ((s + 1) % sections, b, a)
     )
-    handed = lax.ppermute(updated, ("section", "sx", "head"), hand)
+    pieces = 4
+    step = row_count // pieces
+    handed = jnp.concatenate(
+        [
+            lax.ppermute(updated[k * step:(k + 1) * step], ("section", "sx", "head"), hand)
+            for k in range(pieces)
+        ],
+        axis=0,
+    )
     return handed[None]
 
 

time: 163 us -> 169 us (1.037)
  the two profiles are of different devices: /device:TPU:153 before, /device:TPU:6 now
where the time goes in v16:
time: 169 us; the launch traced here: 166 us
  starting transfers between devices  73.5 us (43%)
  waiting for transfers between devices  60.1 us (36%)
  between operations  15.9 us (9%)
  other arithmetic  6.19 us (4%)
  local copies, waits for them, and re-layouts  5.67 us (3%)
  matrix products  5.24 us (3%)
    ppermute x4, starting transfers between devices, on_device(): lax.ppermute(updated[k * step:(k + 1) * step], ('section', 'sx', 'head'),...  18.4 us
    ppermute x3, waiting for transfers between devices, on_device(): mixed = mixed + lax.ppermute(outgoing, 'head', route).astype(jnp.float32)  17.3 us
    ppermute x2, waiting for transfers between devices, on_device(): lax.ppermute((tile_k, tile_v), seq, [(i, i - 2) for i in range(2, seq_cou...  13.7 us
    all_to_all x1, waiting for transfers between devices, on_device(): token_parts = lax.all_to_all(spread, 'sx', 0, 0)  12 us
    ppermute x3, starting transfers between devices, on_device(): mixed = mixed + lax.ppermute(outgoing, 'head', route).astype(jnp.float32)  11.8 us
    ppermute x4, waiting for transfers between devices, on_device(): lax.ppermute(updated[k * step:(k + 1) * step], ('section', 'sx', 'head'),...  9.63 us
    ppermute x3, starting transfers between devices, on_device(): lax.ppermute((partner_half(queries), partner_half(own_keys), partner_half...  9.33 us
    ppermute x2, starting transfers between devices, on_device(): lax.ppermute((tile_k, tile_v), seq, [(i, i + 2) for i in range(seq_count...  7.81 us
  transfers between devices with their start and end apart: 19, of which 8 were waited for; matrix products, arithmetic and copies ran while one was open for 5% of the time, Pallas kernels for 0%

profile of v16, /device:TPU:6, one launch (start us, length us, event | category | flops | bytes accessed | tf_op | source)
XLA Modules:
  0.0 166.5 jit_solution(7879408459406484531)
XLA Ops:
  7.3 1.0 dynamic-slice_bitcast_fusion.5
  8.3 3.5 %collective-permute-start = (bf16[192,384]{1,0:T(8,128)(2,1)S(1)}, bf16[192,384]{1,0:T(8,128)(2,1)S(1)}, u32[]{:S(2)}, u32[]{:S(2)}) collective-permute-start(bf16[192,384]{1,0:T(8,128)(2,1)S(1)} %get-tuple-element.34), channel_id=1, source_target_pairs={{0,4},{4,0},{8,12},{12,8},{16,20},{20,16},{24,28},{28,24},{32,36},... | collective-permute-start | bytes 442376 | tf_op jit(solution)/shard_map/ppermute | solution.py:132
  11.8 1.0 constant_dynamic-slice_fusion.3
  12.8 2.4 %collective-permute-start.1 = (bf16[192,384]{1,0:T(8,128)(2,1)S(1)}, bf16[192,384]{1,0:T(8,128)(2,1)S(1)}, u32[]{:S(2)}, u32[]{:S(2)}) collective-permute-start(bf16[192,384]{1,0:T(8,128)(2,1)S(1)} %get-tuple-element.33), channel_id=1, source_target_pairs={{0,4},{4,0},{8,12},{12,8},{16,20},{20,16},{24,28},{28,24},{32,36},... | collective-permute-start | bytes 442376 | tf_op jit(solution)/shard_map/ppermute | solution.py:132
  15.3 3.5 %collective-permute-start.6 = (bf16[192,384]{1,0:T(8,128)(2,1)S(1)}, bf16[192,384]{1,0:T(8,128)(2,1)S(1)}, u32[]{:S(2)}, u32[]{:S(2)}) collective-permute-start(bf16[192,384]{1,0:T(8,128)(2,1)S(1)} %get-tuple-element.31), channel_id=1, source_target_pairs={{0,4},{4,0},{8,12},{12,8},{16,20},{20,16},{24,28},{28,24},{32,36},... | collective-permute-start | bytes 442376 | tf_op jit(solution)/shard_map/ppermute | solution.py:132
  22.0 0.8 maximum_select_fusion.4
  22.8 4.5 %collective-permute-start.2 = (bf16[384,384]{1,0:T(8,128)(2,1)}, bf16[384,384]{1,0:T(8,128)(2,1)S(1)}, u32[]{:S(2)}, u32[]{:S(2)}) collective-permute-start(bf16[384,384]{1,0:T(8,128)(2,1)} %maximum_select_fusion.4), channel_id=1, source_target_pairs={{0,8},{4,12},{8,16},{12,20},{16,24},{20,28},{24,32},{28,36},{32,40... | collective-permute-start | bytes 884744 | tf_op jit(solution)/shard_map/ppermute | solution.py:146
  27.3 4.4 %collective-permute-start.3 = (bf16[384,384]{1,0:T(8,128)(2,1)}, bf16[384,384]{1,0:T(8,128)(2,1)S(1)}, u32[]{:S(2)}, u32[]{:S(2)}) collective-permute-start(bf16[384,384]{1,0:T(8,128)(2,1)} %maximum_select_fusion.4), channel_id=1, source_target_pairs={{8,0},{12,4},{16,8},{20,12},{24,16},{28,20},{32,24},{36,28},{40,32... | collective-permute-start | bytes 884744 | tf_op jit(solution)/shard_map/ppermute | solution.py:147
  31.7 0.8 maximum_select_fusion.5
  32.5 3.4 %collective-permute-start.8 = (bf16[384,384]{1,0:T(8,128)(2,1)}, bf16[384,384]{1,0:T(8,128)(2,1)S(1)}, u32[]{:S(2)}, u32[]{:S(2)}) collective-permute-start(bf16[384,384]{1,0:T(8,128)(2,1)} %maximum_select_fusion.5), channel_id=1, source_target_pairs={{8,0},{12,4},{16,8},{20,12},{24,16},{28,20},{32,24},{36,28},{40,32... | collective-permute-start | bytes 884744 | tf_op jit(solution)/shard_map/ppermute | solution.py:147
  35.9 3.3 %collective-permute-start.7 = (bf16[384,384]{1,0:T(8,128)(2,1)}, bf16[384,384]{1,0:T(8,128)(2,1)S(1)}, u32[]{:S(2)}, u32[]{:S(2)}) collective-permute-start(bf16[384,384]{1,0:T(8,128)(2,1)} %maximum_select_fusion.5), channel_id=1, source_target_pairs={{0,8},{4,12},{8,16},{12,20},{16,24},{20,28},{24,32},{28,36},{32,40... | collective-permute-start | bytes 884744 | tf_op jit(solution)/shard_map/ppermute | solution.py:146
  40.0 5.4 %collective-permute-start.4 = (bf16[192,768]{1,0:T(8,128)(2,1)}, bf16[192,768]{1,0:T(8,128)(2,1)}, u32[]{:S(2)}, u32[]{:S(2)}) collective-permute-start(bf16[192,768]{1,0:T(8,128)(2,1)} %bitcast.9), channel_id=1, source_target_pairs={{0,0},{1,32},{2,64},{3,96},{32,1},{33,33},{34,65},{35,97},{64,2},{... | collective-permute-start | bytes 884744 | tf_op jit(solution)/shard_map/ppermute | solution.py:169
  46.4 4.3 %collective-permute-start.5 = (f32[768]{0:T(1024)S(1)}, f32[768]{0:T(1024)S(1)}, u32[]{:S(2)}, u32[]{:S(2)}) collective-permute-start(f32[768]{0:T(1024)S(1)} %reduce), channel_id=1, source_target_pairs={{0,0},{1,32},{2,64},{3,96},{32,1},{33,33},{34,65},{35,97},{64,2},{... | collective-permute-start | bytes 9224 | tf_op jit(solution)/shard_map/ppermute | solution.py:170
  51.8 13.7 %collective-permute-done.8 = bf16[384,384]{1,0:T(8,128)(2,1)S(1)} collective-permute-done((bf16[384,384]{1,0:T(8,128)(2,1)}, bf16[384,384]{1,0:T(8,128)(2,1)S(1)}, u32[]{:S(2)}, u32[]{:S(2)}) %collective-permute-start.8) | collective-permute-done | bytes 294944 | tf_op jit(solution)/shard_map/ppermute | solution.py:147
  66.0 2.7 %all-gather.3.cloned.1.call-done = bf16[1,768,768]{1,2,0:T(8,128)(2,1)} async-done(((bf16[1,768,96]{1,2,0:T(8,128)(2,1)}), bf16[1,768,768]{1,2,0:T(8,128)(2,1)}) %all-gather.3.cloned.1.call-update) | async-done | bytes 1179664 | tf_op jit(solution)/shard_map/all_gather | solution.py:166
  72.0 3.7 %collective-permute-start.9 = (bf16[192,384]{0,1:T(8,128)(2,1)S(1)}, bf16[192,384]{0,1:T(8,128)(2,1)S(1)}, u32[]{:S(2)}, u32[]{:S(2)}) collective-permute-start(bf16[192,384]{0,1:T(8,128)(2,1)S(1)} %get-tuple-element.29), channel_id=1, source_target_pairs={{0,4},{4,0},{8,12},{12,8},{16,20},{20,16},{24,28},{28,24},{32,36},... | collective-permute-start | bytes 442376 | tf_op jit(solution)/shard_map/ppermute | solution.py:194
  75.6 4.0 %collective-permute-done.9 = bf16[192,384]{0,1:T(8,128)(2,1)S(1)} collective-permute-done((bf16[192,384]{0,1:T(8,128)(2,1)S(1)}, bf16[192,384]{0,1:T(8,128)(2,1)S(1)}, u32[]{:S(2)}, u32[]{:S(2)}) %collective-permute-start.9) | collective-permute-done | bytes 147488 | tf_op jit(solution)/shard_map/ppermute | solution.py:194
  79.9 1.1 broadcast_in_dim.31
  81.0 5.0 %all-to-all-start = ((bf16[4,192,768]{2,1,0:T(8,128)(2,1)}), bf16[4,192,768]{2,1,0:T(8,128)(2,1)S(1)}, u32[]{:S(2)}, u32[]{:S(2)}) async-start(bf16[4,192,768]{2,1,0:T(8,128)(2,1)} %broadcast_in_dim.31), calls=%async_computation | async-start | bytes 2359296 | tf_op jit(solution)/shard_map/all_to_all | solution.py:201
  86.0 12.0 %all-to-all-done = bf16[4,192,768]{2,1,0:T(8,128)(2,1)S(1)} async-done(((bf16[4,192,768]{2,1,0:T(8,128)(2,1)}), bf16[4,192,768]{2,1,0:T(8,128)(2,1)S(1)}, u32[]{:S(2)}, u32[]{:S(2)}) %all-to-all-start) | async-done | bytes 1179680 | tf_op jit(solution)/shard_map/all_to_all | solution.py:201
  100.5 7.5 %collective-permute-start.12 = (bf16[192,768]{1,0:T(8,128)(2,1)S(1)}, bf16[192,768]{1,0:T(8,128)(2,1)S(1)}, u32[]{:S(2)}, u32[]{:S(2)}) collective-permute-start(bf16[192,768]{1,0:T(8,128)(2,1)S(1)} %get-tuple-element.22), channel_id=1, source_target_pairs={{0,3},{1,0},{2,1},{3,2},{4,7},{5,4},{6,5},{7,6},{8,11},{9,8},{10,9... | collective-permute-start | bytes 884744 | tf_op jit(solution)/shard_map/ppermute | solution.py:217
  107.9 1.9 %collective-permute-start.11 = (bf16[192,768]{1,0:T(8,128)(2,1)S(1)}, bf16[192,768]{1,0:T(8,128)(2,1)S(1)}, u32[]{:S(2)}, u32[]{:S(2)}) collective-permute-start(bf16[192,768]{1,0:T(8,128)(2,1)S(1)} %get-tuple-element.23), channel_id=1, source_target_pairs={{0,2},{1,3},{2,0},{3,1},{4,6},{5,7},{6,4},{7,5},{8,10},{9,11},{10,... | collective-permute-start | bytes 884744 | tf_op jit(solution)/shard_map/ppermute | solution.py:217
  109.9 2.5 %collective-permute-start.10 = (bf16[192,768]{1,0:T(8,128)(2,1)S(1)}, bf16[192,768]{1,0:T(8,128)(2,1)S(1)}, u32[]{:S(2)}, u32[]{:S(2)}) collective-permute-start(bf16[192,768]{1,0:T(8,128)(2,1)S(1)} %get-tuple-element.21), channel_id=1, source_target_pairs={{0,1},{1,2},{2,3},{3,0},{4,5},{5,6},{6,7},{7,4},{8,9},{9,10},{10,1... | collective-permute-start | bytes 884744 | tf_op jit(solution)/shard_map/ppermute | solution.py:217
  112.4 3.0 %collective-permute-done.12 = bf16[192,768]{1,0:T(8,128)(2,1)S(1)} collective-permute-done((bf16[192,768]{1,0:T(8,128)(2,1)S(1)}, bf16[192,768]{1,0:T(8,128)(2,1)S(1)}, u32[]{:S(2)}, u32[]{:S(2)}) %collective-permute-start.12) | collective-permute-done | bytes 294944 | tf_op jit(solution)/shard_map/ppermute | solution.py:217
  115.4 14.2 %collective-permute-done.11 = bf16[192,768]{1,0:T(8,128)(2,1)S(1)} collective-permute-done((bf16[192,768]{1,0:T(8,128)(2,1)S(1)}, bf16[192,768]{1,0:T(8,128)(2,1)S(1)}, u32[]{:S(2)}, u32[]{:S(2)}) %collective-permute-start.11) | collective-permute-done | bytes 294944 | tf_op jit(solution)/shard_map/ppermute | solution.py:217
  129.6 1.2 fusion.17
  130.9 1.9 %collective-permute-start.16 = (bf16[48,768]{1,0:T(8,128)(2,1)S(1)}, bf16[48,768]{1,0:T(8,128)(2,1)S(1)}, u32[]{:S(2)}, u32[]{:S(2)}) collective-permute-start(bf16[48,768]{1,0:T(8,128)(2,1)S(1)} %get-tuple-element.25), channel_id=1, source_target_pairs={{0,128},{1,160},{2,192},{3,224},{32,129},{33,161},{34,193},{35,225... | collective-permute-start | bytes 221192 | tf_op jit(solution)/shard_map/ppermute | solution.py:226
  132.8 11.8 %collective-permute-start.15 = (bf16[48,768]{1,0:T(8,128)(2,1)S(1)}, bf16[48,768]{1,0:T(8,128)(2,1)S(1)}, u32[]{:S(2)}, u32[]{:S(2)}) collective-permute-start(bf16[48,768]{1,0:T(8,128)(2,1)S(1)} %get-tuple-element.26), channel_id=1, source_target_pairs={{0,128},{1,160},{2,192},{3,224},{32,129},{33,161},{34,193},{35,225... | collective-permute-start | bytes 221192 | tf_op jit(solution)/shard_map/ppermute | solution.py:226
  144.5 1.9 %collective-permute-start.14 = (bf16[48,768]{1,0:T(8,128)(2,1)S(1)}, bf16[48,768]{1,0:T(8,128)(2,1)S(1)}, u32[]{:S(2)}, u32[]{:S(2)}) collective-permute-start(bf16[48,768]{1,0:T(8,128)(2,1)S(1)} %get-tuple-element.27), channel_id=1, source_target_pairs={{0,128},{1,160},{2,192},{3,224},{32,129},{33,161},{34,193},{35,225... | collective-permute-start | bytes 221192 | tf_op jit(solution)/shard_map/ppermute | solution.py:226
  146.5 2.8 %collective-permute-start.13 = (bf16[48,768]{1,0:T(8,128)(2,1)S(1)}, bf16[48,768]{1,0:T(8,128)(2,1)S(1)}, u32[]{:S(2)}, u32[]{:S(2)}) collective-permute-start(bf16[48,768]{1,0:T(8,128)(2,1)S(1)} %get-tuple-element.24), channel_id=1, source_target_pairs={{0,128},{1,160},{2,192},{3,224},{32,129},{33,161},{34,193},{35,225... | collective-permute-start | bytes 221192 | tf_op jit(solution)/shard_map/ppermute | solution.py:226
  149.3 8.8 %collective-permute-done.14 = bf16[48,768]{1,0:T(8,128)(2,1)S(1)} collective-permute-done((bf16[48,768]{1,0:T(8,128)(2,1)S(1)}, bf16[48,768]{1,0:T(8,128)(2,1)S(1)}, u32[]{:S(2)}, u32[]{:S(2)}) %collective-permute-start.14) | collective-permute-done | bytes 73760 | tf_op jit(solution)/shard_map/ppermute | solution.py:226
  158.1 0.8 collective-permute-done.13
  (64 shorter events, 11.9 us)
Async XLA Ops:
  6.5 8.7 %copy-start.1 = (bf16[1,192,768]{2,1,0:T(8,128)(2,1)S(1)}, bf16[1,192,768]{2,1,0:T(8,128)(2,1)}, u32[]{:S(2)}) copy-start(bf16[1,192,768]{2,1,0:T(8,128)(2,1)} %param.9) | copy-start | bytes 884740
  6.5 12.2 %copy-start.2 = (s32[16,27]{1,0:T(8,128)S(1)}, s32[16,27]{1,0:T(8,128)}, u32[]{:S(2)}) copy-start(s32[16,27]{1,0:T(8,128)} %param.13) | copy-start | bytes 5188
  6.5 62.1 %all-gather.3.cloned.1.call-start = ((), (), s32[]{:S(2)}) async-start(), calls=%async_computation.1 | async-start | bytes 1327104 | tf_op jit(solution)/shard_map/all_gather | solution.py:166
  8.3 13.7 %copy-start.3 = (f32[1,768]{1,0:T(1,128)S(1)}, f32[1,768]{1,0:T(1,128)}, u32[]{:S(2)}) copy-start(f32[1,768]{1,0:T(1,128)} %param.12) | copy-start | bytes 9220
  8.3 31.7 %collective-permute-start = (bf16[192,384]{1,0:T(8,128)(2,1)S(1)}, bf16[192,384]{1,0:T(8,128)(2,1)S(1)}, u32[]{:S(2)}, u32[]{:S(2)}) collective-permute-start(bf16[192,384]{1,0:T(8,128)(2,1)S(1)} %get-tuple-element.34), channel_id=1, source_target_pairs={{0,4},{4,0},{8,12},{12,8},{16,20},{20,16},{24,28},{28,24},{32,36},... | collective-permute-start | bytes 442376 | tf_op jit(solution)/shard_map/ppermute | solution.py:132
  12.8 9.2 %collective-permute-start.1 = (bf16[192,384]{1,0:T(8,128)(2,1)S(1)}, bf16[192,384]{1,0:T(8,128)(2,1)S(1)}, u32[]{:S(2)}, u32[]{:S(2)}) collective-permute-start(bf16[192,384]{1,0:T(8,128)(2,1)S(1)} %get-tuple-element.33), channel_id=1, source_target_pairs={{0,4},{4,0},{8,12},{12,8},{16,20},{20,16},{24,28},{28,24},{32,36},... | collective-permute-start | bytes 442376 | tf_op jit(solution)/shard_map/ppermute | solution.py:132
  15.3 16.4 %collective-permute-start.6 = (bf16[192,384]{1,0:T(8,128)(2,1)S(1)}, bf16[192,384]{1,0:T(8,128)(2,1)S(1)}, u32[]{:S(2)}, u32[]{:S(2)}) collective-permute-start(bf16[192,384]{1,0:T(8,128)(2,1)S(1)} %get-tuple-element.31), channel_id=1, source_target_pairs={{0,4},{4,0},{8,12},{12,8},{16,20},{20,16},{24,28},{28,24},{32,36},... | collective-permute-start | bytes 442376 | tf_op jit(solution)/shard_map/ppermute | solution.py:132
  22.8 23.6 %collective-permute-start.2 = (bf16[384,384]{1,0:T(8,128)(2,1)}, bf16[384,384]{1,0:T(8,128)(2,1)S(1)}, u32[]{:S(2)}, u32[]{:S(2)}) collective-permute-start(bf16[384,384]{1,0:T(8,128)(2,1)} %maximum_select_fusion.4), channel_id=1, source_target_pairs={{0,8},{4,12},{8,16},{12,20},{16,24},{20,28},{24,32},{28,36},{32,40... | collective-permute-start | bytes 884744 | tf_op jit(solution)/shard_map/ppermute | solution.py:146
  27.3 23.7 %collective-permute-start.3 = (bf16[384,384]{1,0:T(8,128)(2,1)}, bf16[384,384]{1,0:T(8,128)(2,1)S(1)}, u32[]{:S(2)}, u32[]{:S(2)}) collective-permute-start(bf16[384,384]{1,0:T(8,128)(2,1)} %maximum_select_fusion.4), channel_id=1, source_target_pairs={{8,0},{12,4},{16,8},{20,12},{24,16},{28,20},{32,24},{36,28},{40,32... | collective-permute-start | bytes 884744 | tf_op jit(solution)/shard_map/ppermute | solution.py:147
  32.5 33.0 %collective-permute-start.8 = (bf16[384,384]{1,0:T(8,128)(2,1)}, bf16[384,384]{1,0:T(8,128)(2,1)S(1)}, u32[]{:S(2)}, u32[]{:S(2)}) collective-permute-start(bf16[384,384]{1,0:T(8,128)(2,1)} %maximum_select_fusion.5), channel_id=1, source_target_pairs={{8,0},{12,4},{16,8},{20,12},{24,16},{28,20},{32,24},{36,28},{40,32... | collective-permute-start | bytes 884744 | tf_op jit(solution)/shard_map/ppermute | solution.py:147
  35.9 29.8 %collective-permute-start.7 = (bf16[384,384]{1,0:T(8,128)(2,1)}, bf16[384,384]{1,0:T(8,128)(2,1)S(1)}, u32[]{:S(2)}, u32[]{:S(2)}) collective-permute-start(bf16[384,384]{1,0:T(8,128)(2,1)} %maximum_select_fusion.5), channel_id=1, source_target_pairs={{0,8},{4,12},{8,16},{12,20},{16,24},{20,28},{24,32},{28,36},{32,40... | collective-permute-start | bytes 884744 | tf_op jit(solution)/shard_map/ppermute | solution.py:146
  40.0 26.0 %collective-permute-start.4 = (bf16[192,768]{1,0:T(8,128)(2,1)}, bf16[192,768]{1,0:T(8,128)(2,1)}, u32[]{:S(2)}, u32[]{:S(2)}) collective-permute-start(bf16[192,768]{1,0:T(8,128)(2,1)} %bitcast.9), channel_id=1, source_target_pairs={{0,0},{1,32},{2,64},{3,96},{32,1},{33,33},{34,65},{35,97},{64,2},{... | collective-permute-start | bytes 884744 | tf_op jit(solution)/shard_map/ppermute | solution.py:169
  46.4 19.5 %collective-permute-start.5 = (f32[768]{0:T(1024)S(1)}, f32[768]{0:T(1024)S(1)}, u32[]{:S(2)}, u32[]{:S(2)}) collective-permute-start(f32[768]{0:T(1024)S(1)} %reduce), channel_id=1, source_target_pairs={{0,0},{1,32},{2,64},{3,96},{32,1},{33,33},{34,65},{35,97},{64,2},{... | collective-permute-start | bytes 9224 | tf_op jit(solution)/shard_map/ppermute | solution.py:170
  72.0 7.6 %collective-permute-start.9 = (bf16[192,384]{0,1:T(8,128)(2,1)S(1)}, bf16[192,384]{0,1:T(8,128)(2,1)S(1)}, u32[]{:S(2)}, u32[]{:S(2)}) collective-permute-start(bf16[192,384]{0,1:T(8,128)(2,1)S(1)} %get-tuple-element.29), channel_id=1, source_target_pairs={{0,4},{4,0},{8,12},{12,8},{16,20},{20,16},{24,28},{28,24},{32,36},... | collective-permute-start | bytes 442376 | tf_op jit(solution)/shard_map/ppermute | solution.py:194
  81.0 17.0 %copy-start = (bf16[1,768,768]{1,2,0:T(8,128)(2,1)S(1)}, bf16[1,768,768]{1,2,0:T(8,128)(2,1)}, u32[]{:S(2)}) copy-start(bf16[1,768,768]{1,2,0:T(8,128)(2,1)} %all-gather.3.cloned.1.call-done) | copy-start | bytes 3538948
  81.0 17.0 %all-to-all-start = ((bf16[4,192,768]{2,1,0:T(8,128)(2,1)}), bf16[4,192,768]{2,1,0:T(8,128)(2,1)S(1)}, u32[]{:S(2)}, u32[]{:S(2)}) async-start(bf16[4,192,768]{2,1,0:T(8,128)(2,1)} %broadcast_in_dim.31), calls=%async_computation | async-start | bytes 2359296 | tf_op jit(solution)/shard_map/all_to_all | solution.py:201
  100.5 14.9 %collective-permute-start.12 = (bf16[192,768]{1,0:T(8,128)(2,1)S(1)}, bf16[192,768]{1,0:T(8,128)(2,1)S(1)}, u32[]{:S(2)}, u32[]{:S(2)}) collective-permute-start(bf16[192,768]{1,0:T(8,128)(2,1)S(1)} %get-tuple-element.22), channel_id=1, source_target_pairs={{0,3},{1,0},{2,1},{3,2},{4,7},{5,4},{6,5},{7,6},{8,11},{9,8},{10,9... | collective-permute-start | bytes 884744 | tf_op jit(solution)/shard_map/ppermute | solution.py:217
  107.9 21.7 %collective-permute-start.11 = (bf16[192,768]{1,0:T(8,128)(2,1)S(1)}, bf16[192,768]{1,0:T(8,128)(2,1)S(1)}, u32[]{:S(2)}, u32[]{:S(2)}) collective-permute-start(bf16[192,768]{1,0:T(8,128)(2,1)S(1)} %get-tuple-element.23), channel_id=1, source_target_pairs={{0,2},{1,3},{2,0},{3,1},{4,6},{5,7},{6,4},{7,5},{8,10},{9,11},{10,... | collective-permute-start | bytes 884744 | tf_op jit(solution)/shard_map/ppermute | solution.py:217
  109.9 19.8 %collective-permute-start.10 = (bf16[192,768]{1,0:T(8,128)(2,1)S(1)}, bf16[192,768]{1,0:T(8,128)(2,1)S(1)}, u32[]{:S(2)}, u32[]{:S(2)}) collective-permute-start(bf16[192,768]{1,0:T(8,128)(2,1)S(1)} %get-tuple-element.21), channel_id=1, source_target_pairs={{0,1},{1,2},{2,3},{3,0},{4,5},{5,6},{6,7},{7,4},{8,9},{9,10},{10,1... | collective-permute-start | bytes 884744 | tf_op jit(solution)/shard_map/ppermute | solution.py:217
  130.9 18.4 %collective-permute-start.16 = (bf16[48,768]{1,0:T(8,128)(2,1)S(1)}, bf16[48,768]{1,0:T(8,128)(2,1)S(1)}, u32[]{:S(2)}, u32[]{:S(2)}) collective-permute-start(bf16[48,768]{1,0:T(8,128)(2,1)S(1)} %get-tuple-element.25), channel_id=1, source_target_pairs={{0,128},{1,160},{2,192},{3,224},{32,129},{33,161},{34,193},{35,225... | collective-permute-start | bytes 221192 | tf_op jit(solution)/shard_map/ppermute | solution.py:226
  132.8 16.5 %collective-permute-start.15 = (bf16[48,768]{1,0:T(8,128)(2,1)S(1)}, bf16[48,768]{1,0:T(8,128)(2,1)S(1)}, u32[]{:S(2)}, u32[]{:S(2)}) collective-permute-start(bf16[48,768]{1,0:T(8,128)(2,1)S(1)} %get-tuple-element.26), channel_id=1, source_target_pairs={{0,128},{1,160},{2,192},{3,224},{32,129},{33,161},{34,193},{35,225... | collective-permute-start | bytes 221192 | tf_op jit(solution)/shard_map/ppermute | solution.py:226
  144.5 13.5 %collective-permute-start.14 = (bf16[48,768]{1,0:T(8,128)(2,1)S(1)}, bf16[48,768]{1,0:T(8,128)(2,1)S(1)}, u32[]{:S(2)}, u32[]{:S(2)}) collective-permute-start(bf16[48,768]{1,0:T(8,128)(2,1)S(1)} %get-tuple-element.27), channel_id=1, source_target_pairs={{0,128},{1,160},{2,192},{3,224},{32,129},{33,161},{34,193},{35,225... | collective-permute-start | bytes 221192 | tf_op jit(solution)/shard_map/ppermute | solution.py:226
  146.5 12.4 %collective-permute-start.13 = (bf16[48,768]{1,0:T(8,128)(2,1)S(1)}, bf16[48,768]{1,0:T(8,128)(2,1)S(1)}, u32[]{:S(2)}, u32[]{:S(2)}) collective-permute-start(bf16[48,768]{1,0:T(8,128)(2,1)S(1)} %get-tuple-element.24), channel_id=1, source_target_pairs={{0,128},{1,160},{2,192},{3,224},{32,129},{33,161},{34,193},{35,225... | collective-permute-start | bytes 221192 | tf_op jit(solution)/shard_map/ppermute | solution.py:226
Sparse Core Ops, SparseCore 0:
  9.4 59.1 all-gather.2

commit v17 on v14

--- a/solution.py
+++ b/solution.py
@@ -171,27 +171,33 @@
     weight_block, row_bound, stream_block, gate_block = lax.optimization_barrier(
         (weight_block, row_bound, stream_block, gate_block)
     )
-    weighted = jnp.zeros((tile_len, own_heads, HD), jnp.float32)
-    summed = jnp.zeros((own_heads, tile_len), jnp.float32)
-    for (keys, values), keep in zip(key_tiles, keeps):
-        key_parts = keys.reshape(tile_len, own_heads, HD)
-        value_parts = values.reshape(tile_len, own_heads, HD)
-        scores = (
-            jnp.einsum("qhd,khd->hqk", query_parts, key_parts, preferred_element_type=jnp.float32)
-            * score_scale
-        )
-        weights = jnp.where(keep, jnp.exp(scores - row_bound.T[:, :, None]), 0.0)
-        summed = summed + jnp.sum(weights, axis=2)
-        weighted = weighted + jnp.einsum(
-            "hqk,khd->qhd",
-            weights.astype(jnp.bfloat16),
-            value_parts,
-            preferred_element_type=jnp.float32,
-        )
-    tile_out = (weighted / summed.T[:, :, None]).astype(jnp.bfloat16).reshape(tile_len, half)
-    mine_rows = lax.dynamic_slice_in_dim(tile_out, parity * row_count, row_count, 0)
-    their_rows = lax.dynamic_slice_in_dim(tile_out, (1 - parity) * row_count, row_count, 0)
+    def attend_rows(first):
+        rows_q = lax.dynamic_slice_in_dim(query_parts, first, row_count, 0)
+        rows_bound = lax.dynamic_slice_in_dim(row_bound, first, row_count, 0)
+        weighted = jnp.zeros((row_count, own_heads, HD), jnp.float32)
+        summed = jnp.zeros((own_heads, row_count), jnp.float32)
+        for (keys, values), keep in zip(key_tiles, keeps):
+            key_parts = keys.reshape(tile_len, own_heads, HD)
+            value_parts = values.reshape(tile_len, own_heads, HD)
+            scores = (
+                jnp.einsum(
+                    "qhd,khd->hqk", rows_q, key_parts, preferred_element_type=jnp.float32
+                )
+                * score_scale
+            )
+            weights = jnp.where(keep, jnp.exp(scores - rows_bound.T[:, :, None]), 0.0)
+            summed = summed + jnp.sum(weights, axis=2)
+            weighted = weighted + jnp.einsum(
+                "hqk,khd->qhd",
+                weights.astype(jnp.bfloat16),
+                value_parts,
+                preferred_element_type=jnp.float32,
+            )
+        return (weighted / summed.T[:, :, None]).astype(jnp.bfloat16).reshape(row_count, half)
+
+    their_rows = attend_rows((1 - parity) * row_count)
     back = lax.ppermute(their_rows, seq, partner)
+    mine_rows = attend_rows(parity * row_count)
     attended = jnp.where(
         parity == 0,
         jnp.concatenate([mine_rows, back], axis=1),

time: 163 us -> 183 us (1.12)
  the two profiles are of different devices: /device:TPU:153 before, /device:TPU:6 now
where the time goes in v17:
time: 183 us; the launch traced here: 182 us
  starting transfers between devices  76.2 us (42%)
  waiting for transfers between devices  73.7 us (40%)
  between operations  15.8 us (9%)
  matrix products  8.66 us (5%)
  local copies, waits for them, and re-layouts  5.1 us (3%)
  other arithmetic  2.5 us (1%)
    ppermute x3, waiting for transfers between devices, on_device(): mixed = mixed + lax.ppermute(outgoing, 'head', route).astype(jnp.float32)  19.8 us
    ppermute x1, waiting for transfers between devices, on_device(): handed = lax.ppermute(updated, ('section', 'sx', 'head'), hand)  18.4 us
    ppermute x3, starting transfers between devices, on_device(): mixed = mixed + lax.ppermute(outgoing, 'head', route).astype(jnp.float32)  15.8 us
    all_to_all x1, starting transfers between devices, on_device(): token_parts = lax.all_to_all(spread, 'sx', 0, 0)  13.3 us
    all_to_all x1, waiting for transfers between devices, on_device(): token_parts = lax.all_to_all(spread, 'sx', 0, 0)  13.2 us
    ppermute x2, waiting for transfers between devices, on_device(): lax.ppermute((tile_k, tile_v), seq, [(i, i - 2) for i in range(2, seq_cou...  12.6 us
    ppermute x2, starting transfers between devices, on_device(): lax.ppermute((tile_k, tile_v), seq, [(i, i - 2) for i in range(2, seq_cou...  12.4 us
    ppermute x1, starting transfers between devices, on_device(): stream_block = lax.ppermute(stream_in, ('sx', 'head'), swap)  9.77 us
  transfers between devices with their start and end apart: 16, of which 8 were waited for; matrix products, arithmetic and copies ran while one was open for 6% of the time, Pallas kernels for 0%

profile of v17, /device:TPU:6, one launch (start us, length us, event | category | flops | bytes accessed | tf_op | source)
XLA Modules:
  0.0 181.9 jit_solution(12605744993807640302)
XLA Ops:
  6.5 0.7 all-gather.3.cloned.1.call-update
  7.3 1.2 constant_dynamic-slice_fusion.1
  8.6 3.5 %collective-permute-start.6 = (bf16[192,384]{0,1:T(8,128)(2,1)S(1)}, bf16[192,384]{0,1:T(8,128)(2,1)S(1)}, u32[]{:S(2)}, u32[]{:S(2)}) collective-permute-start(bf16[192,384]{0,1:T(8,128)(2,1)S(1)} %bitcast.122), channel_id=1, source_target_pairs={{0,4},{4,0},{8,12},{12,8},{16,20},{20,16},{24,28},{28,24},{32,36},... | collective-permute-start | bytes 442376 | tf_op jit(solution)/shard_map/ppermute | solution.py:132
  12.2 2.4 %collective-permute-start = (bf16[192,384]{1,0:T(8,128)(2,1)S(1)}, bf16[192,384]{1,0:T(8,128)(2,1)S(1)}, u32[]{:S(2)}, u32[]{:S(2)}) collective-permute-start(bf16[192,384]{1,0:T(8,128)(2,1)S(1)} %get-tuple-element.26), channel_id=1, source_target_pairs={{0,4},{4,0},{8,12},{12,8},{16,20},{20,16},{24,28},{28,24},{32,36},... | collective-permute-start | bytes 442376 | tf_op jit(solution)/shard_map/ppermute | solution.py:132
  14.7 3.5 %collective-permute-start.1 = (bf16[192,384]{0,1:T(8,128)(2,1)S(1)}, bf16[192,384]{0,1:T(8,128)(2,1)S(1)}, u32[]{:S(2)}, u32[]{:S(2)}) collective-permute-start(bf16[192,384]{0,1:T(8,128)(2,1)S(1)} %bitcast.123), channel_id=1, source_target_pairs={{0,4},{4,0},{8,12},{12,8},{16,20},{20,16},{24,28},{28,24},{32,36},... | collective-permute-start | bytes 442376 | tf_op jit(solution)/shard_map/ppermute | solution.py:132
  19.2 0.7 fusion.65
  22.1 5.5 %collective-permute-start.8 = (bf16[384,384]{0,1:T(8,128)(2,1)S(1)}, bf16[384,384]{0,1:T(8,128)(2,1)S(1)}, u32[]{:S(2)}, u32[]{:S(2)}) collective-permute-start(bf16[384,384]{0,1:T(8,128)(2,1)S(1)} %maximum_select_fusion.3), channel_id=1, source_target_pairs={{8,0},{12,4},{16,8},{20,12},{24,16},{28,20},{32,24},{36,28},{40,32... | collective-permute-start | bytes 884744 | tf_op jit(solution)/shard_map/ppermute | solution.py:147
  27.6 1.9 %collective-permute-start.7 = (bf16[384,384]{0,1:T(8,128)(2,1)S(1)}, bf16[384,384]{0,1:T(8,128)(2,1)}, u32[]{:S(2)}, u32[]{:S(2)}) collective-permute-start(bf16[384,384]{0,1:T(8,128)(2,1)S(1)} %maximum_select_fusion.3), channel_id=1, source_target_pairs={{0,8},{4,12},{8,16},{12,20},{16,24},{20,28},{24,32},{28,36},{32,40... | collective-permute-start | bytes 884744 | tf_op jit(solution)/shard_map/ppermute | solution.py:146
  29.8 6.9 %collective-permute-start.3 = (bf16[384,384]{0,1:T(8,128)(2,1)S(1)}, bf16[384,384]{0,1:T(8,128)(2,1)S(1)}, u32[]{:S(2)}, u32[]{:S(2)}) collective-permute-start(bf16[384,384]{0,1:T(8,128)(2,1)S(1)} %maximum_select_fusion.1), channel_id=1, source_target_pairs={{8,0},{12,4},{16,8},{20,12},{24,16},{28,20},{32,24},{36,28},{40,32... | collective-permute-start | bytes 884744 | tf_op jit(solution)/shard_map/ppermute | solution.py:147
  36.8 1.9 %collective-permute-start.2 = (bf16[384,384]{0,1:T(8,128)(2,1)S(1)}, bf16[384,384]{0,1:T(8,128)(2,1)S(1)}, u32[]{:S(2)}, u32[]{:S(2)}) collective-permute-start(bf16[384,384]{0,1:T(8,128)(2,1)S(1)} %maximum_select_fusion.1), channel_id=1, source_target_pairs={{0,8},{4,12},{8,16},{12,20},{16,24},{20,28},{24,32},{28,36},{32,40... | collective-permute-start | bytes 884744 | tf_op jit(solution)/shard_map/ppermute | solution.py:146
  38.7 5.9 %collective-permute-start.5 = (f32[768]{0:T(1024)S(1)}, f32[768]{0:T(1024)S(1)}, u32[]{:S(2)}, u32[]{:S(2)}) collective-permute-start(f32[768]{0:T(1024)S(1)} %reduce), channel_id=1, source_target_pairs={{0,0},{1,32},{2,64},{3,96},{32,1},{33,33},{34,65},{35,97},{64,2},{... | collective-permute-start | bytes 9224 | tf_op jit(solution)/shard_map/ppermute | solution.py:170
  45.6 12.6 %collective-permute-done.3 = bf16[384,384]{0,1:T(8,128)(2,1)S(1)} collective-permute-done((bf16[384,384]{0,1:T(8,128)(2,1)S(1)}, bf16[384,384]{0,1:T(8,128)(2,1)S(1)}, u32[]{:S(2)}, u32[]{:S(2)}) %collective-permute-start.3) | collective-permute-done | bytes 294944 | tf_op jit(solution)/shard_map/ppermute | solution.py:147
  58.3 9.8 %collective-permute-start.4 = (bf16[192,768]{1,0:T(8,128)(2,1)S(1)}, bf16[192,768]{1,0:T(8,128)(2,1)S(1)}, u32[]{:S(2)}, u32[]{:S(2)}) collective-permute-start(bf16[192,768]{1,0:T(8,128)(2,1)S(1)} %bitcast.125), channel_id=1, source_target_pairs={{0,0},{1,32},{2,64},{3,96},{32,1},{33,33},{34,65},{35,97},{64,2},{... | collective-permute-start | bytes 884744 | tf_op jit(solution)/shard_map/ppermute | solution.py:169
  68.5 6.7 %collective-permute-done.4 = bf16[192,768]{1,0:T(8,128)(2,1)S(1)} collective-permute-done((bf16[192,768]{1,0:T(8,128)(2,1)S(1)}, bf16[192,768]{1,0:T(8,128)(2,1)S(1)}, u32[]{:S(2)}, u32[]{:S(2)}) %collective-permute-start.4) | collective-permute-done | bytes 294944 | tf_op jit(solution)/shard_map/ppermute | solution.py:169
  79.2 1.3 fusion.31
  80.5 3.4 %collective-permute-start.9 = (bf16[192,384]{1,0:T(8,128)(2,1)S(1)}, bf16[192,384]{1,0:T(8,128)(2,1)S(1)}, u32[]{:S(2)}, u32[]{:S(2)}) collective-permute-start(bf16[192,384]{1,0:T(8,128)(2,1)S(1)} %bitcast.124), channel_id=1, source_target_pairs={{0,4},{4,0},{8,12},{12,8},{16,20},{20,16},{24,28},{28,24},{32,36},... | collective-permute-start | bytes 442376 | tf_op jit(solution)/shard_map/ppermute | solution.py:199
  84.0 1.3 fusion.30
  85.3 2.3 %collective-permute-done.9 = bf16[192,384]{1,0:T(8,128)(2,1)S(1)} collective-permute-done((bf16[192,384]{1,0:T(8,128)(2,1)S(1)}, bf16[192,384]{1,0:T(8,128)(2,1)S(1)}, u32[]{:S(2)}, u32[]{:S(2)}) %collective-permute-start.9) | collective-permute-done | bytes 147488 | tf_op jit(solution)/shard_map/ppermute | solution.py:199
  87.7 1.1 broadcast_in_dim.38
  88.8 13.3 %all-to-all-start = ((bf16[4,192,768]{2,1,0:T(8,128)(2,1)}), bf16[4,192,768]{2,1,0:T(8,128)(2,1)S(1)}, u32[]{:S(2)}, u32[]{:S(2)}) async-start(bf16[4,192,768]{2,1,0:T(8,128)(2,1)} %broadcast_in_dim.38), calls=%async_computation | async-start | bytes 2359296 | tf_op jit(solution)/shard_map/all_to_all | solution.py:207
  102.1 13.2 %all-to-all-done = bf16[4,192,768]{2,1,0:T(8,128)(2,1)S(1)} async-done(((bf16[4,192,768]{2,1,0:T(8,128)(2,1)}), bf16[4,192,768]{2,1,0:T(8,128)(2,1)S(1)}, u32[]{:S(2)}, u32[]{:S(2)}) %all-to-all-start) | async-done | bytes 1179680 | tf_op jit(solution)/shard_map/all_to_all | solution.py:207
  115.9 0.6 fusion.26
  116.4 0.6 fusion.25
  117.8 1.9 %collective-permute-start.10 = (bf16[192,768]{1,0:T(8,128)(2,1)S(1)}, bf16[192,768]{1,0:T(8,128)(2,1)S(1)}, u32[]{:S(2)}, u32[]{:S(2)}) collective-permute-start(bf16[192,768]{1,0:T(8,128)(2,1)S(1)} %get-tuple-element.19), channel_id=1, source_target_pairs={{0,1},{1,2},{2,3},{3,0},{4,5},{5,6},{6,7},{7,4},{8,9},{9,10},{10,1... | collective-permute-start | bytes 884744 | tf_op jit(solution)/shard_map/ppermute | solution.py:223
  119.7 11.4 %collective-permute-start.12 = (bf16[192,768]{1,0:T(8,128)(2,1)S(1)}, bf16[192,768]{1,0:T(8,128)(2,1)S(1)}, u32[]{:S(2)}, u32[]{:S(2)}) collective-permute-start(bf16[192,768]{1,0:T(8,128)(2,1)S(1)} %get-tuple-element.20), channel_id=1, source_target_pairs={{0,3},{1,0},{2,1},{3,2},{4,7},{5,4},{6,5},{7,6},{8,11},{9,8},{10,9... | collective-permute-start | bytes 884744 | tf_op jit(solution)/shard_map/ppermute | solution.py:223
  131.1 2.5 %collective-permute-start.11 = (bf16[192,768]{1,0:T(8,128)(2,1)S(1)}, bf16[192,768]{1,0:T(8,128)(2,1)S(1)}, u32[]{:S(2)}, u32[]{:S(2)}) collective-permute-start(bf16[192,768]{1,0:T(8,128)(2,1)S(1)} %get-tuple-element.21), channel_id=1, source_target_pairs={{0,2},{1,3},{2,0},{3,1},{4,6},{5,7},{6,4},{7,5},{8,10},{9,11},{10,... | collective-permute-start | bytes 884744 | tf_op jit(solution)/shard_map/ppermute | solution.py:223
  133.6 3.5 %collective-permute-done.10 = bf16[192,768]{1,0:T(8,128)(2,1)S(1)} collective-permute-done((bf16[192,768]{1,0:T(8,128)(2,1)S(1)}, bf16[192,768]{1,0:T(8,128)(2,1)S(1)}, u32[]{:S(2)}, u32[]{:S(2)}) %collective-permute-start.10) | collective-permute-done | bytes 294944 | tf_op jit(solution)/shard_map/ppermute | solution.py:223
  137.1 2.8 %collective-permute-done.12 = bf16[192,768]{1,0:T(8,128)(2,1)S(1)} collective-permute-done((bf16[192,768]{1,0:T(8,128)(2,1)S(1)}, bf16[192,768]{1,0:T(8,128)(2,1)S(1)}, u32[]{:S(2)}, u32[]{:S(2)}) %collective-permute-start.12) | collective-permute-done | bytes 294944 | tf_op jit(solution)/shard_map/ppermute | solution.py:223
  139.9 13.4 %collective-permute-done.11 = bf16[192,768]{1,0:T(8,128)(2,1)S(1)} collective-permute-done((bf16[192,768]{1,0:T(8,128)(2,1)S(1)}, bf16[192,768]{1,0:T(8,128)(2,1)S(1)}, u32[]{:S(2)}, u32[]{:S(2)}) %collective-permute-start.11) | collective-permute-done | bytes 294944 | tf_op jit(solution)/shard_map/ppermute | solution.py:223
  153.5 2.4 %collective-permute-start.13 = (bf16[192,768]{1,0:T(8,128)(2,1)S(1)}, bf16[192,768]{1,0:T(8,128)(2,1)S(1)}, u32[]{:S(2)}, u32[]{:S(2)}) collective-permute-start(bf16[192,768]{1,0:T(8,128)(2,1)S(1)} %fusion.36), channel_id=1, source_target_pairs={{0,128},{1,160},{2,192},{3,224},{32,129},{33,161},{34,193},{35,225... | collective-permute-start | bytes 884744 | tf_op jit(solution)/shard_map/ppermute | solution.py:228
  155.9 18.4 %collective-permute-done.13 = bf16[192,768]{1,0:T(8,128)(2,1)S(1)} collective-permute-done((bf16[192,768]{1,0:T(8,128)(2,1)S(1)}, bf16[192,768]{1,0:T(8,128)(2,1)S(1)}, u32[]{:S(2)}, u32[]{:S(2)}) %collective-permute-start.13) | collective-permute-done | bytes 294944 | tf_op jit(solution)/shard_map/ppermute | solution.py:228
  174.4 0.7 copy.115
  (67 shorter events, 8.9 us)
Async XLA Ops:
  6.5 5.6 %copy-start.1 = (bf16[1,192,768]{2,1,0:T(8,128)(2,1)S(1)}, bf16[1,192,768]{2,1,0:T(8,128)(2,1)}, u32[]{:S(2)}) copy-start(bf16[1,192,768]{2,1,0:T(8,128)(2,1)} %param.7) | copy-start | bytes 884740
  6.5 68.7 %all-gather.3.cloned.1.call-start = ((), (), s32[]{:S(2)}) async-start(), calls=%async_computation.1 | async-start | bytes 1327104 | tf_op jit(solution)/shard_map/all_gather | solution.py:166
  7.3 10.9 %copy-start.2 = (s32[16,27]{1,0:T(8,128)S(1)}, s32[16,27]{1,0:T(8,128)}, u32[]{:S(2)}) copy-start(s32[16,27]{1,0:T(8,128)} %param.13) | copy-start | bytes 5188
  8.6 13.2 %collective-permute-start.6 = (bf16[192,384]{0,1:T(8,128)(2,1)S(1)}, bf16[192,384]{0,1:T(8,128)(2,1)S(1)}, u32[]{:S(2)}, u32[]{:S(2)}) collective-permute-start(bf16[192,384]{0,1:T(8,128)(2,1)S(1)} %bitcast.122), channel_id=1, source_target_pairs={{0,4},{4,0},{8,12},{12,8},{16,20},{20,16},{24,28},{28,24},{32,36},... | collective-permute-start | bytes 442376 | tf_op jit(solution)/shard_map/ppermute | solution.py:132
  12.2 26.5 %collective-permute-start = (bf16[192,384]{1,0:T(8,128)(2,1)S(1)}, bf16[192,384]{1,0:T(8,128)(2,1)S(1)}, u32[]{:S(2)}, u32[]{:S(2)}) collective-permute-start(bf16[192,384]{1,0:T(8,128)(2,1)S(1)} %get-tuple-element.26), channel_id=1, source_target_pairs={{0,4},{4,0},{8,12},{12,8},{16,20},{20,16},{24,28},{28,24},{32,36},... | collective-permute-start | bytes 442376 | tf_op jit(solution)/shard_map/ppermute | solution.py:132
  14.7 14.9 %collective-permute-start.1 = (bf16[192,384]{0,1:T(8,128)(2,1)S(1)}, bf16[192,384]{0,1:T(8,128)(2,1)S(1)}, u32[]{:S(2)}, u32[]{:S(2)}) collective-permute-start(bf16[192,384]{0,1:T(8,128)(2,1)S(1)} %bitcast.123), channel_id=1, source_target_pairs={{0,4},{4,0},{8,12},{12,8},{16,20},{20,16},{24,28},{28,24},{32,36},... | collective-permute-start | bytes 442376 | tf_op jit(solution)/shard_map/ppermute | solution.py:132
  18.7 3.1 %copy-start.3 = (f32[1,768]{1,0:T(1,128)S(1)}, f32[1,768]{1,0:T(1,128)}, u32[]{:S(2)}) copy-start(f32[1,768]{1,0:T(1,128)} %param.12) | copy-start | bytes 9220
  22.1 56.5 %collective-permute-start.8 = (bf16[384,384]{0,1:T(8,128)(2,1)S(1)}, bf16[384,384]{0,1:T(8,128)(2,1)S(1)}, u32[]{:S(2)}, u32[]{:S(2)}) collective-permute-start(bf16[384,384]{0,1:T(8,128)(2,1)S(1)} %maximum_select_fusion.3), channel_id=1, source_target_pairs={{8,0},{12,4},{16,8},{20,12},{24,16},{28,20},{32,24},{36,28},{40,32... | collective-permute-start | bytes 884744 | tf_op jit(solution)/shard_map/ppermute | solution.py:147
  27.6 51.6 %collective-permute-start.7 = (bf16[384,384]{0,1:T(8,128)(2,1)S(1)}, bf16[384,384]{0,1:T(8,128)(2,1)}, u32[]{:S(2)}, u32[]{:S(2)}) collective-permute-start(bf16[384,384]{0,1:T(8,128)(2,1)S(1)} %maximum_select_fusion.3), channel_id=1, source_target_pairs={{0,8},{4,12},{8,16},{12,20},{16,24},{20,28},{24,32},{28,36},{32,40... | collective-permute-start | bytes 884744 | tf_op jit(solution)/shard_map/ppermute | solution.py:146
  29.6 28.7 %copy-start.4 = (bf16[1,192,768]{2,1,0:T(8,128)(2,1)S(1)}, bf16[1,192,768]{2,1,0:T(8,128)(2,1)}, u32[]{:S(2)}) copy-start(bf16[1,192,768]{2,1,0:T(8,128)(2,1)} %param.10) | copy-start | bytes 884740
  29.8 28.4 %collective-permute-start.3 = (bf16[384,384]{0,1:T(8,128)(2,1)S(1)}, bf16[384,384]{0,1:T(8,128)(2,1)S(1)}, u32[]{:S(2)}, u32[]{:S(2)}) collective-permute-start(bf16[384,384]{0,1:T(8,128)(2,1)S(1)} %maximum_select_fusion.1), channel_id=1, source_target_pairs={{8,0},{12,4},{16,8},{20,12},{24,16},{28,20},{32,24},{36,28},{40,32... | collective-permute-start | bytes 884744 | tf_op jit(solution)/shard_map/ppermute | solution.py:147
  36.8 31.5 %collective-permute-start.2 = (bf16[384,384]{0,1:T(8,128)(2,1)S(1)}, bf16[384,384]{0,1:T(8,128)(2,1)S(1)}, u32[]{:S(2)}, u32[]{:S(2)}) collective-permute-start(bf16[384,384]{0,1:T(8,128)(2,1)S(1)} %maximum_select_fusion.1), channel_id=1, source_target_pairs={{0,8},{4,12},{8,16},{12,20},{16,24},{20,28},{24,32},{28,36},{32,40... | collective-permute-start | bytes 884744 | tf_op jit(solution)/shard_map/ppermute | solution.py:146
  38.7 29.8 %collective-permute-start.5 = (f32[768]{0:T(1024)S(1)}, f32[768]{0:T(1024)S(1)}, u32[]{:S(2)}, u32[]{:S(2)}) collective-permute-start(f32[768]{0:T(1024)S(1)} %reduce), channel_id=1, source_target_pairs={{0,0},{1,32},{2,64},{3,96},{32,1},{33,33},{34,65},{35,97},{64,2},{... | collective-permute-start | bytes 9224 | tf_op jit(solution)/shard_map/ppermute | solution.py:170
  58.3 16.9 %collective-permute-start.4 = (bf16[192,768]{1,0:T(8,128)(2,1)S(1)}, bf16[192,768]{1,0:T(8,128)(2,1)S(1)}, u32[]{:S(2)}, u32[]{:S(2)}) collective-permute-start(bf16[192,768]{1,0:T(8,128)(2,1)S(1)} %bitcast.125), channel_id=1, source_target_pairs={{0,0},{1,32},{2,64},{3,96},{32,1},{33,33},{34,65},{35,97},{64,2},{... | collective-permute-start | bytes 884744 | tf_op jit(solution)/shard_map/ppermute | solution.py:169
  80.5 7.0 %collective-permute-start.9 = (bf16[192,384]{1,0:T(8,128)(2,1)S(1)}, bf16[192,384]{1,0:T(8,128)(2,1)S(1)}, u32[]{:S(2)}, u32[]{:S(2)}) collective-permute-start(bf16[192,384]{1,0:T(8,128)(2,1)S(1)} %bitcast.124), channel_id=1, source_target_pairs={{0,4},{4,0},{8,12},{12,8},{16,20},{20,16},{24,28},{28,24},{32,36},... | collective-permute-start | bytes 442376 | tf_op jit(solution)/shard_map/ppermute | solution.py:199
  88.8 26.5 %copy-start = (bf16[1,768,768]{1,2,0:T(8,128)(2,1)S(1)}, bf16[1,768,768]{1,2,0:T(8,128)(2,1)}, u32[]{:S(2)}) copy-start(bf16[1,768,768]{1,2,0:T(8,128)(2,1)} %all-gather.3.cloned.1.call-done) | copy-start | bytes 3538948
  88.8 26.5 %all-to-all-start = ((bf16[4,192,768]{2,1,0:T(8,128)(2,1)}), bf16[4,192,768]{2,1,0:T(8,128)(2,1)S(1)}, u32[]{:S(2)}, u32[]{:S(2)}) async-start(bf16[4,192,768]{2,1,0:T(8,128)(2,1)} %broadcast_in_dim.38), calls=%async_computation | async-start | bytes 2359296 | tf_op jit(solution)/shard_map/all_to_all | solution.py:207
  117.8 19.3 %collective-permute-start.10 = (bf16[192,768]{1,0:T(8,128)(2,1)S(1)}, bf16[192,768]{1,0:T(8,128)(2,1)S(1)}, u32[]{:S(2)}, u32[]{:S(2)}) collective-permute-start(bf16[192,768]{1,0:T(8,128)(2,1)S(1)} %get-tuple-element.19), channel_id=1, source_target_pairs={{0,1},{1,2},{2,3},{3,0},{4,5},{5,6},{6,7},{7,4},{8,9},{9,10},{10,1... | collective-permute-start | bytes 884744 | tf_op jit(solution)/shard_map/ppermute | solution.py:223
  119.7 20.2 %collective-permute-start.12 = (bf16[192,768]{1,0:T(8,128)(2,1)S(1)}, bf16[192,768]{1,0:T(8,128)(2,1)S(1)}, u32[]{:S(2)}, u32[]{:S(2)}) collective-permute-start(bf16[192,768]{1,0:T(8,128)(2,1)S(1)} %get-tuple-element.20), channel_id=1, source_target_pairs={{0,3},{1,0},{2,1},{3,2},{4,7},{5,4},{6,5},{7,6},{8,11},{9,8},{10,9... | collective-permute-start | bytes 884744 | tf_op jit(solution)/shard_map/ppermute | solution.py:223
  131.1 22.3 %collective-permute-start.11 = (bf16[192,768]{1,0:T(8,128)(2,1)S(1)}, bf16[192,768]{1,0:T(8,128)(2,1)S(1)}, u32[]{:S(2)}, u32[]{:S(2)}) collective-permute-start(bf16[192,768]{1,0:T(8,128)(2,1)S(1)} %get-tuple-element.21), channel_id=1, source_target_pairs={{0,2},{1,3},{2,0},{3,1},{4,6},{5,7},{6,4},{7,5},{8,10},{9,11},{10,... | collective-permute-start | bytes 884744 | tf_op jit(solution)/shard_map/ppermute | solution.py:223
  153.5 20.8 %collective-permute-start.13 = (bf16[192,768]{1,0:T(8,128)(2,1)S(1)}, bf16[192,768]{1,0:T(8,128)(2,1)S(1)}, u32[]{:S(2)}, u32[]{:S(2)}) collective-permute-start(bf16[192,768]{1,0:T(8,128)(2,1)S(1)} %fusion.36), channel_id=1, source_target_pairs={{0,128},{1,160},{2,192},{3,224},{32,129},{33,161},{34,193},{35,225... | collective-permute-start | bytes 884744 | tf_op jit(solution)/shard_map/ppermute | solution.py:228
Sparse Core Ops, SparseCore 0:
  9.4 58.3 all-gather.2

commit v18 on v14

--- a/solution.py
+++ b/solution.py
@@ -168,8 +168,8 @@
     stream_in, gate_in, _ = lax.optimization_barrier((stream[0], gate_scale[0], tile_k))
     stream_block = lax.ppermute(stream_in, ("sx", "head"), swap)
     gate_block = lax.ppermute(gate_in, ("sx", "head"), swap)
-    weight_block, row_bound, stream_block, gate_block = lax.optimization_barrier(
-        (weight_block, row_bound, stream_block, gate_block)
+    row_bound, stream_block, gate_block = lax.optimization_barrier(
+        (row_bound, stream_block, gate_block)
     )
     weighted = jnp.zeros((tile_len, own_heads, HD), jnp.float32)
     summed = jnp.zeros((own_heads, tile_len), jnp.float32)
@@ -197,6 +197,7 @@
         jnp.concatenate([mine_rows, back], axis=1),
         jnp.concatenate([back, mine_rows], axis=1),
     )
+    weight_block, attended = lax.optimization_barrier((weight_block, attended))
     spread = jnp.broadcast_to(attended[None], (x_count,) + attended.shape)
     token_parts = lax.all_to_all(spread, "sx", 0, 0)
     terms = jnp.stack(

time: 163 us -> 165 us (1.012)
  the two profiles are of different devices: /device:TPU:153 before, /device:TPU:15 now
where the time goes in v18:
time: 165 us; the launch traced here: 164 us
  starting transfers between devices  72 us (44%)
  waiting for transfers between devices  57.8 us (35%)
  between operations  15.7 us (10%)
  local copies, waits for them, and re-layouts  7.14 us (4%)
  matrix products  6.21 us (4%)
  other arithmetic  5.45 us (3%)
    ppermute x1, starting transfers between devices, on_device(): handed = lax.ppermute(updated, ('section', 'sx', 'head'), hand)  20.4 us
    ppermute x3, waiting for transfers between devices, on_device(): mixed = mixed + lax.ppermute(outgoing, 'head', route).astype(jnp.float32)  17.4 us
    ppermute x2, waiting for transfers between devices, on_device(): lax.ppermute((tile_k, tile_v), seq, [(i, i + 2) for i in range(seq_count...  14.2 us
    ppermute x3, starting transfers between devices, on_device(): mixed = mixed + lax.ppermute(outgoing, 'head', route).astype(jnp.float32)  12.7 us
    ppermute x2, starting transfers between devices, on_device(): lax.ppermute((tile_k, tile_v), seq, [(i, i - 2) for i in range(2, seq_cou...  12.5 us
    all_to_all x1, waiting for transfers between devices, on_device(): token_parts = lax.all_to_all(spread, 'sx', 0, 0)  10.2 us
    ppermute x1, waiting for transfers between devices, on_device(): handed = lax.ppermute(updated, ('section', 'sx', 'head'), hand)  9.55 us
    ppermute x3, starting transfers between devices, on_device(): lax.ppermute((partner_half(queries), partner_half(own_keys), partner_half...  7.35 us
  transfers between devices with their start and end apart: 16, of which 9 were waited for; matrix products, arithmetic and copies ran while one was open for 7% of the time, Pallas kernels for 0%

profile of v18, /device:TPU:15, one launch (start us, length us, event | category | flops | bytes accessed | tf_op | source)
XLA Modules:
  0.0 164.4 jit_solution(8940069749521108482)
XLA Ops:
  6.5 1.1 constant_dynamic-slice_fusion.3
  7.6 2.1 %collective-permute-start.1 = (bf16[192,384]{1,0:T(8,128)(2,1)S(1)}, bf16[192,384]{1,0:T(8,128)(2,1)S(1)}, u32[]{:S(2)}, u32[]{:S(2)}) collective-permute-start(bf16[192,384]{1,0:T(8,128)(2,1)S(1)} %get-tuple-element.31), channel_id=1, source_target_pairs={{0,4},{4,0},{8,12},{12,8},{16,20},{20,16},{24,28},{28,24},{32,36},... | collective-permute-start | bytes 442376 | tf_op jit(solution)/shard_map/ppermute | solution.py:132
  9.7 1.0 dynamic-slice_bitcast_fusion.5
  10.7 3.2 %collective-permute-start = (bf16[192,384]{1,0:T(8,128)(2,1)S(1)}, bf16[192,384]{1,0:T(8,128)(2,1)S(1)}, u32[]{:S(2)}, u32[]{:S(2)}) collective-permute-start(bf16[192,384]{1,0:T(8,128)(2,1)S(1)} %get-tuple-element.28), channel_id=1, source_target_pairs={{0,4},{4,0},{8,12},{12,8},{16,20},{20,16},{24,28},{28,24},{32,36},... | collective-permute-start | bytes 442376 | tf_op jit(solution)/shard_map/ppermute | solution.py:132
  14.0 2.1 %collective-permute-start.6 = (bf16[192,384]{1,0:T(8,128)(2,1)S(1)}, bf16[192,384]{1,0:T(8,128)(2,1)S(1)}, u32[]{:S(2)}, u32[]{:S(2)}) collective-permute-start(bf16[192,384]{1,0:T(8,128)(2,1)S(1)} %get-tuple-element.33), channel_id=1, source_target_pairs={{0,4},{4,0},{8,12},{12,8},{16,20},{20,16},{24,28},{28,24},{32,36},... | collective-permute-start | bytes 442376 | tf_op jit(solution)/shard_map/ppermute | solution.py:132
  19.3 0.8 maximum_select_fusion.4
  20.1 6.1 %collective-permute-start.3 = (bf16[384,384]{1,0:T(8,128)(2,1)}, bf16[384,384]{1,0:T(8,128)(2,1)S(1)}, u32[]{:S(2)}, u32[]{:S(2)}) collective-permute-start(bf16[384,384]{1,0:T(8,128)(2,1)} %maximum_select_fusion.4), channel_id=1, source_target_pairs={{8,0},{12,4},{16,8},{20,12},{24,16},{28,20},{32,24},{36,28},{40,32... | collective-permute-start | bytes 884744 | tf_op jit(solution)/shard_map/ppermute | solution.py:147
  26.2 1.9 %collective-permute-start.2 = (bf16[384,384]{1,0:T(8,128)(2,1)}, bf16[384,384]{1,0:T(8,128)(2,1)S(1)}, u32[]{:S(2)}, u32[]{:S(2)}) collective-permute-start(bf16[384,384]{1,0:T(8,128)(2,1)} %maximum_select_fusion.4), channel_id=1, source_target_pairs={{0,8},{4,12},{8,16},{12,20},{16,24},{20,28},{24,32},{28,36},{32,40... | collective-permute-start | bytes 884744 | tf_op jit(solution)/shard_map/ppermute | solution.py:146
  28.2 0.8 maximum_select_fusion.5
  29.0 6.4 %collective-permute-start.8 = (bf16[384,384]{1,0:T(8,128)(2,1)}, bf16[384,384]{1,0:T(8,128)(2,1)S(1)}, u32[]{:S(2)}, u32[]{:S(2)}) collective-permute-start(bf16[384,384]{1,0:T(8,128)(2,1)} %maximum_select_fusion.5), channel_id=1, source_target_pairs={{8,0},{12,4},{16,8},{20,12},{24,16},{28,20},{32,24},{36,28},{40,32... | collective-permute-start | bytes 884744 | tf_op jit(solution)/shard_map/ppermute | solution.py:147
  35.3 1.9 %collective-permute-start.7 = (bf16[384,384]{1,0:T(8,128)(2,1)}, bf16[384,384]{1,0:T(8,128)(2,1)S(1)}, u32[]{:S(2)}, u32[]{:S(2)}) collective-permute-start(bf16[384,384]{1,0:T(8,128)(2,1)} %maximum_select_fusion.5), channel_id=1, source_target_pairs={{0,8},{4,12},{8,16},{12,20},{16,24},{20,28},{24,32},{28,36},{32,40... | collective-permute-start | bytes 884744 | tf_op jit(solution)/shard_map/ppermute | solution.py:146
  37.9 4.7 %collective-permute-start.4 = (bf16[192,768]{1,0:T(8,128)(2,1)}, bf16[192,768]{1,0:T(8,128)(2,1)}, u32[]{:S(2)}, u32[]{:S(2)}) collective-permute-start(bf16[192,768]{1,0:T(8,128)(2,1)} %bitcast.8), channel_id=1, source_target_pairs={{0,0},{1,32},{2,64},{3,96},{32,1},{33,33},{34,65},{35,97},{64,2},{... | collective-permute-start | bytes 884744 | tf_op jit(solution)/shard_map/ppermute | solution.py:169
  43.8 4.5 %collective-permute-start.5 = (f32[768]{0:T(1024)S(1)}, f32[768]{0:T(1024)S(1)}, u32[]{:S(2)}, u32[]{:S(2)}) collective-permute-start(f32[768]{0:T(1024)S(1)} %reduce), channel_id=1, source_target_pairs={{0,0},{1,32},{2,64},{3,96},{32,1},{33,33},{34,65},{35,97},{64,2},{... | collective-permute-start | bytes 9224 | tf_op jit(solution)/shard_map/ppermute | solution.py:170
  48.5 4.4 %collective-permute-done.2 = bf16[384,384]{1,0:T(8,128)(2,1)S(1)} collective-permute-done((bf16[384,384]{1,0:T(8,128)(2,1)}, bf16[384,384]{1,0:T(8,128)(2,1)S(1)}, u32[]{:S(2)}, u32[]{:S(2)}) %collective-permute-start.2) | collective-permute-done | bytes 294944 | tf_op jit(solution)/shard_map/ppermute | solution.py:146
  53.7 1.6 fusion.29
  55.4 2.0 %collective-permute-done.8 = bf16[384,384]{1,0:T(8,128)(2,1)S(1)} collective-permute-done((bf16[384,384]{1,0:T(8,128)(2,1)}, bf16[384,384]{1,0:T(8,128)(2,1)S(1)}, u32[]{:S(2)}, u32[]{:S(2)}) %collective-permute-start.8) | collective-permute-done | bytes 294944 | tf_op jit(solution)/shard_map/ppermute | solution.py:147
  57.6 9.8 %collective-permute-done.7 = bf16[384,384]{1,0:T(8,128)(2,1)S(1)} collective-permute-done((bf16[384,384]{1,0:T(8,128)(2,1)}, bf16[384,384]{1,0:T(8,128)(2,1)S(1)}, u32[]{:S(2)}, u32[]{:S(2)}) %collective-permute-start.7) | collective-permute-done | bytes 294944 | tf_op jit(solution)/shard_map/ppermute | solution.py:146
  69.6 0.8 copy-done.4
  71.0 1.9 %collective-permute-start.9 = (bf16[192,384]{0,1:T(8,128)(2,1)S(1)}, bf16[192,384]{0,1:T(8,128)(2,1)S(1)}, u32[]{:S(2)}, u32[]{:S(2)}) collective-permute-start(bf16[192,384]{0,1:T(8,128)(2,1)S(1)} %get-tuple-element.27), channel_id=1, source_target_pairs={{0,4},{4,0},{8,12},{12,8},{16,20},{20,16},{24,28},{28,24},{32,36},... | collective-permute-start | bytes 442376 | tf_op jit(solution)/shard_map/ppermute | solution.py:194
  72.9 4.5 %collective-permute-done.9 = bf16[192,384]{0,1:T(8,128)(2,1)S(1)} collective-permute-done((bf16[192,384]{0,1:T(8,128)(2,1)S(1)}, bf16[192,384]{0,1:T(8,128)(2,1)S(1)}, u32[]{:S(2)}, u32[]{:S(2)}) %collective-permute-start.9) | collective-permute-done | bytes 147488 | tf_op jit(solution)/shard_map/ppermute | solution.py:194
  77.7 1.1 broadcast_in_dim.31
  78.8 4.1 %all-to-all-start = ((bf16[4,192,768]{2,1,0:T(8,128)(2,1)}), bf16[4,192,768]{2,1,0:T(8,128)(2,1)S(1)}, u32[]{:S(2)}, u32[]{:S(2)}) async-start(bf16[4,192,768]{2,1,0:T(8,128)(2,1)} %broadcast_in_dim.31), calls=%async_computation | async-start | bytes 2359296 | tf_op jit(solution)/shard_map/all_to_all | solution.py:202
  82.9 10.2 %all-to-all-done = bf16[4,192,768]{2,1,0:T(8,128)(2,1)S(1)} async-done(((bf16[4,192,768]{2,1,0:T(8,128)(2,1)}), bf16[4,192,768]{2,1,0:T(8,128)(2,1)S(1)}, u32[]{:S(2)}, u32[]{:S(2)}) %all-to-all-start) | async-done | bytes 1179680 | tf_op jit(solution)/shard_map/all_to_all | solution.py:202
  95.6 4.5 %collective-permute-start.10 = (bf16[192,768]{1,0:T(8,128)(2,1)S(1)}, bf16[192,768]{1,0:T(8,128)(2,1)S(1)}, u32[]{:S(2)}, u32[]{:S(2)}) collective-permute-start(bf16[192,768]{1,0:T(8,128)(2,1)S(1)} %get-tuple-element.23), channel_id=1, source_target_pairs={{0,1},{1,2},{2,3},{3,0},{4,5},{5,6},{6,7},{7,4},{8,9},{9,10},{10,1... | collective-permute-start | bytes 884744 | tf_op jit(solution)/shard_map/ppermute | solution.py:218
  100.1 6.3 %collective-permute-start.11 = (bf16[192,768]{1,0:T(8,128)(2,1)S(1)}, bf16[192,768]{1,0:T(8,128)(2,1)S(1)}, u32[]{:S(2)}, u32[]{:S(2)}) collective-permute-start(bf16[192,768]{1,0:T(8,128)(2,1)S(1)} %get-tuple-element.25), channel_id=1, source_target_pairs={{0,2},{1,3},{2,0},{3,1},{4,6},{5,7},{6,4},{7,5},{8,10},{9,11},{10,... | collective-permute-start | bytes 884744 | tf_op jit(solution)/shard_map/ppermute | solution.py:218
  106.4 1.9 %collective-permute-start.12 = (bf16[192,768]{1,0:T(8,128)(2,1)S(1)}, bf16[192,768]{1,0:T(8,128)(2,1)S(1)}, u32[]{:S(2)}, u32[]{:S(2)}) collective-permute-start(bf16[192,768]{1,0:T(8,128)(2,1)S(1)} %get-tuple-element.24), channel_id=1, source_target_pairs={{0,3},{1,0},{2,1},{3,2},{4,7},{5,4},{6,5},{7,6},{8,11},{9,8},{10,9... | collective-permute-start | bytes 884744 | tf_op jit(solution)/shard_map/ppermute | solution.py:218
  108.4 15.6 %collective-permute-done.11 = bf16[192,768]{1,0:T(8,128)(2,1)S(1)} collective-permute-done((bf16[192,768]{1,0:T(8,128)(2,1)S(1)}, bf16[192,768]{1,0:T(8,128)(2,1)S(1)}, u32[]{:S(2)}, u32[]{:S(2)}) %collective-permute-start.11) | collective-permute-done | bytes 294944 | tf_op jit(solution)/shard_map/ppermute | solution.py:218
  124.0 1.7 %collective-permute-done.12 = bf16[192,768]{1,0:T(8,128)(2,1)S(1)} collective-permute-done((bf16[192,768]{1,0:T(8,128)(2,1)S(1)}, bf16[192,768]{1,0:T(8,128)(2,1)S(1)}, u32[]{:S(2)}, u32[]{:S(2)}) %collective-permute-start.12) | collective-permute-done | bytes 294944 | tf_op jit(solution)/shard_map/ppermute | solution.py:218
  125.7 1.2 fusion.17
  126.9 20.4 %collective-permute-start.13 = (bf16[192,768]{1,0:T(8,128)(2,1)S(1)}, bf16[192,768]{1,0:T(8,128)(2,1)S(1)}, u32[]{:S(2)}, u32[]{:S(2)}) collective-permute-start(bf16[192,768]{1,0:T(8,128)(2,1)S(1)} %fusion.17), channel_id=1, source_target_pairs={{0,128},{1,160},{2,192},{3,224},{32,129},{33,161},{34,193},{35,225... | collective-permute-start | bytes 884744 | tf_op jit(solution)/shard_map/ppermute | solution.py:223
  147.3 9.5 %collective-permute-done.13 = bf16[192,768]{1,0:T(8,128)(2,1)S(1)} collective-permute-done((bf16[192,768]{1,0:T(8,128)(2,1)S(1)}, bf16[192,768]{1,0:T(8,128)(2,1)S(1)}, u32[]{:S(2)}, u32[]{:S(2)}) %collective-permute-start.13) | collective-permute-done | bytes 294944 | tf_op jit(solution)/shard_map/ppermute | solution.py:223
  156.8 0.7 copy.118
  (59 shorter events, 9.8 us)
Async XLA Ops:
  6.5 7.4 %copy-start.1 = (bf16[1,192,768]{2,1,0:T(8,128)(2,1)S(1)}, bf16[1,192,768]{2,1,0:T(8,128)(2,1)}, u32[]{:S(2)}) copy-start(bf16[1,192,768]{2,1,0:T(8,128)(2,1)} %param.9) | copy-start | bytes 884740
  6.5 9.6 %copy-start.2 = (s32[16,27]{1,0:T(8,128)S(1)}, s32[16,27]{1,0:T(8,128)}, u32[]{:S(2)}) copy-start(s32[16,27]{1,0:T(8,128)} %param.13) | copy-start | bytes 5188
  6.5 71.0 %all-gather.3.cloned.1.call-start = ((), (), s32[]{:S(2)}) async-start(), calls=%async_computation.1 | async-start | bytes 1327104 | tf_op jit(solution)/shard_map/all_gather | solution.py:166
  7.6 11.6 %copy-start.3 = (f32[1,768]{1,0:T(1,128)S(1)}, f32[1,768]{1,0:T(1,128)}, u32[]{:S(2)}) copy-start(f32[1,768]{1,0:T(1,128)} %param.12) | copy-start | bytes 9220
  7.6 11.7 %collective-permute-start.1 = (bf16[192,384]{1,0:T(8,128)(2,1)S(1)}, bf16[192,384]{1,0:T(8,128)(2,1)S(1)}, u32[]{:S(2)}, u32[]{:S(2)}) collective-permute-start(bf16[192,384]{1,0:T(8,128)(2,1)S(1)} %get-tuple-element.31), channel_id=1, source_target_pairs={{0,4},{4,0},{8,12},{12,8},{16,20},{20,16},{24,28},{28,24},{32,36},... | collective-permute-start | bytes 442376 | tf_op jit(solution)/shard_map/ppermute | solution.py:132
  10.7 27.2 %collective-permute-start = (bf16[192,384]{1,0:T(8,128)(2,1)S(1)}, bf16[192,384]{1,0:T(8,128)(2,1)S(1)}, u32[]{:S(2)}, u32[]{:S(2)}) collective-permute-start(bf16[192,384]{1,0:T(8,128)(2,1)S(1)} %get-tuple-element.28), channel_id=1, source_target_pairs={{0,4},{4,0},{8,12},{12,8},{16,20},{20,16},{24,28},{28,24},{32,36},... | collective-permute-start | bytes 442376 | tf_op jit(solution)/shard_map/ppermute | solution.py:132
  14.0 14.2 %collective-permute-start.6 = (bf16[192,384]{1,0:T(8,128)(2,1)S(1)}, bf16[192,384]{1,0:T(8,128)(2,1)S(1)}, u32[]{:S(2)}, u32[]{:S(2)}) collective-permute-start(bf16[192,384]{1,0:T(8,128)(2,1)S(1)} %get-tuple-element.33), channel_id=1, source_target_pairs={{0,4},{4,0},{8,12},{12,8},{16,20},{20,16},{24,28},{28,24},{32,36},... | collective-permute-start | bytes 442376 | tf_op jit(solution)/shard_map/ppermute | solution.py:132
  20.1 23.7 %collective-permute-start.3 = (bf16[384,384]{1,0:T(8,128)(2,1)}, bf16[384,384]{1,0:T(8,128)(2,1)S(1)}, u32[]{:S(2)}, u32[]{:S(2)}) collective-permute-start(bf16[384,384]{1,0:T(8,128)(2,1)} %maximum_select_fusion.4), channel_id=1, source_target_pairs={{8,0},{12,4},{16,8},{20,12},{24,16},{28,20},{32,24},{36,28},{40,32... | collective-permute-start | bytes 884744 | tf_op jit(solution)/shard_map/ppermute | solution.py:147
  26.2 26.7 %collective-permute-start.2 = (bf16[384,384]{1,0:T(8,128)(2,1)}, bf16[384,384]{1,0:T(8,128)(2,1)S(1)}, u32[]{:S(2)}, u32[]{:S(2)}) collective-permute-start(bf16[384,384]{1,0:T(8,128)(2,1)} %maximum_select_fusion.4), channel_id=1, source_target_pairs={{0,8},{4,12},{8,16},{12,20},{16,24},{20,28},{24,32},{28,36},{32,40... | collective-permute-start | bytes 884744 | tf_op jit(solution)/shard_map/ppermute | solution.py:146
  29.0 28.4 %collective-permute-start.8 = (bf16[384,384]{1,0:T(8,128)(2,1)}, bf16[384,384]{1,0:T(8,128)(2,1)S(1)}, u32[]{:S(2)}, u32[]{:S(2)}) collective-permute-start(bf16[384,384]{1,0:T(8,128)(2,1)} %maximum_select_fusion.5), channel_id=1, source_target_pairs={{8,0},{12,4},{16,8},{20,12},{24,16},{28,20},{32,24},{36,28},{40,32... | collective-permute-start | bytes 884744 | tf_op jit(solution)/shard_map/ppermute | solution.py:147
  35.3 32.0 %collective-permute-start.7 = (bf16[384,384]{1,0:T(8,128)(2,1)}, bf16[384,384]{1,0:T(8,128)(2,1)S(1)}, u32[]{:S(2)}, u32[]{:S(2)}) collective-permute-start(bf16[384,384]{1,0:T(8,128)(2,1)} %maximum_select_fusion.5), channel_id=1, source_target_pairs={{0,8},{4,12},{8,16},{12,20},{16,24},{20,28},{24,32},{28,36},{32,40... | collective-permute-start | bytes 884744 | tf_op jit(solution)/shard_map/ppermute | solution.py:146
  37.9 15.7 %collective-permute-start.4 = (bf16[192,768]{1,0:T(8,128)(2,1)}, bf16[192,768]{1,0:T(8,128)(2,1)}, u32[]{:S(2)}, u32[]{:S(2)}) collective-permute-start(bf16[192,768]{1,0:T(8,128)(2,1)} %bitcast.8), channel_id=1, source_target_pairs={{0,0},{1,32},{2,64},{3,96},{32,1},{33,33},{34,65},{35,97},{64,2},{... | collective-permute-start | bytes 884744 | tf_op jit(solution)/shard_map/ppermute | solution.py:169
  43.8 9.9 %collective-permute-start.5 = (f32[768]{0:T(1024)S(1)}, f32[768]{0:T(1024)S(1)}, u32[]{:S(2)}, u32[]{:S(2)}) collective-permute-start(f32[768]{0:T(1024)S(1)} %reduce), channel_id=1, source_target_pairs={{0,0},{1,32},{2,64},{3,96},{32,1},{33,33},{34,65},{35,97},{64,2},{... | collective-permute-start | bytes 9224 | tf_op jit(solution)/shard_map/ppermute | solution.py:170
  69.2 1.2 copy-start.4
  71.0 6.4 %collective-permute-start.9 = (bf16[192,384]{0,1:T(8,128)(2,1)S(1)}, bf16[192,384]{0,1:T(8,128)(2,1)S(1)}, u32[]{:S(2)}, u32[]{:S(2)}) collective-permute-start(bf16[192,384]{0,1:T(8,128)(2,1)S(1)} %get-tuple-element.27), channel_id=1, source_target_pairs={{0,4},{4,0},{8,12},{12,8},{16,20},{20,16},{24,28},{28,24},{32,36},... | collective-permute-start | bytes 442376 | tf_op jit(solution)/shard_map/ppermute | solution.py:194
  78.8 14.3 %copy-start = (bf16[1,768,768]{1,2,0:T(8,128)(2,1)S(1)}, bf16[1,768,768]{1,2,0:T(8,128)(2,1)}, u32[]{:S(2)}) copy-start(bf16[1,768,768]{1,2,0:T(8,128)(2,1)} %all-gather.3.cloned.1.call-done) | copy-start | bytes 3538948
  78.8 14.3 %all-to-all-start = ((bf16[4,192,768]{2,1,0:T(8,128)(2,1)}), bf16[4,192,768]{2,1,0:T(8,128)(2,1)S(1)}, u32[]{:S(2)}, u32[]{:S(2)}) async-start(bf16[4,192,768]{2,1,0:T(8,128)(2,1)} %broadcast_in_dim.31), calls=%async_computation | async-start | bytes 2359296 | tf_op jit(solution)/shard_map/all_to_all | solution.py:202
  95.6 12.8 %collective-permute-start.10 = (bf16[192,768]{1,0:T(8,128)(2,1)S(1)}, bf16[192,768]{1,0:T(8,128)(2,1)S(1)}, u32[]{:S(2)}, u32[]{:S(2)}) collective-permute-start(bf16[192,768]{1,0:T(8,128)(2,1)S(1)} %get-tuple-element.23), channel_id=1, source_target_pairs={{0,1},{1,2},{2,3},{3,0},{4,5},{5,6},{6,7},{7,4},{8,9},{9,10},{10,1... | collective-permute-start | bytes 884744 | tf_op jit(solution)/shard_map/ppermute | solution.py:218
  100.1 23.9 %collective-permute-start.11 = (bf16[192,768]{1,0:T(8,128)(2,1)S(1)}, bf16[192,768]{1,0:T(8,128)(2,1)S(1)}, u32[]{:S(2)}, u32[]{:S(2)}) collective-permute-start(bf16[192,768]{1,0:T(8,128)(2,1)S(1)} %get-tuple-element.25), channel_id=1, source_target_pairs={{0,2},{1,3},{2,0},{3,1},{4,6},{5,7},{6,4},{7,5},{8,10},{9,11},{10,... | collective-permute-start | bytes 884744 | tf_op jit(solution)/shard_map/ppermute | solution.py:218
  106.4 19.3 %collective-permute-start.12 = (bf16[192,768]{1,0:T(8,128)(2,1)S(1)}, bf16[192,768]{1,0:T(8,128)(2,1)S(1)}, u32[]{:S(2)}, u32[]{:S(2)}) collective-permute-start(bf16[192,768]{1,0:T(8,128)(2,1)S(1)} %get-tuple-element.24), channel_id=1, source_target_pairs={{0,3},{1,0},{2,1},{3,2},{4,7},{5,4},{6,5},{7,6},{8,11},{9,8},{10,9... | collective-permute-start | bytes 884744 | tf_op jit(solution)/shard_map/ppermute | solution.py:218
  126.9 29.9 %collective-permute-start.13 = (bf16[192,768]{1,0:T(8,128)(2,1)S(1)}, bf16[192,768]{1,0:T(8,128)(2,1)S(1)}, u32[]{:S(2)}, u32[]{:S(2)}) collective-permute-start(bf16[192,768]{1,0:T(8,128)(2,1)S(1)} %fusion.17), channel_id=1, source_target_pairs={{0,128},{1,160},{2,192},{3,224},{32,129},{33,161},{34,193},{35,225... | collective-permute-start | bytes 884744 | tf_op jit(solution)/shard_map/ppermute | solution.py:223
Sparse Core Ops, SparseCore 0:
  16.2 51.3 all-gather.2

commit v19 on v14

--- a/solution.py
+++ b/solution.py
@@ -199,22 +199,22 @@
     )
     spread = jnp.broadcast_to(attended[None], (x_count,) + attended.shape)
     token_parts = lax.all_to_all(spread, "sx", 0, 0)
-    terms = jnp.stack(
-        [
-            jnp.dot(token_parts[j], weight_block, preferred_element_type=jnp.float32).astype(
-                jnp.bfloat16
-            )
-            for j in range(x_count)
-        ]
-    )
     group_index = lax.axis_index("head")
-    mixed = lax.dynamic_index_in_dim(terms, group_index, 0, keepdims=False).astype(jnp.float32)
+
+    def term_for(slab_x):
+        part = lax.dynamic_index_in_dim(token_parts, slab_x, 0, keepdims=False)
+        return jnp.dot(part, weight_block, preferred_element_type=jnp.float32).astype(
+            jnp.bfloat16
+        )
+
+    received = []
     for shift in range(1, head_groups):
-        outgoing = lax.dynamic_index_in_dim(
-            terms, (group_index + shift) % head_groups, 0, keepdims=False
-        )
+        outgoing = term_for((group_index + shift) % head_groups)
         route = [(g, (g + shift) % head_groups) for g in range(head_groups)]
-        mixed = mixed + lax.ppermute(outgoing, "head", route).astype(jnp.float32)
+        received.append(lax.ppermute(outgoing, "head", route))
+    mixed = term_for(group_index).astype(jnp.float32)
+    for term in received:
+        mixed = mixed + term.astype(jnp.float32)
     updated = (stream_block.astype(jnp.float32) + gate_block[None, :] * mixed).astype(jnp.bfloat16)
     hand = linear_pairs(
         (sections, x_count, head_groups), lambda s, a, b: ((s + 1) % sections, b, a)

time: 163 us -> 162 us (level)
  waiting for transfers between devices: 83.6 us -> 80.3 us
  matrix products: 5.25 us -> 7.39 us
    ppermute x3, waiting for transfers between devices: 22.5 us -> 20.2 us  [on_device(): received.append(lax.ppermute(outgoing, 'head', route))]
    dot_general x4, matrix products: 2.22 us -> 4.39 us  [term_for(): jnp.dot(part, weight_block, preferred_element_type=jnp.float32)]
  transfers between devices with their start and end apart: 16 -> 16, of which waited for: 9 -> 9; matrix products, arithmetic and copies ran while one was open for 5% -> 7% of each run, Pallas kernels for 0% -> 0%
where the time goes in v19:
time: 162 us; the launch traced here: 161 us
  waiting for transfers between devices  80.3 us (50%)
  starting transfers between devices  46.2 us (29%)
  between operations  15.8 us (10%)
  matrix products  7.39 us (5%)
  local copies, waits for them, and re-layouts  7.23 us (4%)
  other arithmetic  4.11 us (3%)
    ppermute x3, waiting for transfers between devices, on_device(): received.append(lax.ppermute(outgoing, 'head', route))  20.2 us
    ppermute x1, waiting for transfers between devices, on_device(): handed = lax.ppermute(updated, ('section', 'sx', 'head'), hand)  17.9 us
    all_to_all x1, waiting for transfers between devices, on_device(): token_parts = lax.all_to_all(spread, 'sx', 0, 0)  14.5 us
    ppermute x2, starting transfers between devices, on_device(): lax.ppermute((tile_k, tile_v), seq, [(i, i + 2) for i in range(seq_count...  10.9 us
    ppermute x3, starting transfers between devices, on_device(): received.append(lax.ppermute(outgoing, 'head', route))  9.97 us
    ppermute x2, waiting for transfers between devices, on_device(): lax.ppermute((tile_k, tile_v), seq, [(i, i + 2) for i in range(seq_count...  9.49 us
    ppermute x3, starting transfers between devices, on_device(): lax.ppermute((partner_half(queries), partner_half(own_keys), partner_half...  7.35 us
    all_gather x1, waiting for transfers between devices, on_device(): weight_block = lax.all_gather(out_weight[0], 'sy', axis=1, tiled=True)  7.23 us
  transfers between devices with their start and end apart: 16, of which 9 were waited for; matrix products, arithmetic and copies ran while one was open for 7% of the time, Pallas kernels for 0%

profile of v19, /device:TPU:153, one launch (start us, length us, event | category | flops | bytes accessed | tf_op | source)
XLA Modules:
  0.0 161.0 jit_solution(1921376385303755416)
XLA Ops:
  7.3 1.0 dynamic-slice_bitcast_fusion.2
  8.3 2.1 %collective-permute-start = (bf16[192,384]{1,0:T(8,128)(2,1)S(1)}, bf16[192,384]{1,0:T(8,128)(2,1)S(1)}, u32[]{:S(2)}, u32[]{:S(2)}) collective-permute-start(bf16[192,384]{1,0:T(8,128)(2,1)S(1)} %get-tuple-element.27), channel_id=1, source_target_pairs={{0,4},{4,0},{8,12},{12,8},{16,20},{20,16},{24,28},{28,24},{32,36},... | collective-permute-start | bytes 442376 | tf_op jit(solution)/shard_map/ppermute | solution.py:132
  10.4 1.0 constant_dynamic-slice_fusion.3
  11.4 3.2 %collective-permute-start.1 = (bf16[192,384]{1,0:T(8,128)(2,1)S(1)}, bf16[192,384]{1,0:T(8,128)(2,1)S(1)}, u32[]{:S(2)}, u32[]{:S(2)}) collective-permute-start(bf16[192,384]{1,0:T(8,128)(2,1)S(1)} %get-tuple-element.26), channel_id=1, source_target_pairs={{0,4},{4,0},{8,12},{12,8},{16,20},{20,16},{24,28},{28,24},{32,36},... | collective-permute-start | bytes 442376 | tf_op jit(solution)/shard_map/ppermute | solution.py:132
  14.7 2.1 %collective-permute-start.6 = (bf16[192,384]{1,0:T(8,128)(2,1)S(1)}, bf16[192,384]{1,0:T(8,128)(2,1)S(1)}, u32[]{:S(2)}, u32[]{:S(2)}) collective-permute-start(bf16[192,384]{1,0:T(8,128)(2,1)S(1)} %get-tuple-element.24), channel_id=1, source_target_pairs={{0,4},{4,0},{8,12},{12,8},{16,20},{20,16},{24,28},{28,24},{32,36},... | collective-permute-start | bytes 442376 | tf_op jit(solution)/shard_map/ppermute | solution.py:132
  20.0 0.8 maximum_select_fusion.4
  20.8 5.4 %collective-permute-start.2 = (bf16[384,384]{1,0:T(8,128)(2,1)}, bf16[384,384]{1,0:T(8,128)(2,1)}, u32[]{:S(2)}, u32[]{:S(2)}) collective-permute-start(bf16[384,384]{1,0:T(8,128)(2,1)} %maximum_select_fusion.4), channel_id=1, source_target_pairs={{0,8},{4,12},{8,16},{12,20},{16,24},{20,28},{24,32},{28,36},{32,40... | collective-permute-start | bytes 884744 | tf_op jit(solution)/shard_map/ppermute | solution.py:146
  26.2 1.9 %collective-permute-start.3 = (bf16[384,384]{1,0:T(8,128)(2,1)}, bf16[384,384]{1,0:T(8,128)(2,1)S(1)}, u32[]{:S(2)}, u32[]{:S(2)}) collective-permute-start(bf16[384,384]{1,0:T(8,128)(2,1)} %maximum_select_fusion.4), channel_id=1, source_target_pairs={{8,0},{12,4},{16,8},{20,12},{24,16},{28,20},{32,24},{36,28},{40,32... | collective-permute-start | bytes 884744 | tf_op jit(solution)/shard_map/ppermute | solution.py:147
  29.0 1.9 %collective-permute-start.8 = (bf16[384,384]{1,0:T(8,128)(2,1)}, bf16[384,384]{1,0:T(8,128)(2,1)S(1)}, u32[]{:S(2)}, u32[]{:S(2)}) collective-permute-start(bf16[384,384]{1,0:T(8,128)(2,1)} %maximum_select_fusion.5), channel_id=1, source_target_pairs={{8,0},{12,4},{16,8},{20,12},{24,16},{28,20},{32,24},{36,28},{40,32... | collective-permute-start | bytes 884744 | tf_op jit(solution)/shard_map/ppermute | solution.py:147
  30.9 5.5 %collective-permute-start.7 = (bf16[384,384]{1,0:T(8,128)(2,1)}, bf16[384,384]{1,0:T(8,128)(2,1)S(1)}, u32[]{:S(2)}, u32[]{:S(2)}) collective-permute-start(bf16[384,384]{1,0:T(8,128)(2,1)} %maximum_select_fusion.5), channel_id=1, source_target_pairs={{0,8},{4,12},{8,16},{12,20},{16,24},{20,28},{24,32},{28,36},{32,40... | collective-permute-start | bytes 884744 | tf_op jit(solution)/shard_map/ppermute | solution.py:146
  37.1 2.8 %collective-permute-start.4 = (bf16[192,768]{1,0:T(8,128)(2,1)}, bf16[192,768]{1,0:T(8,128)(2,1)S(1)}, u32[]{:S(2)}, u32[]{:S(2)}) collective-permute-start(bf16[192,768]{1,0:T(8,128)(2,1)} %bitcast.68), channel_id=1, source_target_pairs={{0,0},{1,32},{2,64},{3,96},{32,1},{33,33},{34,65},{35,97},{64,2},{... | collective-permute-start | bytes 884744 | tf_op jit(solution)/shard_map/ppermute | solution.py:169
  41.0 3.3 %collective-permute-done.2 = bf16[384,384]{1,0:T(8,128)(2,1)} collective-permute-done((bf16[384,384]{1,0:T(8,128)(2,1)}, bf16[384,384]{1,0:T(8,128)(2,1)}, u32[]{:S(2)}, u32[]{:S(2)}) %collective-permute-start.2) | collective-permute-done | bytes 294944 | tf_op jit(solution)/shard_map/ppermute | solution.py:146
  44.3 2.4 %collective-permute-start.5 = (f32[768]{0:T(1024)S(1)}, f32[768]{0:T(1024)S(1)}, u32[]{:S(2)}, u32[]{:S(2)}) collective-permute-start(f32[768]{0:T(1024)S(1)} %reduce), channel_id=1, source_target_pairs={{0,0},{1,32},{2,64},{3,96},{32,1},{33,33},{34,65},{35,97},{64,2},{... | collective-permute-start | bytes 9224 | tf_op jit(solution)/shard_map/ppermute | solution.py:170
  46.8 1.2 copy.77
  48.7 5.0 %collective-permute-done.8 = bf16[384,384]{1,0:T(8,128)(2,1)S(1)} collective-permute-done((bf16[384,384]{1,0:T(8,128)(2,1)}, bf16[384,384]{1,0:T(8,128)(2,1)S(1)}, u32[]{:S(2)}, u32[]{:S(2)}) %collective-permute-start.8) | collective-permute-done | bytes 294944 | tf_op jit(solution)/shard_map/ppermute | solution.py:147
  53.9 6.1 %collective-permute-done.7 = bf16[384,384]{1,0:T(8,128)(2,1)S(1)} collective-permute-done((bf16[384,384]{1,0:T(8,128)(2,1)}, bf16[384,384]{1,0:T(8,128)(2,1)S(1)}, u32[]{:S(2)}, u32[]{:S(2)}) %collective-permute-start.7) | collective-permute-done | bytes 294944 | tf_op jit(solution)/shard_map/ppermute | solution.py:146
  60.3 7.2 %all-gather.3.cloned.1.call-done = bf16[1,768,768]{1,2,0:T(8,128)(2,1)} async-done(((bf16[1,768,96]{1,2,0:T(8,128)(2,1)}), bf16[1,768,768]{1,2,0:T(8,128)(2,1)}) %all-gather.3.cloned.1.call-update) | async-done | bytes 1179664 | tf_op jit(solution)/shard_map/all_gather | solution.py:166
  70.8 1.9 %collective-permute-start.9 = (bf16[192,384]{0,1:T(8,128)(2,1)S(1)}, bf16[192,384]{0,1:T(8,128)(2,1)S(1)}, u32[]{:S(2)}, u32[]{:S(2)}) collective-permute-start(bf16[192,384]{0,1:T(8,128)(2,1)S(1)} %get-tuple-element.22), channel_id=1, source_target_pairs={{0,4},{4,0},{8,12},{12,8},{16,20},{20,16},{24,28},{28,24},{32,36},... | collective-permute-start | bytes 442376 | tf_op jit(solution)/shard_map/ppermute | solution.py:194
  72.8 5.2 %collective-permute-done.9 = bf16[192,384]{0,1:T(8,128)(2,1)S(1)} collective-permute-done((bf16[192,384]{0,1:T(8,128)(2,1)S(1)}, bf16[192,384]{0,1:T(8,128)(2,1)S(1)}, u32[]{:S(2)}, u32[]{:S(2)}) %collective-permute-start.9) | collective-permute-done | bytes 147488 | tf_op jit(solution)/shard_map/ppermute | solution.py:194
  78.3 1.1 broadcast_in_dim.31
  79.4 3.9 %all-to-all-start = ((bf16[4,192,768]{2,1,0:T(8,128)(2,1)}), bf16[4,192,768]{2,1,0:T(8,128)(2,1)S(1)}, u32[]{:S(2)}, u32[]{:S(2)}) async-start(bf16[4,192,768]{2,1,0:T(8,128)(2,1)} %broadcast_in_dim.31), calls=%async_computation | async-start | bytes 2359296 | tf_op jit(solution)/shard_map/all_to_all | solution.py:201
  83.3 14.5 %all-to-all-done = bf16[4,192,768]{2,1,0:T(8,128)(2,1)S(1)} async-done(((bf16[4,192,768]{2,1,0:T(8,128)(2,1)}), bf16[4,192,768]{2,1,0:T(8,128)(2,1)S(1)}, u32[]{:S(2)}, u32[]{:S(2)}) %all-to-all-start) | async-done | bytes 1179680 | tf_op jit(solution)/shard_map/all_to_all | solution.py:201
  97.8 1.3 convolution_convert_fusion
  99.1 1.9 %collective-permute-start.12 = (bf16[192,768]{1,0:T(8,128)(2,1)}, bf16[192,768]{1,0:T(8,128)(2,1)S(1)}, u32[]{:S(2)}, u32[]{:S(2)}) collective-permute-start(bf16[192,768]{1,0:T(8,128)(2,1)} %convolution_convert_fusion), channel_id=1, source_target_pairs={{0,3},{1,0},{2,1},{3,2},{4,7},{5,4},{6,5},{7,6},{8,11},{9,8},{10,9... | collective-permute-start | bytes 884744 | tf_op jit(solution)/shard_map/ppermute | solution.py:214
  101.0 1.3 convolution_convert_fusion.1
  102.3 6.2 %collective-permute-start.11 = (bf16[192,768]{1,0:T(8,128)(2,1)}, bf16[192,768]{1,0:T(8,128)(2,1)S(1)}, u32[]{:S(2)}, u32[]{:S(2)}) collective-permute-start(bf16[192,768]{1,0:T(8,128)(2,1)} %convolution_convert_fusion.1), channel_id=1, source_target_pairs={{0,2},{1,3},{2,0},{3,1},{4,6},{5,7},{6,4},{7,5},{8,10},{9,11},{10,... | collective-permute-start | bytes 884744 | tf_op jit(solution)/shard_map/ppermute | solution.py:214
  108.4 1.3 convolution_convert_fusion.2
  109.7 1.9 %collective-permute-start.10 = (bf16[192,768]{1,0:T(8,128)(2,1)}, bf16[192,768]{1,0:T(8,128)(2,1)S(1)}, u32[]{:S(2)}, u32[]{:S(2)}) collective-permute-start(bf16[192,768]{1,0:T(8,128)(2,1)} %convolution_convert_fusion.2), channel_id=1, source_target_pairs={{0,1},{1,2},{2,3},{3,0},{4,5},{5,6},{6,7},{7,4},{8,9},{9,10},{10,1... | collective-permute-start | bytes 884744 | tf_op jit(solution)/shard_map/ppermute | solution.py:214
  111.6 13.7 %collective-permute-done.11 = bf16[192,768]{1,0:T(8,128)(2,1)S(1)} collective-permute-done((bf16[192,768]{1,0:T(8,128)(2,1)}, bf16[192,768]{1,0:T(8,128)(2,1)S(1)}, u32[]{:S(2)}, u32[]{:S(2)}) %collective-permute-start.11) | collective-permute-done | bytes 294944 | tf_op jit(solution)/shard_map/ppermute | solution.py:214
  125.3 6.6 %collective-permute-done.10 = bf16[192,768]{1,0:T(8,128)(2,1)S(1)} collective-permute-done((bf16[192,768]{1,0:T(8,128)(2,1)}, bf16[192,768]{1,0:T(8,128)(2,1)S(1)}, u32[]{:S(2)}, u32[]{:S(2)}) %collective-permute-start.10) | collective-permute-done | bytes 294944 | tf_op jit(solution)/shard_map/ppermute | solution.py:214
  132.5 3.1 %collective-permute-start.13 = (bf16[192,768]{1,0:T(8,128)(2,1)S(1)}, bf16[192,768]{1,0:T(8,128)(2,1)S(1)}, u32[]{:S(2)}, u32[]{:S(2)}) collective-permute-start(bf16[192,768]{1,0:T(8,128)(2,1)S(1)} %add_convert_fusion), channel_id=1, source_target_pairs={{0,128},{1,160},{2,192},{3,224},{32,129},{33,161},{34,193},{35,225... | collective-permute-start | bytes 884744 | tf_op jit(solution)/shard_map/ppermute | solution.py:222
  135.5 17.9 %collective-permute-done.13 = bf16[192,768]{1,0:T(8,128)(2,1)S(1)} collective-permute-done((bf16[192,768]{1,0:T(8,128)(2,1)S(1)}, bf16[192,768]{1,0:T(8,128)(2,1)S(1)}, u32[]{:S(2)}, u32[]{:S(2)}) %collective-permute-start.13) | collective-permute-done | bytes 294944 | tf_op jit(solution)/shard_map/ppermute | solution.py:222
  (54 shorter events, 10.5 us)
Async XLA Ops:
  6.5 8.1 %copy-start.1 = (bf16[1,192,768]{2,1,0:T(8,128)(2,1)S(1)}, bf16[1,192,768]{2,1,0:T(8,128)(2,1)}, u32[]{:S(2)}) copy-start(bf16[1,192,768]{2,1,0:T(8,128)(2,1)} %param.9) | copy-start | bytes 884740
  6.5 10.3 %copy-start.2 = (s32[16,27]{1,0:T(8,128)S(1)}, s32[16,27]{1,0:T(8,128)}, u32[]{:S(2)}) copy-start(s32[16,27]{1,0:T(8,128)} %param.13) | copy-start | bytes 5188
  6.5 61.0 %all-gather.3.cloned.1.call-start = ((), (), s32[]{:S(2)}) async-start(), calls=%async_computation.1 | async-start | bytes 1327104 | tf_op jit(solution)/shard_map/all_gather | solution.py:166
  8.3 11.6 %copy-start.3 = (f32[1,768]{1,0:T(1,128)S(1)}, f32[1,768]{1,0:T(1,128)}, u32[]{:S(2)}) copy-start(f32[1,768]{1,0:T(1,128)} %param.12) | copy-start | bytes 9220
  8.3 28.8 %collective-permute-start = (bf16[192,384]{1,0:T(8,128)(2,1)S(1)}, bf16[192,384]{1,0:T(8,128)(2,1)S(1)}, u32[]{:S(2)}, u32[]{:S(2)}) collective-permute-start(bf16[192,384]{1,0:T(8,128)(2,1)S(1)} %get-tuple-element.27), channel_id=1, source_target_pairs={{0,4},{4,0},{8,12},{12,8},{16,20},{20,16},{24,28},{28,24},{32,36},... | collective-permute-start | bytes 442376 | tf_op jit(solution)/shard_map/ppermute | solution.py:132
  11.4 8.6 %collective-permute-start.1 = (bf16[192,384]{1,0:T(8,128)(2,1)S(1)}, bf16[192,384]{1,0:T(8,128)(2,1)S(1)}, u32[]{:S(2)}, u32[]{:S(2)}) collective-permute-start(bf16[192,384]{1,0:T(8,128)(2,1)S(1)} %get-tuple-element.26), channel_id=1, source_target_pairs={{0,4},{4,0},{8,12},{12,8},{16,20},{20,16},{24,28},{28,24},{32,36},... | collective-permute-start | bytes 442376 | tf_op jit(solution)/shard_map/ppermute | solution.py:132
  14.7 13.5 %collective-permute-start.6 = (bf16[192,384]{1,0:T(8,128)(2,1)S(1)}, bf16[192,384]{1,0:T(8,128)(2,1)S(1)}, u32[]{:S(2)}, u32[]{:S(2)}) collective-permute-start(bf16[192,384]{1,0:T(8,128)(2,1)S(1)} %get-tuple-element.24), channel_id=1, source_target_pairs={{0,4},{4,0},{8,12},{12,8},{16,20},{20,16},{24,28},{28,24},{32,36},... | collective-permute-start | bytes 442376 | tf_op jit(solution)/shard_map/ppermute | solution.py:132
  20.8 23.5 %collective-permute-start.2 = (bf16[384,384]{1,0:T(8,128)(2,1)}, bf16[384,384]{1,0:T(8,128)(2,1)}, u32[]{:S(2)}, u32[]{:S(2)}) collective-permute-start(bf16[384,384]{1,0:T(8,128)(2,1)} %maximum_select_fusion.4), channel_id=1, source_target_pairs={{0,8},{4,12},{8,16},{12,20},{16,24},{20,28},{24,32},{28,36},{32,40... | collective-permute-start | bytes 884744 | tf_op jit(solution)/shard_map/ppermute | solution.py:146
  26.2 21.7 %collective-permute-start.3 = (bf16[384,384]{1,0:T(8,128)(2,1)}, bf16[384,384]{1,0:T(8,128)(2,1)S(1)}, u32[]{:S(2)}, u32[]{:S(2)}) collective-permute-start(bf16[384,384]{1,0:T(8,128)(2,1)} %maximum_select_fusion.4), channel_id=1, source_target_pairs={{8,0},{12,4},{16,8},{20,12},{24,16},{28,20},{32,24},{36,28},{40,32... | collective-permute-start | bytes 884744 | tf_op jit(solution)/shard_map/ppermute | solution.py:147
  29.0 24.7 %collective-permute-start.8 = (bf16[384,384]{1,0:T(8,128)(2,1)}, bf16[384,384]{1,0:T(8,128)(2,1)S(1)}, u32[]{:S(2)}, u32[]{:S(2)}) collective-permute-start(bf16[384,384]{1,0:T(8,128)(2,1)} %maximum_select_fusion.5), channel_id=1, source_target_pairs={{8,0},{12,4},{16,8},{20,12},{24,16},{28,20},{32,24},{36,28},{40,32... | collective-permute-start | bytes 884744 | tf_op jit(solution)/shard_map/ppermute | solution.py:147
  30.9 29.2 %collective-permute-start.7 = (bf16[384,384]{1,0:T(8,128)(2,1)}, bf16[384,384]{1,0:T(8,128)(2,1)S(1)}, u32[]{:S(2)}, u32[]{:S(2)}) collective-permute-start(bf16[384,384]{1,0:T(8,128)(2,1)} %maximum_select_fusion.5), channel_id=1, source_target_pairs={{0,8},{4,12},{8,16},{12,20},{16,24},{20,28},{24,32},{28,36},{32,40... | collective-permute-start | bytes 884744 | tf_op jit(solution)/shard_map/ppermute | solution.py:146
  37.1 23.2 %collective-permute-start.4 = (bf16[192,768]{1,0:T(8,128)(2,1)}, bf16[192,768]{1,0:T(8,128)(2,1)S(1)}, u32[]{:S(2)}, u32[]{:S(2)}) collective-permute-start(bf16[192,768]{1,0:T(8,128)(2,1)} %bitcast.68), channel_id=1, source_target_pairs={{0,0},{1,32},{2,64},{3,96},{32,1},{33,33},{34,65},{35,97},{64,2},{... | collective-permute-start | bytes 884744 | tf_op jit(solution)/shard_map/ppermute | solution.py:169
  44.3 16.0 %collective-permute-start.5 = (f32[768]{0:T(1024)S(1)}, f32[768]{0:T(1024)S(1)}, u32[]{:S(2)}, u32[]{:S(2)}) collective-permute-start(f32[768]{0:T(1024)S(1)} %reduce), channel_id=1, source_target_pairs={{0,0},{1,32},{2,64},{3,96},{32,1},{33,33},{34,65},{35,97},{64,2},{... | collective-permute-start | bytes 9224 | tf_op jit(solution)/shard_map/ppermute | solution.py:170
  70.8 7.2 %collective-permute-start.9 = (bf16[192,384]{0,1:T(8,128)(2,1)S(1)}, bf16[192,384]{0,1:T(8,128)(2,1)S(1)}, u32[]{:S(2)}, u32[]{:S(2)}) collective-permute-start(bf16[192,384]{0,1:T(8,128)(2,1)S(1)} %get-tuple-element.22), channel_id=1, source_target_pairs={{0,4},{4,0},{8,12},{12,8},{16,20},{20,16},{24,28},{28,24},{32,36},... | collective-permute-start | bytes 442376 | tf_op jit(solution)/shard_map/ppermute | solution.py:194
  79.4 18.4 %copy-start = (bf16[1,768,768]{1,2,0:T(8,128)(2,1)S(1)}, bf16[1,768,768]{1,2,0:T(8,128)(2,1)}, u32[]{:S(2)}) copy-start(bf16[1,768,768]{1,2,0:T(8,128)(2,1)} %all-gather.3.cloned.1.call-done) | copy-start | bytes 3538948
  79.4 18.4 %all-to-all-start = ((bf16[4,192,768]{2,1,0:T(8,128)(2,1)}), bf16[4,192,768]{2,1,0:T(8,128)(2,1)S(1)}, u32[]{:S(2)}, u32[]{:S(2)}) async-start(bf16[4,192,768]{2,1,0:T(8,128)(2,1)} %broadcast_in_dim.31), calls=%async_computation | async-start | bytes 2359296 | tf_op jit(solution)/shard_map/all_to_all | solution.py:201
  99.1 12.5 %collective-permute-start.12 = (bf16[192,768]{1,0:T(8,128)(2,1)}, bf16[192,768]{1,0:T(8,128)(2,1)S(1)}, u32[]{:S(2)}, u32[]{:S(2)}) collective-permute-start(bf16[192,768]{1,0:T(8,128)(2,1)} %convolution_convert_fusion), channel_id=1, source_target_pairs={{0,3},{1,0},{2,1},{3,2},{4,7},{5,4},{6,5},{7,6},{8,11},{9,8},{10,9... | collective-permute-start | bytes 884744 | tf_op jit(solution)/shard_map/ppermute | solution.py:214
  102.3 23.0 %collective-permute-start.11 = (bf16[192,768]{1,0:T(8,128)(2,1)}, bf16[192,768]{1,0:T(8,128)(2,1)S(1)}, u32[]{:S(2)}, u32[]{:S(2)}) collective-permute-start(bf16[192,768]{1,0:T(8,128)(2,1)} %convolution_convert_fusion.1), channel_id=1, source_target_pairs={{0,2},{1,3},{2,0},{3,1},{4,6},{5,7},{6,4},{7,5},{8,10},{9,11},{10,... | collective-permute-start | bytes 884744 | tf_op jit(solution)/shard_map/ppermute | solution.py:214
  109.7 22.2 %collective-permute-start.10 = (bf16[192,768]{1,0:T(8,128)(2,1)}, bf16[192,768]{1,0:T(8,128)(2,1)S(1)}, u32[]{:S(2)}, u32[]{:S(2)}) collective-permute-start(bf16[192,768]{1,0:T(8,128)(2,1)} %convolution_convert_fusion.2), channel_id=1, source_target_pairs={{0,1},{1,2},{2,3},{3,0},{4,5},{5,6},{6,7},{7,4},{8,9},{9,10},{10,1... | collective-permute-start | bytes 884744 | tf_op jit(solution)/shard_map/ppermute | solution.py:214
  132.5 21.0 %collective-permute-start.13 = (bf16[192,768]{1,0:T(8,128)(2,1)S(1)}, bf16[192,768]{1,0:T(8,128)(2,1)S(1)}, u32[]{:S(2)}, u32[]{:S(2)}) collective-permute-start(bf16[192,768]{1,0:T(8,128)(2,1)S(1)} %add_convert_fusion), channel_id=1, source_target_pairs={{0,128},{1,160},{2,192},{3,224},{32,129},{33,161},{34,193},{35,225... | collective-permute-start | bytes 884744 | tf_op jit(solution)/shard_map/ppermute | solution.py:222
Sparse Core Ops, SparseCore 0:
  9.4 58.0 all-gather.2

commit v20 on v19

--- a/solution.py
+++ b/solution.py
@@ -208,7 +208,8 @@
         )
 
     received = []
-    for shift in range(1, head_groups):
+    order = sorted(range(1, head_groups), key=lambda d: -min(d, head_groups - d))
+    for shift in order:
         outgoing = term_for((group_index + shift) % head_groups)
         route = [(g, (g + shift) % head_groups) for g in range(head_groups)]
         received.append(lax.ppermute(outgoing, "head", route))

time: 162 us -> 162 us (level)
  the two profiles are of different devices: /device:TPU:153 before, /device:TPU:6 now
where the time goes in v20:
time: 162 us; the launch traced here: 160 us
  waiting for transfers between devices  66.6 us (41%)
  starting transfers between devices  58.6 us (36%)
  between operations  15.8 us (10%)
  matrix products  7.39 us (5%)
  local copies, waits for them, and re-layouts  7.22 us (4%)
  other arithmetic  4.11 us (3%)
    ppermute x3, waiting for transfers between devices, on_device(): received.append(lax.ppermute(outgoing, 'head', route))  16.9 us
    ppermute x1, waiting for transfers between devices, on_device(): handed = lax.ppermute(updated, ('section', 'sx', 'head'), hand)  16.7 us
    ppermute x2, waiting for transfers between devices, on_device(): lax.ppermute((tile_k, tile_v), seq, [(i, i - 2) for i in range(2, seq_cou...  12.9 us
    all_to_all x1, waiting for transfers between devices, on_device(): token_parts = lax.all_to_all(spread, 'sx', 0, 0)  12.4 us
    ppermute x3, starting transfers between devices, on_device(): received.append(lax.ppermute(outgoing, 'head', route))  11.5 us
    ppermute x3, starting transfers between devices, on_device(): lax.ppermute((partner_half(queries), partner_half(own_keys), partner_half...  9.33 us
    ppermute x2, starting transfers between devices, on_device(): lax.ppermute((tile_k, tile_v), seq, [(i, i + 2) for i in range(seq_count...  7.81 us
    ppermute x2, starting transfers between devices, on_device(): lax.ppermute((tile_k, tile_v), seq, [(i, i - 2) for i in range(2, seq_cou...  7.76 us
  transfers between devices with their start and end apart: 16, of which 8 were waited for; matrix products, arithmetic and copies ran while one was open for 7% of the time, Pallas kernels for 0%

profile of v20, /device:TPU:6, one launch (start us, length us, event | category | flops | bytes accessed | tf_op | source)
XLA Modules:
  0.0 159.7 jit_solution(4401008224641691185)
XLA Ops:
  7.3 1.0 dynamic-slice_bitcast_fusion.2
  8.3 3.5 %collective-permute-start = (bf16[192,384]{1,0:T(8,128)(2,1)S(1)}, bf16[192,384]{1,0:T(8,128)(2,1)S(1)}, u32[]{:S(2)}, u32[]{:S(2)}) collective-permute-start(bf16[192,384]{1,0:T(8,128)(2,1)S(1)} %get-tuple-element.27), channel_id=1, source_target_pairs={{0,4},{4,0},{8,12},{12,8},{16,20},{20,16},{24,28},{28,24},{32,36},... | collective-permute-start | bytes 442376 | tf_op jit(solution)/shard_map/ppermute | solution.py:132
  11.8 1.0 constant_dynamic-slice_fusion.3
  12.8 2.4 %collective-permute-start.1 = (bf16[192,384]{1,0:T(8,128)(2,1)S(1)}, bf16[192,384]{1,0:T(8,128)(2,1)S(1)}, u32[]{:S(2)}, u32[]{:S(2)}) collective-permute-start(bf16[192,384]{1,0:T(8,128)(2,1)S(1)} %get-tuple-element.26), channel_id=1, source_target_pairs={{0,4},{4,0},{8,12},{12,8},{16,20},{20,16},{24,28},{28,24},{32,36},... | collective-permute-start | bytes 442376 | tf_op jit(solution)/shard_map/ppermute | solution.py:132
  15.3 3.5 %collective-permute-start.6 = (bf16[192,384]{1,0:T(8,128)(2,1)S(1)}, bf16[192,384]{1,0:T(8,128)(2,1)S(1)}, u32[]{:S(2)}, u32[]{:S(2)}) collective-permute-start(bf16[192,384]{1,0:T(8,128)(2,1)S(1)} %get-tuple-element.24), channel_id=1, source_target_pairs={{0,4},{4,0},{8,12},{12,8},{16,20},{20,16},{24,28},{28,24},{32,36},... | collective-permute-start | bytes 442376 | tf_op jit(solution)/shard_map/ppermute | solution.py:132
  22.0 0.8 maximum_select_fusion.4
  22.8 4.5 %collective-permute-start.2 = (bf16[384,384]{1,0:T(8,128)(2,1)}, bf16[384,384]{1,0:T(8,128)(2,1)}, u32[]{:S(2)}, u32[]{:S(2)}) collective-permute-start(bf16[384,384]{1,0:T(8,128)(2,1)} %maximum_select_fusion.4), channel_id=1, source_target_pairs={{0,8},{4,12},{8,16},{12,20},{16,24},{20,28},{24,32},{28,36},{32,40... | collective-permute-start | bytes 884744 | tf_op jit(solution)/shard_map/ppermute | solution.py:146
  27.3 4.4 %collective-permute-start.3 = (bf16[384,384]{1,0:T(8,128)(2,1)}, bf16[384,384]{1,0:T(8,128)(2,1)S(1)}, u32[]{:S(2)}, u32[]{:S(2)}) collective-permute-start(bf16[384,384]{1,0:T(8,128)(2,1)} %maximum_select_fusion.4), channel_id=1, source_target_pairs={{8,0},{12,4},{16,8},{20,12},{24,16},{28,20},{32,24},{36,28},{40,32... | collective-permute-start | bytes 884744 | tf_op jit(solution)/shard_map/ppermute | solution.py:147
  31.7 0.8 maximum_select_fusion.5
  32.5 3.4 %collective-permute-start.8 = (bf16[384,384]{1,0:T(8,128)(2,1)}, bf16[384,384]{1,0:T(8,128)(2,1)S(1)}, u32[]{:S(2)}, u32[]{:S(2)}) collective-permute-start(bf16[384,384]{1,0:T(8,128)(2,1)} %maximum_select_fusion.5), channel_id=1, source_target_pairs={{8,0},{12,4},{16,8},{20,12},{24,16},{28,20},{32,24},{36,28},{40,32... | collective-permute-start | bytes 884744 | tf_op jit(solution)/shard_map/ppermute | solution.py:147
  35.9 3.3 %collective-permute-start.7 = (bf16[384,384]{1,0:T(8,128)(2,1)}, bf16[384,384]{1,0:T(8,128)(2,1)S(1)}, u32[]{:S(2)}, u32[]{:S(2)}) collective-permute-start(bf16[384,384]{1,0:T(8,128)(2,1)} %maximum_select_fusion.5), channel_id=1, source_target_pairs={{0,8},{4,12},{8,16},{12,20},{16,24},{20,28},{24,32},{28,36},{32,40... | collective-permute-start | bytes 884744 | tf_op jit(solution)/shard_map/ppermute | solution.py:146
  40.0 6.1 %collective-permute-start.4 = (bf16[192,768]{1,0:T(8,128)(2,1)}, bf16[192,768]{1,0:T(8,128)(2,1)S(1)}, u32[]{:S(2)}, u32[]{:S(2)}) collective-permute-start(bf16[192,768]{1,0:T(8,128)(2,1)} %bitcast.68), channel_id=1, source_target_pairs={{0,0},{1,32},{2,64},{3,96},{32,1},{33,33},{34,65},{35,97},{64,2},{... | collective-permute-start | bytes 884744 | tf_op jit(solution)/shard_map/ppermute | solution.py:169
  47.1 3.7 %collective-permute-start.5 = (f32[768]{0:T(1024)S(1)}, f32[768]{0:T(1024)S(1)}, u32[]{:S(2)}, u32[]{:S(2)}) collective-permute-start(f32[768]{0:T(1024)S(1)} %reduce), channel_id=1, source_target_pairs={{0,0},{1,32},{2,64},{3,96},{32,1},{33,33},{34,65},{35,97},{64,2},{... | collective-permute-start | bytes 9224 | tf_op jit(solution)/shard_map/ppermute | solution.py:170
  50.8 1.2 copy.77
  52.7 12.9 %collective-permute-done.8 = bf16[384,384]{1,0:T(8,128)(2,1)S(1)} collective-permute-done((bf16[384,384]{1,0:T(8,128)(2,1)}, bf16[384,384]{1,0:T(8,128)(2,1)S(1)}, u32[]{:S(2)}, u32[]{:S(2)}) %collective-permute-start.8) | collective-permute-done | bytes 294944 | tf_op jit(solution)/shard_map/ppermute | solution.py:147
  66.1 2.7 %all-gather.3.cloned.1.call-done = bf16[1,768,768]{1,2,0:T(8,128)(2,1)} async-done(((bf16[1,768,96]{1,2,0:T(8,128)(2,1)}), bf16[1,768,768]{1,2,0:T(8,128)(2,1)}) %all-gather.3.cloned.1.call-update) | async-done | bytes 1179664 | tf_op jit(solution)/shard_map/all_gather | solution.py:166
  72.1 3.4 %collective-permute-start.9 = (bf16[192,384]{0,1:T(8,128)(2,1)S(1)}, bf16[192,384]{0,1:T(8,128)(2,1)S(1)}, u32[]{:S(2)}, u32[]{:S(2)}) collective-permute-start(bf16[192,384]{0,1:T(8,128)(2,1)S(1)} %get-tuple-element.22), channel_id=1, source_target_pairs={{0,4},{4,0},{8,12},{12,8},{16,20},{20,16},{24,28},{28,24},{32,36},... | collective-permute-start | bytes 442376 | tf_op jit(solution)/shard_map/ppermute | solution.py:194
  75.5 4.2 %collective-permute-done.9 = bf16[192,384]{0,1:T(8,128)(2,1)S(1)} collective-permute-done((bf16[192,384]{0,1:T(8,128)(2,1)S(1)}, bf16[192,384]{0,1:T(8,128)(2,1)S(1)}, u32[]{:S(2)}, u32[]{:S(2)}) %collective-permute-start.9) | collective-permute-done | bytes 147488 | tf_op jit(solution)/shard_map/ppermute | solution.py:194
  80.0 1.1 broadcast_in_dim.31
  81.1 4.8 %all-to-all-start = ((bf16[4,192,768]{2,1,0:T(8,128)(2,1)}), bf16[4,192,768]{2,1,0:T(8,128)(2,1)S(1)}, u32[]{:S(2)}, u32[]{:S(2)}) async-start(bf16[4,192,768]{2,1,0:T(8,128)(2,1)} %broadcast_in_dim.31), calls=%async_computation | async-start | bytes 2359296 | tf_op jit(solution)/shard_map/all_to_all | solution.py:201
  86.0 12.4 %all-to-all-done = bf16[4,192,768]{2,1,0:T(8,128)(2,1)S(1)} async-done(((bf16[4,192,768]{2,1,0:T(8,128)(2,1)}), bf16[4,192,768]{2,1,0:T(8,128)(2,1)S(1)}, u32[]{:S(2)}, u32[]{:S(2)}) %all-to-all-start) | async-done | bytes 1179680 | tf_op jit(solution)/shard_map/all_to_all | solution.py:201
  98.4 1.3 convolution_convert_fusion
  99.7 6.6 %collective-permute-start.12 = (bf16[192,768]{1,0:T(8,128)(2,1)}, bf16[192,768]{1,0:T(8,128)(2,1)S(1)}, u32[]{:S(2)}, u32[]{:S(2)}) collective-permute-start(bf16[192,768]{1,0:T(8,128)(2,1)} %convolution_convert_fusion), channel_id=1, source_target_pairs={{0,3},{1,0},{2,1},{3,2},{4,7},{5,4},{6,5},{7,6},{8,11},{9,8},{10,9... | collective-permute-start | bytes 884744 | tf_op jit(solution)/shard_map/ppermute | solution.py:215
  106.3 1.3 convolution_convert_fusion.1
  107.6 1.9 %collective-permute-start.11 = (bf16[192,768]{1,0:T(8,128)(2,1)}, bf16[192,768]{1,0:T(8,128)(2,1)S(1)}, u32[]{:S(2)}, u32[]{:S(2)}) collective-permute-start(bf16[192,768]{1,0:T(8,128)(2,1)} %convolution_convert_fusion.1), channel_id=1, source_target_pairs={{0,1},{1,2},{2,3},{3,0},{4,5},{5,6},{6,7},{7,4},{8,9},{9,10},{10,1... | collective-permute-start | bytes 884744 | tf_op jit(solution)/shard_map/ppermute | solution.py:215
  109.5 1.3 convolution_convert_fusion.2
  110.8 3.0 %collective-permute-start.10 = (bf16[192,768]{1,0:T(8,128)(2,1)}, bf16[192,768]{1,0:T(8,128)(2,1)S(1)}, u32[]{:S(2)}, u32[]{:S(2)}) collective-permute-start(bf16[192,768]{1,0:T(8,128)(2,1)} %convolution_convert_fusion.2), channel_id=1, source_target_pairs={{0,2},{1,3},{2,0},{3,1},{4,6},{5,7},{6,4},{7,5},{8,10},{9,11},{10,... | collective-permute-start | bytes 884744 | tf_op jit(solution)/shard_map/ppermute | solution.py:215
  114.0 7.4 %collective-permute-done.11 = bf16[192,768]{1,0:T(8,128)(2,1)S(1)} collective-permute-done((bf16[192,768]{1,0:T(8,128)(2,1)}, bf16[192,768]{1,0:T(8,128)(2,1)S(1)}, u32[]{:S(2)}, u32[]{:S(2)}) %collective-permute-start.11) | collective-permute-done | bytes 294944 | tf_op jit(solution)/shard_map/ppermute | solution.py:215
  121.3 9.4 %collective-permute-done.10 = bf16[192,768]{1,0:T(8,128)(2,1)S(1)} collective-permute-done((bf16[192,768]{1,0:T(8,128)(2,1)}, bf16[192,768]{1,0:T(8,128)(2,1)S(1)}, u32[]{:S(2)}, u32[]{:S(2)}) %collective-permute-start.10) | collective-permute-done | bytes 294944 | tf_op jit(solution)/shard_map/ppermute | solution.py:215
  131.3 4.1 %collective-permute-start.13 = (bf16[192,768]{1,0:T(8,128)(2,1)S(1)}, bf16[192,768]{1,0:T(8,128)(2,1)S(1)}, u32[]{:S(2)}, u32[]{:S(2)}) collective-permute-start(bf16[192,768]{1,0:T(8,128)(2,1)S(1)} %add_convert_fusion), channel_id=1, source_target_pairs={{0,128},{1,160},{2,192},{3,224},{32,129},{33,161},{34,193},{35,225... | collective-permute-start | bytes 884744 | tf_op jit(solution)/shard_map/ppermute | solution.py:223
  135.5 16.7 %collective-permute-done.13 = bf16[192,768]{1,0:T(8,128)(2,1)S(1)} collective-permute-done((bf16[192,768]{1,0:T(8,128)(2,1)S(1)}, bf16[192,768]{1,0:T(8,128)(2,1)S(1)}, u32[]{:S(2)}, u32[]{:S(2)}) %collective-permute-start.13) | collective-permute-done | bytes 294944 | tf_op jit(solution)/shard_map/ppermute | solution.py:223
  152.1 0.7 copy.118
  (54 shorter events, 9.2 us)
Async XLA Ops:
  6.5 8.7 %copy-start.1 = (bf16[1,192,768]{2,1,0:T(8,128)(2,1)S(1)}, bf16[1,192,768]{2,1,0:T(8,128)(2,1)}, u32[]{:S(2)}) copy-start(bf16[1,192,768]{2,1,0:T(8,128)(2,1)} %param.9) | copy-start | bytes 884740
  6.5 12.2 %copy-start.2 = (s32[16,27]{1,0:T(8,128)S(1)}, s32[16,27]{1,0:T(8,128)}, u32[]{:S(2)}) copy-start(s32[16,27]{1,0:T(8,128)} %param.13) | copy-start | bytes 5188
  6.5 62.2 %all-gather.3.cloned.1.call-start = ((), (), s32[]{:S(2)}) async-start(), calls=%async_computation.1 | async-start | bytes 1327104 | tf_op jit(solution)/shard_map/all_gather | solution.py:166
  8.3 13.6 %copy-start.3 = (f32[1,768]{1,0:T(1,128)S(1)}, f32[1,768]{1,0:T(1,128)}, u32[]{:S(2)}) copy-start(f32[1,768]{1,0:T(1,128)} %param.12) | copy-start | bytes 9220
  8.3 31.6 %collective-permute-start = (bf16[192,384]{1,0:T(8,128)(2,1)S(1)}, bf16[192,384]{1,0:T(8,128)(2,1)S(1)}, u32[]{:S(2)}, u32[]{:S(2)}) collective-permute-start(bf16[192,384]{1,0:T(8,128)(2,1)S(1)} %get-tuple-element.27), channel_id=1, source_target_pairs={{0,4},{4,0},{8,12},{12,8},{16,20},{20,16},{24,28},{28,24},{32,36},... | collective-permute-start | bytes 442376 | tf_op jit(solution)/shard_map/ppermute | solution.py:132
  12.8 9.1 %collective-permute-start.1 = (bf16[192,384]{1,0:T(8,128)(2,1)S(1)}, bf16[192,384]{1,0:T(8,128)(2,1)S(1)}, u32[]{:S(2)}, u32[]{:S(2)}) collective-permute-start(bf16[192,384]{1,0:T(8,128)(2,1)S(1)} %get-tuple-element.26), channel_id=1, source_target_pairs={{0,4},{4,0},{8,12},{12,8},{16,20},{20,16},{24,28},{28,24},{32,36},... | collective-permute-start | bytes 442376 | tf_op jit(solution)/shard_map/ppermute | solution.py:132
  15.3 16.4 %collective-permute-start.6 = (bf16[192,384]{1,0:T(8,128)(2,1)S(1)}, bf16[192,384]{1,0:T(8,128)(2,1)S(1)}, u32[]{:S(2)}, u32[]{:S(2)}) collective-permute-start(bf16[192,384]{1,0:T(8,128)(2,1)S(1)} %get-tuple-element.24), channel_id=1, source_target_pairs={{0,4},{4,0},{8,12},{12,8},{16,20},{20,16},{24,28},{28,24},{32,36},... | collective-permute-start | bytes 442376 | tf_op jit(solution)/shard_map/ppermute | solution.py:132
  22.8 24.3 %collective-permute-start.2 = (bf16[384,384]{1,0:T(8,128)(2,1)}, bf16[384,384]{1,0:T(8,128)(2,1)}, u32[]{:S(2)}, u32[]{:S(2)}) collective-permute-start(bf16[384,384]{1,0:T(8,128)(2,1)} %maximum_select_fusion.4), channel_id=1, source_target_pairs={{0,8},{4,12},{8,16},{12,20},{16,24},{20,28},{24,32},{28,36},{32,40... | collective-permute-start | bytes 884744 | tf_op jit(solution)/shard_map/ppermute | solution.py:146
  27.3 24.6 %collective-permute-start.3 = (bf16[384,384]{1,0:T(8,128)(2,1)}, bf16[384,384]{1,0:T(8,128)(2,1)S(1)}, u32[]{:S(2)}, u32[]{:S(2)}) collective-permute-start(bf16[384,384]{1,0:T(8,128)(2,1)} %maximum_select_fusion.4), channel_id=1, source_target_pairs={{8,0},{12,4},{16,8},{20,12},{24,16},{28,20},{32,24},{36,28},{40,32... | collective-permute-start | bytes 884744 | tf_op jit(solution)/shard_map/ppermute | solution.py:147
  32.5 33.1 %collective-permute-start.8 = (bf16[384,384]{1,0:T(8,128)(2,1)}, bf16[384,384]{1,0:T(8,128)(2,1)S(1)}, u32[]{:S(2)}, u32[]{:S(2)}) collective-permute-start(bf16[384,384]{1,0:T(8,128)(2,1)} %maximum_select_fusion.5), channel_id=1, source_target_pairs={{8,0},{12,4},{16,8},{20,12},{24,16},{28,20},{32,24},{36,28},{40,32... | collective-permute-start | bytes 884744 | tf_op jit(solution)/shard_map/ppermute | solution.py:147
  35.9 29.9 %collective-permute-start.7 = (bf16[384,384]{1,0:T(8,128)(2,1)}, bf16[384,384]{1,0:T(8,128)(2,1)S(1)}, u32[]{:S(2)}, u32[]{:S(2)}) collective-permute-start(bf16[384,384]{1,0:T(8,128)(2,1)} %maximum_select_fusion.5), channel_id=1, source_target_pairs={{0,8},{4,12},{8,16},{12,20},{16,24},{20,28},{24,32},{28,36},{32,40... | collective-permute-start | bytes 884744 | tf_op jit(solution)/shard_map/ppermute | solution.py:146
  40.0 26.1 %collective-permute-start.4 = (bf16[192,768]{1,0:T(8,128)(2,1)}, bf16[192,768]{1,0:T(8,128)(2,1)S(1)}, u32[]{:S(2)}, u32[]{:S(2)}) collective-permute-start(bf16[192,768]{1,0:T(8,128)(2,1)} %bitcast.68), channel_id=1, source_target_pairs={{0,0},{1,32},{2,64},{3,96},{32,1},{33,33},{34,65},{35,97},{64,2},{... | collective-permute-start | bytes 884744 | tf_op jit(solution)/shard_map/ppermute | solution.py:169
  47.1 19.0 %collective-permute-start.5 = (f32[768]{0:T(1024)S(1)}, f32[768]{0:T(1024)S(1)}, u32[]{:S(2)}, u32[]{:S(2)}) collective-permute-start(f32[768]{0:T(1024)S(1)} %reduce), channel_id=1, source_target_pairs={{0,0},{1,32},{2,64},{3,96},{32,1},{33,33},{34,65},{35,97},{64,2},{... | collective-permute-start | bytes 9224 | tf_op jit(solution)/shard_map/ppermute | solution.py:170
  72.1 7.7 %collective-permute-start.9 = (bf16[192,384]{0,1:T(8,128)(2,1)S(1)}, bf16[192,384]{0,1:T(8,128)(2,1)S(1)}, u32[]{:S(2)}, u32[]{:S(2)}) collective-permute-start(bf16[192,384]{0,1:T(8,128)(2,1)S(1)} %get-tuple-element.22), channel_id=1, source_target_pairs={{0,4},{4,0},{8,12},{12,8},{16,20},{20,16},{24,28},{28,24},{32,36},... | collective-permute-start | bytes 442376 | tf_op jit(solution)/shard_map/ppermute | solution.py:194
  81.1 17.3 %copy-start = (bf16[1,768,768]{1,2,0:T(8,128)(2,1)S(1)}, bf16[1,768,768]{1,2,0:T(8,128)(2,1)}, u32[]{:S(2)}) copy-start(bf16[1,768,768]{1,2,0:T(8,128)(2,1)} %all-gather.3.cloned.1.call-done) | copy-start | bytes 3538948
  81.1 17.3 %all-to-all-start = ((bf16[4,192,768]{2,1,0:T(8,128)(2,1)}), bf16[4,192,768]{2,1,0:T(8,128)(2,1)S(1)}, u32[]{:S(2)}, u32[]{:S(2)}) async-start(bf16[4,192,768]{2,1,0:T(8,128)(2,1)} %broadcast_in_dim.31), calls=%async_computation | async-start | bytes 2359296 | tf_op jit(solution)/shard_map/all_to_all | solution.py:201
  99.7 14.3 %collective-permute-start.12 = (bf16[192,768]{1,0:T(8,128)(2,1)}, bf16[192,768]{1,0:T(8,128)(2,1)S(1)}, u32[]{:S(2)}, u32[]{:S(2)}) collective-permute-start(bf16[192,768]{1,0:T(8,128)(2,1)} %convolution_convert_fusion), channel_id=1, source_target_pairs={{0,3},{1,0},{2,1},{3,2},{4,7},{5,4},{6,5},{7,6},{8,11},{9,8},{10,9... | collective-permute-start | bytes 884744 | tf_op jit(solution)/shard_map/ppermute | solution.py:215
  107.6 13.8 %collective-permute-start.11 = (bf16[192,768]{1,0:T(8,128)(2,1)}, bf16[192,768]{1,0:T(8,128)(2,1)S(1)}, u32[]{:S(2)}, u32[]{:S(2)}) collective-permute-start(bf16[192,768]{1,0:T(8,128)(2,1)} %convolution_convert_fusion.1), channel_id=1, source_target_pairs={{0,1},{1,2},{2,3},{3,0},{4,5},{5,6},{6,7},{7,4},{8,9},{9,10},{10,1... | collective-permute-start | bytes 884744 | tf_op jit(solution)/shard_map/ppermute | solution.py:215
  110.8 19.9 %collective-permute-start.10 = (bf16[192,768]{1,0:T(8,128)(2,1)}, bf16[192,768]{1,0:T(8,128)(2,1)S(1)}, u32[]{:S(2)}, u32[]{:S(2)}) collective-permute-start(bf16[192,768]{1,0:T(8,128)(2,1)} %convolution_convert_fusion.2), channel_id=1, source_target_pairs={{0,2},{1,3},{2,0},{3,1},{4,6},{5,7},{6,4},{7,5},{8,10},{9,11},{10,... | collective-permute-start | bytes 884744 | tf_op jit(solution)/shard_map/ppermute | solution.py:215
  131.3 20.8 %collective-permute-start.13 = (bf16[192,768]{1,0:T(8,128)(2,1)S(1)}, bf16[192,768]{1,0:T(8,128)(2,1)S(1)}, u32[]{:S(2)}, u32[]{:S(2)}) collective-permute-start(bf16[192,768]{1,0:T(8,128)(2,1)S(1)} %add_convert_fusion), channel_id=1, source_target_pairs={{0,128},{1,160},{2,192},{3,224},{32,129},{33,161},{34,193},{35,225... | collective-permute-start | bytes 884744 | tf_op jit(solution)/shard_map/ppermute | solution.py:223
Sparse Core Ops, SparseCore 0:
  9.4 59.2 all-gather.2
